TPU v7x, 256 devices: a whole 4x4x8 slice. The times are simulated.
256 devices in a mesh: dp: 8 (over z), seq: 32 (over x, y, core).
Axes of the slice: x: 4, y: 4, z: 8, core: 2. Of those that a mesh axis runs over, the one named last changes fastest.
Arguments:
- inputs: bfloat16 [8, 8192, 5120], P('dp', 'seq'), may hold values from -6 to 6
- gate_proj: bfloat16 [8, 8192, 5120], P('dp', 'seq'), may hold values from -6 to 6
- write_proj: bfloat16 [8, 8192, 128], P('dp', 'seq'), may hold values from -6 to 6
- read_proj: bfloat16 [8, 8192, 128], P('dp', 'seq'), may hold values from -6 to 6
- step_size: float32 [8, 80, 8192], P('dp', None, 'seq'), may hold values from 0 to 0.4, as said below
- log_forget: float32 [8, 80, 8192], P('dp', None, 'seq'), may hold values from -0.8 to 0, as said below
- conv_weight: float32 [4, 5376], replicated, may hold values from -3 to 3
- conv_bias: float32 [5376], replicated, may hold values from -3 to 3
- skip_gain: float32 [80], replicated, may hold values from 0.5 to 1.5
- norm_gain: float32 [5120], replicated, may hold values from 0.1 to 1.9
- code_weight: bfloat16 [5120, 256], P('dp'), may hold values from -0.5 to 0.5
- prior_draw: float32 [2048, 256], P(('dp', 'seq')), may hold values from -6 to 6
Outputs:
- mixed: bfloat16 [8, 8192, 5120], P('dp', 'seq')
- codes: float32 [2048, 256], P(('dp', 'seq'))
- kernel: float32 [2048, 4096], P(('dp', 'seq'))
Inputs may be any that keep to these rules, and one draw needn't show every extreme that they name: `step_size`: positive step sizes, per document, head and position. `log_forget`: never positive.
All inputs are finite; a program needn't handle non-finite values.
Results may differ from a plain program's by a relative error of at most 0.008.
Values may be sent and summed in bfloat16 or wider, within the bound.
No kernel may reach another device: no remote copies, remote signals or barrier semaphores. Data moves between devices by JAX's collectives and lax.ppermute only.
A program may use at most 256 MiB of HBM per device.

v0:
```python
import jax
import jax.numpy as jnp
from jax import lax
from jax.sharding import PartitionSpec as P

SPAN = 128
SEG = 32


def passed_along(block, axis, distance):
    devices = range(lax.axis_size(axis))
    route = [(i - distance, i) for i in devices if i - distance in devices]
    return lax.ppermute(block, axis, route)


def carried_in(part, axis, combine, identity):
    place = lax.axis_index(axis)
    gathered = jax.tree.map(lambda a: lax.all_gather(a, axis), part)
    state = jax.tree.map(lambda a, e: jnp.zeros_like(a) + jnp.asarray(e, a.dtype), part, identity)

    def one(step, state):
        return combine(
            state, jax.tree.map(lambda a: lax.dynamic_index_in_dim(a, step, 0, False), gathered)
        )

    return lax.fori_loop(0, place, one, state)


def block_terms(values, write_rows, read_rows, steps, logs):
    cum_log = jnp.cumsum(logs, axis=1)
    length = logs.shape[1]
    causal = jnp.arange(length)[:, None] >= jnp.arange(length)[None, :]
    scores = jnp.dot(read_rows, write_rows.T, preferred_element_type=jnp.float32)
    decay = jnp.exp(jnp.where(causal[None], cum_log[:, :, None] - cum_log[:, None, :], -jnp.inf))
    mixing = (scores[None] * decay * steps[:, None, :]).astype(jnp.bfloat16)
    inner_out = jnp.einsum("hts,shp->thp", mixing, values, preferred_element_type=jnp.float32)
    tail_decay = jnp.exp(cum_log[:, -1:] - cum_log) * steps
    weighted = (tail_decay[:, :, None] * write_rows.astype(jnp.float32)[None]).astype(jnp.bfloat16)
    states = jnp.einsum("hsn,shp->hpn", weighted, values, preferred_element_type=jnp.float32)
    return (inner_out, states, cum_log)


def join_states(first, second):
    return (first[0] + second[0], jnp.exp(second[0])[:, None, None] * first[1] + second[1])


def per_device(
    inputs,
    gate_proj,
    write_proj,
    read_proj,
    step_size,
    log_forget,
    conv_weight,
    conv_bias,
    skip_gain,
    norm_gain,
    code_weight,
    prior_draw,
):
    length = inputs.shape[1]
    width = inputs.shape[2]
    state_dim = write_proj.shape[2]
    heads = step_size.shape[1]
    head_dim = width // heads
    taps = conv_weight.shape[0]
    joined = jnp.concatenate([inputs[0], write_proj[0], read_proj[0]], axis=1)
    rim_rows = passed_along(joined[length - (taps - 1) :], "seq", 1)
    padded = jnp.concatenate([rim_rows, joined], axis=0)
    summed = conv_bias[None, :] + conv_weight[0][None, :] * padded[0:length].astype(jnp.float32)
    for offset in range(1, taps):
        summed = summed + conv_weight[offset][None, :] * padded[offset : offset + length].astype(
            jnp.float32
        )
    active = jax.nn.silu(summed).astype(jnp.bfloat16)
    values = active[:, :width].reshape(length, heads, head_dim)
    write_all = active[:, width : width + state_dim]
    read_all = active[:, width + state_dim :]
    steps = step_size[0]
    logs = log_forget[0]
    blocks = length // SPAN
    inner_list = []
    state_list = []
    cum_list = []
    for block in range(blocks):
        lower = block * SPAN
        upper = lower + SPAN
        inner_out, states, cum_log = block_terms(
            values[lower:upper],
            write_all[lower:upper],
            read_all[lower:upper],
            steps[:, lower:upper],
            logs[:, lower:upper],
        )
        inner_list.append(inner_out)
        state_list.append(states)
        cum_list.append(cum_log)
    running = jnp.zeros((heads, head_dim, state_dim), jnp.float32)
    before = jnp.zeros((heads,), jnp.float32)
    start_list = []
    before_list = []
    for block in range(blocks):
        start_list.append(running)
        before_list.append(before)
        block_total = cum_list[block][:, -1]
        running = jnp.exp(block_total)[:, None, None] * running + state_list[block]
        before = before + block_total
    identity = (jnp.zeros_like(before), jnp.zeros_like(running))
    decay_in, carry_in = carried_in((before, running), "seq", join_states, identity)
    outputs = []
    for block in range(blocks):
        lower = block * SPAN
        upper = lower + SPAN
        start = start_list[block] + jnp.exp(before_list[block])[:, None, None] * carry_in
        read_block = read_all[lower:upper].astype(jnp.float32)
        outer_out = jnp.exp(cum_list[block]).T[:, :, None] * jnp.einsum(
            "tn,hpn->thp", read_block, start, precision=lax.Precision.HIGHEST
        )
        outputs.append(inner_list[block] + outer_out)
    ssd_out = jnp.concatenate(outputs, axis=0)
    total = ssd_out + skip_gain[None, :, None] * values.astype(jnp.float32)
    gated = total.reshape(length, width) * jax.nn.silu(gate_proj[0].astype(jnp.float32))
    scale = lax.rsqrt(jnp.mean(gated * gated, axis=1, keepdims=True) + 1e-05)
    mixed = (gated * scale * norm_gain[None, :]).astype(jnp.bfloat16)
    pooled = jnp.mean(mixed.astype(jnp.float32).reshape(length // SEG, SEG, width), axis=1).astype(
        jnp.bfloat16
    )
    codes_local = jnp.dot(
        pooled,
        lax.all_gather(code_weight, "dp", axis=0, tiled=True),
        preferred_element_type=jnp.float32,
    )
    all_codes, all_prior = (
        lax.all_gather(codes_local, ("dp", "seq"), axis=0, tiled=True),
        lax.all_gather(prior_draw, ("dp", "seq"), axis=0, tiled=True),
    )
    columns = jnp.concatenate([all_codes, all_prior], axis=0)
    cross = jnp.dot(codes_local, columns.T, precision=lax.Precision.HIGHEST)
    row_sq = jnp.sum(codes_local * codes_local, axis=1)
    col_sq = jnp.sum(columns * columns, axis=1)
    dist_sq = row_sq[:, None] + col_sq[None, :] - 2.0 * cross
    code_dim = codes_local.shape[1]
    kernel = 2.0 * code_dim / (2.0 * code_dim + dist_sq)
    return (mixed[None], codes_local, kernel)


def solution(mesh):
    in_specs = (
        P("dp", "seq", None),
        P("dp", "seq", None),
        P("dp", "seq", None),
        P("dp", "seq", None),
        P("dp", None, "seq"),
        P("dp", None, "seq"),
        P(),
        P(),
        P(),
        P(),
        P("dp", None),
        P(("dp", "seq"), None),
    )
    out_specs = (P("dp", "seq", None), P(("dp", "seq"), None), P(("dp", "seq"), None))
    return jax.shard_map(
        per_device, mesh=mesh, in_specs=in_specs, out_specs=out_specs, check_vma=False
    )
```

profile of v0, /device:TPU:1, one launch (start us, length us, event | category | flops | bytes accessed | tf_op | source)
XLA Modules:
  0.0 618.8 jit_solution(9493338200007290373)
XLA Ops:
  7.2 0.0 all-gather.13.cloned.1.call-start
  7.2 0.0 copy-start.13
  7.2 0.0 copy-start.14
  7.2 0.0 copy-start.11
  7.2 0.0 copy-start.4
  7.3 0.0 copy-start.9
  7.3 0.0 copy-start.10
  7.3 2.1 pad_maximum_fusion
  9.5 4.6 collective-permute-start
  14.1 0.3 reduce_window_sum.17
  14.4 0.3 reduce_window_sum.18
  14.7 0.2 slice_reduce_fusion
  14.9 0.1 fusion.53
  15.0 0.2 slice_reduce_fusion.5
  15.3 0.0 copy-start.5
  15.3 0.0 copy-start.16
  15.3 0.0 collective-permute-done
  15.3 2.4 maximum_maximum_fusion
  17.7 4.4 multiply_convert_fusion
  22.2 2.0 fusion.52
  24.2 2.4 copy.31
  26.6 2.4 copy.32
  29.0 3.9 fusion.9
  33.0 0.0 copy-start.6
  33.0 1.5 copy-done.6
  34.4 4.0 multiply_add_fusion
  38.5 0.0 all-gather.13.cloned.1.call-update
  38.5 0.0 all-gather.7.cloned.1.call-start
  38.5 0.7 all-gather.7.cloned.1.call-update
  39.3 0.0 all-gather.9.cloned.1.call-start
  39.3 0.6 dynamic-slice
  40.6 0.3 dynamic-update-slice
  40.9 126.3 %all-reduce = f32[2560]{0:T(1024)S(1)} all-reduce(f32[2560]{0:T(1024)S(1)} %dynamic-update-slice), channel_id=2, replica_groups=mesh['dp'=8,'seq'=32] {'seq'}, use_global_device_ids=true, to_apply=%add | all-reduce | flops 2560 | bytes 20480
  167.2 0.1 reshape.99
  167.2 0.1 mul.251
  167.3 0.1 mul.252
  167.4 0.1 fusion.43
  167.5 4.5 fusion.7
  172.0 0.1 fusion.40
  172.2 4.1 fusion.8
  176.2 116.8 %all-gather.13.cloned.1.call-done = f32[2560,64,128]{2,1,0:T(8,128)} async-done(((f32[80,64,128]{2,1,0:T(8,128)}), f32[2560,64,128]{2,1,0:T(8,128)}) %all-gather.13.cloned.1.call-update) | async-done | bytes 83886096 | tf_op jit(solution)/shard_map/all_gather | solution.py:18
  293.0 0.3 broadcast.52
  293.4 2.4 while.12
  293.4 2.2 bitcast_add_fusion.4
  295.8 4.6 bitcast_add_fusion.2
  300.4 3.2 copy.37
  303.6 5.7 bitcast_add_fusion.1
  309.3 3.4 copy.38
  312.7 5.3 multiply_reduce_fusion
  318.1 2.3 copy-done
  320.3 1.0 convert_reduce_fusion
  321.3 11.0 %all-gather.7.cloned.1.call-done = bf16[5120,256]{1,0:T(8,128)(2,1)} async-done(((bf16[640,256]{1,0:T(8,128)(2,1)}), bf16[5120,256]{1,0:T(8,128)(2,1)}) %all-gather.7.cloned.1.call-update) | async-done | bytes 2621456 | tf_op jit(solution)/shard_map/all_gather | solution.py:130
  332.3 2.9 multiply_reduce_fusion.2
  335.2 0.0 all-gather.9.cloned.1.call-update
  335.3 0.0 all-gather.11.cloned.1.call-start
  335.3 0.5 all-gather.11.cloned.1.call-update
  335.8 4.7 fusion.50
  340.5 154.3 %all-gather.9.cloned.1.call-done = f32[2048,256]{1,0:T(8,128)} async-done(((f32[8,256]{1,0:T(8,128)}), f32[2048,256]{1,0:T(8,128)}) %all-gather.9.cloned.1.call-update) | async-done | bytes 2097168 | tf_op jit(solution)/shard_map/all_gather | solution.py:134
  494.8 3.1 constant_dynamic-update-slice_fusion.1
  497.9 103.6 %all-gather.11.cloned.1.call-done = f32[2048,256]{1,0:T(8,128)} async-done(((f32[8,256]{1,0:T(8,128)}), f32[2048,256]{1,0:T(8,128)}) %all-gather.11.cloned.1.call-update) | async-done | bytes 2097168 | tf_op jit(solution)/shard_map/all_gather | solution.py:135
  601.5 3.0 constant_dynamic-update-slice_fusion
  604.6 3.0 multiply_reduce_fusion.1
  607.5 0.5 copy-done.1
  608.0 4.2 fusion.6
  (35 shorter events, 0.1 us)
Async XLA Ops:
  7.2 285.9 %all-gather.13.cloned.1.call-start = ((), (), s32[]{:S(2)}) async-start(), calls=%async_computation.3 | async-start | bytes 86507520 | tf_op jit(solution)/shard_map/all_gather | solution.py:18
  7.2 6.8 %copy-start.13 = (f32[1,80,256]{2,1,0:T(8,128)S(1)}, f32[1,80,256]{2,1,0:T(8,128)}, u32[]{:S(2)}) copy-start(f32[1,80,256]{2,1,0:T(8,128)} %param.19) | copy-start | bytes 245764
  7.2 7.7 %copy-start.14 = (f32[1,80,256]{2,1,0:T(8,128)S(1)}, f32[1,80,256]{2,1,0:T(8,128)}, u32[]{:S(2)}) copy-start(f32[1,80,256]{2,1,0:T(8,128)} %param.18) | copy-start | bytes 245764
  7.2 7.8 %copy-start.11 = (f32[4,5376]{1,0:T(4,128)S(1)}, f32[4,5376]{1,0:T(4,128)}, u32[]{:S(2)}) copy-start(f32[4,5376]{1,0:T(4,128)} %param.20) | copy-start | bytes 258052
  7.2 8.1 %copy-start.4 = (bf16[1,256,5120]{2,1,0:T(8,128)(2,1)S(1)}, bf16[1,256,5120]{2,1,0:T(8,128)(2,1)}, u32[]{:S(2)}) copy-start(bf16[1,256,5120]{2,1,0:T(8,128)(2,1)} %param.14) | copy-start | bytes 7864324
  7.3 8.1 %copy-start.9 = (bf16[1,256,128]{2,1,0:T(8,128)(2,1)S(1)}, bf16[1,256,128]{2,1,0:T(8,128)(2,1)}, u32[]{:S(2)}) copy-start(bf16[1,256,128]{2,1,0:T(8,128)(2,1)} %param.17) | copy-start | bytes 196612
  7.3 8.1 %copy-start.10 = (bf16[1,256,128]{2,1,0:T(8,128)(2,1)S(1)}, bf16[1,256,128]{2,1,0:T(8,128)(2,1)}, u32[]{:S(2)}) copy-start(bf16[1,256,128]{2,1,0:T(8,128)(2,1)} %param.16) | copy-start | bytes 196612
  9.5 5.8 collective-permute-start
  15.3 2.4 copy-start.5
  15.3 2.4 copy-start.16
  22.2 149.9 %copy-start.2 = (bf16[256,5376]{1,0:T(8,128)(2,1)}, bf16[256,5376]{1,0:T(8,128)(2,1)S(1)}, u32[]{:S(2)}) copy-start(bf16[256,5376]{1,0:T(8,128)(2,1)S(1)} %multiply_convert_fusion) | copy-start | bytes 8257540
  29.0 5.4 copy-start.7
  33.0 1.5 copy-start.6
  38.5 0.9 copy-start.18
  38.5 128.8 %copy-start.17 = (f32[80]{0:T(128)S(1)}, f32[80]{0:T(128)}, u32[]{:S(2)}) copy-start(f32[80]{0:T(128)} %param.22) | copy-start | bytes 964
  38.5 293.8 %all-gather.7.cloned.1.call-start = ((), (), s32[]{:S(2)}) async-start(), calls=%async_computation | async-start | bytes 2949120 | tf_op jit(solution)/shard_map/all_gather | solution.py:130
  39.3 455.6 %all-gather.9.cloned.1.call-start = ((), (), s32[]{:S(2)}) async-start(), calls=%async_computation.1 | async-start | bytes 2105344 | tf_op jit(solution)/shard_map/all_gather | solution.py:134
  167.5 4.7 copy-start.8
  309.3 3.4 copy-start.3
  312.7 7.6 %copy-start.12 = (f32[5120]{0:T(1024)S(1)}, f32[5120]{0:T(1024)}, u32[]{:S(2)}) copy-start(f32[5120]{0:T(1024)} %param.23) | copy-start | bytes 61444
  318.0 2.3 copy-start
  335.3 266.3 %all-gather.11.cloned.1.call-start = ((), (), s32[]{:S(2)}) async-start(), calls=%async_computation.2 | async-start | bytes 2105344 | tf_op jit(solution)/shard_map/all_gather | solution.py:135
  604.6 3.4 copy-start.1
  604.6 3.4 copy-start.15
Sparse Core Ops, SparseCore 0:
  38.6 254.3 all-gather.12
  294.8 37.4 all-gather.6
  336.6 158.1 all-gather.8
  498.4 103.0 all-gather.10
where the time goes:
time: 620 us; the launch traced here: 619 us
  waiting for transfers between devices  387 us (62%)
  blocking collectives  126 us (20%)
  matrix products  34.3 us (6%)
  other arithmetic  26 us (4%)
  local copies, waits for them, and re-layouts  25.5 us (4%)
  between operations  14.8 us (2%)
    all_gather x1, waiting for transfers between devices, per_device(): lax.all_gather(codes_local, ('dp', 'seq'), axis=0, tiled=True)  154 us
    unnamed x1, blocking collectives  126 us
    all_gather x1, waiting for transfers between devices, carried_in(): gathered = jax.tree.map(lambda a: lax.all_gather(a, axis), part)  117 us
    all_gather x1, waiting for transfers between devices, per_device(): lax.all_gather(prior_draw, ('dp', 'seq'), axis=0, tiled=True)  104 us
  transfers between devices with their start and end apart: 5, of which 4 were waited for; matrix products, arithmetic and copies ran while one was open for 7% of the time, Pallas kernels for 0%

commit v1 on v0

--- a/solution.py
+++ b/solution.py
@@ -5,25 +5,15 @@
 
 SPAN = 128
 SEG = 32
+CORES = 2
+RING = 4
+XFER = jnp.bfloat16
 
 
 def passed_along(block, axis, distance):
     devices = range(lax.axis_size(axis))
     route = [(i - distance, i) for i in devices if i - distance in devices]
     return lax.ppermute(block, axis, route)
-
-
-def carried_in(part, axis, combine, identity):
-    place = lax.axis_index(axis)
-    gathered = jax.tree.map(lambda a: lax.all_gather(a, axis), part)
-    state = jax.tree.map(lambda a, e: jnp.zeros_like(a) + jnp.asarray(e, a.dtype), part, identity)
-
-    def one(step, state):
-        return combine(
-            state, jax.tree.map(lambda a: lax.dynamic_index_in_dim(a, step, 0, False), gathered)
-        )
-
-    return lax.fori_loop(0, place, one, state)
 
 
 def block_terms(values, write_rows, read_rows, steps, logs):
@@ -40,8 +30,88 @@
     return (inner_out, states, cum_log)
 
 
-def join_states(first, second):
-    return (first[0] + second[0], jnp.exp(second[0])[:, None, None] * first[1] + second[1])
+def chip_routes(seq):
+    rows = seq // (CORES * RING)
+
+    def at(x, y, c):
+        return (x * RING + y) * CORES + c
+
+    cells = [(x, y) for x in range(rows) for y in range(RING)]
+    up = [(at(x, y, 0), at(x, y, 1)) for x, y in cells]
+    down = [(b, a) for a, b in up]
+    y_fwd = [(at(x, y, 1), at(x, (y + 1) % RING, 1)) for x, y in cells]
+    y_bwd = [(at(x, y, 1), at(x, (y - 1) % RING, 1)) for x, y in cells]
+    x_fwd = [(at(x, y, 1), at((x + 1) % rows, y, 1)) for x, y in cells]
+    x_bwd = [(at(x, y, 1), at((x - 1) % rows, y, 1)) for x, y in cells]
+    return rows, up, down, (y_fwd, y_bwd), (x_fwd, x_bwd)
+
+
+def ring_of_four(state, logsum, fwd, bwd):
+    half = state.shape[0] // 2
+    sent = state.astype(XFER)
+    prev_state, prev_log = lax.ppermute((sent, logsum), "seq", fwd)
+    next_state, next_log = lax.ppermute((sent, logsum), "seq", bwd)
+    far_a, far_log = lax.ppermute((next_state[:half], next_log), "seq", bwd)
+    far_b = lax.ppermute(prev_state[half:], "seq", fwd)
+    far_state = jnp.concatenate([far_a, far_b], axis=0)
+    return [
+        (state, logsum, 0),
+        (prev_state, prev_log, RING - 1),
+        (next_state, next_log, 1),
+        (far_state, far_log, 2),
+    ]
+
+
+def fold_ring(slots, pos):
+    places = [(pos + k) % RING for (_, _, k) in slots]
+    logs = [l for (_, l, _) in slots]
+    zero = jnp.zeros_like(logs[0])
+    before = None
+    total = None
+    for i, (value, _, _) in enumerate(slots):
+        between = zero
+        after = zero
+        for j in range(len(slots)):
+            if j == i:
+                continue
+            inside = (places[i] < places[j]) & (places[j] < pos)
+            between = between + jnp.where(inside, logs[j], 0.0)
+            after = after + jnp.where(places[i] < places[j], logs[j], 0.0)
+        w_before = jnp.where(places[i] < pos, jnp.exp(between), 0.0)[:, None, None]
+        w_total = jnp.exp(after)[:, None, None]
+        v = value.astype(jnp.float32)
+        before = w_before * v if before is None else before + w_before * v
+        total = w_total * v if total is None else total + w_total * v
+    lead = zero
+    for j in range(len(slots)):
+        lead = lead + jnp.where(places[j] < pos, logs[j], 0.0)
+    total_log = sum(logs[1:], logs[0])
+    return before, jnp.exp(lead), total, total_log
+
+
+def carried_in(own_state, own_log):
+    seq = lax.axis_size("seq")
+    rows, up, down, y_routes, x_routes = chip_routes(seq)
+    assert rows == RING and seq == rows * RING * CORES
+    place = lax.axis_index("seq")
+    core = place % CORES
+    y_pos = (place // CORES) % RING
+    x_pos = place // (CORES * RING)
+    low_state, low_log = lax.ppermute((own_state, own_log), "seq", up)
+    chip_state = jnp.exp(own_log)[:, None, None] * low_state + own_state
+    chip_log = low_log + own_log
+    slots = ring_of_four(chip_state, chip_log, *y_routes)
+    row_before, row_lead, row_total, row_log = fold_ring(slots, y_pos)
+    slots = ring_of_four(row_total, row_log, *x_routes)
+    rows_before, _, _, _ = fold_ring(slots, x_pos)
+    chip_in = row_lead[:, None, None] * rows_before + row_before
+    chip_in_low = lax.ppermute(chip_in, "seq", down)
+    high_in = jnp.exp(low_log)[:, None, None] * chip_in + low_state
+    return jnp.where(core == 0, chip_in_low, high_in)
+
+
+def gathered_rows(block):
+    return lax.all_gather(lax.all_gather(block, "seq", axis=0, tiled=True), "dp", axis=0, tiled=True)
 
 
 def per_device(
@@ -64,6 +134,8 @@
     heads = step_size.shape[1]
     head_dim = width // heads
     taps = conv_weight.shape[0]
+    all_prior = gathered_rows(prior_draw)
+    full_code_weight = lax.all_gather(code_weight, "dp", axis=0, tiled=True)
     joined = jnp.concatenate([inputs[0], write_proj[0], read_proj[0]], axis=1)
     rim_rows = passed_along(joined[length - (taps - 1) :], "seq", 1)
     padded = jnp.concatenate([rim_rows, joined], axis=0)
@@ -105,8 +177,7 @@
         block_total = cum_list[block][:, -1]
         running = jnp.exp(block_total)[:, None, None] * running + state_list[block]
         before = before + block_total
-    identity = (jnp.zeros_like(before), jnp.zeros_like(running))
-    decay_in, carry_in = carried_in((before, running), "seq", join_states, identity)
+    carry_in = carried_in(running, before)
     outputs = []
     for block in range(blocks):
         lower = block * SPAN
@@ -125,15 +196,8 @@
     pooled = jnp.mean(mixed.astype(jnp.float32).reshape(length // SEG, SEG, width), axis=1).astype(
         jnp.bfloat16
     )
-    codes_local = jnp.dot(
-        pooled,
-        lax.all_gather(code_weight, "dp", axis=0, tiled=True),
-        preferred_element_type=jnp.float32,
-    )
-    all_codes, all_prior = (
-        lax.all_gather(codes_local, ("dp", "seq"), axis=0, tiled=True),
-        lax.all_gather(prior_draw, ("dp", "seq"), axis=0, tiled=True),
-    )
+    codes_local = jnp.dot(pooled, full_code_weight, preferred_element_type=jnp.float32)
+    all_codes = gathered_rows(codes_local)
     columns = jnp.concatenate([all_codes, all_prior], axis=0)
     cross = jnp.dot(codes_local, columns.T, precision=lax.Precision.HIGHEST)
     row_sq = jnp.sum(codes_local * codes_local, axis=1)

time: 620 us -> 311 us (0.50)
  waiting for transfers between devices: 387 us -> 73.7 us
  blocking collectives: 126 us -> 57.1 us
  starting transfers between devices: 4.74 us -> 57.5 us
  other arithmetic: 26 us -> 43.6 us
    all_gather x4 -> x3, waiting for transfers between devices: 386 us -> 40 us  [the longest x2 39.5 us: gathered_rows(): lax.all_gather(lax.all_gather(block, 'seq', axis=0, tiled=True), 'dp', ax...]
    unnamed x1 -> x0, blocking collectives: 126 us -> none
    all_gather x0 -> x2, blocking collectives: none -> 57.1 us  [gathered_rows(): lax.all_gather(block, 'seq', axis=0, tiled=True)]
    ppermute x0 -> x17, starting transfers between devices: none -> 52.8 us  [the longest x4 17.1 us: ring_of_four(): next_state, next_log = lax.ppermute((sent, logsum), 'seq', bwd)]
    ppermute x0 -> x17, waiting for transfers between devices: none -> 33.6 us  [the longest x4 15.9 us: ring_of_four(): next_state, next_log = lax.ppermute((sent, logsum), 'seq', bwd)]
  transfers between devices with their start and end apart: 5 -> 21, of which waited for: 4 -> 11; matrix products, arithmetic and copies ran while one was open for 7% -> 17% of each run, Pallas kernels for 0% -> 0%
where the time goes in v1:
time: 311 us; the launch traced here: 306 us
  waiting for transfers between devices  73.7 us (24%)
  starting transfers between devices  57.5 us (18%)
  blocking collectives  57.1 us (18%)
  other arithmetic  43.6 us (14%)
  matrix products  30.6 us (10%)
  local copies, waits for them, and re-layouts  29.2 us (9%)
  between operations  14.8 us (5%)
    all_gather x2, blocking collectives, gathered_rows(): lax.all_gather(block, 'seq', axis=0, tiled=True)  57.1 us
    all_gather x2, waiting for transfers between devices, gathered_rows(): lax.all_gather(lax.all_gather(block, 'seq', axis=0, tiled=True), 'dp', ax...  39.5 us
    ppermute x4, starting transfers between devices, ring_of_four(): next_state, next_log = lax.ppermute((sent, logsum), 'seq', bwd)  17.1 us
    ppermute x4, starting transfers between devices, ring_of_four(): far_a, far_log = lax.ppermute((next_state[:half], next_log), 'seq', bwd)  16.8 us
    ppermute x4, waiting for transfers between devices, ring_of_four(): next_state, next_log = lax.ppermute((sent, logsum), 'seq', bwd)  15.9 us
    dot_general x2, matrix products, per_device(): jnp.einsum('tn,hpn->thp', read_block, start, precision=lax.Precision.HIGH...  9.41 us
    dot_general x2, matrix products, block_terms(): jnp.einsum('hts,shp->thp', mixing, values, preferred_element_type=jnp.flo...  8.69 us
    unnamed x63, local copies, waits for them, and re-layouts  8.32 us
  transfers between devices with their start and end apart: 21, of which 11 were waited for; matrix products, arithmetic and copies ran while one was open for 17% of the time, Pallas kernels for 0%

profile of v1, /device:TPU:1, one launch (start us, length us, event | category | flops | bytes accessed | tf_op | source)
XLA Modules:
  0.0 306.4 jit_solution(16940590945961895119)
XLA Ops:
  7.3 2.1 pad_maximum_fusion
  9.5 4.6 %collective-permute-start = (bf16[3,5376]{1,0:T(4,128)(2,1)S(1)}, bf16[3,5376]{1,0:T(4,128)(2,1)S(1)}, u32[]{:S(2)}, u32[]{:S(2)}) collective-permute-start(bf16[3,5376]{1,0:T(4,128)(2,1)S(1)} %slice.120), channel_id=1, source_target_pairs={{0,1},{1,2},{2,3},{3,4},{4,5},{5,6},{6,7},{7,8},{8,9},{9,10},{10,1... | collective-permute-start | bytes 96776 | tf_op jit(solution)/shard_map/ppermute | solution.py:16
  16.3 2.4 maximum_maximum_fusion
  18.7 4.4 %multiply_convert_fusion = bf16[256,5376]{1,0:T(8,128)(2,1)S(1)} fusion(bf16[259,5376]{1,0:T(8,128)(2,1)S(1)} %maximum_maximum_fusion, f32[5376]{0:T(1024)S(1)} %get-tuple-element.5, f32[5376]{0:T(1024)S(1)} %get-tuple-element.6, f32[5376]{0:T(1024)S(1)} %get-tuple-element.4, f32[5376]{0:T(1024)S(1)} %get-tuple-element.3, f32[5376]{0:T(1024)S(1)} %copy-done.23, ...), kind=kLoop, calls=%fused_computation.2 | loop fusion | flops 30277632 | bytes 13870080 | tf_op jit(solution)/shard_map/convert_element_type | solution.py:147
  23.2 1.8 fusion.94
  25.0 2.4 copy.23
  27.4 2.4 copy.24
  29.9 3.9 %fusion.16 = f32[80,64,128]{2,1,0:T(8,128)S(1)} fusion(bf16[128,80,64]{0,2,1:T(8,128)(2,1)} %bitcast.45, f32[128,128]{1,0:T(8,128)S(1)} %get-tuple-element.14, f32[80,128]{1,0:T(8,128)S(1)} %get-tuple-element.18), kind=kOutput, calls=%fused_computation.37 | convolution fusion | flops 170393600 | bytes 4038656 | tf_op jit(solution)/shard_map/hsn,shp->hpn/dot_general | solution.py:29
  33.8 1.8 multiply_add_fusion.1
  35.6 1.3 collective-permute-start.8
  36.9 5.5 %collective-permute-done.8 = f32[80,64,128]{2,1,0:T(8,128)S(1)} collective-permute-done((f32[80,64,128]{2,1,0:T(8,128)S(1)}, f32[80,64,128]{2,1,0:T(8,128)S(1)}, u32[]{:S(2)}, u32[]{:S(2)}) %collective-permute-start.8) | collective-permute-done | bytes 2621472 | tf_op jit(solution)/shard_map/ppermute | solution.py:100
  42.4 2.6 fusion.92
  45.1 4.2 %collective-permute-start.10 = (bf16[80,64,128]{2,1,0:T(8,128)(2,1)}, bf16[80,64,128]{2,1,0:T(8,128)(2,1)}, u32[]{:S(2)}, u32[]{:S(2)}) collective-permute-start(bf16[80,64,128]{2,1,0:T(8,128)(2,1)} %get-tuple-element.9), channel_id=1, source_target_pairs={{1,7},{3,1},{5,3},{7,5},{9,15},{11,9},{13,11},{15,13},{17,23},{19,... | collective-permute-start | bytes 3932168 | tf_op jit(solution)/shard_map/ppermute | solution.py:53
  49.4 1.9 collective-permute-start.9
  51.3 1.3 collective-permute-start.1
  52.7 1.6 collective-permute-done.1
  54.9 4.6 %collective-permute-start.3 = (f32[80]{0:T(128)S(1)}, f32[80]{0:T(128)S(1)}, u32[]{:S(2)}, u32[]{:S(2)}) collective-permute-start(f32[80]{0:T(128)S(1)} %get-tuple-element.45), channel_id=1, source_target_pairs={{1,7},{3,1},{5,3},{7,5},{9,15},{11,9},{13,11},{15,13},{17,23},{19,... | collective-permute-start | bytes 968 | tf_op jit(solution)/shard_map/ppermute | solution.py:53
  59.5 2.2 collective-permute-start.2
  61.7 2.5 collective-permute-done.3
  64.2 5.0 %collective-permute-start.4 = (f32[80]{0:T(128)S(1)}, f32[80]{0:T(128)S(1)}, u32[]{:S(2)}, u32[]{:S(2)}) collective-permute-start(f32[80]{0:T(128)S(1)} %collective-permute-done.3), channel_id=1, source_target_pairs={{1,7},{3,1},{5,3},{7,5},{9,15},{11,9},{13,11},{15,13},{17,23},{19,... | collective-permute-start | bytes 968 | tf_op jit(solution)/shard_map/ppermute | solution.py:54
  69.2 1.1 slice.135
  70.4 1.9 collective-permute-start.11
  72.3 1.1 slice.136
  73.4 3.4 %collective-permute-start.12 = (bf16[40,64,128]{2,1,0:T(8,128)(2,1)S(1)}, bf16[40,64,128]{2,1,0:T(8,128)(2,1)S(1)}, u32[]{:S(2)}, u32[]{:S(2)}) collective-permute-start(bf16[40,64,128]{2,1,0:T(8,128)(2,1)S(1)} %slice.136), channel_id=1, source_target_pairs={{1,3},{3,5},{5,7},{7,1},{9,11},{11,13},{13,15},{15,9},{17,19},{19,... | collective-permute-start | bytes 1966088 | tf_op jit(solution)/shard_map/ppermute | solution.py:55
  77.5 1.3 fusion.86
  78.8 2.9 collective-permute-done.11
  81.7 4.3 %collective-permute-done.12 = bf16[40,64,128]{2,1,0:T(8,128)(2,1)S(1)} collective-permute-done((bf16[40,64,128]{2,1,0:T(8,128)(2,1)S(1)}, bf16[40,64,128]{2,1,0:T(8,128)(2,1)S(1)}, u32[]{:S(2)}, u32[]{:S(2)}) %collective-permute-start.12) | collective-permute-done | bytes 655392 | tf_op jit(solution)/shard_map/ppermute | solution.py:55
  86.0 3.3 %fusion.25 = bf16[80,64,128]{2,1,0:T(8,128)(2,1)S(1)} fusion(bf16[80,64,128]{2,1,0:T(8,128)(2,1)} %collective-permute-done.10, bf16[80,64,128]{2,1,0:T(8,128)(2,1)} %collective-permute-done.9, f32[80,64,128]{2,1,0:T(8,128)S(1)} %copy-done.2, f32[80]{0:T(128)S(1)} %get-tuple-element.27, f32[80]{0:T(128)S(1)} %fusion.83, f32[80]{0:T(128)S(1)} %get-tuple-element.37, ...), kind=kLoop, calls=%fused_computation.49 | loop fusion | flops 7864320 | bytes 7865600 | tf_op jit(solution)/shard_map/convert_element_type | solution.py:51
  89.3 3.8 %collective-permute-start.14 = (bf16[80,64,128]{2,1,0:T(8,128)(2,1)S(1)}, bf16[80,64,128]{2,1,0:T(8,128)(2,1)S(1)}, u32[]{:S(2)}, u32[]{:S(2)}) collective-permute-start(bf16[80,64,128]{2,1,0:T(8,128)(2,1)S(1)} %fusion.25), channel_id=1, source_target_pairs={{1,25},{3,27},{5,29},{7,31},{9,1},{11,3},{13,5},{15,7},{17,9},{19,... | collective-permute-start | bytes 3932168 | tf_op jit(solution)/shard_map/ppermute | solution.py:53
  93.1 1.9 collective-permute-start.13
  95.0 12.6 %collective-permute-done.14 = bf16[80,64,128]{2,1,0:T(8,128)(2,1)S(1)} collective-permute-done((bf16[80,64,128]{2,1,0:T(8,128)(2,1)S(1)}, bf16[80,64,128]{2,1,0:T(8,128)(2,1)S(1)}, u32[]{:S(2)}, u32[]{:S(2)}) %collective-permute-start.14) | collective-permute-done | bytes 1310752 | tf_op jit(solution)/shard_map/ppermute | solution.py:53
  107.7 1.0 copy-done.11
  108.7 0.9 slice.137
  109.6 5.0 %collective-permute-start.15 = (bf16[40,64,128]{2,1,0:T(8,128)(2,1)}, bf16[40,64,128]{2,1,0:T(8,128)(2,1)}, u32[]{:S(2)}, u32[]{:S(2)}) collective-permute-start(bf16[40,64,128]{2,1,0:T(8,128)(2,1)} %slice.137), channel_id=1, source_target_pairs={{1,25},{3,27},{5,29},{7,31},{9,1},{11,3},{13,5},{15,7},{17,9},{19,... | collective-permute-start | bytes 1966088 | tf_op jit(solution)/shard_map/ppermute | solution.py:54
  114.6 1.1 copy-done.12
  115.7 0.9 slice.138
  116.6 1.9 collective-permute-start.16
  118.6 4.6 %collective-permute-start.6 = (f32[80]{0:T(128)S(1)}, f32[80]{0:T(128)}, u32[]{:S(2)}, u32[]{:S(2)}) collective-permute-start(f32[80]{0:T(128)S(1)} %get-tuple-element.26), channel_id=1, source_target_pairs={{1,25},{3,27},{5,29},{7,31},{9,1},{11,3},{13,5},{15,7},{17,9},{19,... | collective-permute-start | bytes 968 | tf_op jit(solution)/shard_map/ppermute | solution.py:53
  123.2 0.7 collective-permute-done.6
  123.9 4.9 %collective-permute-start.7 = (f32[80]{0:T(128)}, f32[80]{0:T(128)}, u32[]{:S(2)}, u32[]{:S(2)}) collective-permute-start(f32[80]{0:T(128)} %collective-permute-done.6), channel_id=1, source_target_pairs={{1,25},{3,27},{5,29},{7,31},{9,1},{11,3},{13,5},{15,7},{17,9},{19,... | collective-permute-start | bytes 968 | tf_op jit(solution)/shard_map/ppermute | solution.py:54
  128.8 2.1 collective-permute-start.5
  131.0 3.4 %collective-permute-done.5 = f32[80]{0:T(128)S(1)} collective-permute-done((f32[80]{0:T(128)S(1)}, f32[80]{0:T(128)S(1)}, u32[]{:S(2)}, u32[]{:S(2)}) %collective-permute-start.5) | collective-permute-done | bytes 352 | tf_op jit(solution)/shard_map/ppermute | solution.py:52
  135.1 7.6 %fusion.15 = f32[80,64,128]{2,1,0:T(8,128)} fusion(bf16[80,64,128]{2,1,0:T(8,128)(2,1)} %collective-permute-done.9, bf16[80,64,128]{2,1,0:T(8,128)(2,1)} %collective-permute-done.10, f32[80,64,128]{2,1,0:T(8,128)} %get-tuple-element.10, bf16[80,64,128]{2,1,0:T(8,128)(2,1)} %copy-done.11, bf16[80,64,128]{2,1,0:T(8,128)(2,1)} %copy-done.12, ...), kind=kLoop, calls=%fused_computation.36 | loop fusion | flops 20316160 | bytes 13111360 | tf_op jit(solution)/shard_map/add | solution.py:107
  142.7 2.9 collective-permute-start.17
  146.1 4.6 %fusion.7 = f32[80,64,128]{2,1,0:T(8,128)S(1)} fusion(bf16[128,80,64]{0,2,1:T(8,128)(2,1)} %bitcast.46, f32[80,128]{1,0:T(8,128)} %get-tuple-element.17, f32[80,128]{1,0:T(8,128)S(1)} %reduce_window_sum.17, f32[128,128]{1,0:T(8,128)S(1)} %fusion.51, pred[128,128]{1,0:T(8,128)(4,1)S(1)} %iota_compare_fusion), kind=kOutput, calls=%fused_computation.28 | convolution fusion | flops 174325760 | bytes 4096000 | tf_op jit(solution)/shard_map/hts,shp->thp/dot_general | solution.py:26
  150.8 4.1 %fusion.8 = f32[80,64,128]{2,1,0:T(8,128)} fusion(bf16[128,80,64]{0,2,1:T(8,128)(2,1)S(1)} %bitcast.48, f32[80,128]{1,0:T(8,128)S(1)} %copy-done.22, f32[80,128]{1,0:T(8,128)S(1)} %reduce_window_sum.18, f32[128,128]{1,0:T(8,128)S(1)} %fusion.48, pred[128,128]{1,0:T(8,128)(4,1)S(1)} %iota_compare_fusion), kind=kOutput, calls=%fused_computation.29 | convolution fusion | flops 174325760 | bytes 4096000 | tf_op jit(solution)/shard_map/hts,shp->thp/dot_general | solution.py:26
  154.9 2.3 add_select_fusion
  157.2 3.0 bitcast_add_fusion.1
  160.2 3.2 %copy.29 = f32[128,5120]{1,0:T(8,128)} copy(f32[128,5120]{0,1:T(8,128)} %bitcast.43) | data formatting | bytes 5242880 | tf_op jit(solution)/shard_map/concatenate | solution.py:191
  163.4 6.5 %bitcast_add_fusion = f32[128,80,64]{0,2,1:T(8,128)} fusion(f32[80,64,128]{2,1,0:T(8,128)} %fusion.8, f32[80,64,128]{2,1,0:T(8,128)} %copy-done.6, f32[80,64,128]{2,1,0:T(8,128)} %copy-done.5, f32[80]{0:T(128)S(1)} %copy-done.27, f32[128,80]{0,1:T(8,128)S(1)} %get-tuple-element.23, f32[80]{0:T(128)S(1)} %get-tuple-element.40, ...), kind=kOutput, calls=%fused_computation.39 | convolution fusion | flops 1009909760 | bytes 10560512 | tf_op jit(solution)/shard_map/tn,hpn->thp/dot_general | solution.py:187
  169.9 3.2 %copy.30 = f32[128,5120]{1,0:T(8,128)} copy(f32[128,5120]{0,1:T(8,128)} %bitcast.44) | data formatting | bytes 5242880 | tf_op jit(solution)/shard_map/concatenate | solution.py:191
  173.1 5.3 %multiply_reduce_fusion = (f32[256]{0:T(256)S(1)}, f32[256,5120]{1,0:T(8,128)S(1)}) fusion(bf16[1,256,5120]{2,1,0:T(8,128)(2,1)} %param.13, bf16[256,5376]{1,0:T(8,128)(2,1)S(1)} %multiply_convert_fusion, f32[5120]{0:T(1024)S(1)} %mul.390, f32[128,5120]{1,0:T(8,128)} %copy.30, f32[128,5120]{1,0:T(8,128)} %copy.29), kind=kLoop, calls=%fused_computation.10 | loop fusion | flops 15728384 | bytes 15750144 | tf_op jit(solution)/shard_map/reduce_sum | solution.py:194
  178.4 2.3 copy-done
  180.7 1.0 convert_reduce_fusion
  182.3 2.3 multiply_reduce_fusion.2
  184.6 30.7 %all_gather.16 = f32[256,256]{1,0:T(8,128)} all-gather(f32[8,256]{1,0:T(8,128)S(1)} %get-tuple-element.47), channel_id=1, replica_groups=mesh['dp'=8,'seq'=32] {'seq'}, dimensions={0}, use_global_device_ids=true | all-gather | bytes 270336 | tf_op jit(solution)/shard_map/all_gather | solution.py:114
  215.4 26.4 %all_gather.18 = f32[256,256]{1,0:T(8,128)} all-gather(f32[8,256]{1,0:T(8,128)S(1)} %copy-done.24), channel_id=1, replica_groups=mesh['dp'=8,'seq'=32] {'seq'}, dimensions={0}, use_global_device_ids=true | all-gather | bytes 270336 | tf_op jit(solution)/shard_map/all_gather | solution.py:114
  241.8 4.7 %fusion.90 = bf16[1,256,5120]{2,1,0:T(8,128)(2,1)} fusion(f32[5120]{0:T(1024)S(1)} %copy-done.18, f32[256,5120]{1,0:T(8,128)} %copy-done, f32[256]{0:T(256)S(1)} %add_rsqrt_fusion), kind=kLoop, calls=%fused_computation.183 | loop fusion | flops 3932160 | bytes 7885824 | tf_op jit(solution)/shard_map/broadcast_in_dim | solution.py:208
  246.6 1.3 all-gather.6.cloned.1.call-done
  247.9 3.1 %constant_dynamic-update-slice_fusion.1 = f32[4096,256]{1,0:T(8,128)} fusion(f32[2048,256]{1,0:T(8,128)} %all-gather.6.cloned.1.call-done), kind=kLoop, calls=%fused_computation.96 | loop fusion | bytes 4194304
  250.9 38.2 %all-gather.8.cloned.1.call-done = f32[2048,256]{1,0:T(8,128)} async-done(((f32[256,256]{1,0:T(8,128)}), f32[2048,256]{1,0:T(8,128)}) %all-gather.8.cloned.1.call-update) | async-done | bytes 2097168 | tf_op jit(solution)/shard_map/all_gather | solution.py:114
  289.1 3.0 constant_dynamic-update-slice_fusion
  292.2 3.0 multiply_reduce_fusion.1
  295.6 4.2 %fusion.6 = f32[8,4096]{1,0:T(8,128)} fusion(f32[8,256]{1,0:T(8,128)S(1)} %get-tuple-element.47, f32[4096,256]{1,0:T(8,128)S(1)} %copy-done.1, f32[4096]{0:T(1024)S(1)} %multiply_reduce_fusion.1, f32[8]{0:T(128)S(1)} %get-tuple-element.46), kind=kOutput, calls=%fused_computation.18 | convolution fusion | flops 100827136 | bytes 4349984 | tf_op jit(solution)/shard_map/dot_general | solution.py:202
  (96 shorter events, 6.1 us)
Async XLA Ops:
  7.2 175.1 %all-gather.4.cloned.1.call-start = ((), (), s32[]{:S(2)}) async-start(), calls=%async_computation | async-start | bytes 2949120 | tf_op jit(solution)/shard_map/all_gather | solution.py:138
  7.2 6.8 %copy-start.19 = (f32[1,80,256]{2,1,0:T(8,128)S(1)}, f32[1,80,256]{2,1,0:T(8,128)}, u32[]{:S(2)}) copy-start(f32[1,80,256]{2,1,0:T(8,128)} %param.17) | copy-start | bytes 245764
  7.2 8.2 %copy-start.20 = (f32[1,80,256]{2,1,0:T(8,128)S(1)}, f32[1,80,256]{2,1,0:T(8,128)}, u32[]{:S(2)}) copy-start(f32[1,80,256]{2,1,0:T(8,128)} %param.16) | copy-start | bytes 245764
  7.2 8.8 %copy-start.17 = (f32[4,5376]{1,0:T(4,128)S(1)}, f32[4,5376]{1,0:T(4,128)}, u32[]{:S(2)}) copy-start(f32[4,5376]{1,0:T(4,128)} %param.18) | copy-start | bytes 258052
  7.2 9.1 %copy-start.3 = (bf16[1,256,5120]{2,1,0:T(8,128)(2,1)S(1)}, bf16[1,256,5120]{2,1,0:T(8,128)(2,1)}, u32[]{:S(2)}) copy-start(bf16[1,256,5120]{2,1,0:T(8,128)(2,1)} %param.12) | copy-start | bytes 7864324
  7.3 9.1 %copy-start.14 = (bf16[1,256,128]{2,1,0:T(8,128)(2,1)S(1)}, bf16[1,256,128]{2,1,0:T(8,128)(2,1)}, u32[]{:S(2)}) copy-start(bf16[1,256,128]{2,1,0:T(8,128)(2,1)} %param.15) | copy-start | bytes 196612
  7.3 9.1 %copy-start.15 = (bf16[1,256,128]{2,1,0:T(8,128)(2,1)S(1)}, bf16[1,256,128]{2,1,0:T(8,128)(2,1)}, u32[]{:S(2)}) copy-start(bf16[1,256,128]{2,1,0:T(8,128)(2,1)} %param.14) | copy-start | bytes 196612
  9.5 6.8 %collective-permute-start = (bf16[3,5376]{1,0:T(4,128)(2,1)S(1)}, bf16[3,5376]{1,0:T(4,128)(2,1)S(1)}, u32[]{:S(2)}, u32[]{:S(2)}) collective-permute-start(bf16[3,5376]{1,0:T(4,128)(2,1)S(1)} %slice.120), channel_id=1, source_target_pairs={{0,1},{1,2},{2,3},{3,4},{4,5},{5,6},{6,7},{7,8},{8,9},{9,10},{10,1... | collective-permute-start | bytes 96776 | tf_op jit(solution)/shard_map/ppermute | solution.py:16
  16.3 2.4 copy-start.4
  16.3 2.4 copy-start.23
  29.9 3.9 %copy-start.9 = (bf16[128,5120]{0,1:T(8,128)(2,1)S(1)}, bf16[128,5120]{0,1:T(8,128)(2,1)}, u32[]{:S(2)}) copy-start(bf16[128,5120]{0,1:T(8,128)(2,1)} %copy.24) | copy-start | bytes 3932164
  33.8 1.8 copy-start.5
  35.6 6.8 %collective-permute-start.8 = (f32[80,64,128]{2,1,0:T(8,128)S(1)}, f32[80,64,128]{2,1,0:T(8,128)S(1)}, u32[]{:S(2)}, u32[]{:S(2)}) collective-permute-start(f32[80,64,128]{2,1,0:T(8,128)S(1)} %multiply_add_fusion.1), channel_id=1, source_target_pairs={{0,1},{2,3},{4,5},{6,7},{8,9},{10,11},{12,13},{14,15},{16,17},{18,... | collective-permute-start | bytes 7864328 | tf_op jit(solution)/shard_map/ppermute | solution.py:100
  42.4 2.8 copy-start.7
  45.1 24.1 %collective-permute-start.10 = (bf16[80,64,128]{2,1,0:T(8,128)(2,1)}, bf16[80,64,128]{2,1,0:T(8,128)(2,1)}, u32[]{:S(2)}, u32[]{:S(2)}) collective-permute-start(bf16[80,64,128]{2,1,0:T(8,128)(2,1)} %get-tuple-element.9), channel_id=1, source_target_pairs={{1,7},{3,1},{5,3},{7,5},{9,15},{11,9},{13,11},{15,13},{17,23},{19,... | collective-permute-start | bytes 3932168 | tf_op jit(solution)/shard_map/ppermute | solution.py:53
  49.4 22.9 %collective-permute-start.9 = (bf16[80,64,128]{2,1,0:T(8,128)(2,1)}, bf16[80,64,128]{2,1,0:T(8,128)(2,1)}, u32[]{:S(2)}, u32[]{:S(2)}) collective-permute-start(bf16[80,64,128]{2,1,0:T(8,128)(2,1)} %get-tuple-element.9), channel_id=1, source_target_pairs={{1,3},{3,5},{5,7},{7,1},{9,11},{11,13},{13,15},{15,9},{17,19},{19,... | collective-permute-start | bytes 3932168 | tf_op jit(solution)/shard_map/ppermute | solution.py:52
  51.3 3.1 collective-permute-start.1
  54.9 9.3 %collective-permute-start.3 = (f32[80]{0:T(128)S(1)}, f32[80]{0:T(128)S(1)}, u32[]{:S(2)}, u32[]{:S(2)}) collective-permute-start(f32[80]{0:T(128)S(1)} %get-tuple-element.45), channel_id=1, source_target_pairs={{1,7},{3,1},{5,3},{7,5},{9,15},{11,9},{13,11},{15,13},{17,23},{19,... | collective-permute-start | bytes 968 | tf_op jit(solution)/shard_map/ppermute | solution.py:53
  59.5 26.5 %copy-start.2 = (f32[80,64,128]{2,1,0:T(8,128)S(1)}, f32[80,64,128]{2,1,0:T(8,128)}, u32[]{:S(2)}) copy-start(f32[80,64,128]{2,1,0:T(8,128)} %get-tuple-element.10) | copy-start | bytes 7864324
  59.5 17.3 %collective-permute-start.2 = (f32[80]{0:T(128)S(1)}, f32[80]{0:T(128)S(1)}, u32[]{:S(2)}, u32[]{:S(2)}) collective-permute-start(f32[80]{0:T(128)S(1)} %get-tuple-element.45), channel_id=1, source_target_pairs={{1,3},{3,5},{5,7},{7,1},{9,11},{11,13},{13,15},{15,9},{17,19},{19,... | collective-permute-start | bytes 968 | tf_op jit(solution)/shard_map/ppermute | solution.py:52
  64.2 12.7 %copy-start.29 = (f32[80]{0:T(128)}, f32[80]{0:T(128)S(1)}, u32[]{:S(2)}) copy-start(f32[80]{0:T(128)S(1)} %collective-permute-done.3) | copy-start | bytes 964
  64.2 12.6 %collective-permute-start.4 = (f32[80]{0:T(128)S(1)}, f32[80]{0:T(128)S(1)}, u32[]{:S(2)}, u32[]{:S(2)}) collective-permute-start(f32[80]{0:T(128)S(1)} %collective-permute-done.3), channel_id=1, source_target_pairs={{1,7},{3,1},{5,3},{7,5},{9,15},{11,9},{13,11},{15,13},{17,23},{19,... | collective-permute-start | bytes 968 | tf_op jit(solution)/shard_map/ppermute | solution.py:54
  70.4 11.3 %collective-permute-start.11 = (bf16[40,64,128]{2,1,0:T(8,128)(2,1)S(1)}, bf16[40,64,128]{2,1,0:T(8,128)(2,1)S(1)}, u32[]{:S(2)}, u32[]{:S(2)}) collective-permute-start(bf16[40,64,128]{2,1,0:T(8,128)(2,1)S(1)} %slice.135), channel_id=1, source_target_pairs={{1,7},{3,1},{5,3},{7,5},{9,15},{11,9},{13,11},{15,13},{17,23},{19,... | collective-permute-start | bytes 1966088 | tf_op jit(solution)/shard_map/ppermute | solution.py:54
  73.4 12.5 %collective-permute-start.12 = (bf16[40,64,128]{2,1,0:T(8,128)(2,1)S(1)}, bf16[40,64,128]{2,1,0:T(8,128)(2,1)S(1)}, u32[]{:S(2)}, u32[]{:S(2)}) collective-permute-start(bf16[40,64,128]{2,1,0:T(8,128)(2,1)S(1)} %slice.136), channel_id=1, source_target_pairs={{1,3},{3,5},{5,7},{7,1},{9,11},{11,13},{13,15},{15,9},{17,19},{19,... | collective-permute-start | bytes 1966088 | tf_op jit(solution)/shard_map/ppermute | solution.py:55
  78.8 10.5 %copy-start.25 = (f32[80]{0:T(128)}, f32[80]{0:T(128)S(1)}, u32[]{:S(2)}) copy-start(f32[80]{0:T(128)S(1)} %get-tuple-element.27) | copy-start | bytes 964
  86.0 3.3 %copy-start.13 = (bf16[40,64,128]{2,1,0:T(8,128)(2,1)}, bf16[40,64,128]{2,1,0:T(8,128)(2,1)S(1)}, u32[]{:S(2)}) copy-start(bf16[40,64,128]{2,1,0:T(8,128)(2,1)S(1)} %collective-permute-done.12) | copy-start | bytes 1966084
  89.3 18.4 %collective-permute-start.14 = (bf16[80,64,128]{2,1,0:T(8,128)(2,1)S(1)}, bf16[80,64,128]{2,1,0:T(8,128)(2,1)S(1)}, u32[]{:S(2)}, u32[]{:S(2)}) collective-permute-start(bf16[80,64,128]{2,1,0:T(8,128)(2,1)S(1)} %fusion.25), channel_id=1, source_target_pairs={{1,25},{3,27},{5,29},{7,31},{9,1},{11,3},{13,5},{15,7},{17,9},{19,... | collective-permute-start | bytes 3932168 | tf_op jit(solution)/shard_map/ppermute | solution.py:53
  93.1 42.0 %copy-start.26 = (f32[80]{0:T(128)S(1)}, f32[80]{0:T(128)}, u32[]{:S(2)}) copy-start(f32[80]{0:T(128)} %copy-done.25) | copy-start | bytes 964
  93.1 21.5 %collective-permute-start.13 = (bf16[80,64,128]{2,1,0:T(8,128)(2,1)S(1)}, bf16[80,64,128]{2,1,0:T(8,128)(2,1)S(1)}, u32[]{:S(2)}, u32[]{:S(2)}) collective-permute-start(bf16[80,64,128]{2,1,0:T(8,128)(2,1)S(1)} %fusion.25), channel_id=1, source_target_pairs={{1,9},{3,11},{5,13},{7,15},{9,17},{11,19},{13,21},{15,23},{17,25},... | collective-permute-start | bytes 3932168 | tf_op jit(solution)/shard_map/ppermute | solution.py:52
  107.7 1.0 copy-start.11
  109.6 25.4 %collective-permute-start.15 = (bf16[40,64,128]{2,1,0:T(8,128)(2,1)}, bf16[40,64,128]{2,1,0:T(8,128)(2,1)}, u32[]{:S(2)}, u32[]{:S(2)}) collective-permute-start(bf16[40,64,128]{2,1,0:T(8,128)(2,1)} %slice.137), channel_id=1, source_target_pairs={{1,25},{3,27},{5,29},{7,31},{9,1},{11,3},{13,5},{15,7},{17,9},{19,... | collective-permute-start | bytes 1966088 | tf_op jit(solution)/shard_map/ppermute | solution.py:54
  114.6 1.1 copy-start.12
  116.6 18.5 %collective-permute-start.16 = (bf16[40,64,128]{2,1,0:T(8,128)(2,1)}, bf16[40,64,128]{2,1,0:T(8,128)(2,1)}, u32[]{:S(2)}, u32[]{:S(2)}) collective-permute-start(bf16[40,64,128]{2,1,0:T(8,128)(2,1)} %slice.138), channel_id=1, source_target_pairs={{1,9},{3,11},{5,13},{7,15},{9,17},{11,19},{13,21},{15,23},{17,25},... | collective-permute-start | bytes 1966088 | tf_op jit(solution)/shard_map/ppermute | solution.py:55
  118.6 5.3 %collective-permute-start.6 = (f32[80]{0:T(128)S(1)}, f32[80]{0:T(128)}, u32[]{:S(2)}, u32[]{:S(2)}) collective-permute-start(f32[80]{0:T(128)S(1)} %get-tuple-element.26), channel_id=1, source_target_pairs={{1,25},{3,27},{5,29},{7,31},{9,1},{11,3},{13,5},{15,7},{17,9},{19,... | collective-permute-start | bytes 968 | tf_op jit(solution)/shard_map/ppermute | solution.py:53
  123.9 7.1 %collective-permute-start.7 = (f32[80]{0:T(128)}, f32[80]{0:T(128)}, u32[]{:S(2)}, u32[]{:S(2)}) collective-permute-start(f32[80]{0:T(128)} %collective-permute-done.6), channel_id=1, source_target_pairs={{1,25},{3,27},{5,29},{7,31},{9,1},{11,3},{13,5},{15,7},{17,9},{19,... | collective-permute-start | bytes 968 | tf_op jit(solution)/shard_map/ppermute | solution.py:54
  128.8 5.5 %collective-permute-start.5 = (f32[80]{0:T(128)S(1)}, f32[80]{0:T(128)S(1)}, u32[]{:S(2)}, u32[]{:S(2)}) collective-permute-start(f32[80]{0:T(128)S(1)} %get-tuple-element.26), channel_id=1, source_target_pairs={{1,9},{3,11},{5,13},{7,15},{9,17},{11,19},{13,21},{15,23},{17,25},... | collective-permute-start | bytes 968 | tf_op jit(solution)/shard_map/ppermute | solution.py:52
  135.1 10.6 %copy-start.30 = (f32[80]{0:T(128)S(1)}, f32[80]{0:T(128)}, u32[]{:S(2)}) copy-start(f32[80]{0:T(128)} %param.20) | copy-start | bytes 964
  142.7 12.2 %collective-permute-start.17 = (f32[80,64,128]{2,1,0:T(8,128)}, f32[80,64,128]{2,1,0:T(8,128)}, u32[]{:S(2)}, u32[]{:S(2)}) collective-permute-start(f32[80,64,128]{2,1,0:T(8,128)} %fusion.15), channel_id=1, source_target_pairs={{1,0},{3,2},{5,4},{7,6},{9,8},{11,10},{13,12},{15,14},{17,16},{19,... | collective-permute-start | bytes 7864328 | tf_op jit(solution)/shard_map/ppermute | solution.py:108
  145.6 102.3 %all-gather.6.cloned.1.call-start = ((), (), s32[]{:S(2)}) async-start(), calls=%async_computation.1 | async-start | bytes 2359296 | tf_op jit(solution)/shard_map/all_gather | solution.py:114
  146.1 4.7 %copy-start.10 = (bf16[128,5120]{0,1:T(8,128)(2,1)S(1)}, bf16[128,5120]{0,1:T(8,128)(2,1)}, u32[]{:S(2)}) copy-start(bf16[128,5120]{0,1:T(8,128)(2,1)} %copy.24) | copy-start | bytes 3932164
  146.1 4.7 %copy-start.22 = (f32[80,128]{1,0:T(8,128)S(1)}, f32[80,128]{1,0:T(8,128)}, u32[]{:S(2)}) copy-start(f32[80,128]{1,0:T(8,128)} %get-tuple-element.20) | copy-start | bytes 122884
  150.8 4.1 %copy-start.8 = (f32[80,64,128]{2,1,0:T(8,128)S(1)}, f32[80,64,128]{2,1,0:T(8,128)}, u32[]{:S(2)}) copy-start(f32[80,64,128]{2,1,0:T(8,128)} %copy-done.7) | copy-start | bytes 7864324
  150.8 4.1 %copy-start.28 = (f32[80]{0:T(128)S(1)}, f32[80]{0:T(128)}, u32[]{:S(2)}) copy-start(f32[80]{0:T(128)} %get-tuple-element.44) | copy-start | bytes 964
  154.9 2.3 copy-start.16
  157.2 3.0 copy-start.6
  160.2 3.2 %copy-start.27 = (f32[80]{0:T(128)S(1)}, f32[80]{0:T(128)}, u32[]{:S(2)}) copy-start(f32[80]{0:T(128)} %get-tuple-element.39) | copy-start | bytes 964
  173.1 7.6 %copy-start.18 = (f32[5120]{0:T(1024)S(1)}, f32[5120]{0:T(1024)}, u32[]{:S(2)}) copy-start(f32[5120]{0:T(1024)} %param.21) | copy-start | bytes 61444
  178.4 2.3 copy-start
  181.7 33.6 %copy-start.24 = (f32[8,256]{1,0:T(8,128)S(1)}, f32[8,256]{1,0:T(8,128)}, u32[]{:S(2)}) copy-start(f32[8,256]{1,0:T(8,128)} %param.23) | copy-start | bytes 24580
  184.6 110.5 %copy-start.21 = (f32[8,256]{1,0:T(8,128)}, f32[8,256]{1,0:T(8,128)S(1)}, u32[]{:S(2)}) copy-start(f32[8,256]{1,0:T(8,128)S(1)} %get-tuple-element.47) | copy-start | bytes 24580
  215.3 73.8 %all-gather.8.cloned.1.call-start = ((), (), s32[]{:S(2)}) async-start(), calls=%async_computation.2 | async-start | bytes 2359296 | tf_op jit(solution)/shard_map/all_gather | solution.py:114
  292.2 3.4 %copy-start.1 = (f32[4096,256]{1,0:T(8,128)S(1)}, f32[4096,256]{1,0:T(8,128)}, u32[]{:S(2)}) copy-start(f32[4096,256]{1,0:T(8,128)} %constant_dynamic-update-slice_fusion) | copy-start | bytes 12582916
Sparse Core Ops, SparseCore 0:
  145.7 36.5 all-gather.3
  215.4 32.3 all-gather.5
  249.7 39.3 all-gather.7

commit v2 on v1

--- a/solution.py
+++ b/solution.py
@@ -46,29 +46,24 @@
     return rows, up, down, (y_fwd, y_bwd), (x_fwd, x_bwd)
 
 
-def ring_of_four(state, logsum, fwd, bwd):
+def ring_of_four(state, fwd, bwd):
     half = state.shape[0] // 2
     sent = state.astype(XFER)
-    prev_state, prev_log = lax.ppermute((sent, logsum), "seq", fwd)
-    next_state, next_log = lax.ppermute((sent, logsum), "seq", bwd)
-    far_a, far_log = lax.ppermute((next_state[:half], next_log), "seq", bwd)
+    prev_state = lax.ppermute(sent, "seq", fwd)
+    next_state = lax.ppermute(sent, "seq", bwd)
+    far_a = lax.ppermute(next_state[:half], "seq", bwd)
     far_b = lax.ppermute(prev_state[half:], "seq", fwd)
     far_state = jnp.concatenate([far_a, far_b], axis=0)
-    return [
-        (state, logsum, 0),
-        (prev_state, prev_log, RING - 1),
-        (next_state, next_log, 1),
-        (far_state, far_log, 2),
-    ]
-
-
-def fold_ring(slots, pos):
-    places = [(pos + k) % RING for (_, _, k) in slots]
-    logs = [l for (_, l, _) in slots]
+    return [(state, 0), (prev_state, RING - 1), (next_state, 1), (far_state, 2)]
+
+
+def fold_ring(slots, pos, ring_logs):
+    places = [(pos + k) % RING for (_, k) in slots]
+    logs = [lax.dynamic_index_in_dim(ring_logs, p, 0, False) for p in places]
     zero = jnp.zeros_like(logs[0])
     before = None
     total = None
-    for i, (value, _, _) in enumerate(slots):
+    for i, (value, _) in enumerate(slots):
         between = zero
         after = zero
         for j in range(len(slots)):
@@ -85,11 +80,10 @@
     lead = zero
     for j in range(len(slots)):
         lead = lead + jnp.where(places[j] < pos, logs[j], 0.0)
-    total_log = sum(logs[1:], logs[0])
-    return before, jnp.exp(lead), total, total_log
-
-
-def carried_in(own_state, own_log):
+    return before, jnp.exp(lead), total
+
+
+def carried_in(own_state, shard_logs):
     seq = lax.axis_size("seq")
     rows, up, down, y_routes, x_routes = chip_routes(seq)
     assert rows == RING and seq == rows * RING * CORES
@@ -97,21 +91,33 @@
     core = place % CORES
     y_pos = (place // CORES) % RING
     x_pos = place // (CORES * RING)
-    low_state, low_log = lax.ppermute((own_state, own_log), "seq", up)
+    grid_logs = shard_logs.reshape(rows, RING, CORES, -1)
+    chip_logs = grid_logs[:, :, 0] + grid_logs[:, :, 1]
+    own_log = lax.dynamic_index_in_dim(shard_logs, place, 0, False)
+    low_log = lax.dynamic_index_in_dim(shard_logs, place - 1, 0, False)
+    low_state = lax.ppermute(own_state, "seq", up)
     chip_state = jnp.exp(own_log)[:, None, None] * low_state + own_state
-    chip_log = low_log + own_log
-    slots = ring_of_four(chip_state, chip_log, *y_routes)
-    row_before, row_lead, row_total, row_log = fold_ring(slots, y_pos)
-    slots = ring_of_four(row_total, row_log, *x_routes)
-    rows_before, _, _, _ = fold_ring(slots, x_pos)
+    slots = ring_of_four(chip_state, *y_routes)
+    row_logs = lax.dynamic_index_in_dim(chip_logs, x_pos, 0, False)
+    row_before, row_lead, row_total = fold_ring(slots, y_pos, row_logs)
+    slots = ring_of_four(row_total, *x_routes)
+    rows_before, _, _ = fold_ring(slots, x_pos, jnp.sum(chip_logs, axis=1))
     chip_in = row_lead[:, None, None] * rows_before + row_before
     chip_in_low = lax.ppermute(chip_in, "seq", down)
     high_in = jnp.exp(low_log)[:, None, None] * chip_in + low_state
     return jnp.where(core == 0, chip_in_low, high_in)
 
 
-def gathered_rows(block):
-    return lax.all_gather(lax.all_gather(block, "seq", axis=0, tiled=True), "dp", axis=0, tiled=True)
+def placed(block, slots, index):
+    held = jnp.zeros((slots,) + block.shape, block.dtype)
+    return lax.dynamic_update_index_in_dim(held, block, index, 0)
+
+
+def everywhere(block):
+    flat = lax.axis_index("dp") * lax.axis_size("seq") + lax.axis_index("seq")
+    count = lax.axis_size("dp") * lax.axis_size("seq")
+    summed = lax.psum(placed(block, count, flat), ("dp", "seq"))
+    return summed.reshape((count * block.shape[0],) + block.shape[1:])
 
 
 def per_device(
@@ -134,7 +140,6 @@
     heads = step_size.shape[1]
     head_dim = width // heads
     taps = conv_weight.shape[0]
-    all_prior = gathered_rows(prior_draw)
     full_code_weight = lax.all_gather(code_weight, "dp", axis=0, tiled=True)
     joined = jnp.concatenate([inputs[0], write_proj[0], read_proj[0]], axis=1)
     rim_rows = passed_along(joined[length - (taps - 1) :], "seq", 1)
@@ -177,7 +182,14 @@
         block_total = cum_list[block][:, -1]
         running = jnp.exp(block_total)[:, None, None] * running + state_list[block]
         before = before + block_total
-    carry_in = carried_in(running, before)
+    seq = lax.axis_size("seq")
+    code_dim = prior_draw.shape[1]
+    prior_size = prior_draw.shape[0] * code_dim
+    shared = everywhere(jnp.concatenate([prior_draw.reshape(-1), before]))
+    shared = shared.reshape(-1, prior_size + heads)
+    all_prior = shared[:, :prior_size].reshape(-1, code_dim)
+    shard_logs = lax.dynamic_slice_in_dim(shared[:, prior_size:], lax.axis_index("dp") * seq, seq, 0)
+    carry_in = carried_in(running, shard_logs)
     outputs = []
     for block in range(blocks):
         lower = block * SPAN
@@ -197,13 +209,12 @@
         jnp.bfloat16
     )
     codes_local = jnp.dot(pooled, full_code_weight, preferred_element_type=jnp.float32)
-    all_codes = gathered_rows(codes_local)
+    all_codes = everywhere(codes_local)
     columns = jnp.concatenate([all_codes, all_prior], axis=0)
     cross = jnp.dot(codes_local, columns.T, precision=lax.Precision.HIGHEST)
     row_sq = jnp.sum(codes_local * codes_local, axis=1)
     col_sq = jnp.sum(columns * columns, axis=1)
     dist_sq = row_sq[:, None] + col_sq[None, :] - 2.0 * cross
-    code_dim = codes_local.shape[1]
     kernel = 2.0 * code_dim / (2.0 * code_dim + dist_sq)
     return (mixed[None], codes_local, kernel)
 

time: 311 us -> 727 us (2.34)
  waiting for transfers between devices: 73.7 us -> 564 us
  blocking collectives: 57.1 us -> 0 us
  starting transfers between devices: 57.5 us -> 34.5 us
    psum x0 -> x2, waiting for transfers between devices: none -> 519 us  [everywhere(): summed = lax.psum(placed(block, count, flat), ('dp', 'seq'))]
    all_gather x2 -> x0, blocking collectives: 57.1 us -> none  [gathered_rows(): lax.all_gather(block, 'seq', axis=0, tiled=True)]
    all_gather x2 -> x0, waiting for transfers between devices: 39.5 us -> none  [gathered_rows(): lax.all_gather(lax.all_gather(block, 'seq', axis=0, tiled=True), 'dp', ax...]
    ppermute x14 -> x7, starting transfers between devices: 44.6 us -> 23 us  [the longest x2 9.99 us: ring_of_four(): far_a = lax.ppermute(next_state[:half], 'seq', bwd)]
    ppermute x2, waiting for transfers between devices: 4.29 us -> 13.2 us  [ring_of_four(): far_b = lax.ppermute(prev_state[half:], 'seq', fwd)]
    ppermute x14 -> x7, waiting for transfers between devices: 29.3 us -> 31.8 us  [the longest x2 25.3 us: ring_of_four(): next_state = lax.ppermute(sent, 'seq', bwd)]
  transfers between devices with their start and end apart: 21 -> 14, of which waited for: 11 -> 8; matrix products, arithmetic and copies ran while one was open for 17% -> 8% of each run, Pallas kernels for 0% -> 0%
where the time goes in v2:
time: 727 us; the launch traced here: 726 us
  waiting for transfers between devices  564 us (78%)
  other arithmetic  43.2 us (6%)
  local copies, waits for them, and re-layouts  34.9 us (5%)
  starting transfers between devices  34.5 us (5%)
  matrix products  32.8 us (5%)
  between operations  16.5 us (2%)
    psum x2, waiting for transfers between devices, everywhere(): summed = lax.psum(placed(block, count, flat), ('dp', 'seq'))  519 us
    ppermute x2, waiting for transfers between devices, ring_of_four(): next_state = lax.ppermute(sent, 'seq', bwd)  25.3 us
  transfers between devices with their start and end apart: 14, of which 8 were waited for; matrix products, arithmetic and copies ran while one was open for 8% of the time, Pallas kernels for 0%

profile of v2, /device:TPU:1, one launch (start us, length us, event | category | flops | bytes accessed | tf_op | source)
XLA Modules:
  0.0 725.8 jit_solution(3509531131960660864)
XLA Ops:
  8.1 2.1 pad_maximum_fusion
  10.3 4.6 collective-permute-start
  15.2 0.3 reduce_window_sum.18
  15.7 0.5 fusion.104
  16.2 0.6 fusion.102
  17.2 2.4 maximum_maximum_fusion
  19.6 4.4 multiply_convert_fusion
  24.0 1.8 fusion.101
  25.8 2.4 copy.23
  28.3 2.4 copy.24
  30.7 3.9 fusion.16
  34.7 4.3 multiply_add_fusion.1
  38.9 1.3 collective-permute-start.1
  40.3 1.5 broadcast_in_dim.137
  41.8 1.5 dynamic_update_slice.8
  43.4 266.4 %all-reduce.3.cloned.1.call-done = f32[256,2128]{1,0:T(8,128)} async-done(((f32[256,2128]{1,0:T(8,128)}), f32[256,2128]{1,0:T(8,128)}) %all-reduce.3.cloned.1.call-update) | async-done | bytes 2179088 | tf_op jit(solution)/shard_map/psum | solution.py:119
  309.8 0.9 slice.148
  310.8 0.6 fusion.93
  311.3 4.9 fusion.100
  316.2 4.1 collective-permute-start.3
  320.3 1.9 collective-permute-start.2
  322.5 12.7 %collective-permute-done.3 = bf16[80,64,128]{2,1,0:T(8,128)(2,1)} collective-permute-done((bf16[80,64,128]{2,1,0:T(8,128)(2,1)}, bf16[80,64,128]{2,1,0:T(8,128)(2,1)}, u32[]{:S(2)}, u32[]{:S(2)}) %collective-permute-start.3) | collective-permute-done | bytes 1310752 | tf_op jit(solution)/shard_map/ppermute | solution.py:53
  335.2 1.1 slice.154
  336.3 5.0 collective-permute-start.4
  341.4 1.1 slice.155
  342.5 1.9 collective-permute-start.5
  344.5 0.5 exponential_bitcast_fusion.2
  345.0 0.5 fusion.59
  345.5 0.6 fusion.58
  346.1 2.7 collective-permute-done.4
  348.9 6.2 collective-permute-done.5
  355.0 3.3 fusion.25
  358.4 3.8 collective-permute-start.7
  362.1 1.9 collective-permute-start.6
  364.1 12.7 %collective-permute-done.7 = bf16[80,64,128]{2,1,0:T(8,128)(2,1)S(1)} collective-permute-done((bf16[80,64,128]{2,1,0:T(8,128)(2,1)S(1)}, bf16[80,64,128]{2,1,0:T(8,128)(2,1)S(1)}, u32[]{:S(2)}, u32[]{:S(2)}) %collective-permute-start.7) | collective-permute-done | bytes 1310752 | tf_op jit(solution)/shard_map/ppermute | solution.py:53
  376.7 1.1 copy-done.10
  377.8 0.9 slice.156
  378.7 5.0 collective-permute-start.8
  383.7 1.1 copy-done.11
  384.8 0.9 slice.157
  385.7 1.9 collective-permute-start.9
  387.8 3.7 collective-permute-done.8
  391.5 7.0 collective-permute-done.9
  398.5 7.6 %fusion.15 = f32[80,64,128]{2,1,0:T(8,128)} fusion(bf16[80,64,128]{2,1,0:T(8,128)(2,1)} %collective-permute-done.2, bf16[80,64,128]{2,1,0:T(8,128)(2,1)} %collective-permute-done.3, f32[80,64,128]{2,1,0:T(8,128)} %get-tuple-element.17, bf16[80,64,128]{2,1,0:T(8,128)(2,1)} %copy-done.10, bf16[80,64,128]{2,1,0:T(8,128)(2,1)} %copy-done.11, ...), kind=kLoop, calls=%fused_computation.36 | loop fusion | flops 20316160 | bytes 13111360 | tf_op jit(solution)/shard_map/add | solution.py:105
  406.1 2.8 collective-permute-start.10
  409.6 4.5 fusion.7
  414.1 4.1 fusion.8
  418.2 1.6 slice.160
  419.8 2.8 reshape.622
  422.6 3.2 add_select_fusion
  426.0 2.9 bitcast_add_fusion.1
  428.8 3.3 copy.29
  432.1 6.5 bitcast_add_fusion
  438.6 3.2 copy.30
  441.8 5.4 multiply_reduce_fusion
  447.3 2.3 copy-done
  449.6 1.0 convert_reduce_fusion
  450.8 2.2 bitcast_dynamic-update-slice_fusion
  452.9 1.3 copy-done.7
  454.4 4.7 fusion.97
  459.1 252.5 %all-reduce.5.cloned.1.call-done = f32[2048,256]{1,0:T(8,128)} async-done(((f32[2048,256]{1,0:T(8,128)}), f32[2048,256]{1,0:T(8,128)}) %all-reduce.5.cloned.1.call-update) | async-done | bytes 2097168 | tf_op jit(solution)/shard_map/psum | solution.py:119
  711.6 1.7 constant_dynamic-update-slice_fusion.1
  713.5 0.6 multiply_reduce_fusion.1
  714.1 4.2 fusion.6
  (88 shorter events, 2.4 us)
Async XLA Ops:
  8.0 301.8 %all-reduce.3.cloned.1.call-start = ((), (), s32[]{:S(2)}) async-start(), calls=%async_computation | async-start | bytes 4456448 | tf_op jit(solution)/shard_map/psum | solution.py:119
  8.0 6.8 copy-start.20
  8.1 8.2 %copy-start.21 = (f32[1,80,256]{2,1,0:T(8,128)S(1)}, f32[1,80,256]{2,1,0:T(8,128)}, u32[]{:S(2)}) copy-start(f32[1,80,256]{2,1,0:T(8,128)} %param.16) | copy-start | bytes 245764
  8.1 8.8 %copy-start.18 = (f32[4,5376]{1,0:T(4,128)S(1)}, f32[4,5376]{1,0:T(4,128)}, u32[]{:S(2)}) copy-start(f32[4,5376]{1,0:T(4,128)} %param.18) | copy-start | bytes 258052
  8.1 9.1 %copy-start.2 = (bf16[1,256,5120]{2,1,0:T(8,128)(2,1)S(1)}, bf16[1,256,5120]{2,1,0:T(8,128)(2,1)}, u32[]{:S(2)}) copy-start(bf16[1,256,5120]{2,1,0:T(8,128)(2,1)} %param.12) | copy-start | bytes 7864324
  8.1 9.1 %copy-start.15 = (bf16[1,256,128]{2,1,0:T(8,128)(2,1)S(1)}, bf16[1,256,128]{2,1,0:T(8,128)(2,1)}, u32[]{:S(2)}) copy-start(bf16[1,256,128]{2,1,0:T(8,128)(2,1)} %param.15) | copy-start | bytes 196612
  8.1 9.1 %copy-start.16 = (bf16[1,256,128]{2,1,0:T(8,128)(2,1)S(1)}, bf16[1,256,128]{2,1,0:T(8,128)(2,1)}, u32[]{:S(2)}) copy-start(bf16[1,256,128]{2,1,0:T(8,128)(2,1)} %param.14) | copy-start | bytes 196612
  10.3 6.8 collective-permute-start
  17.1 2.4 copy-start.3
  17.1 2.4 copy-start.24
  30.7 3.9 copy-start.8
  34.6 4.3 copy-start.4
  34.6 5.6 copy-start.25
  38.9 272.4 %collective-permute-start.1 = (f32[80,64,128]{2,1,0:T(8,128)}, f32[80,64,128]{2,1,0:T(8,128)}, u32[]{:S(2)}, u32[]{:S(2)}) collective-permute-start(f32[80,64,128]{2,1,0:T(8,128)} %multiply_add_fusion.1), channel_id=1, source_target_pairs={{0,1},{2,3},{4,5},{6,7},{8,9},{10,11},{12,13},{14,15},{16,17},{18,... | collective-permute-start | bytes 7864328 | tf_op jit(solution)/shard_map/ppermute | solution.py:98
  43.3 407.3 %all-gather.2.cloned.1.call-start = ((), (), s32[]{:S(2)}) async-start(), calls=%async_computation.1 | async-start | bytes 2949120 | tf_op jit(solution)/shard_map/all_gather | solution.py:143
  316.2 19.0 %collective-permute-start.3 = (bf16[80,64,128]{2,1,0:T(8,128)(2,1)}, bf16[80,64,128]{2,1,0:T(8,128)(2,1)}, u32[]{:S(2)}, u32[]{:S(2)}) collective-permute-start(bf16[80,64,128]{2,1,0:T(8,128)(2,1)} %get-tuple-element.16), channel_id=1, source_target_pairs={{1,7},{3,1},{5,3},{7,5},{9,15},{11,9},{13,11},{15,13},{17,23},{19,... | collective-permute-start | bytes 3932168 | tf_op jit(solution)/shard_map/ppermute | solution.py:53
  320.3 21.0 %collective-permute-start.2 = (bf16[80,64,128]{2,1,0:T(8,128)(2,1)}, bf16[80,64,128]{2,1,0:T(8,128)(2,1)}, u32[]{:S(2)}, u32[]{:S(2)}) collective-permute-start(bf16[80,64,128]{2,1,0:T(8,128)(2,1)} %get-tuple-element.16), channel_id=1, source_target_pairs={{1,3},{3,5},{5,7},{7,1},{9,11},{11,13},{13,15},{15,9},{17,19},{19,... | collective-permute-start | bytes 3932168 | tf_op jit(solution)/shard_map/ppermute | solution.py:52
  322.5 32.6 %copy-start.1 = (f32[80,64,128]{2,1,0:T(8,128)S(1)}, f32[80,64,128]{2,1,0:T(8,128)}, u32[]{:S(2)}) copy-start(f32[80,64,128]{2,1,0:T(8,128)} %get-tuple-element.17) | copy-start | bytes 7864324
  336.3 12.5 %collective-permute-start.4 = (bf16[40,64,128]{2,1,0:T(8,128)(2,1)S(1)}, bf16[40,64,128]{2,1,0:T(8,128)(2,1)S(1)}, u32[]{:S(2)}, u32[]{:S(2)}) collective-permute-start(bf16[40,64,128]{2,1,0:T(8,128)(2,1)S(1)} %slice.154), channel_id=1, source_target_pairs={{1,7},{3,1},{5,3},{7,5},{9,15},{11,9},{13,11},{15,13},{17,23},{19,... | collective-permute-start | bytes 1966088 | tf_op jit(solution)/shard_map/ppermute | solution.py:54
  342.5 12.5 %collective-permute-start.5 = (bf16[40,64,128]{2,1,0:T(8,128)(2,1)S(1)}, bf16[40,64,128]{2,1,0:T(8,128)(2,1)S(1)}, u32[]{:S(2)}, u32[]{:S(2)}) collective-permute-start(bf16[40,64,128]{2,1,0:T(8,128)(2,1)S(1)} %slice.155), channel_id=1, source_target_pairs={{1,3},{3,5},{5,7},{7,1},{9,11},{11,13},{13,15},{15,9},{17,19},{19,... | collective-permute-start | bytes 1966088 | tf_op jit(solution)/shard_map/ppermute | solution.py:55
  355.0 3.3 copy-start.13
  358.4 18.4 %collective-permute-start.7 = (bf16[80,64,128]{2,1,0:T(8,128)(2,1)S(1)}, bf16[80,64,128]{2,1,0:T(8,128)(2,1)S(1)}, u32[]{:S(2)}, u32[]{:S(2)}) collective-permute-start(bf16[80,64,128]{2,1,0:T(8,128)(2,1)S(1)} %fusion.25), channel_id=1, source_target_pairs={{1,25},{3,27},{5,29},{7,31},{9,1},{11,3},{13,5},{15,7},{17,9},{19,... | collective-permute-start | bytes 3932168 | tf_op jit(solution)/shard_map/ppermute | solution.py:53
  362.1 21.5 %collective-permute-start.6 = (bf16[80,64,128]{2,1,0:T(8,128)(2,1)S(1)}, bf16[80,64,128]{2,1,0:T(8,128)(2,1)S(1)}, u32[]{:S(2)}, u32[]{:S(2)}) collective-permute-start(bf16[80,64,128]{2,1,0:T(8,128)(2,1)S(1)} %fusion.25), channel_id=1, source_target_pairs={{1,9},{3,11},{5,13},{7,15},{9,17},{11,19},{13,21},{15,23},{17,25},... | collective-permute-start | bytes 3932168 | tf_op jit(solution)/shard_map/ppermute | solution.py:52
  376.7 1.1 copy-start.10
  378.7 12.8 %collective-permute-start.8 = (bf16[40,64,128]{2,1,0:T(8,128)(2,1)}, bf16[40,64,128]{2,1,0:T(8,128)(2,1)}, u32[]{:S(2)}, u32[]{:S(2)}) collective-permute-start(bf16[40,64,128]{2,1,0:T(8,128)(2,1)} %slice.156), channel_id=1, source_target_pairs={{1,25},{3,27},{5,29},{7,31},{9,1},{11,3},{13,5},{15,7},{17,9},{19,... | collective-permute-start | bytes 1966088 | tf_op jit(solution)/shard_map/ppermute | solution.py:54
  383.7 1.1 copy-start.11
  385.7 12.8 %collective-permute-start.9 = (bf16[40,64,128]{2,1,0:T(8,128)(2,1)}, bf16[40,64,128]{2,1,0:T(8,128)(2,1)}, u32[]{:S(2)}, u32[]{:S(2)}) collective-permute-start(bf16[40,64,128]{2,1,0:T(8,128)(2,1)} %slice.157), channel_id=1, source_target_pairs={{1,9},{3,11},{5,13},{7,15},{9,17},{11,19},{13,21},{15,23},{17,25},... | collective-permute-start | bytes 1966088 | tf_op jit(solution)/shard_map/ppermute | solution.py:55
  398.5 10.6 %copy-start.28 = (f32[80]{0:T(128)S(1)}, f32[80]{0:T(128)}, u32[]{:S(2)}) copy-start(f32[80]{0:T(128)} %param.20) | copy-start | bytes 964
  406.1 16.5 %collective-permute-start.10 = (f32[80,64,128]{2,1,0:T(8,128)}, f32[80,64,128]{2,1,0:T(8,128)}, u32[]{:S(2)}, u32[]{:S(2)}) collective-permute-start(f32[80,64,128]{2,1,0:T(8,128)} %fusion.15), channel_id=1, source_target_pairs={{1,0},{3,2},{5,4},{7,6},{9,8},{11,10},{13,12},{15,14},{17,16},{19,... | collective-permute-start | bytes 7864328 | tf_op jit(solution)/shard_map/ppermute | solution.py:106
  408.9 302.7 %all-reduce.5.cloned.1.call-start = ((), (), s32[]{:S(2)}) async-start(), calls=%async_computation.2 | async-start | bytes 4194304 | tf_op jit(solution)/shard_map/psum | solution.py:119
  409.6 4.5 copy-start.9
  409.6 4.5 copy-start.23
  414.1 4.1 copy-start.14
  419.8 2.8 copy-start.27
  422.6 3.4 copy-start.12
  422.6 3.4 copy-start.17
  425.7 3.1 copy-start.5
  428.8 3.3 copy-start.26
  441.8 7.8 %copy-start.19 = (f32[5120]{0:T(1024)S(1)}, f32[5120]{0:T(1024)}, u32[]{:S(2)}) copy-start(f32[5120]{0:T(1024)} %param.21) | copy-start | bytes 61444
  447.3 2.3 copy-start
  452.9 1.3 copy-start.7
  452.9 261.2 %copy-start.22 = (f32[8,256]{1,0:T(8,128)}, f32[8,256]{1,0:T(8,128)S(1)}, u32[]{:S(2)}) copy-start(f32[8,256]{1,0:T(8,128)S(1)} %get-tuple-element.52) | copy-start | bytes 24580
  459.1 254.2 %copy-start.6 = (f32[2048,256]{1,0:T(8,128)S(1)}, f32[2048,256]{1,0:T(8,128)}, u32[]{:S(2)}) copy-start(f32[2048,256]{1,0:T(8,128)} %reshape.622) | copy-start | bytes 6291460
Sparse Core Ops, SparseCore 0:
  43.5 266.3 all-reduce.2
  454.4 257.1 all-reduce.4
Sparse Core Ops, SparseCore 1:
  409.0 33.4 all-gather.1

commit v3 on v2

--- a/solution.py
+++ b/solution.py
@@ -114,10 +114,10 @@
 
 
 def everywhere(block):
-    flat = lax.axis_index("dp") * lax.axis_size("seq") + lax.axis_index("seq")
     count = lax.axis_size("dp") * lax.axis_size("seq")
-    summed = lax.psum(placed(block, count, flat), ("dp", "seq"))
-    return summed.reshape((count * block.shape[0],) + block.shape[1:])
+    spread = jnp.broadcast_to(block[None], (count,) + block.shape)
+    got = lax.all_to_all(spread, ("dp", "seq"), 0, 0)
+    return got.reshape((count * block.shape[0],) + block.shape[1:])
 
 
 def per_device(

time: 727 us -> 304 us (0.42)
  waiting for transfers between devices: 564 us -> 111 us
  starting transfers between devices: 34.5 us -> 56.4 us
  local copies, waits for them, and re-layouts: 34.9 us -> 44.7 us
    psum x2 -> x0, waiting for transfers between devices: 519 us -> none  [everywhere(): summed = lax.psum(placed(block, count, flat), ('dp', 'seq'))]
    all_to_all x0 -> x2, waiting for transfers between devices: none -> 66.4 us  [everywhere(): got = lax.all_to_all(spread, ('dp', 'seq'), 0, 0)]
    all_to_all x0 -> x2, starting transfers between devices: none -> 24.8 us  [everywhere(): got = lax.all_to_all(spread, ('dp', 'seq'), 0, 0)]
  transfers between devices with their start and end apart: 14 -> 14, of which waited for: 8 -> 9; matrix products, arithmetic and copies ran while one was open for 8% -> 28% of each run, Pallas kernels for 0% -> 0%
where the time goes in v3:
time: 304 us; the launch traced here: 303 us
  waiting for transfers between devices  111 us (37%)
  starting transfers between devices  56.4 us (19%)
  local copies, waits for them, and re-layouts  44.7 us (15%)
  other arithmetic  42.6 us (14%)
  matrix products  33.1 us (11%)
  between operations  15 us (5%)
    all_to_all x2, waiting for transfers between devices, everywhere(): got = lax.all_to_all(spread, ('dp', 'seq'), 0, 0)  66.4 us
    ppermute x2, waiting for transfers between devices, ring_of_four(): next_state = lax.ppermute(sent, 'seq', bwd)  25.6 us
    all_to_all x2, starting transfers between devices, everywhere(): got = lax.all_to_all(spread, ('dp', 'seq'), 0, 0)  24.8 us
    ppermute x2, waiting for transfers between devices, ring_of_four(): far_b = lax.ppermute(prev_state[half:], 'seq', fwd)  12.6 us
    dot_general x2, matrix products, per_device(): jnp.einsum('tn,hpn->thp', read_block, start, precision=lax.Precision.HIGH...  9.42 us
    dot_general x2, matrix products, block_terms(): jnp.einsum('hts,shp->thp', mixing, values, preferred_element_type=jnp.flo...  8.69 us
    dot_general x2, matrix products, block_terms(): jnp.einsum('hsn,shp->hpn', weighted, values, preferred_element_type=jnp.f...  8.21 us
    convert_element_type x2, other arithmetic, ring_of_four(): sent = state.astype(XFER)  8.19 us
  transfers between devices with their start and end apart: 14, of which 9 were waited for; matrix products, arithmetic and copies ran while one was open for 28% of the time, Pallas kernels for 0%

profile of v3, /device:TPU:1, one launch (start us, length us, event | category | flops | bytes accessed | tf_op | source)
XLA Modules:
  0.0 303.1 jit_solution(18234892965178526706)
XLA Ops:
  7.2 0.8 fusion.100
  8.6 0.7 copy.63
  10.0 2.6 broadcast_in_dim.135
  12.6 16.5 %all-to-all-start = ((f32[256,1,2128]{2,1,0:T(1,128)}), f32[256,1,2128]{2,1,0:T(1,128)}, u32[]{:S(2)}, u32[]{:S(2)}) async-start(f32[256,1,2128]{2,1,0:T(1,128)} %broadcast_in_dim.135), calls=%async_computation | async-start | bytes 4456448 | tf_op jit(solution)/shard_map/all_to_all | solution.py:119
  29.4 3.5 %collective-permute-start = (bf16[3,5376]{1,0:T(4,128)(2,1)S(1)}, bf16[3,5376]{1,0:T(4,128)(2,1)S(1)}, u32[]{:S(2)}, u32[]{:S(2)}) collective-permute-start(bf16[3,5376]{1,0:T(4,128)(2,1)S(1)} %slice.136), channel_id=1, source_target_pairs={{0,1},{1,2},{2,3},{3,4},{4,5},{5,6},{6,7},{7,8},{8,9},{9,10},{10,1... | collective-permute-start | bytes 96776 | tf_op jit(solution)/shard_map/ppermute | solution.py:16
  33.0 0.7 fusion.99
  34.1 2.4 maximum_maximum_fusion
  36.5 4.4 %multiply_convert_fusion = bf16[256,5376]{1,0:T(8,128)(2,1)S(1)} fusion(bf16[259,5376]{1,0:T(8,128)(2,1)S(1)} %maximum_maximum_fusion, f32[5376]{0:T(1024)S(1)} %get-tuple-element.5, f32[5376]{0:T(1024)S(1)} %get-tuple-element.6, f32[5376]{0:T(1024)S(1)} %get-tuple-element.4, f32[5376]{0:T(1024)S(1)} %get-tuple-element.3, f32[5376]{0:T(1024)S(1)} %copy-done.20, ...), kind=kLoop, calls=%fused_computation.2 | loop fusion | flops 30277632 | bytes 13870080 | tf_op jit(solution)/shard_map/convert_element_type | solution.py:152
  40.9 1.8 fusion.98
  42.7 2.4 copy.48
  45.2 2.4 copy.51
  47.6 3.9 %fusion.16 = f32[80,64,128]{2,1,0:T(8,128)S(1)} fusion(bf16[128,80,64]{0,2,1:T(8,128)(2,1)} %bitcast.79, f32[128,128]{1,0:T(8,128)S(1)} %get-tuple-element.21, f32[80,128]{1,0:T(8,128)S(1)} %get-tuple-element.25), kind=kOutput, calls=%fused_computation.38 | convolution fusion | flops 170393600 | bytes 4038656 | tf_op jit(solution)/shard_map/hsn,shp->hpn/dot_general | solution.py:29
  51.6 4.3 %multiply_add_fusion.1 = f32[80,64,128]{2,1,0:T(8,128)} fusion(f32[80,64,128]{2,1,0:T(8,128)S(1)} %fusion.16, bf16[128,80,64]{0,2,1:T(8,128)(2,1)S(1)} %bitcast.81, f32[128,128]{1,0:T(8,128)S(1)} %get-tuple-element.20, f32[80,128]{1,0:T(8,128)S(1)} %get-tuple-element.26, f32[80]{0:T(128)S(1)} %get-tuple-element.48, f32[80]{0:T(128)S(1)} %get-tuple-element.50), kind=kOutput, calls=%fused_computation.54 | convolution fusion | flops 172359680 | bytes 6660736 | tf_op jit(solution)/shard_map/hsn,shp->hpn/dot_general | solution.py:29
  55.8 1.3 collective-permute-start.1
  57.1 26.9 %all-to-all-done = f32[256,1,2128]{2,1,0:T(1,128)} async-done(((f32[256,1,2128]{2,1,0:T(1,128)}), f32[256,1,2128]{2,1,0:T(1,128)}, u32[]{:S(2)}, u32[]{:S(2)}) %all-to-all-start) | async-done | bytes 2179104 | tf_op jit(solution)/shard_map/all_to_all | solution.py:119
  84.0 6.3 %copy.49 = f32[256,1,2128]{0,2,1:T(8,128)} copy(f32[256,1,2128]{2,1,0:T(1,128)} %all-to-all-done) | data formatting | bytes 4358144 | tf_op jit(solution)/shard_map/all_to_all | solution.py:119
  90.3 0.9 slice.148
  91.2 0.7 exponential_reduce_fusion
  91.9 4.9 %fusion.97 = (bf16[80,64,128]{2,1,0:T(8,128)(2,1)}, f32[80,64,128]{2,1,0:T(8,128)}) fusion(f32[80,64,128]{2,1,0:T(8,128)} %multiply_add_fusion.1, f32[80,64,128]{2,1,0:T(8,128)} %collective-permute-done.1, f32[80]{0:T(128)S(1)} %get-tuple-element.8), kind=kLoop, calls=%fused_computation.205 | loop fusion | flops 1966080 | bytes 9175360 | tf_op jit(solution)/shard_map/convert_element_type | solution.py:51
  96.8 4.3 %collective-permute-start.3 = (bf16[80,64,128]{2,1,0:T(8,128)(2,1)}, bf16[80,64,128]{2,1,0:T(8,128)(2,1)}, u32[]{:S(2)}, u32[]{:S(2)}) collective-permute-start(bf16[80,64,128]{2,1,0:T(8,128)(2,1)} %get-tuple-element.18), channel_id=1, source_target_pairs={{1,7},{3,1},{5,3},{7,5},{9,15},{11,9},{13,11},{15,13},{17,23},{19,... | collective-permute-start | bytes 3932168 | tf_op jit(solution)/shard_map/ppermute | solution.py:53
  101.1 1.9 collective-permute-start.2
  103.4 12.5 %collective-permute-done.3 = bf16[80,64,128]{2,1,0:T(8,128)(2,1)} collective-permute-done((bf16[80,64,128]{2,1,0:T(8,128)(2,1)}, bf16[80,64,128]{2,1,0:T(8,128)(2,1)}, u32[]{:S(2)}, u32[]{:S(2)}) %collective-permute-start.3) | collective-permute-done | bytes 1310752 | tf_op jit(solution)/shard_map/ppermute | solution.py:53
  115.9 1.1 slice.154
  117.0 5.0 %collective-permute-start.4 = (bf16[40,64,128]{2,1,0:T(8,128)(2,1)S(1)}, bf16[40,64,128]{2,1,0:T(8,128)(2,1)S(1)}, u32[]{:S(2)}, u32[]{:S(2)}) collective-permute-start(bf16[40,64,128]{2,1,0:T(8,128)(2,1)S(1)} %slice.154), channel_id=1, source_target_pairs={{1,7},{3,1},{5,3},{7,5},{9,15},{11,9},{13,11},{15,13},{17,23},{19,... | collective-permute-start | bytes 1966088 | tf_op jit(solution)/shard_map/ppermute | solution.py:54
  122.1 1.1 slice.155
  123.2 1.9 collective-permute-start.5
  125.7 0.6 fusion.59
  126.3 0.6 fusion.58
  126.9 2.7 collective-permute-done.4
  129.6 6.2 %collective-permute-done.5 = bf16[40,64,128]{2,1,0:T(8,128)(2,1)S(1)} collective-permute-done((bf16[40,64,128]{2,1,0:T(8,128)(2,1)S(1)}, bf16[40,64,128]{2,1,0:T(8,128)(2,1)S(1)}, u32[]{:S(2)}, u32[]{:S(2)}) %collective-permute-start.5) | collective-permute-done | bytes 655392 | tf_op jit(solution)/shard_map/ppermute | solution.py:55
  135.8 3.3 %fusion.25 = bf16[80,64,128]{2,1,0:T(8,128)(2,1)S(1)} fusion(bf16[80,64,128]{2,1,0:T(8,128)(2,1)} %collective-permute-done.3, bf16[80,64,128]{2,1,0:T(8,128)(2,1)} %collective-permute-done.2, f32[80,64,128]{2,1,0:T(8,128)S(1)} %copy-done.1, f32[80]{0:T(128)S(1)} %get-tuple-element.43, f32[80]{0:T(128)S(1)} %get-tuple-element.45, ...), kind=kLoop, calls=%fused_computation.50 | loop fusion | flops 7864320 | bytes 7865600 | tf_op jit(solution)/shard_map/convert_element_type | solution.py:51
  139.1 1.9 collective-permute-start.7
  141.1 3.4 %collective-permute-start.6 = (bf16[80,64,128]{2,1,0:T(8,128)(2,1)S(1)}, bf16[80,64,128]{2,1,0:T(8,128)(2,1)S(1)}, u32[]{:S(2)}, u32[]{:S(2)}) collective-permute-start(bf16[80,64,128]{2,1,0:T(8,128)(2,1)S(1)} %fusion.25), channel_id=1, source_target_pairs={{1,9},{3,11},{5,13},{7,15},{9,17},{11,19},{13,21},{15,23},{17,25},... | collective-permute-start | bytes 3932168 | tf_op jit(solution)/shard_map/ppermute | solution.py:52
  144.5 13.0 %collective-permute-done.7 = bf16[80,64,128]{2,1,0:T(8,128)(2,1)S(1)} collective-permute-done((bf16[80,64,128]{2,1,0:T(8,128)(2,1)S(1)}, bf16[80,64,128]{2,1,0:T(8,128)(2,1)S(1)}, u32[]{:S(2)}, u32[]{:S(2)}) %collective-permute-start.7) | collective-permute-done | bytes 1310752 | tf_op jit(solution)/shard_map/ppermute | solution.py:53
  157.5 1.1 copy-done.9
  158.5 0.9 slice.156
  159.4 3.1 %collective-permute-start.8 = (bf16[40,64,128]{2,1,0:T(8,128)(2,1)}, bf16[40,64,128]{2,1,0:T(8,128)(2,1)}, u32[]{:S(2)}, u32[]{:S(2)}) collective-permute-start(bf16[40,64,128]{2,1,0:T(8,128)(2,1)} %slice.156), channel_id=1, source_target_pairs={{1,25},{3,27},{5,29},{7,31},{9,1},{11,3},{13,5},{15,7},{17,9},{19,... | collective-permute-start | bytes 1966088 | tf_op jit(solution)/shard_map/ppermute | solution.py:54
  162.6 1.1 copy-done.10
  163.7 0.9 slice.157
  164.6 2.3 collective-permute-start.9
  167.1 3.9 %collective-permute-done.8 = bf16[40,64,128]{2,1,0:T(8,128)(2,1)} collective-permute-done((bf16[40,64,128]{2,1,0:T(8,128)(2,1)}, bf16[40,64,128]{2,1,0:T(8,128)(2,1)}, u32[]{:S(2)}, u32[]{:S(2)}) %collective-permute-start.8) | collective-permute-done | bytes 655392 | tf_op jit(solution)/shard_map/ppermute | solution.py:54
  171.1 6.4 %collective-permute-done.9 = bf16[40,64,128]{2,1,0:T(8,128)(2,1)} collective-permute-done((bf16[40,64,128]{2,1,0:T(8,128)(2,1)}, bf16[40,64,128]{2,1,0:T(8,128)(2,1)}, u32[]{:S(2)}, u32[]{:S(2)}) %collective-permute-start.9) | collective-permute-done | bytes 655392 | tf_op jit(solution)/shard_map/ppermute | solution.py:55
  177.5 7.6 %fusion.15 = f32[80,64,128]{2,1,0:T(8,128)} fusion(bf16[80,64,128]{2,1,0:T(8,128)(2,1)} %collective-permute-done.2, bf16[80,64,128]{2,1,0:T(8,128)(2,1)} %collective-permute-done.3, f32[80,64,128]{2,1,0:T(8,128)} %get-tuple-element.19, bf16[80,64,128]{2,1,0:T(8,128)(2,1)} %copy-done.9, bf16[80,64,128]{2,1,0:T(8,128)(2,1)} %copy-done.10, ...), kind=kLoop, calls=%fused_computation.37 | loop fusion | flops 20316160 | bytes 13111360 | tf_op jit(solution)/shard_map/add | solution.py:105
  185.0 2.9 collective-permute-start.10
  188.4 4.6 %fusion.7 = f32[80,64,128]{2,1,0:T(8,128)S(1)} fusion(bf16[128,80,64]{0,2,1:T(8,128)(2,1)} %bitcast.80, f32[80,128]{1,0:T(8,128)} %get-tuple-element.24, f32[80,128]{1,0:T(8,128)S(1)} %reduce_window_sum.17, f32[128,128]{1,0:T(8,128)S(1)} %fusion.51, pred[128,128]{1,0:T(8,128)(4,1)S(1)} %iota_compare_fusion), kind=kOutput, calls=%fused_computation.29 | convolution fusion | flops 174325760 | bytes 4096000 | tf_op jit(solution)/shard_map/hts,shp->thp/dot_general | solution.py:26
  193.1 4.1 %fusion.8 = f32[80,64,128]{2,1,0:T(8,128)} fusion(bf16[128,80,64]{0,2,1:T(8,128)(2,1)S(1)} %bitcast.82, f32[80,128]{1,0:T(8,128)S(1)} %copy-done.19, f32[80,128]{1,0:T(8,128)S(1)} %reduce_window_sum.18, f32[128,128]{1,0:T(8,128)S(1)} %fusion.48, pred[128,128]{1,0:T(8,128)(4,1)S(1)} %iota_compare_fusion), kind=kOutput, calls=%fused_computation.30 | convolution fusion | flops 174325760 | bytes 4096000 | tf_op jit(solution)/shard_map/hts,shp->thp/dot_general | solution.py:26
  197.2 3.0 add_select_fusion
  200.2 3.0 bitcast_add_fusion.1
  203.2 3.2 %copy.56 = f32[128,5120]{1,0:T(8,128)} copy(f32[128,5120]{0,1:T(8,128)} %bitcast.75) | data formatting | bytes 5242880 | tf_op jit(solution)/shard_map/concatenate | solution.py:203
  206.4 6.5 %bitcast_add_fusion = f32[128,80,64]{0,2,1:T(8,128)} fusion(f32[80,64,128]{2,1,0:T(8,128)} %fusion.8, f32[80,64,128]{2,1,0:T(8,128)} %copy-done.5, f32[80,64,128]{2,1,0:T(8,128)} %copy-done.4, f32[80]{0:T(128)S(1)} %copy-done.30, f32[128,80]{0,1:T(8,128)S(1)} %get-tuple-element.30, f32[80]{0:T(128)S(1)} %get-tuple-element.48, ...), kind=kOutput, calls=%fused_computation.40 | convolution fusion | flops 1009909760 | bytes 10560512 | tf_op jit(solution)/shard_map/tn,hpn->thp/dot_general | solution.py:199
  212.9 3.2 %copy.57 = f32[128,5120]{1,0:T(8,128)} copy(f32[128,5120]{0,1:T(8,128)} %bitcast.76) | data formatting | bytes 5242880 | tf_op jit(solution)/shard_map/concatenate | solution.py:203
  216.1 5.2 %multiply_reduce_fusion = (f32[256]{0:T(256)S(1)}, f32[256,5120]{1,0:T(8,128)S(1)}) fusion(bf16[1,256,5120]{2,1,0:T(8,128)(2,1)} %param.13, bf16[256,5376]{1,0:T(8,128)(2,1)S(1)} %multiply_convert_fusion, f32[5120]{0:T(1024)S(1)} %mul.394, f32[128,5120]{1,0:T(8,128)} %copy.57, f32[128,5120]{1,0:T(8,128)} %copy.56), kind=kLoop, calls=%fused_computation.10 | loop fusion | flops 15728384 | bytes 15750144 | tf_op jit(solution)/shard_map/reduce_sum | solution.py:206
  221.4 2.3 copy-done
  223.7 1.0 convert_reduce_fusion
  224.7 2.3 multiply_reduce_fusion.2
  227.0 1.5 broadcast_in_dim.140
  228.5 8.3 %all-to-all-start.1 = ((f32[256,8,256]{2,1,0:T(8,128)}), f32[256,8,256]{2,1,0:T(8,128)S(1)}, u32[]{:S(2)}, u32[]{:S(2)}) async-start(f32[256,8,256]{2,1,0:T(8,128)} %broadcast_in_dim.140), calls=%async_computation.1 | async-start | bytes 4194304 | tf_op jit(solution)/shard_map/all_to_all | solution.py:119
  236.8 3.0 %slice.160 = f32[256,2048]{0,1:T(8,128)} slice(f32[256,2128]{0,1:T(8,128)} %bitcast.78), slice={[0:256], [0:2048]} | slice | bytes 4194304 | tf_op jit(solution)/shard_map/slice | solution.py:190
  239.8 2.9 copy.58
  242.7 2.8 reshape.629
  245.5 4.7 %fusion.94 = bf16[1,256,5120]{2,1,0:T(8,128)(2,1)} fusion(f32[5120]{0:T(1024)S(1)} %copy-done.16, f32[256,5120]{1,0:T(8,128)} %copy-done, f32[256]{0:T(256)S(1)} %add_rsqrt_fusion), kind=kLoop, calls=%fused_computation.203 | loop fusion | flops 3932160 | bytes 7885824 | tf_op jit(solution)/shard_map/broadcast_in_dim | solution.py:219
  250.2 39.5 %all-to-all-done.1 = f32[256,8,256]{2,1,0:T(8,128)S(1)} async-done(((f32[256,8,256]{2,1,0:T(8,128)}), f32[256,8,256]{2,1,0:T(8,128)S(1)}, u32[]{:S(2)}, u32[]{:S(2)}) %all-to-all-start.1) | async-done | bytes 2097184 | tf_op jit(solution)/shard_map/all_to_all | solution.py:119
  289.7 2.4 multiply_reduce_fusion.1
  292.1 4.2 %fusion.6 = f32[8,4096]{1,0:T(8,128)} fusion(f32[8,256]{1,0:T(8,128)S(1)} %get-tuple-element.52, f32[2048,256]{1,0:T(8,128)S(1)} %copy-done.6, f32[2048,256]{1,0:T(8,128)S(1)} %bitcast.74, f32[4096]{0:T(1024)S(1)} %multiply_reduce_fusion.1, f32[8]{0:T(128)S(1)} %get-tuple-element.51), kind=kOutput, calls=%fused_computation.18 | convolution fusion | flops 101875712 | bytes 4349984 | tf_op jit(solution)/shard_map/dot_general | solution.py:214
  (90 shorter events, 3.4 us)
Async XLA Ops:
  12.6 16.6 %copy-start.2 = (bf16[1,256,5120]{2,1,0:T(8,128)(2,1)S(1)}, bf16[1,256,5120]{2,1,0:T(8,128)(2,1)}, u32[]{:S(2)}) copy-start(bf16[1,256,5120]{2,1,0:T(8,128)(2,1)} %param.12) | copy-start | bytes 7864324
  12.6 16.6 %copy-start.12 = (bf16[1,256,128]{2,1,0:T(8,128)(2,1)S(1)}, bf16[1,256,128]{2,1,0:T(8,128)(2,1)}, u32[]{:S(2)}) copy-start(bf16[1,256,128]{2,1,0:T(8,128)(2,1)} %param.15) | copy-start | bytes 196612
  12.6 16.6 %copy-start.13 = (bf16[1,256,128]{2,1,0:T(8,128)(2,1)S(1)}, bf16[1,256,128]{2,1,0:T(8,128)(2,1)}, u32[]{:S(2)}) copy-start(bf16[1,256,128]{2,1,0:T(8,128)(2,1)} %param.14) | copy-start | bytes 196612
  12.6 71.4 %all-to-all-start = ((f32[256,1,2128]{2,1,0:T(1,128)}), f32[256,1,2128]{2,1,0:T(1,128)}, u32[]{:S(2)}, u32[]{:S(2)}) async-start(f32[256,1,2128]{2,1,0:T(1,128)} %broadcast_in_dim.135), calls=%async_computation | async-start | bytes 4456448 | tf_op jit(solution)/shard_map/all_to_all | solution.py:119
  29.1 195.6 %all-gather.2.cloned.1.call-start = ((), (), s32[]{:S(2)}) async-start(), calls=%async_computation.2 | async-start | bytes 2949120 | tf_op jit(solution)/shard_map/all_gather | solution.py:143
  29.2 3.8 %copy-start.17 = (f32[1,80,256]{2,1,0:T(8,128)S(1)}, f32[1,80,256]{2,1,0:T(8,128)}, u32[]{:S(2)}) copy-start(f32[1,80,256]{2,1,0:T(8,128)} %param.16) | copy-start | bytes 245764
  29.2 4.5 %copy-start.15 = (f32[4,5376]{1,0:T(4,128)S(1)}, f32[4,5376]{1,0:T(4,128)}, u32[]{:S(2)}) copy-start(f32[4,5376]{1,0:T(4,128)} %param.18) | copy-start | bytes 258052
  29.4 4.6 %collective-permute-start = (bf16[3,5376]{1,0:T(4,128)(2,1)S(1)}, bf16[3,5376]{1,0:T(4,128)(2,1)S(1)}, u32[]{:S(2)}, u32[]{:S(2)}) collective-permute-start(bf16[3,5376]{1,0:T(4,128)(2,1)S(1)} %slice.136), channel_id=1, source_target_pairs={{0,1},{1,2},{2,3},{3,4},{4,5},{5,6},{6,7},{7,8},{8,9},{9,10},{10,1... | collective-permute-start | bytes 96776 | tf_op jit(solution)/shard_map/ppermute | solution.py:16
  33.9 2.6 copy-start.3
  33.9 2.6 copy-start.20
  47.6 4.0 %copy-start.7 = (bf16[128,5120]{0,1:T(8,128)(2,1)S(1)}, bf16[128,5120]{0,1:T(8,128)(2,1)}, u32[]{:S(2)}) copy-start(bf16[128,5120]{0,1:T(8,128)(2,1)} %copy.51) | copy-start | bytes 3932164
  51.5 4.3 %copy-start.4 = (f32[80,64,128]{2,1,0:T(8,128)}, f32[80,64,128]{2,1,0:T(8,128)S(1)}, u32[]{:S(2)}) copy-start(f32[80,64,128]{2,1,0:T(8,128)S(1)} %fusion.16) | copy-start | bytes 7864324
  55.8 36.0 %collective-permute-start.1 = (f32[80,64,128]{2,1,0:T(8,128)}, f32[80,64,128]{2,1,0:T(8,128)}, u32[]{:S(2)}, u32[]{:S(2)}) collective-permute-start(f32[80,64,128]{2,1,0:T(8,128)} %multiply_add_fusion.1), channel_id=1, source_target_pairs={{0,1},{2,3},{4,5},{6,7},{8,9},{10,11},{12,13},{14,15},{16,17},{18,... | collective-permute-start | bytes 7864328 | tf_op jit(solution)/shard_map/ppermute | solution.py:98
  96.8 19.2 %collective-permute-start.3 = (bf16[80,64,128]{2,1,0:T(8,128)(2,1)}, bf16[80,64,128]{2,1,0:T(8,128)(2,1)}, u32[]{:S(2)}, u32[]{:S(2)}) collective-permute-start(bf16[80,64,128]{2,1,0:T(8,128)(2,1)} %get-tuple-element.18), channel_id=1, source_target_pairs={{1,7},{3,1},{5,3},{7,5},{9,15},{11,9},{13,11},{15,13},{17,23},{19,... | collective-permute-start | bytes 3932168 | tf_op jit(solution)/shard_map/ppermute | solution.py:53
  101.1 21.0 %collective-permute-start.2 = (bf16[80,64,128]{2,1,0:T(8,128)(2,1)}, bf16[80,64,128]{2,1,0:T(8,128)(2,1)}, u32[]{:S(2)}, u32[]{:S(2)}) collective-permute-start(bf16[80,64,128]{2,1,0:T(8,128)(2,1)} %get-tuple-element.18), channel_id=1, source_target_pairs={{1,3},{3,5},{5,7},{7,1},{9,11},{11,13},{13,15},{15,9},{17,19},{19,... | collective-permute-start | bytes 3932168 | tf_op jit(solution)/shard_map/ppermute | solution.py:52
  103.4 32.4 %copy-start.1 = (f32[80,64,128]{2,1,0:T(8,128)S(1)}, f32[80,64,128]{2,1,0:T(8,128)}, u32[]{:S(2)}) copy-start(f32[80,64,128]{2,1,0:T(8,128)} %get-tuple-element.19) | copy-start | bytes 7864324
  117.0 12.5 %collective-permute-start.4 = (bf16[40,64,128]{2,1,0:T(8,128)(2,1)S(1)}, bf16[40,64,128]{2,1,0:T(8,128)(2,1)S(1)}, u32[]{:S(2)}, u32[]{:S(2)}) collective-permute-start(bf16[40,64,128]{2,1,0:T(8,128)(2,1)S(1)} %slice.154), channel_id=1, source_target_pairs={{1,7},{3,1},{5,3},{7,5},{9,15},{11,9},{13,11},{15,13},{17,23},{19,... | collective-permute-start | bytes 1966088 | tf_op jit(solution)/shard_map/ppermute | solution.py:54
  123.2 12.5 %collective-permute-start.5 = (bf16[40,64,128]{2,1,0:T(8,128)(2,1)S(1)}, bf16[40,64,128]{2,1,0:T(8,128)(2,1)S(1)}, u32[]{:S(2)}, u32[]{:S(2)}) collective-permute-start(bf16[40,64,128]{2,1,0:T(8,128)(2,1)S(1)} %slice.155), channel_id=1, source_target_pairs={{1,3},{3,5},{5,7},{7,1},{9,11},{11,13},{13,15},{15,9},{17,19},{19,... | collective-permute-start | bytes 1966088 | tf_op jit(solution)/shard_map/ppermute | solution.py:55
  126.3 12.8 %copy-start.21 = (f32[80]{0:T(128)}, f32[80]{0:T(128)S(1)}, u32[]{:S(2)}) copy-start(f32[80]{0:T(128)S(1)} %get-tuple-element.38) | copy-start | bytes 964
  126.3 12.8 %copy-start.23 = (f32[80]{0:T(128)}, f32[80]{0:T(128)S(1)}, u32[]{:S(2)}) copy-start(f32[80]{0:T(128)S(1)} %get-tuple-element.45) | copy-start | bytes 964
  126.9 12.2 %copy-start.25 = (f32[80]{0:T(128)}, f32[80]{0:T(128)S(1)}, u32[]{:S(2)}) copy-start(f32[80]{0:T(128)S(1)} %get-tuple-element.36) | copy-start | bytes 964
  126.9 12.2 %copy-start.27 = (f32[80]{0:T(128)}, f32[80]{0:T(128)S(1)}, u32[]{:S(2)}) copy-start(f32[80]{0:T(128)S(1)} %get-tuple-element.43) | copy-start | bytes 964
  135.8 3.3 %copy-start.11 = (bf16[40,64,128]{2,1,0:T(8,128)(2,1)}, bf16[40,64,128]{2,1,0:T(8,128)(2,1)S(1)}, u32[]{:S(2)}) copy-start(bf16[40,64,128]{2,1,0:T(8,128)(2,1)S(1)} %collective-permute-done.5) | copy-start | bytes 1966084
  139.1 18.4 %collective-permute-start.7 = (bf16[80,64,128]{2,1,0:T(8,128)(2,1)S(1)}, bf16[80,64,128]{2,1,0:T(8,128)(2,1)S(1)}, u32[]{:S(2)}, u32[]{:S(2)}) collective-permute-start(bf16[80,64,128]{2,1,0:T(8,128)(2,1)S(1)} %fusion.25), channel_id=1, source_target_pairs={{1,25},{3,27},{5,29},{7,31},{9,1},{11,3},{13,5},{15,7},{17,9},{19,... | collective-permute-start | bytes 3932168 | tf_op jit(solution)/shard_map/ppermute | solution.py:53
  141.1 36.4 %copy-start.22 = (f32[80]{0:T(128)S(1)}, f32[80]{0:T(128)}, u32[]{:S(2)}) copy-start(f32[80]{0:T(128)} %copy-done.21) | copy-start | bytes 964
  141.1 36.4 %copy-start.24 = (f32[80]{0:T(128)S(1)}, f32[80]{0:T(128)}, u32[]{:S(2)}) copy-start(f32[80]{0:T(128)} %copy-done.23) | copy-start | bytes 964
  141.1 36.4 %copy-start.26 = (f32[80]{0:T(128)S(1)}, f32[80]{0:T(128)}, u32[]{:S(2)}) copy-start(f32[80]{0:T(128)} %copy-done.25) | copy-start | bytes 964
  141.1 36.4 %copy-start.28 = (f32[80]{0:T(128)S(1)}, f32[80]{0:T(128)}, u32[]{:S(2)}) copy-start(f32[80]{0:T(128)} %copy-done.27) | copy-start | bytes 964
  141.1 21.5 %collective-permute-start.6 = (bf16[80,64,128]{2,1,0:T(8,128)(2,1)S(1)}, bf16[80,64,128]{2,1,0:T(8,128)(2,1)S(1)}, u32[]{:S(2)}, u32[]{:S(2)}) collective-permute-start(bf16[80,64,128]{2,1,0:T(8,128)(2,1)S(1)} %fusion.25), channel_id=1, source_target_pairs={{1,9},{3,11},{5,13},{7,15},{9,17},{11,19},{13,21},{15,23},{17,25},... | collective-permute-start | bytes 3932168 | tf_op jit(solution)/shard_map/ppermute | solution.py:52
  157.5 1.1 copy-start.9
  159.4 11.6 %collective-permute-start.8 = (bf16[40,64,128]{2,1,0:T(8,128)(2,1)}, bf16[40,64,128]{2,1,0:T(8,128)(2,1)}, u32[]{:S(2)}, u32[]{:S(2)}) collective-permute-start(bf16[40,64,128]{2,1,0:T(8,128)(2,1)} %slice.156), channel_id=1, source_target_pairs={{1,25},{3,27},{5,29},{7,31},{9,1},{11,3},{13,5},{15,7},{17,9},{19,... | collective-permute-start | bytes 1966088 | tf_op jit(solution)/shard_map/ppermute | solution.py:54
  162.6 1.1 copy-start.10
  164.6 12.8 %collective-permute-start.9 = (bf16[40,64,128]{2,1,0:T(8,128)(2,1)}, bf16[40,64,128]{2,1,0:T(8,128)(2,1)}, u32[]{:S(2)}, u32[]{:S(2)}) collective-permute-start(bf16[40,64,128]{2,1,0:T(8,128)(2,1)} %slice.157), channel_id=1, source_target_pairs={{1,9},{3,11},{5,13},{7,15},{9,17},{11,19},{13,21},{15,23},{17,25},... | collective-permute-start | bytes 1966088 | tf_op jit(solution)/shard_map/ppermute | solution.py:55
  177.5 10.5 %copy-start.31 = (f32[80]{0:T(128)S(1)}, f32[80]{0:T(128)}, u32[]{:S(2)}) copy-start(f32[80]{0:T(128)} %param.20) | copy-start | bytes 964
  185.0 12.1 %collective-permute-start.10 = (f32[80,64,128]{2,1,0:T(8,128)}, f32[80,64,128]{2,1,0:T(8,128)}, u32[]{:S(2)}, u32[]{:S(2)}) collective-permute-start(f32[80,64,128]{2,1,0:T(8,128)} %fusion.15), channel_id=1, source_target_pairs={{1,0},{3,2},{5,4},{7,6},{9,8},{11,10},{13,12},{15,14},{17,16},{19,... | collective-permute-start | bytes 7864328 | tf_op jit(solution)/shard_map/ppermute | solution.py:106
  188.4 4.7 %copy-start.8 = (bf16[128,5120]{0,1:T(8,128)(2,1)S(1)}, bf16[128,5120]{0,1:T(8,128)(2,1)}, u32[]{:S(2)}) copy-start(bf16[128,5120]{0,1:T(8,128)(2,1)} %copy.51) | copy-start | bytes 3932164
  188.4 4.7 %copy-start.19 = (f32[80,128]{1,0:T(8,128)S(1)}, f32[80,128]{1,0:T(8,128)}, u32[]{:S(2)}) copy-start(f32[80,128]{1,0:T(8,128)} %get-tuple-element.27) | copy-start | bytes 122884
  193.1 4.1 %copy-start.29 = (f32[80]{0:T(128)S(1)}, f32[80]{0:T(128)}, u32[]{:S(2)}) copy-start(f32[80]{0:T(128)} %get-tuple-element.7) | copy-start | bytes 964
  197.2 3.0 copy-start.14
  200.2 3.0 copy-start.5
  203.2 3.2 %copy-start.30 = (f32[80]{0:T(128)S(1)}, f32[80]{0:T(128)}, u32[]{:S(2)}) copy-start(f32[80]{0:T(128)} %get-tuple-element.47) | copy-start | bytes 964
  216.1 7.6 %copy-start.16 = (f32[5120]{0:T(1024)S(1)}, f32[5120]{0:T(1024)}, u32[]{:S(2)}) copy-start(f32[5120]{0:T(1024)} %param.21) | copy-start | bytes 61444
  221.4 2.3 copy-start
  227.0 65.1 %copy-start.18 = (f32[8,256]{1,0:T(8,128)}, f32[8,256]{1,0:T(8,128)S(1)}, u32[]{:S(2)}) copy-start(f32[8,256]{1,0:T(8,128)S(1)} %get-tuple-element.52) | copy-start | bytes 24580
  228.5 61.2 %all-to-all-start.1 = ((f32[256,8,256]{2,1,0:T(8,128)}), f32[256,8,256]{2,1,0:T(8,128)S(1)}, u32[]{:S(2)}, u32[]{:S(2)}) async-start(f32[256,8,256]{2,1,0:T(8,128)} %broadcast_in_dim.140), calls=%async_computation.1 | async-start | bytes 4194304 | tf_op jit(solution)/shard_map/all_to_all | solution.py:119
  289.7 2.4 copy-start.6
Sparse Core Ops, SparseCore 0:
  188.1 31.2 all-gather.1

commit v4 on v3

--- a/solution.py
+++ b/solution.py
@@ -113,11 +113,20 @@
     return lax.dynamic_update_index_in_dim(held, block, index, 0)
 
 
-def everywhere(block):
-    count = lax.axis_size("dp") * lax.axis_size("seq")
-    spread = jnp.broadcast_to(block[None], (count,) + block.shape)
-    got = lax.all_to_all(spread, ("dp", "seq"), 0, 0)
-    return got.reshape((count * block.shape[0],) + block.shape[1:])
+def spread_over(block, axis):
+    count = lax.axis_size(axis)
+    return lax.all_to_all(jnp.broadcast_to(block[None], (count,) + block.shape), axis, 0, 0)
+
+
+def prior_everywhere(block):
+    rows = spread_over(block, "seq").reshape((-1,) + block.shape[1:])
+    return lax.all_gather(rows, "dp", axis=0, tiled=True)
+
+
+def codes_everywhere(block):
+    rows = lax.all_gather(block, "dp", axis=0, tiled=False)
+    got = spread_over(rows, "seq")
+    return jnp.swapaxes(got, 0, 1).reshape((-1,) + block.shape[1:])
 
 
 def per_device(
@@ -182,14 +191,10 @@
         block_total = cum_list[block][:, -1]
         running = jnp.exp(block_total)[:, None, None] * running + state_list[block]
         before = before + block_total
-    seq = lax.axis_size("seq")
-    code_dim = prior_draw.shape[1]
-    prior_size = prior_draw.shape[0] * code_dim
-    shared = everywhere(jnp.concatenate([prior_draw.reshape(-1), before]))
-    shared = shared.reshape(-1, prior_size + heads)
-    all_prior = shared[:, :prior_size].reshape(-1, code_dim)
-    shard_logs = lax.dynamic_slice_in_dim(shared[:, prior_size:], lax.axis_index("dp") * seq, seq, 0)
+    all_prior = prior_everywhere(prior_draw)
+    shard_logs = spread_over(before, "seq")
     carry_in = carried_in(running, shard_logs)
+    all_prior, carry_in = lax.optimization_barrier((all_prior, carry_in))
     outputs = []
     for block in range(blocks):
         lower = block * SPAN
@@ -209,12 +214,13 @@
         jnp.bfloat16
     )
     codes_local = jnp.dot(pooled, full_code_weight, preferred_element_type=jnp.float32)
-    all_codes = everywhere(codes_local)
+    all_codes = codes_everywhere(codes_local)
     columns = jnp.concatenate([all_codes, all_prior], axis=0)
     cross = jnp.dot(codes_local, columns.T, precision=lax.Precision.HIGHEST)
     row_sq = jnp.sum(codes_local * codes_local, axis=1)
     col_sq = jnp.sum(columns * columns, axis=1)
     dist_sq = row_sq[:, None] + col_sq[None, :] - 2.0 * cross
+    code_dim = codes_local.shape[1]
     kernel = 2.0 * code_dim / (2.0 * code_dim + dist_sq)
     return (mixed[None], codes_local, kernel)
 

time: 304 us -> 276 us (0.908)
  waiting for transfers between devices: 111 us -> 74.1 us
  blocking collectives: 0 us -> 21.7 us
  local copies, waits for them, and re-layouts: 44.7 us -> 29.7 us
    all_to_all x2 -> x3, waiting for transfers between devices: 66.4 us -> 30.7 us  [spread_over(): lax.all_to_all(jnp.broadcast_to(block[None], (count,) + block.shape), axi...]
    all_gather x0 -> x1, blocking collectives: none -> 21.7 us  [codes_everywhere(): rows = lax.all_gather(block, 'dp', axis=0, tiled=False)]
    slice x3 -> x0, local copies, waits for them, and re-layouts: 6.82 us -> none  [the longest x2 5.93 us: per_device(): all_prior = shared[:, :prior_size].reshape(-1, code_dim)]
    all_to_all x1, local copies, waits for them, and re-layouts: 6.25 us -> 1.93 us  [spread_over(): lax.all_to_all(jnp.broadcast_to(block[None], (count,) + block.shape), axi...]
    all_to_all x2 -> x3, starting transfers between devices: 24.8 us -> 23.2 us  [spread_over(): lax.all_to_all(jnp.broadcast_to(block[None], (count,) + block.shape), axi...]
  transfers between devices with their start and end apart: 14 -> 16, of which waited for: 9 -> 8; matrix products, arithmetic and copies ran while one was open for 28% -> 24% of each run, Pallas kernels for 0% -> 0%
where the time goes in v4:
time: 276 us; the launch traced here: 275 us
  waiting for transfers between devices  74.1 us (27%)
  starting transfers between devices  54.3 us (20%)
  other arithmetic  44.6 us (16%)
  matrix products  35.4 us (13%)
  local copies, waits for them, and re-layouts  29.7 us (11%)
  blocking collectives  21.7 us (8%)
  between operations  15 us (5%)
    all_to_all x3, waiting for transfers between devices, spread_over(): lax.all_to_all(jnp.broadcast_to(block[None], (count,) + block.shape), axi...  30.7 us
    ppermute x2, waiting for transfers between devices, ring_of_four(): next_state = lax.ppermute(sent, 'seq', bwd)  23.7 us
    all_to_all x3, starting transfers between devices, spread_over(): lax.all_to_all(jnp.broadcast_to(block[None], (count,) + block.shape), axi...  23.2 us
    all_gather x1, blocking collectives, codes_everywhere(): rows = lax.all_gather(block, 'dp', axis=0, tiled=False)  21.7 us
    ppermute x2, waiting for transfers between devices, ring_of_four(): far_b = lax.ppermute(prev_state[half:], 'seq', fwd)  14 us
    dot_general x2, matrix products, per_device(): jnp.einsum('tn,hpn->thp', read_block, start, precision=lax.Precision.HIGH...  11.8 us
    dot_general x2, matrix products, block_terms(): jnp.einsum('hts,shp->thp', mixing, values, preferred_element_type=jnp.flo...  8.55 us
    convert_element_type x2, other arithmetic, ring_of_four(): sent = state.astype(XFER)  8.5 us
  transfers between devices with their start and end apart: 16, of which 8 were waited for; matrix products, arithmetic and copies ran while one was open for 24% of the time, Pallas kernels for 0%

profile of v4, /device:TPU:1, one launch (start us, length us, event | category | flops | bytes accessed | tf_op | source)
XLA Modules:
  0.0 274.9 jit_solution(4578410870770445581)
XLA Ops:
  7.2 2.1 pad_maximum_fusion.2
  9.4 4.6 %collective-permute-start = (bf16[3,5376]{1,0:T(4,128)(2,1)S(1)}, bf16[3,5376]{1,0:T(4,128)(2,1)S(1)}, u32[]{:S(2)}, u32[]{:S(2)}) collective-permute-start(bf16[3,5376]{1,0:T(4,128)(2,1)S(1)} %slice.128), channel_id=1, source_target_pairs={{0,1},{1,2},{2,3},{3,4},{4,5},{5,6},{6,7},{7,8},{8,9},{9,10},{10,1... | collective-permute-start | bytes 96776 | tf_op jit(solution)/shard_map/ppermute | solution.py:16
  14.8 0.5 fusion.105
  15.3 0.7 fusion.103
  16.3 2.4 maximum_maximum_fusion
  18.7 4.4 %multiply_convert_fusion = bf16[256,5376]{1,0:T(8,128)(2,1)S(1)} fusion(bf16[259,5376]{1,0:T(8,128)(2,1)S(1)} %maximum_maximum_fusion, f32[5376]{0:T(1024)S(1)} %get-tuple-element.9, f32[5376]{0:T(1024)S(1)} %get-tuple-element.10, f32[5376]{0:T(1024)S(1)} %get-tuple-element.8, f32[5376]{0:T(1024)S(1)} %get-tuple-element.7, f32[5376]{0:T(1024)S(1)} %copy-done.18, ...), kind=kLoop, calls=%fused_computation.2 | loop fusion | flops 30277632 | bytes 13870080 | tf_op jit(solution)/shard_map/convert_element_type | solution.py:161
  23.1 1.8 fusion.102
  24.9 2.4 copy.39
  27.4 2.4 copy.40
  29.8 3.9 %fusion.16 = f32[80,64,128]{2,1,0:T(8,128)S(1)} fusion(bf16[128,80,64]{0,2,1:T(8,128)(2,1)} %bitcast.82, f32[128,128]{1,0:T(8,128)S(1)} %get-tuple-element.23, f32[80,128]{1,0:T(8,128)S(1)} %get-tuple-element.27), kind=kOutput, calls=%fused_computation.38 | convolution fusion | flops 170393600 | bytes 4038656 | tf_op jit(solution)/shard_map/hsn,shp->hpn/dot_general | solution.py:29
  33.8 4.3 %multiply_add_fusion.1 = f32[80,64,128]{2,1,0:T(8,128)} fusion(f32[80,64,128]{2,1,0:T(8,128)S(1)} %fusion.16, bf16[128,80,64]{0,2,1:T(8,128)(2,1)S(1)} %bitcast.84, f32[128,128]{1,0:T(8,128)S(1)} %get-tuple-element.22, f32[80,128]{1,0:T(8,128)S(1)} %get-tuple-element.28, f32[80]{0:T(128)S(1)} %get-tuple-element.52, f32[80]{0:T(128)S(1)} %get-tuple-element.54), kind=kOutput, calls=%fused_computation.54 | convolution fusion | flops 172359680 | bytes 6660736 | tf_op jit(solution)/shard_map/hsn,shp->hpn/dot_general | solution.py:29
  38.0 1.3 collective-permute-start.1
  39.3 0.6 broadcast_in_dim.142
  39.9 9.5 %all-to-all-start.1 = ((f32[32,1,80]{2,1,0:T(1,128)}), f32[32,1,80]{2,1,0:T(1,128)S(1)}, u32[]{:S(2)}, u32[]{:S(2)}) async-start(f32[32,1,80]{2,1,0:T(1,128)} %broadcast_in_dim.142), calls=%async_computation.1 | async-start | bytes 32768 | tf_op jit(solution)/shard_map/all_to_all | solution.py:118
  49.4 7.0 %all-to-all-done.1 = f32[32,1,80]{2,1,0:T(1,128)S(1)} async-done(((f32[32,1,80]{2,1,0:T(1,128)}), f32[32,1,80]{2,1,0:T(1,128)S(1)}, u32[]{:S(2)}, u32[]{:S(2)}) %all-to-all-start.1) | async-done | bytes 10272 | tf_op jit(solution)/shard_map/all_to_all | solution.py:118
  56.4 0.5 fusion.93
  56.9 4.9 %fusion.101 = (bf16[80,64,128]{2,1,0:T(8,128)(2,1)}, f32[80,64,128]{2,1,0:T(8,128)}) fusion(f32[80,64,128]{2,1,0:T(8,128)} %multiply_add_fusion.1, f32[80,64,128]{2,1,0:T(8,128)} %collective-permute-done.1, f32[80]{0:T(128)S(1)} %get-tuple-element.35), kind=kLoop, calls=%fused_computation.207 | loop fusion | flops 1966080 | bytes 9175360 | tf_op jit(solution)/shard_map/convert_element_type | solution.py:51
  61.9 2.8 %collective-permute-start.3 = (bf16[80,64,128]{2,1,0:T(8,128)(2,1)}, bf16[80,64,128]{2,1,0:T(8,128)(2,1)}, u32[]{:S(2)}, u32[]{:S(2)}) collective-permute-start(bf16[80,64,128]{2,1,0:T(8,128)(2,1)} %get-tuple-element.20), channel_id=1, source_target_pairs={{1,7},{3,1},{5,3},{7,5},{9,15},{11,9},{13,11},{15,13},{17,23},{19,... | collective-permute-start | bytes 3932168 | tf_op jit(solution)/shard_map/ppermute | solution.py:53
  64.7 2.5 collective-permute-start.2
  67.2 0.7 broadcast_in_dim.141
  67.9 4.6 %all-to-all-start = ((f32[32,8,256]{2,1,0:T(8,128)}), f32[32,8,256]{2,1,0:T(8,128)}, u32[]{:S(2)}, u32[]{:S(2)}) async-start(f32[32,8,256]{2,1,0:T(8,128)} %broadcast_in_dim.141), calls=%async_computation | async-start | bytes 524288 | tf_op jit(solution)/shard_map/all_to_all | solution.py:118
  72.8 10.2 %collective-permute-done.3 = bf16[80,64,128]{2,1,0:T(8,128)(2,1)} collective-permute-done((bf16[80,64,128]{2,1,0:T(8,128)(2,1)}, bf16[80,64,128]{2,1,0:T(8,128)(2,1)}, u32[]{:S(2)}, u32[]{:S(2)}) %collective-permute-start.3) | collective-permute-done | bytes 1310752 | tf_op jit(solution)/shard_map/ppermute | solution.py:53
  83.0 2.0 slice.145
  85.0 4.0 %collective-permute-start.4 = (bf16[40,64,128]{2,1,0:T(8,128)(2,1)}, bf16[40,64,128]{2,1,0:T(8,128)(2,1)S(1)}, u32[]{:S(2)}, u32[]{:S(2)}) collective-permute-start(bf16[40,64,128]{2,1,0:T(8,128)(2,1)} %slice.145), channel_id=1, source_target_pairs={{1,7},{3,1},{5,3},{7,5},{9,15},{11,9},{13,11},{15,13},{17,23},{19,... | collective-permute-start | bytes 1966088 | tf_op jit(solution)/shard_map/ppermute | solution.py:54
  89.0 2.0 slice.146
  91.0 1.9 collective-permute-start.5
  92.9 0.6 exponential_bitcast_fusion.2
  93.5 0.6 fusion.59
  94.1 0.6 fusion.58
  94.8 2.0 collective-permute-done.4
  96.8 7.0 %collective-permute-done.5 = bf16[40,64,128]{2,1,0:T(8,128)(2,1)} collective-permute-done((bf16[40,64,128]{2,1,0:T(8,128)(2,1)}, bf16[40,64,128]{2,1,0:T(8,128)(2,1)}, u32[]{:S(2)}, u32[]{:S(2)}) %collective-permute-start.5) | collective-permute-done | bytes 655392 | tf_op jit(solution)/shard_map/ppermute | solution.py:55
  103.8 3.6 %fusion.25 = bf16[80,64,128]{2,1,0:T(8,128)(2,1)S(1)} fusion(bf16[80,64,128]{2,1,0:T(8,128)(2,1)} %collective-permute-done.3, bf16[80,64,128]{2,1,0:T(8,128)(2,1)} %collective-permute-done.2, f32[80,64,128]{2,1,0:T(8,128)} %get-tuple-element.21, f32[80]{0:T(128)} %get-tuple-element.47, f32[80]{0:T(128)} %get-tuple-element.49, f32[80]{0:T(128)} %get-tuple-element.42, ...), kind=kLoop, calls=%fused_computation.50 | loop fusion | flops 7864320 | bytes 7865600 | tf_op jit(solution)/shard_map/convert_element_type | solution.py:51
  107.4 2.8 %collective-permute-start.7 = (bf16[80,64,128]{2,1,0:T(8,128)(2,1)S(1)}, bf16[80,64,128]{2,1,0:T(8,128)(2,1)S(1)}, u32[]{:S(2)}, u32[]{:S(2)}) collective-permute-start(bf16[80,64,128]{2,1,0:T(8,128)(2,1)S(1)} %fusion.25), channel_id=1, source_target_pairs={{1,25},{3,27},{5,29},{7,31},{9,1},{11,3},{13,5},{15,7},{17,9},{19,... | collective-permute-start | bytes 3932168 | tf_op jit(solution)/shard_map/ppermute | solution.py:53
  110.2 2.5 collective-permute-start.6
  112.7 13.5 %collective-permute-done.7 = bf16[80,64,128]{2,1,0:T(8,128)(2,1)S(1)} collective-permute-done((bf16[80,64,128]{2,1,0:T(8,128)(2,1)S(1)}, bf16[80,64,128]{2,1,0:T(8,128)(2,1)S(1)}, u32[]{:S(2)}, u32[]{:S(2)}) %collective-permute-start.7) | collective-permute-done | bytes 1310752 | tf_op jit(solution)/shard_map/ppermute | solution.py:53
  126.2 1.1 copy-done.7
  127.2 0.9 slice.147
  128.1 4.0 %collective-permute-start.8 = (bf16[40,64,128]{2,1,0:T(8,128)(2,1)}, bf16[40,64,128]{2,1,0:T(8,128)(2,1)}, u32[]{:S(2)}, u32[]{:S(2)}) collective-permute-start(bf16[40,64,128]{2,1,0:T(8,128)(2,1)} %slice.147), channel_id=1, source_target_pairs={{1,25},{3,27},{5,29},{7,31},{9,1},{11,3},{13,5},{15,7},{17,9},{19,... | collective-permute-start | bytes 1966088 | tf_op jit(solution)/shard_map/ppermute | solution.py:54
  132.1 1.1 copy-done.8
  133.2 0.9 slice.148
  134.1 1.9 collective-permute-start.9
  136.2 3.7 %collective-permute-done.8 = bf16[40,64,128]{2,1,0:T(8,128)(2,1)} collective-permute-done((bf16[40,64,128]{2,1,0:T(8,128)(2,1)}, bf16[40,64,128]{2,1,0:T(8,128)(2,1)}, u32[]{:S(2)}, u32[]{:S(2)}) %collective-permute-start.8) | collective-permute-done | bytes 655392 | tf_op jit(solution)/shard_map/ppermute | solution.py:54
  139.9 7.0 %collective-permute-done.9 = bf16[40,64,128]{2,1,0:T(8,128)(2,1)} collective-permute-done((bf16[40,64,128]{2,1,0:T(8,128)(2,1)}, bf16[40,64,128]{2,1,0:T(8,128)(2,1)}, u32[]{:S(2)}, u32[]{:S(2)}) %collective-permute-start.9) | collective-permute-done | bytes 655392 | tf_op jit(solution)/shard_map/ppermute | solution.py:55
  146.9 7.6 %fusion.15 = f32[80,64,128]{2,1,0:T(8,128)} fusion(bf16[80,64,128]{2,1,0:T(8,128)(2,1)} %collective-permute-done.2, bf16[80,64,128]{2,1,0:T(8,128)(2,1)} %collective-permute-done.3, f32[80,64,128]{2,1,0:T(8,128)} %get-tuple-element.21, bf16[80,64,128]{2,1,0:T(8,128)(2,1)} %copy-done.7, bf16[80,64,128]{2,1,0:T(8,128)(2,1)} %copy-done.8, ...), kind=kLoop, calls=%fused_computation.37 | loop fusion | flops 20316160 | bytes 13111360 | tf_op jit(solution)/shard_map/add | solution.py:105
  154.5 2.8 %collective-permute-start.10 = (f32[80,64,128]{2,1,0:T(8,128)}, f32[80,64,128]{2,1,0:T(8,128)}, u32[]{:S(2)}, u32[]{:S(2)}) collective-permute-start(f32[80,64,128]{2,1,0:T(8,128)} %fusion.15), channel_id=1, source_target_pairs={{1,0},{3,2},{5,4},{7,6},{9,8},{11,10},{13,12},{15,14},{17,16},{19,... | collective-permute-start | bytes 7864328 | tf_op jit(solution)/shard_map/ppermute | solution.py:106
  157.8 4.5 %fusion.7 = f32[80,64,128]{2,1,0:T(8,128)} fusion(bf16[128,80,64]{0,2,1:T(8,128)(2,1)} %bitcast.83, f32[80,128]{1,0:T(8,128)} %get-tuple-element.26, f32[80,128]{1,0:T(8,128)S(1)} %reduce_window_sum.17, f32[128,128]{1,0:T(8,128)S(1)} %fusion.51, pred[128,128]{1,0:T(8,128)(4,1)S(1)} %iota_compare_fusion), kind=kOutput, calls=%fused_computation.29 | convolution fusion | flops 174325760 | bytes 4096000 | tf_op jit(solution)/shard_map/hts,shp->thp/dot_general | solution.py:26
  162.3 4.1 %fusion.8 = f32[80,64,128]{2,1,0:T(8,128)} fusion(bf16[128,80,64]{0,2,1:T(8,128)(2,1)S(1)} %bitcast.85, f32[80,128]{1,0:T(8,128)S(1)} %copy-done.17, f32[80,128]{1,0:T(8,128)S(1)} %reduce_window_sum.18, f32[128,128]{1,0:T(8,128)S(1)} %fusion.48, pred[128,128]{1,0:T(8,128)(4,1)S(1)} %iota_compare_fusion), kind=kOutput, calls=%fused_computation.30 | convolution fusion | flops 174325760 | bytes 4096000 | tf_op jit(solution)/shard_map/hts,shp->thp/dot_general | solution.py:26
  166.4 4.4 %add_select_fusion = f32[80,64,128]{2,1,0:T(8,128)} fusion(f32[80,64,128]{2,1,0:T(8,128)} %collective-permute-done.10, f32[80,64,128]{2,1,0:T(8,128)} %collective-permute-done.1, f32[80,64,128]{2,1,0:T(8,128)} %fusion.15, f32[80]{0:T(128)S(1)} %copy-done.25, pred[]{:T(512)S(6)} %eq.14), kind=kLoop, calls=%fused_computation.49 | loop fusion | flops 1966080 | bytes 10486081 | tf_op jit(solution)/shard_map/jit(_where)/select_n | solution.py:108
  170.8 5.4 %bitcast_add_fusion.1 = f32[128,80,64]{0,2,1:T(8,128)} fusion(f32[80,64,128]{2,1,0:T(8,128)} %fusion.7, f32[80,64,128]{2,1,0:T(8,128)} %add_select_fusion, f32[128,80]{0,1:T(8,128)S(1)} %copy-done.11, bf16[256,5376]{1,0:T(8,128)(2,1)S(1)} %multiply_convert_fusion), kind=kOutput, calls=%fused_computation.41 | convolution fusion | flops 1007943680 | bytes 7938048 | tf_op jit(solution)/shard_map/tn,hpn->thp/dot_general | solution.py:204
  176.2 3.3 %copy.45 = f32[128,5120]{1,0:T(8,128)} copy(f32[128,5120]{0,1:T(8,128)} %bitcast.80) | data formatting | bytes 5242880 | tf_op jit(solution)/shard_map/concatenate | solution.py:208
  179.5 6.5 %bitcast_add_fusion = f32[128,80,64]{0,2,1:T(8,128)} fusion(f32[80,64,128]{2,1,0:T(8,128)} %fusion.8, f32[80,64,128]{2,1,0:T(8,128)} %add_select_fusion, f32[80,64,128]{2,1,0:T(8,128)} %copy-done.3, f32[80]{0:T(128)S(1)} %copy-done.24, f32[128,80]{0,1:T(8,128)S(1)} %get-tuple-element.32, f32[80]{0:T(128)S(1)} %get-tuple-element.52, ...), kind=kOutput, calls=%fused_computation.40 | convolution fusion | flops 1009909760 | bytes 10560512 | tf_op jit(solution)/shard_map/tn,hpn->thp/dot_general | solution.py:204
  186.0 3.3 %copy.46 = f32[128,5120]{1,0:T(8,128)} copy(f32[128,5120]{0,1:T(8,128)} %bitcast.81) | data formatting | bytes 5242880 | tf_op jit(solution)/shard_map/concatenate | solution.py:208
  189.3 5.3 %multiply_reduce_fusion = (f32[256]{0:T(256)S(1)}, f32[256,5120]{1,0:T(8,128)S(1)}) fusion(bf16[1,256,5120]{2,1,0:T(8,128)(2,1)} %param.13, bf16[256,5376]{1,0:T(8,128)(2,1)S(1)} %multiply_convert_fusion, f32[5120]{0:T(1024)S(1)} %mul.390, f32[128,5120]{1,0:T(8,128)} %copy.46, f32[128,5120]{1,0:T(8,128)} %copy.45), kind=kLoop, calls=%fused_computation.10 | loop fusion | flops 15728384 | bytes 15750144 | tf_op jit(solution)/shard_map/reduce_sum | solution.py:211
  194.6 2.3 copy-done
  196.9 1.0 convert_reduce_fusion
  197.9 2.3 multiply_reduce_fusion.2
  200.2 21.7 %all-gather = f32[64,256]{1,0:T(8,128)S(1)} all-gather(f32[8,256]{1,0:T(8,128)S(1)} %get-tuple-element.56), channel_id=2, replica_groups=mesh['dp'=8,'seq'=32] {'dp'}, dimensions={0}, use_global_device_ids=true | all-gather | bytes 73728 | tf_op jit(solution)/shard_map/all_gather | solution.py:127
  222.0 1.5 broadcast_in_dim.147
  223.5 9.2 %all-to-all-start.2 = ((f32[32,8,8,256]{3,2,1,0:T(8,128)}), f32[32,8,8,256]{3,2,1,0:T(8,128)}, u32[]{:S(2)}, u32[]{:S(2)}) async-start(f32[32,8,8,256]{3,2,1,0:T(8,128)} %broadcast_in_dim.147), calls=%async_computation.2 | async-start | bytes 4194304 | tf_op jit(solution)/shard_map/all_to_all | solution.py:118
  232.7 4.7 %fusion.98 = bf16[1,256,5120]{2,1,0:T(8,128)(2,1)} fusion(f32[5120]{0:T(1024)S(1)} %copy-done.13, f32[256,5120]{1,0:T(8,128)} %copy-done, f32[256]{0:T(256)S(1)} %add_rsqrt_fusion), kind=kLoop, calls=%fused_computation.205 | loop fusion | flops 3932160 | bytes 7885824 | tf_op jit(solution)/shard_map/broadcast_in_dim | solution.py:225
  237.4 23.7 %all-to-all-done.2 = f32[32,8,8,256]{3,2,1,0:T(8,128)} async-done(((f32[32,8,8,256]{3,2,1,0:T(8,128)}), f32[32,8,8,256]{3,2,1,0:T(8,128)}, u32[]{:S(2)}, u32[]{:S(2)}) %all-to-all-start.2) | async-done | bytes 2097184 | tf_op jit(solution)/shard_map/all_to_all | solution.py:118
  261.1 1.9 copy.47
  263.3 0.6 multiply_reduce_fusion.1
  263.9 4.2 %fusion.6 = f32[8,4096]{1,0:T(8,128)} fusion(f32[8,256]{1,0:T(8,128)S(1)} %get-tuple-element.56, f32[2048,256]{1,0:T(8,128)S(1)} %copy-done.4, f32[2048,256]{1,0:T(8,128)S(1)} %bitcast.79, f32[4096]{0:T(1024)S(1)} %multiply_reduce_fusion.1, f32[8]{0:T(128)S(1)} %get-tuple-element.55), kind=kOutput, calls=%fused_computation.18 | convolution fusion | flops 101875712 | bytes 4349984 | tf_op jit(solution)/shard_map/dot_general | solution.py:219
  (79 shorter events, 2.1 us)
Async XLA Ops:
  7.2 6.8 %copy-start.14 = (f32[1,80,256]{2,1,0:T(8,128)S(1)}, f32[1,80,256]{2,1,0:T(8,128)}, u32[]{:S(2)}) copy-start(f32[1,80,256]{2,1,0:T(8,128)} %param.17) | copy-start | bytes 245764
  7.2 8.2 %copy-start.15 = (f32[1,80,256]{2,1,0:T(8,128)S(1)}, f32[1,80,256]{2,1,0:T(8,128)}, u32[]{:S(2)}) copy-start(f32[1,80,256]{2,1,0:T(8,128)} %param.16) | copy-start | bytes 245764
  7.2 8.8 %copy-start.12 = (f32[4,5376]{1,0:T(4,128)S(1)}, f32[4,5376]{1,0:T(4,128)}, u32[]{:S(2)}) copy-start(f32[4,5376]{1,0:T(4,128)} %param.18) | copy-start | bytes 258052
  7.2 9.1 %copy-start.1 = (bf16[1,256,5120]{2,1,0:T(8,128)(2,1)S(1)}, bf16[1,256,5120]{2,1,0:T(8,128)(2,1)}, u32[]{:S(2)}) copy-start(bf16[1,256,5120]{2,1,0:T(8,128)(2,1)} %param.12) | copy-start | bytes 7864324
  7.2 9.1 %copy-start.9 = (bf16[1,256,128]{2,1,0:T(8,128)(2,1)S(1)}, bf16[1,256,128]{2,1,0:T(8,128)(2,1)}, u32[]{:S(2)}) copy-start(bf16[1,256,128]{2,1,0:T(8,128)(2,1)} %param.15) | copy-start | bytes 196612
  7.2 9.1 %copy-start.10 = (bf16[1,256,128]{2,1,0:T(8,128)(2,1)S(1)}, bf16[1,256,128]{2,1,0:T(8,128)(2,1)}, u32[]{:S(2)}) copy-start(bf16[1,256,128]{2,1,0:T(8,128)(2,1)} %param.14) | copy-start | bytes 196612
  9.4 6.8 %collective-permute-start = (bf16[3,5376]{1,0:T(4,128)(2,1)S(1)}, bf16[3,5376]{1,0:T(4,128)(2,1)S(1)}, u32[]{:S(2)}, u32[]{:S(2)}) collective-permute-start(bf16[3,5376]{1,0:T(4,128)(2,1)S(1)} %slice.128), channel_id=1, source_target_pairs={{0,1},{1,2},{2,3},{3,4},{4,5},{5,6},{6,7},{7,8},{8,9},{9,10},{10,1... | collective-permute-start | bytes 96776 | tf_op jit(solution)/shard_map/ppermute | solution.py:16
  16.2 2.4 copy-start.2
  16.2 2.4 copy-start.18
  29.8 3.9 %copy-start.5 = (bf16[128,5120]{0,1:T(8,128)(2,1)S(1)}, bf16[128,5120]{0,1:T(8,128)(2,1)}, u32[]{:S(2)}) copy-start(bf16[128,5120]{0,1:T(8,128)(2,1)} %copy.40) | copy-start | bytes 3932164
  33.7 4.3 %copy-start.3 = (f32[80,64,128]{2,1,0:T(8,128)}, f32[80,64,128]{2,1,0:T(8,128)S(1)}, u32[]{:S(2)}) copy-start(f32[80,64,128]{2,1,0:T(8,128)S(1)} %fusion.16) | copy-start | bytes 7864324
  38.0 18.9 %collective-permute-start.1 = (f32[80,64,128]{2,1,0:T(8,128)}, f32[80,64,128]{2,1,0:T(8,128)}, u32[]{:S(2)}, u32[]{:S(2)}) collective-permute-start(f32[80,64,128]{2,1,0:T(8,128)} %multiply_add_fusion.1), channel_id=1, source_target_pairs={{0,1},{2,3},{4,5},{6,7},{8,9},{10,11},{12,13},{14,15},{16,17},{18,... | collective-permute-start | bytes 7864328 | tf_op jit(solution)/shard_map/ppermute | solution.py:98
  39.9 16.4 %all-to-all-start.1 = ((f32[32,1,80]{2,1,0:T(1,128)}), f32[32,1,80]{2,1,0:T(1,128)S(1)}, u32[]{:S(2)}, u32[]{:S(2)}) async-start(f32[32,1,80]{2,1,0:T(1,128)} %broadcast_in_dim.142), calls=%async_computation.1 | async-start | bytes 32768 | tf_op jit(solution)/shard_map/all_to_all | solution.py:118
  56.9 10.2 %copy-start.19 = (f32[8,256]{1,0:T(8,128)S(1)}, f32[8,256]{1,0:T(8,128)}, u32[]{:S(2)}) copy-start(f32[8,256]{1,0:T(8,128)} %param.23) | copy-start | bytes 24580
  61.9 21.1 %collective-permute-start.3 = (bf16[80,64,128]{2,1,0:T(8,128)(2,1)}, bf16[80,64,128]{2,1,0:T(8,128)(2,1)}, u32[]{:S(2)}, u32[]{:S(2)}) collective-permute-start(bf16[80,64,128]{2,1,0:T(8,128)(2,1)} %get-tuple-element.20), channel_id=1, source_target_pairs={{1,7},{3,1},{5,3},{7,5},{9,15},{11,9},{13,11},{15,13},{17,23},{19,... | collective-permute-start | bytes 3932168 | tf_op jit(solution)/shard_map/ppermute | solution.py:53
  64.7 24.3 %collective-permute-start.2 = (bf16[80,64,128]{2,1,0:T(8,128)(2,1)}, bf16[80,64,128]{2,1,0:T(8,128)(2,1)}, u32[]{:S(2)}, u32[]{:S(2)}) collective-permute-start(bf16[80,64,128]{2,1,0:T(8,128)(2,1)} %get-tuple-element.20), channel_id=1, source_target_pairs={{1,3},{3,5},{5,7},{7,1},{9,11},{11,13},{13,15},{15,9},{17,19},{19,... | collective-permute-start | bytes 3932168 | tf_op jit(solution)/shard_map/ppermute | solution.py:52
  67.9 26.8 %all-to-all-start = ((f32[32,8,256]{2,1,0:T(8,128)}), f32[32,8,256]{2,1,0:T(8,128)}, u32[]{:S(2)}, u32[]{:S(2)}) async-start(f32[32,8,256]{2,1,0:T(8,128)} %broadcast_in_dim.141), calls=%async_computation | async-start | bytes 524288 | tf_op jit(solution)/shard_map/all_to_all | solution.py:118
  72.5 98.3 %all-gather.4.cloned.1.call-start = ((), (), s32[]{:S(2)}) async-start(), calls=%async_computation.3 | async-start | bytes 2359296 | tf_op jit(solution)/shard_map/all_gather | solution.py:123
  85.0 11.8 %collective-permute-start.4 = (bf16[40,64,128]{2,1,0:T(8,128)(2,1)}, bf16[40,64,128]{2,1,0:T(8,128)(2,1)S(1)}, u32[]{:S(2)}, u32[]{:S(2)}) collective-permute-start(bf16[40,64,128]{2,1,0:T(8,128)(2,1)} %slice.145), channel_id=1, source_target_pairs={{1,7},{3,1},{5,3},{7,5},{9,15},{11,9},{13,11},{15,13},{17,23},{19,... | collective-permute-start | bytes 1966088 | tf_op jit(solution)/shard_map/ppermute | solution.py:54
  91.0 12.8 %collective-permute-start.5 = (bf16[40,64,128]{2,1,0:T(8,128)(2,1)}, bf16[40,64,128]{2,1,0:T(8,128)(2,1)}, u32[]{:S(2)}, u32[]{:S(2)}) collective-permute-start(bf16[40,64,128]{2,1,0:T(8,128)(2,1)} %slice.146), channel_id=1, source_target_pairs={{1,3},{3,5},{5,7},{7,1},{9,11},{11,13},{13,15},{15,9},{17,19},{19,... | collective-permute-start | bytes 1966088 | tf_op jit(solution)/shard_map/ppermute | solution.py:55
  94.7 103.1 %all-gather.6.cloned.1.call-start = ((), (), s32[]{:S(2)}) async-start(), calls=%async_computation.4 | async-start | bytes 2949120 | tf_op jit(solution)/shard_map/all_gather | solution.py:152
  107.4 39.6 %copy-start.20 = (f32[80]{0:T(128)S(1)}, f32[80]{0:T(128)}, u32[]{:S(2)}) copy-start(f32[80]{0:T(128)} %get-tuple-element.42) | copy-start | bytes 964
  107.4 39.5 %copy-start.21 = (f32[80]{0:T(128)S(1)}, f32[80]{0:T(128)}, u32[]{:S(2)}) copy-start(f32[80]{0:T(128)} %get-tuple-element.49) | copy-start | bytes 964
  107.4 39.5 %copy-start.22 = (f32[80]{0:T(128)S(1)}, f32[80]{0:T(128)}, u32[]{:S(2)}) copy-start(f32[80]{0:T(128)} %get-tuple-element.40) | copy-start | bytes 964
  107.4 39.5 %copy-start.23 = (f32[80]{0:T(128)S(1)}, f32[80]{0:T(128)}, u32[]{:S(2)}) copy-start(f32[80]{0:T(128)} %get-tuple-element.47) | copy-start | bytes 964
  107.4 18.8 %collective-permute-start.7 = (bf16[80,64,128]{2,1,0:T(8,128)(2,1)S(1)}, bf16[80,64,128]{2,1,0:T(8,128)(2,1)S(1)}, u32[]{:S(2)}, u32[]{:S(2)}) collective-permute-start(bf16[80,64,128]{2,1,0:T(8,128)(2,1)S(1)} %fusion.25), channel_id=1, source_target_pairs={{1,25},{3,27},{5,29},{7,31},{9,1},{11,3},{13,5},{15,7},{17,9},{19,... | collective-permute-start | bytes 3932168 | tf_op jit(solution)/shard_map/ppermute | solution.py:53
  110.2 21.9 %collective-permute-start.6 = (bf16[80,64,128]{2,1,0:T(8,128)(2,1)S(1)}, bf16[80,64,128]{2,1,0:T(8,128)(2,1)S(1)}, u32[]{:S(2)}, u32[]{:S(2)}) collective-permute-start(bf16[80,64,128]{2,1,0:T(8,128)(2,1)S(1)} %fusion.25), channel_id=1, source_target_pairs={{1,9},{3,11},{5,13},{7,15},{9,17},{11,19},{13,21},{15,23},{17,25},... | collective-permute-start | bytes 3932168 | tf_op jit(solution)/shard_map/ppermute | solution.py:52
  126.2 1.1 copy-start.7
  128.1 11.8 %collective-permute-start.8 = (bf16[40,64,128]{2,1,0:T(8,128)(2,1)}, bf16[40,64,128]{2,1,0:T(8,128)(2,1)}, u32[]{:S(2)}, u32[]{:S(2)}) collective-permute-start(bf16[40,64,128]{2,1,0:T(8,128)(2,1)} %slice.147), channel_id=1, source_target_pairs={{1,25},{3,27},{5,29},{7,31},{9,1},{11,3},{13,5},{15,7},{17,9},{19,... | collective-permute-start | bytes 1966088 | tf_op jit(solution)/shard_map/ppermute | solution.py:54
  132.1 1.1 copy-start.8
  134.1 12.8 %collective-permute-start.9 = (bf16[40,64,128]{2,1,0:T(8,128)(2,1)}, bf16[40,64,128]{2,1,0:T(8,128)(2,1)}, u32[]{:S(2)}, u32[]{:S(2)}) collective-permute-start(bf16[40,64,128]{2,1,0:T(8,128)(2,1)} %slice.148), channel_id=1, source_target_pairs={{1,9},{3,11},{5,13},{7,15},{9,17},{11,19},{13,21},{15,23},{17,25},... | collective-permute-start | bytes 1966088 | tf_op jit(solution)/shard_map/ppermute | solution.py:55
  146.9 10.4 %copy-start.26 = (f32[80]{0:T(128)S(1)}, f32[80]{0:T(128)}, u32[]{:S(2)}) copy-start(f32[80]{0:T(128)} %param.20) | copy-start | bytes 964
  154.5 11.9 %collective-permute-start.10 = (f32[80,64,128]{2,1,0:T(8,128)}, f32[80,64,128]{2,1,0:T(8,128)}, u32[]{:S(2)}, u32[]{:S(2)}) collective-permute-start(f32[80,64,128]{2,1,0:T(8,128)} %fusion.15), channel_id=1, source_target_pairs={{1,0},{3,2},{5,4},{7,6},{9,8},{11,10},{13,12},{15,14},{17,16},{19,... | collective-permute-start | bytes 7864328 | tf_op jit(solution)/shard_map/ppermute | solution.py:106
  157.8 4.5 %copy-start.6 = (bf16[128,5120]{0,1:T(8,128)(2,1)S(1)}, bf16[128,5120]{0,1:T(8,128)(2,1)}, u32[]{:S(2)}) copy-start(bf16[128,5120]{0,1:T(8,128)(2,1)} %copy.40) | copy-start | bytes 3932164
  157.8 4.5 %copy-start.17 = (f32[80,128]{1,0:T(8,128)S(1)}, f32[80,128]{1,0:T(8,128)}, u32[]{:S(2)}) copy-start(f32[80,128]{1,0:T(8,128)} %get-tuple-element.29) | copy-start | bytes 122884
  162.3 4.1 %copy-start.25 = (f32[80]{0:T(128)S(1)}, f32[80]{0:T(128)}, u32[]{:S(2)}) copy-start(f32[80]{0:T(128)} %get-tuple-element.34) | copy-start | bytes 964
  166.4 4.4 %copy-start.11 = (f32[128,80]{0,1:T(8,128)S(1)}, f32[128,80]{0,1:T(8,128)}, u32[]{:S(2)}) copy-start(f32[128,80]{0,1:T(8,128)} %get-tuple-element.33) | copy-start | bytes 122884
  176.2 3.3 %copy-start.24 = (f32[80]{0:T(128)S(1)}, f32[80]{0:T(128)}, u32[]{:S(2)}) copy-start(f32[80]{0:T(128)} %get-tuple-element.51) | copy-start | bytes 964
  189.3 7.6 %copy-start.13 = (f32[5120]{0:T(1024)S(1)}, f32[5120]{0:T(1024)}, u32[]{:S(2)}) copy-start(f32[5120]{0:T(1024)} %param.21) | copy-start | bytes 61444
  194.5 2.3 copy-start
  200.2 63.7 %copy-start.16 = (f32[8,256]{1,0:T(8,128)}, f32[8,256]{1,0:T(8,128)S(1)}, u32[]{:S(2)}) copy-start(f32[8,256]{1,0:T(8,128)S(1)} %get-tuple-element.56) | copy-start | bytes 24580
  223.5 37.6 %all-to-all-start.2 = ((f32[32,8,8,256]{3,2,1,0:T(8,128)}), f32[32,8,8,256]{3,2,1,0:T(8,128)}, u32[]{:S(2)}, u32[]{:S(2)}) async-start(f32[32,8,8,256]{3,2,1,0:T(8,128)} %broadcast_in_dim.147), calls=%async_computation.2 | async-start | bytes 4194304 | tf_op jit(solution)/shard_map/all_to_all | solution.py:118
  261.0 2.2 copy-start.4
Sparse Core Ops, SparseCore 0:
  94.9 36.9 all-gather.3
  157.4 35.9 all-gather.5

commit v5 on v4

--- a/solution.py
+++ b/solution.py
@@ -16,18 +16,21 @@
     return lax.ppermute(block, axis, route)
 
 
-def block_terms(values, write_rows, read_rows, steps, logs):
+def block_states(values, write_rows, steps, logs):
     cum_log = jnp.cumsum(logs, axis=1)
-    length = logs.shape[1]
+    tail_decay = jnp.exp(cum_log[:, -1:] - cum_log) * steps
+    weighted = (tail_decay[:, :, None] * write_rows.astype(jnp.float32)[None]).astype(jnp.bfloat16)
+    states = jnp.einsum("hsn,shp->hpn", weighted, values, preferred_element_type=jnp.float32)
+    return (states, cum_log)
+
+
+def block_inner(values, write_rows, read_rows, steps, cum_log):
+    length = cum_log.shape[1]
     causal = jnp.arange(length)[:, None] >= jnp.arange(length)[None, :]
     scores = jnp.dot(read_rows, write_rows.T, preferred_element_type=jnp.float32)
     decay = jnp.exp(jnp.where(causal[None], cum_log[:, :, None] - cum_log[:, None, :], -jnp.inf))
     mixing = (scores[None] * decay * steps[:, None, :]).astype(jnp.bfloat16)
-    inner_out = jnp.einsum("hts,shp->thp", mixing, values, preferred_element_type=jnp.float32)
-    tail_decay = jnp.exp(cum_log[:, -1:] - cum_log) * steps
-    weighted = (tail_decay[:, :, None] * write_rows.astype(jnp.float32)[None]).astype(jnp.bfloat16)
-    states = jnp.einsum("hsn,shp->hpn", weighted, values, preferred_element_type=jnp.float32)
-    return (inner_out, states, cum_log)
+    return jnp.einsum("hts,shp->thp", mixing, values, preferred_element_type=jnp.float32)
 
 
 def chip_routes(seq):
@@ -46,24 +49,46 @@
     return rows, up, down, (y_fwd, y_bwd), (x_fwd, x_bwd)
 
 
-def ring_of_four(state, fwd, bwd):
+def exact_pieces(log):
+    hi = lax.reduce_precision(log, exponent_bits=8, mantissa_bits=7)
+    mid = lax.reduce_precision(log - hi, exponent_bits=8, mantissa_bits=7)
+    return [hi, mid, log - hi - mid]
+
+
+def packed(state, log):
+    pieces = jnp.stack(exact_pieces(log), axis=-1)
+    row = jnp.zeros((state.shape[0], 1, state.shape[2]), jnp.float32)
+    row = row.at[:, 0, : pieces.shape[1]].set(pieces)
+    return jnp.concatenate([state, row], axis=1).astype(XFER)
+
+
+def unpacked(block):
+    pieces = block[:, -1, :3].astype(jnp.float32)
+    return block[:, :-1], (pieces[:, 0] + pieces[:, 1]) + pieces[:, 2]
+
+
+def ring_of_four(state, log, fwd, bwd):
     half = state.shape[0] // 2
-    sent = state.astype(XFER)
-    prev_state = lax.ppermute(sent, "seq", fwd)
-    next_state = lax.ppermute(sent, "seq", bwd)
-    far_a = lax.ppermute(next_state[:half], "seq", bwd)
-    far_b = lax.ppermute(prev_state[half:], "seq", fwd)
-    far_state = jnp.concatenate([far_a, far_b], axis=0)
-    return [(state, 0), (prev_state, RING - 1), (next_state, 1), (far_state, 2)]
-
-
-def fold_ring(slots, pos, ring_logs):
-    places = [(pos + k) % RING for (_, k) in slots]
-    logs = [lax.dynamic_index_in_dim(ring_logs, p, 0, False) for p in places]
+    sent = packed(state, log)
+    prev_block = lax.ppermute(sent, "seq", fwd)
+    next_block = lax.ppermute(sent, "seq", bwd)
+    far_a = lax.ppermute(next_block[:half], "seq", bwd)
+    far_b = lax.ppermute(prev_block[half:], "seq", fwd)
+    far_block = jnp.concatenate([far_a, far_b], axis=0)
+    slots = [(state, log, 0)]
+    for block, k in ((prev_block, RING - 1), (next_block, 1), (far_block, 2)):
+        value, value_log = unpacked(block)
+        slots.append((value, value_log, k))
+    return slots
+
+
+def fold_ring(slots, pos):
+    places = [(pos + k) % RING for (_, _, k) in slots]
+    logs = [l for (_, l, _) in slots]
     zero = jnp.zeros_like(logs[0])
     before = None
     total = None
-    for i, (value, _) in enumerate(slots):
+    for i, (value, _, _) in enumerate(slots):
         between = zero
         after = zero
         for j in range(len(slots)):
@@ -80,28 +105,29 @@
     lead = zero
     for j in range(len(slots)):
         lead = lead + jnp.where(places[j] < pos, logs[j], 0.0)
-    return before, jnp.exp(lead), total
-
-
-def carried_in(own_state, shard_logs):
+    return before, jnp.exp(lead), total, sum(logs[1:], logs[0])
+
+
+def chip_ends(own_state, own_log):
     seq = lax.axis_size("seq")
-    rows, up, down, y_routes, x_routes = chip_routes(seq)
+    _, up, _, _, _ = chip_routes(seq)
+    low_block = lax.ppermute(jnp.concatenate([own_state, jnp.broadcast_to(own_log[:, None, None], (own_state.shape[0], 1, own_state.shape[2]))], axis=1), "seq", up)
+    return low_block[:, :-1], low_block[:, -1, 0]
+
+
+def carried_in(own_state, own_log, low_state, low_log):
+    seq = lax.axis_size("seq")
+    rows, _, down, y_routes, x_routes = chip_routes(seq)
     assert rows == RING and seq == rows * RING * CORES
     place = lax.axis_index("seq")
     core = place % CORES
     y_pos = (place // CORES) % RING
     x_pos = place // (CORES * RING)
-    grid_logs = shard_logs.reshape(rows, RING, CORES, -1)
-    chip_logs = grid_logs[:, :, 0] + grid_logs[:, :, 1]
-    own_log = lax.dynamic_index_in_dim(shard_logs, place, 0, False)
-    low_log = lax.dynamic_index_in_dim(shard_logs, place - 1, 0, False)
-    low_state = lax.ppermute(own_state, "seq", up)
     chip_state = jnp.exp(own_log)[:, None, None] * low_state + own_state
-    slots = ring_of_four(chip_state, *y_routes)
-    row_logs = lax.dynamic_index_in_dim(chip_logs, x_pos, 0, False)
-    row_before, row_lead, row_total = fold_ring(slots, y_pos, row_logs)
-    slots = ring_of_four(row_total, *x_routes)
-    rows_before, _, _ = fold_ring(slots, x_pos, jnp.sum(chip_logs, axis=1))
+    slots = ring_of_four(chip_state, low_log + own_log, *y_routes)
+    row_before, row_lead, row_total, row_log = fold_ring(slots, y_pos)
+    slots = ring_of_four(row_total, row_log, *x_routes)
+    rows_before, _, _, _ = fold_ring(slots, x_pos)
     chip_in = row_lead[:, None, None] * rows_before + row_before
     chip_in_low = lax.ppermute(chip_in, "seq", down)
     high_in = jnp.exp(low_log)[:, None, None] * chip_in + low_state
@@ -165,20 +191,14 @@
     steps = step_size[0]
     logs = log_forget[0]
     blocks = length // SPAN
-    inner_list = []
     state_list = []
     cum_list = []
     for block in range(blocks):
         lower = block * SPAN
         upper = lower + SPAN
-        inner_out, states, cum_log = block_terms(
-            values[lower:upper],
-            write_all[lower:upper],
-            read_all[lower:upper],
-            steps[:, lower:upper],
-            logs[:, lower:upper],
-        )
-        inner_list.append(inner_out)
+        states, cum_log = block_states(
+            values[lower:upper], write_all[lower:upper], steps[:, lower:upper], logs[:, lower:upper]
+        )
         state_list.append(states)
         cum_list.append(cum_log)
     running = jnp.zeros((heads, head_dim, state_dim), jnp.float32)
@@ -192,8 +212,22 @@
         running = jnp.exp(block_total)[:, None, None] * running + state_list[block]
         before = before + block_total
     all_prior = prior_everywhere(prior_draw)
-    shard_logs = spread_over(before, "seq")
-    carry_in = carried_in(running, shard_logs)
+    low_state, low_log = chip_ends(running, before)
+    read_all, low_log = lax.optimization_barrier((read_all, low_log))
+    inner_list = []
+    for block in range(blocks):
+        lower = block * SPAN
+        upper = lower + SPAN
+        inner_list.append(
+            block_inner(
+                values[lower:upper],
+                write_all[lower:upper],
+                read_all[lower:upper],
+                steps[:, lower:upper],
+                cum_list[block],
+            )
+        )
+    carry_in = carried_in(running, before, low_state, low_log)
     all_prior, carry_in = lax.optimization_barrier((all_prior, carry_in))
     outputs = []
     for block in range(blocks):

time: 276 us -> 291 us (1.054)
  local copies, waits for them, and re-layouts: 29.7 us -> 37.4 us
  other arithmetic: 44.6 us -> 52.2 us
  waiting for transfers between devices: 74.1 us -> 77.9 us
  blocking collectives: 21.7 us -> 18.4 us
    all_gather x1, waiting for transfers between devices: 0.02 us -> 8.88 us  [per_device(): full_code_weight = lax.all_gather(code_weight, 'dp', axis=0, tiled=True)]
    another operation x2 -> x9, other arithmetic: 0.59 us -> 8.33 us  [block_terms(): cum_log = jnp.cumsum(logs, axis=1)]
    all_to_all x3 -> x2, waiting for transfers between devices: 30.7 us -> 23.7 us  [spread_over(): lax.all_to_all(jnp.broadcast_to(block[None], (count,) + block.shape), axi...]
    convert_element_type x3 -> x7, other arithmetic: 8.51 us -> 2.98 us  [the longest x6 2.97 us: unpacked(): pieces = block[:, -1, :3].astype(jnp.float32)]
    add x0 -> x5, other arithmetic: none -> 4.04 us  [the longest x1 2.6 us: fold_ring(): before = w_before * v if before is None else before + w_before * v]
    concatenate x0 -> x3, other arithmetic: none -> 3.96 us  [the longest x2 3.71 us: packed(): return jnp.concatenate([state, row], axis=1).astype(XFER)]
    unnamed x54 -> x90, local copies, waits for them, and re-layouts: 4.85 us -> 8.68 us
    ppermute x9, starting transfers between devices: 23.7 us -> 27.3 us  [the longest x2 10.3 us: ring_of_four(): far_a = lax.ppermute(next_block[:half], 'seq', bwd)]
  transfers between devices with their start and end apart: 16 -> 15, of which waited for: 8 -> 9; matrix products, arithmetic and copies ran while one was open for 24% -> 23% of each run, Pallas kernels for 0% -> 0%
where the time goes in v5:
time: 291 us; the launch traced here: 290 us
  waiting for transfers between devices  77.9 us (27%)
  starting transfers between devices  55.1 us (19%)
  other arithmetic  52.2 us (18%)
  local copies, waits for them, and re-layouts  37.4 us (13%)
  matrix products  33.6 us (12%)
  blocking collectives  18.4 us (6%)
  between operations  15.2 us (5%)
    all_to_all x2, waiting for transfers between devices, spread_over(): lax.all_to_all(jnp.broadcast_to(block[None], (count,) + block.shape), axi...  23.7 us
    ppermute x2, waiting for transfers between devices, ring_of_four(): next_block = lax.ppermute(sent, 'seq', bwd)  22.5 us
    all_to_all x2, starting transfers between devices, spread_over(): lax.all_to_all(jnp.broadcast_to(block[None], (count,) + block.shape), axi...  21.5 us
    all_gather x1, blocking collectives, codes_everywhere(): rows = lax.all_gather(block, 'dp', axis=0, tiled=False)  18.4 us
    ppermute x2, waiting for transfers between devices, ring_of_four(): far_b = lax.ppermute(prev_block[half:], 'seq', fwd)  13 us
    dot_general x2, matrix products, per_device(): jnp.einsum('tn,hpn->thp', read_block, start, precision=lax.Precision.HIGH...  11 us
    ppermute x2, starting transfers between devices, ring_of_four(): far_a = lax.ppermute(next_block[:half], 'seq', bwd)  10.3 us
    all_gather x1, waiting for transfers between devices, per_device(): full_code_weight = lax.all_gather(code_weight, 'dp', axis=0, tiled=True)  8.88 us
  transfers between devices with their start and end apart: 15, of which 9 were waited for; matrix products, arithmetic and copies ran while one was open for 23% of the time, Pallas kernels for 0%

profile of v5, /device:TPU:1, one launch (start us, length us, event | category | flops | bytes accessed | tf_op | source)
XLA Modules:
  0.0 289.6 jit_solution(6367670647310966073)
XLA Ops:
  7.2 2.1 pad_maximum_fusion.3
  9.4 4.6 %collective-permute-start = (bf16[3,5376]{1,0:T(4,128)(2,1)S(1)}, bf16[3,5376]{1,0:T(4,128)(2,1)S(1)}, u32[]{:S(2)}, u32[]{:S(2)}) collective-permute-start(bf16[3,5376]{1,0:T(4,128)(2,1)S(1)} %slice.301), channel_id=1, source_target_pairs={{0,1},{1,2},{2,3},{3,4},{4,5},{5,6},{6,7},{7,8},{8,9},{9,10},{10,1... | collective-permute-start | bytes 96776 | tf_op jit(solution)/shard_map/ppermute | solution.py:16
  16.3 2.4 maximum_maximum_fusion
  18.8 4.4 %multiply_convert_fusion = bf16[256,5376]{1,0:T(8,128)(2,1)S(1)} fusion(bf16[259,5376]{1,0:T(8,128)(2,1)S(1)} %maximum_maximum_fusion, f32[5376]{0:T(1024)S(1)} %get-tuple-element.37, f32[5376]{0:T(1024)S(1)} %get-tuple-element.38, f32[5376]{0:T(1024)S(1)} %get-tuple-element.36, f32[5376]{0:T(1024)S(1)} %get-tuple-element.35, f32[5376]{0:T(1024)S(1)} %copy-done.36, ...), kind=kLoop, calls=%fused_computation.2 | loop fusion | flops 30277632 | bytes 13870080 | tf_op jit(solution)/shard_map/convert_element_type | solution.py:187
  23.2 2.1 fusion.111
  25.3 2.5 copy.79
  27.7 2.4 copy.80
  30.2 3.9 %fusion.14 = f32[80,64,128]{2,1,0:T(8,128)S(1)} fusion(bf16[128,80,64]{0,2,1:T(8,128)(2,1)} %bitcast.91, f32[128,128]{1,0:T(8,128)S(1)} %get-tuple-element.57, f32[80,128]{1,0:T(8,128)S(1)} %get-tuple-element.64), kind=kOutput, calls=%fused_computation.38 | convolution fusion | flops 170393600 | bytes 4038656 | tf_op jit(solution)/shard_map/hsn,shp->hpn/dot_general | solution.py:23
  34.1 1.8 multiply_add_fusion.2
  36.8 1.3 collective-permute-start.1
  38.8 4.9 %collective-permute-done.1 = f32[80,65,128]{2,0,1:T(8,128)S(1)} collective-permute-done((f32[80,65,128]{2,0,1:T(8,128)S(1)}, f32[80,65,128]{2,0,1:T(8,128)S(1)}, u32[]{:S(2)}, u32[]{:S(2)}) %collective-permute-start.1) | collective-permute-done | bytes 2662432 | tf_op jit(solution)/shard_map/ppermute | solution.py:114
  43.9 0.9 multiply_add_fusion.1
  45.4 2.6 copy.125
  48.8 2.5 fusion.40
  51.3 4.2 %collective-permute-start.3 = (bf16[80,65,128]{2,0,1:T(8,128)(2,1)}, bf16[80,65,128]{2,0,1:T(8,128)(2,1)}, u32[]{:S(2)}, u32[]{:S(2)}) collective-permute-start(bf16[80,65,128]{2,0,1:T(8,128)(2,1)} %fusion.40), channel_id=1, source_target_pairs={{1,7},{3,1},{5,3},{7,5},{9,15},{11,9},{13,11},{15,13},{17,23},{19,... | collective-permute-start | bytes 3993608 | tf_op jit(solution)/shard_map/ppermute | solution.py:74
  55.5 1.9 collective-permute-start.2
  57.6 13.0 %collective-permute-done.3 = bf16[80,65,128]{2,0,1:T(8,128)(2,1)} collective-permute-done((bf16[80,65,128]{2,0,1:T(8,128)(2,1)}, bf16[80,65,128]{2,0,1:T(8,128)(2,1)}, u32[]{:S(2)}, u32[]{:S(2)}) %collective-permute-start.3) | collective-permute-done | bytes 1331232 | tf_op jit(solution)/shard_map/ppermute | solution.py:74
  70.6 1.2 slice.326
  71.7 5.0 %collective-permute-start.4 = (bf16[40,65,128]{2,0,1:T(8,128)(2,1)S(1)}, bf16[40,65,128]{2,0,1:T(8,128)(2,1)S(1)}, u32[]{:S(2)}, u32[]{:S(2)}) collective-permute-start(bf16[40,65,128]{2,0,1:T(8,128)(2,1)S(1)} %slice.326), channel_id=1, source_target_pairs={{1,7},{3,1},{5,3},{7,5},{9,15},{11,9},{13,11},{15,13},{17,23},{19,... | collective-permute-start | bytes 1996808 | tf_op jit(solution)/shard_map/ppermute | solution.py:75
  76.8 1.2 slice.327
  77.9 2.1 collective-permute-start.5
  80.9 0.7 fusion.63
  81.9 2.5 collective-permute-done.4
  84.4 6.1 %collective-permute-done.5 = bf16[40,65,128]{2,0,1:T(8,128)(2,1)S(1)} collective-permute-done((bf16[40,65,128]{2,0,1:T(8,128)(2,1)S(1)}, bf16[40,65,128]{2,0,1:T(8,128)(2,1)S(1)}, u32[]{:S(2)}, u32[]{:S(2)}) %collective-permute-start.5) | collective-permute-done | bytes 665632 | tf_op jit(solution)/shard_map/ppermute | solution.py:76
  90.7 1.1 copy-done.17
  93.2 6.6 %fusion.108 = (bf16[80,64,128]{2,0,1:T(8,128)(2,1)S(1)}, f32[80,64,128]{2,0,1:T(8,128)}, f32[80,64,128]{2,0,1:T(8,128)}, f32[80,64,128]{2,0,1:T(8,128)}, f32[80,64,128]{2,0,1:T(8,128)}) fusion(bf16[80,65,128]{2,0,1:T(8,128)(2,1)} %copy-done.17, f32[80]{0:T(128)S(1)} %get-tuple-element.79, bf16[80,65,128]{2,0,1:T(8,128)(2,1)} %collective-permute-done.3, ...), kind=kLoop, calls=%fused_computation.236 | loop fusion | flops 9175040 | bytes 18352320 | tf_op jit(solution)/shard_map/convert.8
  99.8 1.2 fusion.41
  101.1 3.6 %collective-permute-start.7 = (bf16[80,65,128]{2,0,1:T(8,128)(2,1)}, bf16[80,65,128]{2,0,1:T(8,128)(2,1)}, u32[]{:S(2)}, u32[]{:S(2)}) collective-permute-start(bf16[80,65,128]{2,0,1:T(8,128)(2,1)} %fusion.41), channel_id=1, source_target_pairs={{1,25},{3,27},{5,29},{7,31},{9,1},{11,3},{13,5},{15,7},{17,9},{19,... | collective-permute-start | bytes 3993608 | tf_op jit(solution)/shard_map/ppermute | solution.py:74
  104.7 1.9 collective-permute-start.6
  107.3 4.5 %all-to-all-start = ((f32[32,8,256]{2,1,0:T(8,128)}), f32[32,8,256]{2,1,0:T(8,128)S(1)}, u32[]{:S(2)}, u32[]{:S(2)}) async-start(f32[32,8,256]{2,1,0:T(8,128)} %broadcast_in_dim.141), calls=%async_computation | async-start | bytes 524288 | tf_op jit(solution)/shard_map/all_to_all | solution.py:144
  111.9 9.6 %collective-permute-done.7 = bf16[80,65,128]{2,0,1:T(8,128)(2,1)} collective-permute-done((bf16[80,65,128]{2,0,1:T(8,128)(2,1)}, bf16[80,65,128]{2,0,1:T(8,128)(2,1)}, u32[]{:S(2)}, u32[]{:S(2)}) %collective-permute-start.7) | collective-permute-done | bytes 1331232 | tf_op jit(solution)/shard_map/ppermute | solution.py:74
  121.4 2.0 slice.343
  123.4 5.3 %collective-permute-start.8 = (bf16[40,65,128]{2,0,1:T(8,128)(2,1)}, bf16[40,65,128]{2,0,1:T(8,128)(2,1)S(1)}, u32[]{:S(2)}, u32[]{:S(2)}) collective-permute-start(bf16[40,65,128]{2,0,1:T(8,128)(2,1)} %slice.343), channel_id=1, source_target_pairs={{1,25},{3,27},{5,29},{7,31},{9,1},{11,3},{13,5},{15,7},{17,9},{19,... | collective-permute-start | bytes 1996808 | tf_op jit(solution)/shard_map/ppermute | solution.py:75
  129.7 1.3 slice.344
  131.0 1.9 collective-permute-start.9
  134.4 2.3 collective-permute-done.8
  136.8 6.9 %collective-permute-done.9 = bf16[40,65,128]{2,0,1:T(8,128)(2,1)S(1)} collective-permute-done((bf16[40,65,128]{2,0,1:T(8,128)(2,1)S(1)}, bf16[40,65,128]{2,0,1:T(8,128)(2,1)S(1)}, u32[]{:S(2)}, u32[]{:S(2)}) %collective-permute-start.9) | collective-permute-done | bytes 665632 | tf_op jit(solution)/shard_map/ppermute | solution.py:76
  144.9 2.6 multiply_add_fusion
  147.5 0.7 copy-done.11
  148.2 0.8 copy-done.12
  149.1 7.2 %fusion.16 = f32[80,64,128]{2,1,0:T(8,128)} fusion(f32[80,64,128]{2,0,1:T(8,128)S(1)} %copy-done.12, f32[80,64,128]{2,0,1:T(8,128)S(1)} %copy-done.11, f32[80,64,128]{2,0,1:T(8,128)S(1)} %copy-done.10, f32[80,64,128]{2,0,1:T(8,128)S(1)} %multiply_add_fusion, f32[80,64,128]{2,1,0:T(8,128)S(1)} %multiply_add_fusion.1, ...), kind=kLoop, calls=%fused_computation.43 | loop fusion | flops 5898240 | bytes 17040320 | tf_op jit(solution)/shard_map/add | solution.py:131
  156.2 1.7 collective-permute-start.10
  158.1 0.9 fusion.53
  159.0 0.9 fusion.51
  160.0 4.5 %fusion.9 = f32[80,64,128]{2,1,0:T(8,128)} fusion(bf16[128,80,64]{0,2,1:T(8,128)(2,1)} %bitcast.92, f32[80,128]{1,0:T(8,128)S(1)} %copy-done.35, f32[80,128]{1,0:T(8,128)S(1)} %copy-done.26, f32[128,128]{1,0:T(8,128)S(1)} %fusion.53, pred[128,128]{1,0:T(8,128)(4,1)S(1)} %iota_compare_fusion.1), kind=kOutput, calls=%fused_computation.33 | convolution fusion | flops 174325760 | bytes 4096000 | tf_op jit(solution)/shard_map/hts,shp->thp/dot_general | solution.py:33
  164.5 4.1 %fusion.10 = f32[80,64,128]{2,1,0:T(8,128)} fusion(bf16[128,80,64]{0,2,1:T(8,128)(2,1)S(1)} %bitcast.94, f32[80,128]{1,0:T(8,128)S(1)} %copy-done.34, f32[80,128]{1,0:T(8,128)S(1)} %copy-done.24, f32[128,128]{1,0:T(8,128)S(1)} %fusion.51, pred[128,128]{1,0:T(8,128)(4,1)S(1)} %iota_compare_fusion.1), kind=kOutput, calls=%fused_computation.34 | convolution fusion | flops 174325760 | bytes 4096000 | tf_op jit(solution)/shard_map/hts,shp->thp/dot_general | solution.py:33
  168.6 1.5 copy-done.18
  170.1 3.0 %add_select_fusion = f32[80,64,128]{2,1,0:T(8,128)S(1)} fusion(f32[80,64,128]{2,1,0:T(8,128)} %copy-done.18, f32[80,64,128]{2,1,0:T(8,128)} %fusion.16, f32[80,64,128]{2,0,1:T(8,128)S(1)} %copy-done.8, f32[80]{0:T(128)S(1)} %copy-done.41, pred[]{:T(512)S(6)} %eq.14), kind=kLoop, calls=%fused_computation.55 | loop fusion | flops 1966080 | bytes 10486081 | tf_op jit(solution)/shard_map/jit(_where)/select_n | solution.py:134
  173.2 5.4 %bitcast_add_fusion.1 = f32[128,80,64]{0,2,1:T(8,128)} fusion(f32[80,64,128]{2,1,0:T(8,128)} %fusion.9, f32[80,64,128]{2,1,0:T(8,128)S(1)} %add_select_fusion, f32[128,80]{0,1:T(8,128)S(1)} %copy-done.28, bf16[256,128]{1,0:T(8,128)(2,1)S(1)} %copy-done.22), kind=kOutput, calls=%fused_computation.41 | convolution fusion | flops 1007943680 | bytes 7938048 | tf_op jit(solution)/shard_map/tn,hpn->thp/dot_general | solution.py:238
  178.6 3.4 %copy.97 = f32[128,5120]{1,0:T(8,128)} copy(f32[128,5120]{0,1:T(8,128)} %bitcast.89) | data formatting | bytes 5242880 | tf_op jit(solution)/shard_map/concatenate | solution.py:242
  182.0 5.6 %bitcast_add_fusion = f32[128,80,64]{0,2,1:T(8,128)} fusion(f32[80,64,128]{2,1,0:T(8,128)} %fusion.10, f32[80,64,128]{2,1,0:T(8,128)} %copy-done.9, f32[80,64,128]{2,1,0:T(8,128)S(1)} %copy-done.6, f32[80]{0:T(128)S(1)} %copy-done.40, f32[128,80]{0,1:T(8,128)S(1)} %copy-done.27, f32[80]{0:T(128)S(1)} %get-tuple-element.81, bf16[256,128]{1,0:T(8,128)(2,1)S(1)} %copy-done.22), kind=kOutput, calls=%fused_computation.40 | convolution fusion | flops 1009909760 | bytes 10560512 | tf_op jit(solution)/shard_map/tn,hpn->thp/dot_general | solution.py:238
  187.7 3.4 %copy.98 = f32[128,5120]{1,0:T(8,128)} copy(f32[128,5120]{0,1:T(8,128)} %bitcast.90) | data formatting | bytes 5242880 | tf_op jit(solution)/shard_map/concatenate | solution.py:242
  191.1 5.3 %multiply_reduce_fusion = (f32[256]{0:T(256)S(1)}, f32[256,5120]{1,0:T(8,128)S(1)}) fusion(bf16[1,256,5120]{2,1,0:T(8,128)(2,1)} %param.17, bf16[256,5376]{1,0:T(8,128)(2,1)S(1)} %copy-done.2, f32[5120]{0:T(1024)S(1)} %mul.390, f32[128,5120]{1,0:T(8,128)} %copy.98, f32[128,5120]{1,0:T(8,128)} %copy.97), kind=kLoop, calls=%fused_computation.10 | loop fusion | flops 15728384 | bytes 15750144 | tf_op jit(solution)/shard_map/reduce_sum | solution.py:245
  196.4 2.3 copy-done
  198.7 1.0 convert_reduce_fusion
  199.7 8.9 %all-gather.6.cloned.1.call-done = bf16[5120,256]{1,0:T(8,128)(2,1)} async-done(((bf16[640,256]{1,0:T(8,128)(2,1)}), bf16[5120,256]{1,0:T(8,128)(2,1)}) %all-gather.6.cloned.1.call-update) | async-done | bytes 2621456 | tf_op jit(solution)/shard_map/all_gather | solution.py:178
  208.6 2.3 multiply_reduce_fusion.2
  210.9 18.4 %all-gather = f32[64,256]{1,0:T(8,128)S(1)} all-gather(f32[8,256]{1,0:T(8,128)S(1)} %get-tuple-element.94), channel_id=2, replica_groups=mesh['dp'=8,'seq'=32] {'dp'}, dimensions={0}, use_global_device_ids=true | all-gather | bytes 73728 | tf_op jit(solution)/shard_map/all_gather | solution.py:153
  229.2 1.6 broadcast_in_dim.144
  230.8 17.0 %all-to-all-start.1 = ((f32[32,8,8,256]{3,2,1,0:T(8,128)}), f32[32,8,8,256]{3,2,1,0:T(8,128)}, u32[]{:S(2)}, u32[]{:S(2)}) async-start(f32[32,8,8,256]{3,2,1,0:T(8,128)} %broadcast_in_dim.144), calls=%async_computation.1 | async-start | bytes 4194304 | tf_op jit(solution)/shard_map/all_to_all | solution.py:144
  247.8 4.7 %fusion.106 = bf16[1,256,5120]{2,1,0:T(8,128)(2,1)} fusion(f32[5120]{0:T(1024)S(1)} %copy-done.30, f32[256,5120]{1,0:T(8,128)} %copy-done, f32[256]{0:T(256)S(1)} %add_rsqrt_fusion), kind=kLoop, calls=%fused_computation.235 | loop fusion | flops 3932160 | bytes 7885824 | tf_op jit(solution)/shard_map/broadcast_in_dim | solution.py:259
  252.5 23.7 %all-to-all-done.1 = f32[32,8,8,256]{3,2,1,0:T(8,128)} async-done(((f32[32,8,8,256]{3,2,1,0:T(8,128)}), f32[32,8,8,256]{3,2,1,0:T(8,128)}, u32[]{:S(2)}, u32[]{:S(2)}) %all-to-all-start.1) | async-done | bytes 2097184 | tf_op jit(solution)/shard_map/all_to_all | solution.py:144
  276.2 1.8 copy.99
  278.6 4.2 %fusion.6 = f32[8,4096]{1,0:T(8,128)} fusion(f32[8,256]{1,0:T(8,128)S(1)} %get-tuple-element.94, f32[2048,256]{1,0:T(8,128)S(1)} %copy-done.14, f32[2048,256]{1,0:T(8,128)S(1)} %bitcast.88, f32[4096]{0:T(1024)S(1)} %multiply_reduce_fusion.1, f32[8]{0:T(128)S(1)} %get-tuple-element.93), kind=kOutput, calls=%fused_computation.18 | convolution fusion | flops 101875712 | bytes 4349984 | tf_op jit(solution)/shard_map/dot_general | solution.py:253
  (138 shorter events, 13.4 us)
Async XLA Ops:
  7.2 6.8 %copy-start.31 = (f32[1,80,256]{2,1,0:T(8,128)S(1)}, f32[1,80,256]{2,1,0:T(8,128)}, u32[]{:S(2)}) copy-start(f32[1,80,256]{2,1,0:T(8,128)} %param.21) | copy-start | bytes 245764
  7.2 8.2 %copy-start.32 = (f32[1,80,256]{2,1,0:T(8,128)S(1)}, f32[1,80,256]{2,1,0:T(8,128)}, u32[]{:S(2)}) copy-start(f32[1,80,256]{2,1,0:T(8,128)} %param.20) | copy-start | bytes 245764
  7.2 8.9 %copy-start.29 = (f32[4,5376]{1,0:T(4,128)S(1)}, f32[4,5376]{1,0:T(4,128)}, u32[]{:S(2)}) copy-start(f32[4,5376]{1,0:T(4,128)} %param.22) | copy-start | bytes 258052
  7.2 9.1 %copy-start.3 = (bf16[1,256,5120]{2,1,0:T(8,128)(2,1)S(1)}, bf16[1,256,5120]{2,1,0:T(8,128)(2,1)}, u32[]{:S(2)}) copy-start(bf16[1,256,5120]{2,1,0:T(8,128)(2,1)} %param.16) | copy-start | bytes 7864324
  7.2 9.1 %copy-start.20 = (bf16[1,256,128]{2,1,0:T(8,128)(2,1)S(1)}, bf16[1,256,128]{2,1,0:T(8,128)(2,1)}, u32[]{:S(2)}) copy-start(bf16[1,256,128]{2,1,0:T(8,128)(2,1)} %param.19) | copy-start | bytes 196612
  7.2 9.1 %copy-start.21 = (bf16[1,256,128]{2,1,0:T(8,128)(2,1)S(1)}, bf16[1,256,128]{2,1,0:T(8,128)(2,1)}, u32[]{:S(2)}) copy-start(bf16[1,256,128]{2,1,0:T(8,128)(2,1)} %param.18) | copy-start | bytes 196612
  9.4 6.9 %collective-permute-start = (bf16[3,5376]{1,0:T(4,128)(2,1)S(1)}, bf16[3,5376]{1,0:T(4,128)(2,1)S(1)}, u32[]{:S(2)}, u32[]{:S(2)}) collective-permute-start(bf16[3,5376]{1,0:T(4,128)(2,1)S(1)} %slice.301), channel_id=1, source_target_pairs={{0,1},{1,2},{2,3},{3,4},{4,5},{5,6},{6,7},{7,8},{8,9},{9,10},{10,1... | collective-permute-start | bytes 96776 | tf_op jit(solution)/shard_map/ppermute | solution.py:16
  14.3 4.4 %copy-start.23 = (f32[80,128]{1,0:T(8,128)}, f32[80,128]{1,0:T(8,128)S(1)}, u32[]{:S(2)}) copy-start(f32[80,128]{1,0:T(8,128)S(1)} %reduce_window_sum.17) | copy-start | bytes 122884
  14.6 4.1 %copy-start.25 = (f32[80,128]{1,0:T(8,128)}, f32[80,128]{1,0:T(8,128)S(1)}, u32[]{:S(2)}) copy-start(f32[80,128]{1,0:T(8,128)S(1)} %reduce_window_sum.18) | copy-start | bytes 122884
  16.3 2.5 copy-start.4
  16.3 2.5 copy-start.36
  23.2 14.9 %copy-start.1 = (bf16[256,5376]{1,0:T(8,128)(2,1)}, bf16[256,5376]{1,0:T(8,128)(2,1)S(1)}, u32[]{:S(2)}) copy-start(bf16[256,5376]{1,0:T(8,128)(2,1)S(1)} %multiply_convert_fusion) | copy-start | bytes 8257540
  30.2 3.9 %copy-start.15 = (bf16[128,5120]{0,1:T(8,128)(2,1)S(1)}, bf16[128,5120]{0,1:T(8,128)(2,1)}, u32[]{:S(2)}) copy-start(bf16[128,5120]{0,1:T(8,128)(2,1)} %copy.80) | copy-start | bytes 3932164
  34.1 1.8 copy-start.5
  36.8 6.9 %collective-permute-start.1 = (f32[80,65,128]{2,0,1:T(8,128)S(1)}, f32[80,65,128]{2,0,1:T(8,128)S(1)}, u32[]{:S(2)}, u32[]{:S(2)}) collective-permute-start(f32[80,65,128]{2,0,1:T(8,128)S(1)} %copy.81), channel_id=1, source_target_pairs={{0,1},{2,3},{4,5},{6,7},{8,9},{10,11},{12,13},{14,15},{16,17},{18,... | collective-permute-start | bytes 7987208 | tf_op jit(solution)/shard_map/ppermute | solution.py:114
  43.8 1.6 copy-start.7
  51.3 19.3 %collective-permute-start.3 = (bf16[80,65,128]{2,0,1:T(8,128)(2,1)}, bf16[80,65,128]{2,0,1:T(8,128)(2,1)}, u32[]{:S(2)}, u32[]{:S(2)}) collective-permute-start(bf16[80,65,128]{2,0,1:T(8,128)(2,1)} %fusion.40), channel_id=1, source_target_pairs={{1,7},{3,1},{5,3},{7,5},{9,15},{11,9},{13,11},{15,13},{17,23},{19,... | collective-permute-start | bytes 3993608 | tf_op jit(solution)/shard_map/ppermute | solution.py:74
  55.5 21.3 %collective-permute-start.2 = (bf16[80,65,128]{2,0,1:T(8,128)(2,1)}, bf16[80,65,128]{2,0,1:T(8,128)(2,1)}, u32[]{:S(2)}, u32[]{:S(2)}) collective-permute-start(bf16[80,65,128]{2,0,1:T(8,128)(2,1)} %fusion.40), channel_id=1, source_target_pairs={{1,3},{3,5},{5,7},{7,1},{9,11},{11,13},{13,15},{15,9},{17,19},{19,... | collective-permute-start | bytes 3993608 | tf_op jit(solution)/shard_map/ppermute | solution.py:73
  71.7 12.7 %collective-permute-start.4 = (bf16[40,65,128]{2,0,1:T(8,128)(2,1)S(1)}, bf16[40,65,128]{2,0,1:T(8,128)(2,1)S(1)}, u32[]{:S(2)}, u32[]{:S(2)}) collective-permute-start(bf16[40,65,128]{2,0,1:T(8,128)(2,1)S(1)} %slice.326), channel_id=1, source_target_pairs={{1,7},{3,1},{5,3},{7,5},{9,15},{11,9},{13,11},{15,13},{17,23},{19,... | collective-permute-start | bytes 1996808 | tf_op jit(solution)/shard_map/ppermute | solution.py:75
  77.9 12.7 %collective-permute-start.5 = (bf16[40,65,128]{2,0,1:T(8,128)(2,1)S(1)}, bf16[40,65,128]{2,0,1:T(8,128)(2,1)S(1)}, u32[]{:S(2)}, u32[]{:S(2)}) collective-permute-start(bf16[40,65,128]{2,0,1:T(8,128)(2,1)S(1)} %slice.327), channel_id=1, source_target_pairs={{1,3},{3,5},{5,7},{7,1},{9,11},{11,13},{13,15},{15,9},{17,19},{19,... | collective-permute-start | bytes 1996808 | tf_op jit(solution)/shard_map/ppermute | solution.py:76
  90.7 1.1 copy-start.17
  92.5 0.5 copy-start.42
  99.8 6.8 %copy-start.37 = (f32[8,256]{1,0:T(8,128)S(1)}, f32[8,256]{1,0:T(8,128)}, u32[]{:S(2)}) copy-start(f32[8,256]{1,0:T(8,128)} %param.27) | copy-start | bytes 24580
  101.1 20.4 %collective-permute-start.7 = (bf16[80,65,128]{2,0,1:T(8,128)(2,1)}, bf16[80,65,128]{2,0,1:T(8,128)(2,1)}, u32[]{:S(2)}, u32[]{:S(2)}) collective-permute-start(bf16[80,65,128]{2,0,1:T(8,128)(2,1)} %fusion.41), channel_id=1, source_target_pairs={{1,25},{3,27},{5,29},{7,31},{9,1},{11,3},{13,5},{15,7},{17,9},{19,... | collective-permute-start | bytes 3993608 | tf_op jit(solution)/shard_map/ppermute | solution.py:74
  104.7 25.0 %collective-permute-start.6 = (bf16[80,65,128]{2,0,1:T(8,128)(2,1)}, bf16[80,65,128]{2,0,1:T(8,128)(2,1)}, u32[]{:S(2)}, u32[]{:S(2)}) collective-permute-start(bf16[80,65,128]{2,0,1:T(8,128)(2,1)} %fusion.41), channel_id=1, source_target_pairs={{1,9},{3,11},{5,13},{7,15},{9,17},{11,19},{13,21},{15,23},{17,25},... | collective-permute-start | bytes 3993608 | tf_op jit(solution)/shard_map/ppermute | solution.py:73
  107.3 21.4 %all-to-all-start = ((f32[32,8,256]{2,1,0:T(8,128)}), f32[32,8,256]{2,1,0:T(8,128)S(1)}, u32[]{:S(2)}, u32[]{:S(2)}) async-start(f32[32,8,256]{2,1,0:T(8,128)} %broadcast_in_dim.141), calls=%async_computation | async-start | bytes 524288 | tf_op jit(solution)/shard_map/all_to_all | solution.py:144
  111.8 61.4 %all-gather.4.cloned.1.call-start = ((), (), s32[]{:S(2)}) async-start(), calls=%async_computation.2 | async-start | bytes 2359296 | tf_op jit(solution)/shard_map/all_gather | solution.py:149
  123.4 13.2 %collective-permute-start.8 = (bf16[40,65,128]{2,0,1:T(8,128)(2,1)}, bf16[40,65,128]{2,0,1:T(8,128)(2,1)S(1)}, u32[]{:S(2)}, u32[]{:S(2)}) collective-permute-start(bf16[40,65,128]{2,0,1:T(8,128)(2,1)} %slice.343), channel_id=1, source_target_pairs={{1,25},{3,27},{5,29},{7,31},{9,1},{11,3},{13,5},{15,7},{17,9},{19,... | collective-permute-start | bytes 1996808 | tf_op jit(solution)/shard_map/ppermute | solution.py:75
  128.7 0.7 copy-start.19
  129.5 79.1 %all-gather.6.cloned.1.call-start = ((), (), s32[]{:S(2)}) async-start(), calls=%async_computation.3 | async-start | bytes 2949120 | tf_op jit(solution)/shard_map/all_gather | solution.py:178
  129.6 15.2 %copy-start.13 = (f32[80,64,128]{2,0,1:T(8,128)S(1)}, f32[80,64,128]{2,0,1:T(8,128)}, u32[]{:S(2)}) copy-start(f32[80,64,128]{2,0,1:T(8,128)} %get-tuple-element.49) | copy-start | bytes 7864324
  131.0 12.7 %collective-permute-start.9 = (bf16[40,65,128]{2,0,1:T(8,128)(2,1)S(1)}, bf16[40,65,128]{2,0,1:T(8,128)(2,1)S(1)}, u32[]{:S(2)}, u32[]{:S(2)}) collective-permute-start(bf16[40,65,128]{2,0,1:T(8,128)(2,1)S(1)} %slice.344), channel_id=1, source_target_pairs={{1,9},{3,11},{5,13},{7,15},{9,17},{11,19},{13,21},{15,23},{17,25},... | collective-permute-start | bytes 1996808 | tf_op jit(solution)/shard_map/ppermute | solution.py:76
  144.8 2.7 copy-start.10
  144.8 3.4 %copy-start.11 = (f32[80,64,128]{2,0,1:T(8,128)S(1)}, f32[80,64,128]{2,0,1:T(8,128)}, u32[]{:S(2)}) copy-start(f32[80,64,128]{2,0,1:T(8,128)} %get-tuple-element.61) | copy-start | bytes 7864324
  144.8 4.2 %copy-start.12 = (f32[80,64,128]{2,0,1:T(8,128)S(1)}, f32[80,64,128]{2,0,1:T(8,128)}, u32[]{:S(2)}) copy-start(f32[80,64,128]{2,0,1:T(8,128)} %get-tuple-element.62) | copy-start | bytes 7864324
  144.9 4.2 %copy-start.38 = (f32[80]{0:T(128)S(1)}, f32[80]{0:T(128)}, u32[]{:S(2)}) copy-start(f32[80]{0:T(128)} %get-tuple-element.71) | copy-start | bytes 964
  144.9 4.2 %copy-start.39 = (f32[80]{0:T(128)S(1)}, f32[80]{0:T(128)}, u32[]{:S(2)}) copy-start(f32[80]{0:T(128)} %get-tuple-element.72) | copy-start | bytes 964
  149.0 8.9 %copy-start.43 = (f32[80]{0:T(128)S(1)}, f32[80]{0:T(128)}, u32[]{:S(2)}) copy-start(f32[80]{0:T(128)} %param.24) | copy-start | bytes 964
  149.0 9.1 %copy-start.22 = (bf16[256,128]{1,0:T(8,128)(2,1)S(1)}, bf16[256,128]{1,0:T(8,128)(2,1)}, u32[]{:S(2)}) copy-start(bf16[256,128]{1,0:T(8,128)(2,1)} %slice.306) | copy-start | bytes 196612
  149.1 10.9 %copy-start.26 = (f32[80,128]{1,0:T(8,128)S(1)}, f32[80,128]{1,0:T(8,128)}, u32[]{:S(2)}) copy-start(f32[80,128]{1,0:T(8,128)} %copy-done.25) | copy-start | bytes 122884
  149.1 10.9 %copy-start.35 = (f32[80,128]{1,0:T(8,128)S(1)}, f32[80,128]{1,0:T(8,128)}, u32[]{:S(2)}) copy-start(f32[80,128]{1,0:T(8,128)} %get-tuple-element.63) | copy-start | bytes 122884
  156.2 12.3 %collective-permute-start.10 = (f32[80,64,128]{2,1,0:T(8,128)}, f32[80,64,128]{2,1,0:T(8,128)S(1)}, u32[]{:S(2)}, u32[]{:S(2)}) collective-permute-start(f32[80,64,128]{2,1,0:T(8,128)} %fusion.16), channel_id=1, source_target_pairs={{1,0},{3,2},{5,4},{7,6},{9,8},{11,10},{13,12},{15,14},{17,16},{19,... | collective-permute-start | bytes 7864328 | tf_op jit(solution)/shard_map/ppermute | solution.py:132
  160.0 4.5 %copy-start.16 = (bf16[128,5120]{0,1:T(8,128)(2,1)S(1)}, bf16[128,5120]{0,1:T(8,128)(2,1)}, u32[]{:S(2)}) copy-start(bf16[128,5120]{0,1:T(8,128)(2,1)} %copy.80) | copy-start | bytes 3932164
  160.0 4.5 %copy-start.24 = (f32[80,128]{1,0:T(8,128)S(1)}, f32[80,128]{1,0:T(8,128)}, u32[]{:S(2)}) copy-start(f32[80,128]{1,0:T(8,128)} %copy-done.23) | copy-start | bytes 122884
  160.0 4.5 %copy-start.34 = (f32[80,128]{1,0:T(8,128)S(1)}, f32[80,128]{1,0:T(8,128)}, u32[]{:S(2)}) copy-start(f32[80,128]{1,0:T(8,128)} %get-tuple-element.66) | copy-start | bytes 122884
  164.5 5.6 %copy-start.8 = (f32[80,64,128]{2,0,1:T(8,128)S(1)}, f32[80,64,128]{2,0,1:T(8,128)}, u32[]{:S(2)}) copy-start(f32[80,64,128]{2,0,1:T(8,128)} %copy-done.7) | copy-start | bytes 7864324
  164.5 5.6 %copy-start.41 = (f32[80]{0:T(128)S(1)}, f32[80]{0:T(128)}, u32[]{:S(2)}) copy-start(f32[80]{0:T(128)} %get-tuple-element.85) | copy-start | bytes 964
  168.6 1.5 copy-start.18
  170.1 3.0 %copy-start.28 = (f32[128,80]{0,1:T(8,128)S(1)}, f32[128,80]{0,1:T(8,128)}, u32[]{:S(2)}) copy-start(f32[128,80]{0,1:T(8,128)} %get-tuple-element.70) | copy-start | bytes 122884
  173.1 5.5 %copy-start.9 = (f32[80,64,128]{2,1,0:T(8,128)}, f32[80,64,128]{2,1,0:T(8,128)S(1)}, u32[]{:S(2)}) copy-start(f32[80,64,128]{2,1,0:T(8,128)S(1)} %add_select_fusion) | copy-start | bytes 7864324
  178.6 3.4 %copy-start.6 = (f32[80,64,128]{2,1,0:T(8,128)S(1)}, f32[80,64,128]{2,1,0:T(8,128)}, u32[]{:S(2)}) copy-start(f32[80,64,128]{2,1,0:T(8,128)} %copy-done.5) | copy-start | bytes 7864324
  178.6 3.4 %copy-start.27 = (f32[128,80]{0,1:T(8,128)S(1)}, f32[128,80]{0,1:T(8,128)}, u32[]{:S(2)}) copy-start(f32[128,80]{0,1:T(8,128)} %get-tuple-element.69) | copy-start | bytes 122884
  178.6 3.4 %copy-start.40 = (f32[80]{0:T(128)S(1)}, f32[80]{0:T(128)}, u32[]{:S(2)}) copy-start(f32[80]{0:T(128)} %get-tuple-element.80) | copy-start | bytes 964
  187.7 3.4 %copy-start.2 = (bf16[256,5376]{1,0:T(8,128)(2,1)S(1)}, bf16[256,5376]{1,0:T(8,128)(2,1)}, u32[]{:S(2)}) copy-start(bf16[256,5376]{1,0:T(8,128)(2,1)} %copy-done.1) | copy-start | bytes 8257540
  191.1 7.6 %copy-start.30 = (f32[5120]{0:T(1024)S(1)}, f32[5120]{0:T(1024)}, u32[]{:S(2)}) copy-start(f32[5120]{0:T(1024)} %param.25) | copy-start | bytes 61444
  196.4 2.3 copy-start
  210.9 67.7 %copy-start.33 = (f32[8,256]{1,0:T(8,128)}, f32[8,256]{1,0:T(8,128)S(1)}, u32[]{:S(2)}) copy-start(f32[8,256]{1,0:T(8,128)S(1)} %get-tuple-element.94) | copy-start | bytes 24580
  230.8 45.4 %all-to-all-start.1 = ((f32[32,8,8,256]{3,2,1,0:T(8,128)}), f32[32,8,8,256]{3,2,1,0:T(8,128)}, u32[]{:S(2)}, u32[]{:S(2)}) async-start(f32[32,8,8,256]{3,2,1,0:T(8,128)} %broadcast_in_dim.144), calls=%async_computation.1 | async-start | bytes 4194304 | tf_op jit(solution)/shard_map/all_to_all | solution.py:144
  252.5 25.5 %copy-start.14 = (f32[2048,256]{1,0:T(8,128)S(1)}, f32[2048,256]{1,0:T(8,128)}, u32[]{:S(2)}) copy-start(f32[2048,256]{1,0:T(8,128)} %all-gather.4.cloned.1.call-done) | copy-start | bytes 6291460
Sparse Core Ops, SparseCore 0:
  129.6 35.2 all-gather.3
  166.7 41.8 all-gather.5

commit v6 on v4

--- a/solution.py
+++ b/solution.py
@@ -124,9 +124,9 @@
 
 
 def codes_everywhere(block):
-    rows = lax.all_gather(block, "dp", axis=0, tiled=False)
+    rows = spread_over(block.astype(XFER), "dp")
     got = spread_over(rows, "seq")
-    return jnp.swapaxes(got, 0, 1).reshape((-1,) + block.shape[1:])
+    return jnp.swapaxes(got, 0, 1).reshape((-1,) + block.shape[1:]).astype(jnp.float32)
 
 
 def per_device(

time: 276 us -> 251 us (0.909)
  waiting for transfers between devices: 74.1 us -> 62 us
  blocking collectives: 21.7 us -> 14.4 us
  starting transfers between devices: 54.3 us -> 49.8 us
    all_gather x1 -> x0, blocking collectives: 21.7 us -> none  [codes_everywhere(): rows = lax.all_gather(block, 'dp', axis=0, tiled=False)]
    all_to_all x0 -> x1, blocking collectives: none -> 14.4 us  [spread_over(): lax.all_to_all(jnp.broadcast_to(block[None], (count,) + block.shape), axi...]
    all_to_all x3, waiting for transfers between devices: 30.7 us -> 18.5 us  [spread_over(): lax.all_to_all(jnp.broadcast_to(block[None], (count,) + block.shape), axi...]
    all_to_all x3, starting transfers between devices: 23.2 us -> 18.7 us  [spread_over(): lax.all_to_all(jnp.broadcast_to(block[None], (count,) + block.shape), axi...]
  transfers between devices with their start and end apart: 16 -> 16, of which waited for: 8 -> 8; matrix products, arithmetic and copies ran while one was open for 24% -> 26% of each run, Pallas kernels for 0% -> 0%
where the time goes in v6:
time: 251 us; the launch traced here: 250 us
  waiting for transfers between devices  62 us (25%)
  starting transfers between devices  49.8 us (20%)
  other arithmetic  46.2 us (18%)
  matrix products  35.4 us (14%)
  local copies, waits for them, and re-layouts  27.4 us (11%)
  between operations  15 us (6%)
  blocking collectives  14.4 us (6%)
    ppermute x2, waiting for transfers between devices, ring_of_four(): next_state = lax.ppermute(sent, 'seq', bwd)  23.7 us
    all_to_all x3, starting transfers between devices, spread_over(): lax.all_to_all(jnp.broadcast_to(block[None], (count,) + block.shape), axi...  18.7 us
    all_to_all x3, waiting for transfers between devices, spread_over(): lax.all_to_all(jnp.broadcast_to(block[None], (count,) + block.shape), axi...  18.5 us
    all_to_all x1, blocking collectives, spread_over(): lax.all_to_all(jnp.broadcast_to(block[None], (count,) + block.shape), axi...  14.4 us
    ppermute x2, waiting for transfers between devices, ring_of_four(): far_b = lax.ppermute(prev_state[half:], 'seq', fwd)  14 us
    dot_general x2, matrix products, per_device(): jnp.einsum('tn,hpn->thp', read_block, start, precision=lax.Precision.HIGH...  11.8 us
    dot_general x2, matrix products, block_terms(): jnp.einsum('hts,shp->thp', mixing, values, preferred_element_type=jnp.flo...  8.55 us
    convert_element_type x2, other arithmetic, ring_of_four(): sent = state.astype(XFER)  8.5 us
  transfers between devices with their start and end apart: 16, of which 8 were waited for; matrix products, arithmetic and copies ran while one was open for 26% of the time, Pallas kernels for 0%

profile of v6, /device:TPU:1, one launch (start us, length us, event | category | flops | bytes accessed | tf_op | source)
XLA Modules:
  0.0 250.2 jit_solution(4655904653025436980)
XLA Ops:
  7.2 2.1 pad_maximum_fusion.2
  9.4 4.6 %collective-permute-start = (bf16[3,5376]{1,0:T(4,128)(2,1)S(1)}, bf16[3,5376]{1,0:T(4,128)(2,1)S(1)}, u32[]{:S(2)}, u32[]{:S(2)}) collective-permute-start(bf16[3,5376]{1,0:T(4,128)(2,1)S(1)} %slice.128), channel_id=1, source_target_pairs={{0,1},{1,2},{2,3},{3,4},{4,5},{5,6},{6,7},{7,8},{8,9},{9,10},{10,1... | collective-permute-start | bytes 96776 | tf_op jit(solution)/shard_map/ppermute | solution.py:16
  14.8 0.5 fusion.105
  15.3 0.7 fusion.103
  16.3 2.4 maximum_maximum_fusion
  18.7 4.4 %multiply_convert_fusion = bf16[256,5376]{1,0:T(8,128)(2,1)S(1)} fusion(bf16[259,5376]{1,0:T(8,128)(2,1)S(1)} %maximum_maximum_fusion, f32[5376]{0:T(1024)S(1)} %get-tuple-element.9, f32[5376]{0:T(1024)S(1)} %get-tuple-element.10, f32[5376]{0:T(1024)S(1)} %get-tuple-element.8, f32[5376]{0:T(1024)S(1)} %get-tuple-element.7, f32[5376]{0:T(1024)S(1)} %copy-done.18, ...), kind=kLoop, calls=%fused_computation.2 | loop fusion | flops 30277632 | bytes 13870080 | tf_op jit(solution)/shard_map/convert_element_type | solution.py:161
  23.1 1.8 fusion.102
  24.9 2.4 copy.39
  27.4 2.4 copy.40
  29.8 3.9 %fusion.16 = f32[80,64,128]{2,1,0:T(8,128)S(1)} fusion(bf16[128,80,64]{0,2,1:T(8,128)(2,1)} %bitcast.81, f32[128,128]{1,0:T(8,128)S(1)} %get-tuple-element.23, f32[80,128]{1,0:T(8,128)S(1)} %get-tuple-element.27), kind=kOutput, calls=%fused_computation.38 | convolution fusion | flops 170393600 | bytes 4038656 | tf_op jit(solution)/shard_map/hsn,shp->hpn/dot_general | solution.py:29
  33.8 4.3 %multiply_add_fusion.1 = f32[80,64,128]{2,1,0:T(8,128)} fusion(f32[80,64,128]{2,1,0:T(8,128)S(1)} %fusion.16, bf16[128,80,64]{0,2,1:T(8,128)(2,1)S(1)} %bitcast.83, f32[128,128]{1,0:T(8,128)S(1)} %get-tuple-element.22, f32[80,128]{1,0:T(8,128)S(1)} %get-tuple-element.28, f32[80]{0:T(128)S(1)} %get-tuple-element.54, f32[80]{0:T(128)S(1)} %get-tuple-element.56), kind=kOutput, calls=%fused_computation.54 | convolution fusion | flops 172359680 | bytes 6660736 | tf_op jit(solution)/shard_map/hsn,shp->hpn/dot_general | solution.py:29
  38.0 1.3 collective-permute-start.1
  39.3 0.6 broadcast_in_dim.148
  39.9 9.5 %all-to-all-start.1 = ((f32[32,1,80]{2,1,0:T(1,128)}), f32[32,1,80]{2,1,0:T(1,128)S(1)}, u32[]{:S(2)}, u32[]{:S(2)}) async-start(f32[32,1,80]{2,1,0:T(1,128)} %broadcast_in_dim.148), calls=%async_computation.1 | async-start | bytes 32768 | tf_op jit(solution)/shard_map/all_to_all | solution.py:118
  49.4 7.0 %all-to-all-done.1 = f32[32,1,80]{2,1,0:T(1,128)S(1)} async-done(((f32[32,1,80]{2,1,0:T(1,128)}), f32[32,1,80]{2,1,0:T(1,128)S(1)}, u32[]{:S(2)}, u32[]{:S(2)}) %all-to-all-start.1) | async-done | bytes 10272 | tf_op jit(solution)/shard_map/all_to_all | solution.py:118
  56.4 0.5 fusion.93
  56.9 4.9 %fusion.101 = (bf16[80,64,128]{2,1,0:T(8,128)(2,1)}, f32[80,64,128]{2,1,0:T(8,128)}) fusion(f32[80,64,128]{2,1,0:T(8,128)} %multiply_add_fusion.1, f32[80,64,128]{2,1,0:T(8,128)} %collective-permute-done.1, f32[80]{0:T(128)S(1)} %get-tuple-element.35), kind=kLoop, calls=%fused_computation.208 | loop fusion | flops 1966080 | bytes 9175360 | tf_op jit(solution)/shard_map/convert_element_type | solution.py:51
  61.9 2.8 %collective-permute-start.3 = (bf16[80,64,128]{2,1,0:T(8,128)(2,1)}, bf16[80,64,128]{2,1,0:T(8,128)(2,1)}, u32[]{:S(2)}, u32[]{:S(2)}) collective-permute-start(bf16[80,64,128]{2,1,0:T(8,128)(2,1)} %get-tuple-element.20), channel_id=1, source_target_pairs={{1,7},{3,1},{5,3},{7,5},{9,15},{11,9},{13,11},{15,13},{17,23},{19,... | collective-permute-start | bytes 3932168 | tf_op jit(solution)/shard_map/ppermute | solution.py:53
  64.7 2.5 collective-permute-start.2
  67.2 0.7 broadcast_in_dim.147
  67.9 4.6 %all-to-all-start = ((f32[32,8,256]{2,1,0:T(8,128)}), f32[32,8,256]{2,1,0:T(8,128)}, u32[]{:S(2)}, u32[]{:S(2)}) async-start(f32[32,8,256]{2,1,0:T(8,128)} %broadcast_in_dim.147), calls=%async_computation | async-start | bytes 524288 | tf_op jit(solution)/shard_map/all_to_all | solution.py:118
  72.8 10.2 %collective-permute-done.3 = bf16[80,64,128]{2,1,0:T(8,128)(2,1)} collective-permute-done((bf16[80,64,128]{2,1,0:T(8,128)(2,1)}, bf16[80,64,128]{2,1,0:T(8,128)(2,1)}, u32[]{:S(2)}, u32[]{:S(2)}) %collective-permute-start.3) | collective-permute-done | bytes 1310752 | tf_op jit(solution)/shard_map/ppermute | solution.py:53
  83.0 2.0 slice.145
  85.0 4.0 %collective-permute-start.4 = (bf16[40,64,128]{2,1,0:T(8,128)(2,1)}, bf16[40,64,128]{2,1,0:T(8,128)(2,1)S(1)}, u32[]{:S(2)}, u32[]{:S(2)}) collective-permute-start(bf16[40,64,128]{2,1,0:T(8,128)(2,1)} %slice.145), channel_id=1, source_target_pairs={{1,7},{3,1},{5,3},{7,5},{9,15},{11,9},{13,11},{15,13},{17,23},{19,... | collective-permute-start | bytes 1966088 | tf_op jit(solution)/shard_map/ppermute | solution.py:54
  89.0 2.0 slice.146
  91.0 1.9 collective-permute-start.5
  92.9 0.6 exponential_bitcast_fusion.2
  93.5 0.6 fusion.59
  94.1 0.6 fusion.58
  94.8 2.0 collective-permute-done.4
  96.8 7.0 %collective-permute-done.5 = bf16[40,64,128]{2,1,0:T(8,128)(2,1)} collective-permute-done((bf16[40,64,128]{2,1,0:T(8,128)(2,1)}, bf16[40,64,128]{2,1,0:T(8,128)(2,1)}, u32[]{:S(2)}, u32[]{:S(2)}) %collective-permute-start.5) | collective-permute-done | bytes 655392 | tf_op jit(solution)/shard_map/ppermute | solution.py:55
  103.8 3.6 %fusion.25 = bf16[80,64,128]{2,1,0:T(8,128)(2,1)S(1)} fusion(bf16[80,64,128]{2,1,0:T(8,128)(2,1)} %collective-permute-done.3, bf16[80,64,128]{2,1,0:T(8,128)(2,1)} %collective-permute-done.2, f32[80,64,128]{2,1,0:T(8,128)} %get-tuple-element.21, f32[80]{0:T(128)} %get-tuple-element.49, f32[80]{0:T(128)} %get-tuple-element.51, f32[80]{0:T(128)} %get-tuple-element.44, ...), kind=kLoop, calls=%fused_computation.50 | loop fusion | flops 7864320 | bytes 7865600 | tf_op jit(solution)/shard_map/convert_element_type | solution.py:51
  107.4 2.8 %collective-permute-start.7 = (bf16[80,64,128]{2,1,0:T(8,128)(2,1)S(1)}, bf16[80,64,128]{2,1,0:T(8,128)(2,1)S(1)}, u32[]{:S(2)}, u32[]{:S(2)}) collective-permute-start(bf16[80,64,128]{2,1,0:T(8,128)(2,1)S(1)} %fusion.25), channel_id=1, source_target_pairs={{1,25},{3,27},{5,29},{7,31},{9,1},{11,3},{13,5},{15,7},{17,9},{19,... | collective-permute-start | bytes 3932168 | tf_op jit(solution)/shard_map/ppermute | solution.py:53
  110.2 2.5 collective-permute-start.6
  112.7 13.5 %collective-permute-done.7 = bf16[80,64,128]{2,1,0:T(8,128)(2,1)S(1)} collective-permute-done((bf16[80,64,128]{2,1,0:T(8,128)(2,1)S(1)}, bf16[80,64,128]{2,1,0:T(8,128)(2,1)S(1)}, u32[]{:S(2)}, u32[]{:S(2)}) %collective-permute-start.7) | collective-permute-done | bytes 1310752 | tf_op jit(solution)/shard_map/ppermute | solution.py:53
  126.2 1.1 copy-done.7
  127.2 0.9 slice.147
  128.1 4.0 %collective-permute-start.8 = (bf16[40,64,128]{2,1,0:T(8,128)(2,1)}, bf16[40,64,128]{2,1,0:T(8,128)(2,1)}, u32[]{:S(2)}, u32[]{:S(2)}) collective-permute-start(bf16[40,64,128]{2,1,0:T(8,128)(2,1)} %slice.147), channel_id=1, source_target_pairs={{1,25},{3,27},{5,29},{7,31},{9,1},{11,3},{13,5},{15,7},{17,9},{19,... | collective-permute-start | bytes 1966088 | tf_op jit(solution)/shard_map/ppermute | solution.py:54
  132.1 1.1 copy-done.8
  133.2 0.9 slice.148
  134.1 1.9 collective-permute-start.9
  136.2 3.7 %collective-permute-done.8 = bf16[40,64,128]{2,1,0:T(8,128)(2,1)} collective-permute-done((bf16[40,64,128]{2,1,0:T(8,128)(2,1)}, bf16[40,64,128]{2,1,0:T(8,128)(2,1)}, u32[]{:S(2)}, u32[]{:S(2)}) %collective-permute-start.8) | collective-permute-done | bytes 655392 | tf_op jit(solution)/shard_map/ppermute | solution.py:54
  139.9 7.0 %collective-permute-done.9 = bf16[40,64,128]{2,1,0:T(8,128)(2,1)} collective-permute-done((bf16[40,64,128]{2,1,0:T(8,128)(2,1)}, bf16[40,64,128]{2,1,0:T(8,128)(2,1)}, u32[]{:S(2)}, u32[]{:S(2)}) %collective-permute-start.9) | collective-permute-done | bytes 655392 | tf_op jit(solution)/shard_map/ppermute | solution.py:55
  146.9 7.6 %fusion.15 = f32[80,64,128]{2,1,0:T(8,128)} fusion(bf16[80,64,128]{2,1,0:T(8,128)(2,1)} %collective-permute-done.2, bf16[80,64,128]{2,1,0:T(8,128)(2,1)} %collective-permute-done.3, f32[80,64,128]{2,1,0:T(8,128)} %get-tuple-element.21, bf16[80,64,128]{2,1,0:T(8,128)(2,1)} %copy-done.7, bf16[80,64,128]{2,1,0:T(8,128)(2,1)} %copy-done.8, ...), kind=kLoop, calls=%fused_computation.37 | loop fusion | flops 20316160 | bytes 13111360 | tf_op jit(solution)/shard_map/add | solution.py:105
  154.5 2.8 %collective-permute-start.10 = (f32[80,64,128]{2,1,0:T(8,128)}, f32[80,64,128]{2,1,0:T(8,128)}, u32[]{:S(2)}, u32[]{:S(2)}) collective-permute-start(f32[80,64,128]{2,1,0:T(8,128)} %fusion.15), channel_id=1, source_target_pairs={{1,0},{3,2},{5,4},{7,6},{9,8},{11,10},{13,12},{15,14},{17,16},{19,... | collective-permute-start | bytes 7864328 | tf_op jit(solution)/shard_map/ppermute | solution.py:106
  157.8 4.5 %fusion.7 = f32[80,64,128]{2,1,0:T(8,128)} fusion(bf16[128,80,64]{0,2,1:T(8,128)(2,1)} %bitcast.82, f32[80,128]{1,0:T(8,128)} %get-tuple-element.26, f32[80,128]{1,0:T(8,128)S(1)} %reduce_window_sum.17, f32[128,128]{1,0:T(8,128)S(1)} %fusion.51, pred[128,128]{1,0:T(8,128)(4,1)S(1)} %iota_compare_fusion), kind=kOutput, calls=%fused_computation.29 | convolution fusion | flops 174325760 | bytes 4096000 | tf_op jit(solution)/shard_map/hts,shp->thp/dot_general | solution.py:26
  162.3 4.1 %fusion.8 = f32[80,64,128]{2,1,0:T(8,128)} fusion(bf16[128,80,64]{0,2,1:T(8,128)(2,1)S(1)} %bitcast.84, f32[80,128]{1,0:T(8,128)S(1)} %copy-done.16, f32[80,128]{1,0:T(8,128)S(1)} %reduce_window_sum.18, f32[128,128]{1,0:T(8,128)S(1)} %fusion.48, pred[128,128]{1,0:T(8,128)(4,1)S(1)} %iota_compare_fusion), kind=kOutput, calls=%fused_computation.30 | convolution fusion | flops 174325760 | bytes 4096000 | tf_op jit(solution)/shard_map/hts,shp->thp/dot_general | solution.py:26
  166.4 4.4 %add_select_fusion = f32[80,64,128]{2,1,0:T(8,128)} fusion(f32[80,64,128]{2,1,0:T(8,128)} %collective-permute-done.10, f32[80,64,128]{2,1,0:T(8,128)} %collective-permute-done.1, f32[80,64,128]{2,1,0:T(8,128)} %fusion.15, f32[80]{0:T(128)S(1)} %copy-done.25, pred[]{:T(512)S(6)} %eq.14), kind=kLoop, calls=%fused_computation.49 | loop fusion | flops 1966080 | bytes 10486081 | tf_op jit(solution)/shard_map/jit(_where)/select_n | solution.py:108
  170.8 5.4 %bitcast_add_fusion.1 = f32[128,80,64]{0,2,1:T(8,128)} fusion(f32[80,64,128]{2,1,0:T(8,128)} %fusion.7, f32[80,64,128]{2,1,0:T(8,128)} %add_select_fusion, f32[128,80]{0,1:T(8,128)S(1)} %copy-done.11, bf16[256,5376]{1,0:T(8,128)(2,1)S(1)} %multiply_convert_fusion), kind=kOutput, calls=%fused_computation.41 | convolution fusion | flops 1007943680 | bytes 7938048 | tf_op jit(solution)/shard_map/tn,hpn->thp/dot_general | solution.py:204
  176.2 3.3 %copy.45 = f32[128,5120]{1,0:T(8,128)} copy(f32[128,5120]{0,1:T(8,128)} %bitcast.79) | data formatting | bytes 5242880 | tf_op jit(solution)/shard_map/concatenate | solution.py:208
  179.5 6.5 %bitcast_add_fusion = f32[128,80,64]{0,2,1:T(8,128)} fusion(f32[80,64,128]{2,1,0:T(8,128)} %fusion.8, f32[80,64,128]{2,1,0:T(8,128)} %add_select_fusion, f32[80,64,128]{2,1,0:T(8,128)} %copy-done.3, f32[80]{0:T(128)S(1)} %copy-done.24, f32[128,80]{0,1:T(8,128)S(1)} %get-tuple-element.32, f32[80]{0:T(128)S(1)} %get-tuple-element.54, ...), kind=kOutput, calls=%fused_computation.40 | convolution fusion | flops 1009909760 | bytes 10560512 | tf_op jit(solution)/shard_map/tn,hpn->thp/dot_general | solution.py:204
  186.0 3.3 %copy.46 = f32[128,5120]{1,0:T(8,128)} copy(f32[128,5120]{0,1:T(8,128)} %bitcast.80) | data formatting | bytes 5242880 | tf_op jit(solution)/shard_map/concatenate | solution.py:208
  189.3 5.3 %multiply_reduce_fusion = (f32[256]{0:T(256)S(1)}, f32[256,5120]{1,0:T(8,128)S(1)}) fusion(bf16[1,256,5120]{2,1,0:T(8,128)(2,1)} %param.13, bf16[256,5376]{1,0:T(8,128)(2,1)S(1)} %multiply_convert_fusion, f32[5120]{0:T(1024)S(1)} %mul.390, f32[128,5120]{1,0:T(8,128)} %copy.46, f32[128,5120]{1,0:T(8,128)} %copy.45), kind=kLoop, calls=%fused_computation.10 | loop fusion | flops 15728384 | bytes 15750144 | tf_op jit(solution)/shard_map/reduce_sum | solution.py:211
  194.6 2.3 copy-done
  196.9 1.0 convert_reduce_fusion
  197.9 2.3 multiply_reduce_fusion.2
  200.2 14.4 %all_to_all.21 = bf16[8,8,256]{2,1,0:T(8,128)(2,1)S(1)} all-to-all(bf16[8,8,256]{2,1,0:T(8,128)(2,1)S(1)} %broadcast_in_dim.153), channel_id=1, replica_groups=mesh['dp'=8,'seq'=32] {'dp'}, dimensions={0} | all-to-all | bytes 65536 | tf_op jit(solution)/shard_map/all_to_all | solution.py:118
  214.7 1.1 broadcast_in_dim.154
  215.7 4.7 %all-to-all-start.3 = ((bf16[32,8,8,256]{3,2,1,0:T(8,128)(2,1)}), bf16[32,8,8,256]{3,2,1,0:T(8,128)(2,1)}, u32[]{:S(2)}, u32[]{:S(2)}) async-start(bf16[32,8,8,256]{3,2,1,0:T(8,128)(2,1)} %broadcast_in_dim.154), calls=%async_computation.3 | async-start | bytes 2097152 | tf_op jit(solution)/shard_map/all_to_all | solution.py:118
  220.4 4.7 %fusion.98 = bf16[1,256,5120]{2,1,0:T(8,128)(2,1)} fusion(f32[5120]{0:T(1024)S(1)} %copy-done.13, f32[256,5120]{1,0:T(8,128)} %copy-done, f32[256]{0:T(256)S(1)} %add_rsqrt_fusion), kind=kLoop, calls=%fused_computation.206 | loop fusion | flops 3932160 | bytes 7885824 | tf_op jit(solution)/shard_map/broadcast_in_dim | solution.py:225
  225.1 11.5 %all-to-all-done.3 = bf16[32,8,8,256]{3,2,1,0:T(8,128)(2,1)} async-done(((bf16[32,8,8,256]{3,2,1,0:T(8,128)(2,1)}), bf16[32,8,8,256]{3,2,1,0:T(8,128)(2,1)}, u32[]{:S(2)}, u32[]{:S(2)}) %all-to-all-start.3) | async-done | bytes 1048608 | tf_op jit(solution)/shard_map/all_to_all | solution.py:118
  236.6 1.6 copy_convert_fusion
  238.5 0.6 multiply_reduce_fusion.1
  239.1 4.2 %fusion.6 = f32[8,4096]{1,0:T(8,128)} fusion(f32[8,256]{1,0:T(8,128)S(1)} %get-tuple-element.57, f32[2048,256]{1,0:T(8,128)S(1)} %copy-done.4, f32[2048,256]{1,0:T(8,128)S(1)} %bitcast.78, f32[4096]{0:T(1024)S(1)} %multiply_reduce_fusion.1, f32[8]{0:T(128)S(1)} %get-tuple-element.36), kind=kOutput, calls=%fused_computation.18 | convolution fusion | flops 101875712 | bytes 4349984 | tf_op jit(solution)/shard_map/dot_general | solution.py:219
  (80 shorter events, 2.2 us)
Async XLA Ops:
  7.2 6.8 %copy-start.14 = (f32[1,80,256]{2,1,0:T(8,128)S(1)}, f32[1,80,256]{2,1,0:T(8,128)}, u32[]{:S(2)}) copy-start(f32[1,80,256]{2,1,0:T(8,128)} %param.17) | copy-start | bytes 245764
  7.2 8.2 %copy-start.15 = (f32[1,80,256]{2,1,0:T(8,128)S(1)}, f32[1,80,256]{2,1,0:T(8,128)}, u32[]{:S(2)}) copy-start(f32[1,80,256]{2,1,0:T(8,128)} %param.16) | copy-start | bytes 245764
  7.2 8.8 %copy-start.12 = (f32[4,5376]{1,0:T(4,128)S(1)}, f32[4,5376]{1,0:T(4,128)}, u32[]{:S(2)}) copy-start(f32[4,5376]{1,0:T(4,128)} %param.18) | copy-start | bytes 258052
  7.2 9.1 %copy-start.1 = (bf16[1,256,5120]{2,1,0:T(8,128)(2,1)S(1)}, bf16[1,256,5120]{2,1,0:T(8,128)(2,1)}, u32[]{:S(2)}) copy-start(bf16[1,256,5120]{2,1,0:T(8,128)(2,1)} %param.12) | copy-start | bytes 7864324
  7.2 9.1 %copy-start.9 = (bf16[1,256,128]{2,1,0:T(8,128)(2,1)S(1)}, bf16[1,256,128]{2,1,0:T(8,128)(2,1)}, u32[]{:S(2)}) copy-start(bf16[1,256,128]{2,1,0:T(8,128)(2,1)} %param.15) | copy-start | bytes 196612
  7.2 9.1 %copy-start.10 = (bf16[1,256,128]{2,1,0:T(8,128)(2,1)S(1)}, bf16[1,256,128]{2,1,0:T(8,128)(2,1)}, u32[]{:S(2)}) copy-start(bf16[1,256,128]{2,1,0:T(8,128)(2,1)} %param.14) | copy-start | bytes 196612
  9.4 6.8 %collective-permute-start = (bf16[3,5376]{1,0:T(4,128)(2,1)S(1)}, bf16[3,5376]{1,0:T(4,128)(2,1)S(1)}, u32[]{:S(2)}, u32[]{:S(2)}) collective-permute-start(bf16[3,5376]{1,0:T(4,128)(2,1)S(1)} %slice.128), channel_id=1, source_target_pairs={{0,1},{1,2},{2,3},{3,4},{4,5},{5,6},{6,7},{7,8},{8,9},{9,10},{10,1... | collective-permute-start | bytes 96776 | tf_op jit(solution)/shard_map/ppermute | solution.py:16
  16.2 2.4 copy-start.2
  16.2 2.4 copy-start.18
  29.8 3.9 %copy-start.5 = (bf16[128,5120]{0,1:T(8,128)(2,1)S(1)}, bf16[128,5120]{0,1:T(8,128)(2,1)}, u32[]{:S(2)}) copy-start(bf16[128,5120]{0,1:T(8,128)(2,1)} %copy.40) | copy-start | bytes 3932164
  33.7 4.3 %copy-start.3 = (f32[80,64,128]{2,1,0:T(8,128)}, f32[80,64,128]{2,1,0:T(8,128)S(1)}, u32[]{:S(2)}) copy-start(f32[80,64,128]{2,1,0:T(8,128)S(1)} %fusion.16) | copy-start | bytes 7864324
  38.0 18.9 %collective-permute-start.1 = (f32[80,64,128]{2,1,0:T(8,128)}, f32[80,64,128]{2,1,0:T(8,128)}, u32[]{:S(2)}, u32[]{:S(2)}) collective-permute-start(f32[80,64,128]{2,1,0:T(8,128)} %multiply_add_fusion.1), channel_id=1, source_target_pairs={{0,1},{2,3},{4,5},{6,7},{8,9},{10,11},{12,13},{14,15},{16,17},{18,... | collective-permute-start | bytes 7864328 | tf_op jit(solution)/shard_map/ppermute | solution.py:98
  39.9 16.4 %all-to-all-start.1 = ((f32[32,1,80]{2,1,0:T(1,128)}), f32[32,1,80]{2,1,0:T(1,128)S(1)}, u32[]{:S(2)}, u32[]{:S(2)}) async-start(f32[32,1,80]{2,1,0:T(1,128)} %broadcast_in_dim.148), calls=%async_computation.1 | async-start | bytes 32768 | tf_op jit(solution)/shard_map/all_to_all | solution.py:118
  56.9 10.2 %copy-start.19 = (f32[8,256]{1,0:T(8,128)S(1)}, f32[8,256]{1,0:T(8,128)}, u32[]{:S(2)}) copy-start(f32[8,256]{1,0:T(8,128)} %param.23) | copy-start | bytes 24580
  61.9 21.1 %collective-permute-start.3 = (bf16[80,64,128]{2,1,0:T(8,128)(2,1)}, bf16[80,64,128]{2,1,0:T(8,128)(2,1)}, u32[]{:S(2)}, u32[]{:S(2)}) collective-permute-start(bf16[80,64,128]{2,1,0:T(8,128)(2,1)} %get-tuple-element.20), channel_id=1, source_target_pairs={{1,7},{3,1},{5,3},{7,5},{9,15},{11,9},{13,11},{15,13},{17,23},{19,... | collective-permute-start | bytes 3932168 | tf_op jit(solution)/shard_map/ppermute | solution.py:53
  64.7 24.3 %collective-permute-start.2 = (bf16[80,64,128]{2,1,0:T(8,128)(2,1)}, bf16[80,64,128]{2,1,0:T(8,128)(2,1)}, u32[]{:S(2)}, u32[]{:S(2)}) collective-permute-start(bf16[80,64,128]{2,1,0:T(8,128)(2,1)} %get-tuple-element.20), channel_id=1, source_target_pairs={{1,3},{3,5},{5,7},{7,1},{9,11},{11,13},{13,15},{15,9},{17,19},{19,... | collective-permute-start | bytes 3932168 | tf_op jit(solution)/shard_map/ppermute | solution.py:52
  67.9 26.8 %all-to-all-start = ((f32[32,8,256]{2,1,0:T(8,128)}), f32[32,8,256]{2,1,0:T(8,128)}, u32[]{:S(2)}, u32[]{:S(2)}) async-start(f32[32,8,256]{2,1,0:T(8,128)} %broadcast_in_dim.147), calls=%async_computation | async-start | bytes 524288 | tf_op jit(solution)/shard_map/all_to_all | solution.py:118
  72.5 98.3 %all-gather.3.cloned.1.call-start = ((), (), s32[]{:S(2)}) async-start(), calls=%async_computation.4 | async-start | bytes 2359296 | tf_op jit(solution)/shard_map/all_gather | solution.py:123
  85.0 11.8 %collective-permute-start.4 = (bf16[40,64,128]{2,1,0:T(8,128)(2,1)}, bf16[40,64,128]{2,1,0:T(8,128)(2,1)S(1)}, u32[]{:S(2)}, u32[]{:S(2)}) collective-permute-start(bf16[40,64,128]{2,1,0:T(8,128)(2,1)} %slice.145), channel_id=1, source_target_pairs={{1,7},{3,1},{5,3},{7,5},{9,15},{11,9},{13,11},{15,13},{17,23},{19,... | collective-permute-start | bytes 1966088 | tf_op jit(solution)/shard_map/ppermute | solution.py:54
  91.0 12.8 %collective-permute-start.5 = (bf16[40,64,128]{2,1,0:T(8,128)(2,1)}, bf16[40,64,128]{2,1,0:T(8,128)(2,1)}, u32[]{:S(2)}, u32[]{:S(2)}) collective-permute-start(bf16[40,64,128]{2,1,0:T(8,128)(2,1)} %slice.146), channel_id=1, source_target_pairs={{1,3},{3,5},{5,7},{7,1},{9,11},{11,13},{13,15},{15,9},{17,19},{19,... | collective-permute-start | bytes 1966088 | tf_op jit(solution)/shard_map/ppermute | solution.py:55
  94.7 103.1 %all-gather.5.cloned.1.call-start = ((), (), s32[]{:S(2)}) async-start(), calls=%async_computation.5 | async-start | bytes 2949120 | tf_op jit(solution)/shard_map/all_gather | solution.py:152
  107.4 39.6 %copy-start.20 = (f32[80]{0:T(128)S(1)}, f32[80]{0:T(128)}, u32[]{:S(2)}) copy-start(f32[80]{0:T(128)} %get-tuple-element.44) | copy-start | bytes 964
  107.4 39.5 %copy-start.21 = (f32[80]{0:T(128)S(1)}, f32[80]{0:T(128)}, u32[]{:S(2)}) copy-start(f32[80]{0:T(128)} %get-tuple-element.51) | copy-start | bytes 964
  107.4 39.5 %copy-start.22 = (f32[80]{0:T(128)S(1)}, f32[80]{0:T(128)}, u32[]{:S(2)}) copy-start(f32[80]{0:T(128)} %get-tuple-element.42) | copy-start | bytes 964
  107.4 39.5 %copy-start.23 = (f32[80]{0:T(128)S(1)}, f32[80]{0:T(128)}, u32[]{:S(2)}) copy-start(f32[80]{0:T(128)} %get-tuple-element.49) | copy-start | bytes 964
  107.4 18.8 %collective-permute-start.7 = (bf16[80,64,128]{2,1,0:T(8,128)(2,1)S(1)}, bf16[80,64,128]{2,1,0:T(8,128)(2,1)S(1)}, u32[]{:S(2)}, u32[]{:S(2)}) collective-permute-start(bf16[80,64,128]{2,1,0:T(8,128)(2,1)S(1)} %fusion.25), channel_id=1, source_target_pairs={{1,25},{3,27},{5,29},{7,31},{9,1},{11,3},{13,5},{15,7},{17,9},{19,... | collective-permute-start | bytes 3932168 | tf_op jit(solution)/shard_map/ppermute | solution.py:53
  110.2 21.9 %collective-permute-start.6 = (bf16[80,64,128]{2,1,0:T(8,128)(2,1)S(1)}, bf16[80,64,128]{2,1,0:T(8,128)(2,1)S(1)}, u32[]{:S(2)}, u32[]{:S(2)}) collective-permute-start(bf16[80,64,128]{2,1,0:T(8,128)(2,1)S(1)} %fusion.25), channel_id=1, source_target_pairs={{1,9},{3,11},{5,13},{7,15},{9,17},{11,19},{13,21},{15,23},{17,25},... | collective-permute-start | bytes 3932168 | tf_op jit(solution)/shard_map/ppermute | solution.py:52
  126.2 1.1 copy-start.7
  128.1 11.8 %collective-permute-start.8 = (bf16[40,64,128]{2,1,0:T(8,128)(2,1)}, bf16[40,64,128]{2,1,0:T(8,128)(2,1)}, u32[]{:S(2)}, u32[]{:S(2)}) collective-permute-start(bf16[40,64,128]{2,1,0:T(8,128)(2,1)} %slice.147), channel_id=1, source_target_pairs={{1,25},{3,27},{5,29},{7,31},{9,1},{11,3},{13,5},{15,7},{17,9},{19,... | collective-permute-start | bytes 1966088 | tf_op jit(solution)/shard_map/ppermute | solution.py:54
  132.1 1.1 copy-start.8
  134.1 12.8 %collective-permute-start.9 = (bf16[40,64,128]{2,1,0:T(8,128)(2,1)}, bf16[40,64,128]{2,1,0:T(8,128)(2,1)}, u32[]{:S(2)}, u32[]{:S(2)}) collective-permute-start(bf16[40,64,128]{2,1,0:T(8,128)(2,1)} %slice.148), channel_id=1, source_target_pairs={{1,9},{3,11},{5,13},{7,15},{9,17},{11,19},{13,21},{15,23},{17,25},... | collective-permute-start | bytes 1966088 | tf_op jit(solution)/shard_map/ppermute | solution.py:55
  146.9 10.4 %copy-start.26 = (f32[80]{0:T(128)S(1)}, f32[80]{0:T(128)}, u32[]{:S(2)}) copy-start(f32[80]{0:T(128)} %param.20) | copy-start | bytes 964
  154.5 11.9 %collective-permute-start.10 = (f32[80,64,128]{2,1,0:T(8,128)}, f32[80,64,128]{2,1,0:T(8,128)}, u32[]{:S(2)}, u32[]{:S(2)}) collective-permute-start(f32[80,64,128]{2,1,0:T(8,128)} %fusion.15), channel_id=1, source_target_pairs={{1,0},{3,2},{5,4},{7,6},{9,8},{11,10},{13,12},{15,14},{17,16},{19,... | collective-permute-start | bytes 7864328 | tf_op jit(solution)/shard_map/ppermute | solution.py:106
  157.8 4.5 %copy-start.6 = (bf16[128,5120]{0,1:T(8,128)(2,1)S(1)}, bf16[128,5120]{0,1:T(8,128)(2,1)}, u32[]{:S(2)}) copy-start(bf16[128,5120]{0,1:T(8,128)(2,1)} %copy.40) | copy-start | bytes 3932164
  157.8 4.5 %copy-start.16 = (f32[80,128]{1,0:T(8,128)S(1)}, f32[80,128]{1,0:T(8,128)}, u32[]{:S(2)}) copy-start(f32[80,128]{1,0:T(8,128)} %get-tuple-element.29) | copy-start | bytes 122884
  162.3 4.1 %copy-start.25 = (f32[80]{0:T(128)S(1)}, f32[80]{0:T(128)}, u32[]{:S(2)}) copy-start(f32[80]{0:T(128)} %get-tuple-element.34) | copy-start | bytes 964
  166.4 4.4 %copy-start.11 = (f32[128,80]{0,1:T(8,128)S(1)}, f32[128,80]{0,1:T(8,128)}, u32[]{:S(2)}) copy-start(f32[128,80]{0,1:T(8,128)} %get-tuple-element.33) | copy-start | bytes 122884
  176.2 3.3 %copy-start.24 = (f32[80]{0:T(128)S(1)}, f32[80]{0:T(128)}, u32[]{:S(2)}) copy-start(f32[80]{0:T(128)} %get-tuple-element.53) | copy-start | bytes 964
  189.3 7.6 %copy-start.13 = (f32[5120]{0:T(1024)S(1)}, f32[5120]{0:T(1024)}, u32[]{:S(2)}) copy-start(f32[5120]{0:T(1024)} %param.21) | copy-start | bytes 61444
  194.5 2.3 copy-start
  200.2 38.9 %copy-start.17 = (f32[8,256]{1,0:T(8,128)}, f32[8,256]{1,0:T(8,128)S(1)}, u32[]{:S(2)}) copy-start(f32[8,256]{1,0:T(8,128)S(1)} %get-tuple-element.57) | copy-start | bytes 24580
  215.7 20.9 %all-to-all-start.3 = ((bf16[32,8,8,256]{3,2,1,0:T(8,128)(2,1)}), bf16[32,8,8,256]{3,2,1,0:T(8,128)(2,1)}, u32[]{:S(2)}, u32[]{:S(2)}) async-start(bf16[32,8,8,256]{3,2,1,0:T(8,128)(2,1)} %broadcast_in_dim.154), calls=%async_computation.3 | async-start | bytes 2097152 | tf_op jit(solution)/shard_map/all_to_all | solution.py:118
  236.6 1.9 copy-start.4
Sparse Core Ops, SparseCore 0:
  94.9 36.9 all-gather.2
  157.4 35.9 all-gather.4

commit v7 on v5

--- a/solution.py
+++ b/solution.py
@@ -16,21 +16,18 @@
     return lax.ppermute(block, axis, route)
 
 
-def block_states(values, write_rows, steps, logs):
+def block_terms(values, write_rows, read_rows, steps, logs):
     cum_log = jnp.cumsum(logs, axis=1)
-    tail_decay = jnp.exp(cum_log[:, -1:] - cum_log) * steps
-    weighted = (tail_decay[:, :, None] * write_rows.astype(jnp.float32)[None]).astype(jnp.bfloat16)
-    states = jnp.einsum("hsn,shp->hpn", weighted, values, preferred_element_type=jnp.float32)
-    return (states, cum_log)
-
-
-def block_inner(values, write_rows, read_rows, steps, cum_log):
-    length = cum_log.shape[1]
+    length = logs.shape[1]
     causal = jnp.arange(length)[:, None] >= jnp.arange(length)[None, :]
     scores = jnp.dot(read_rows, write_rows.T, preferred_element_type=jnp.float32)
     decay = jnp.exp(jnp.where(causal[None], cum_log[:, :, None] - cum_log[:, None, :], -jnp.inf))
     mixing = (scores[None] * decay * steps[:, None, :]).astype(jnp.bfloat16)
-    return jnp.einsum("hts,shp->thp", mixing, values, preferred_element_type=jnp.float32)
+    inner_out = jnp.einsum("hts,shp->thp", mixing, values, preferred_element_type=jnp.float32)
+    tail_decay = jnp.exp(cum_log[:, -1:] - cum_log) * steps
+    weighted = (tail_decay[:, :, None] * write_rows.astype(jnp.float32)[None]).astype(jnp.bfloat16)
+    states = jnp.einsum("hsn,shp->hpn", weighted, values, preferred_element_type=jnp.float32)
+    return (inner_out, states, cum_log)
 
 
 def chip_routes(seq):
@@ -150,9 +147,9 @@
 
 
 def codes_everywhere(block):
-    rows = lax.all_gather(block, "dp", axis=0, tiled=False)
+    rows = spread_over(block.astype(XFER), "dp")
     got = spread_over(rows, "seq")
-    return jnp.swapaxes(got, 0, 1).reshape((-1,) + block.shape[1:])
+    return jnp.swapaxes(got, 0, 1).reshape((-1,) + block.shape[1:]).astype(jnp.float32)
 
 
 def per_device(
@@ -191,14 +188,20 @@
     steps = step_size[0]
     logs = log_forget[0]
     blocks = length // SPAN
+    inner_list = []
     state_list = []
     cum_list = []
     for block in range(blocks):
         lower = block * SPAN
         upper = lower + SPAN
-        states, cum_log = block_states(
-            values[lower:upper], write_all[lower:upper], steps[:, lower:upper], logs[:, lower:upper]
+        inner_out, states, cum_log = block_terms(
+            values[lower:upper],
+            write_all[lower:upper],
+            read_all[lower:upper],
+            steps[:, lower:upper],
+            logs[:, lower:upper],
         )
+        inner_list.append(inner_out)
         state_list.append(states)
         cum_list.append(cum_log)
     running = jnp.zeros((heads, head_dim, state_dim), jnp.float32)
@@ -213,20 +216,6 @@
         before = before + block_total
     all_prior = prior_everywhere(prior_draw)
     low_state, low_log = chip_ends(running, before)
-    read_all, low_log = lax.optimization_barrier((read_all, low_log))
-    inner_list = []
-    for block in range(blocks):
-        lower = block * SPAN
-        upper = lower + SPAN
-        inner_list.append(
-            block_inner(
-                values[lower:upper],
-                write_all[lower:upper],
-                read_all[lower:upper],
-                steps[:, lower:upper],
-                cum_list[block],
-            )
-        )
     carry_in = carried_in(running, before, low_state, low_log)
     all_prior, carry_in = lax.optimization_barrier((all_prior, carry_in))
     outputs = []

time: 291 us -> 258 us (0.89)
  waiting for transfers between devices: 77.9 us -> 65.1 us
  blocking collectives: 18.4 us -> 10.7 us
  starting transfers between devices: 55.1 us -> 50.6 us
  local copies, waits for them, and re-layouts: 37.4 us -> 33.5 us
    all_gather x1 -> x0, blocking collectives: 18.4 us -> none  [codes_everywhere(): rows = lax.all_gather(block, 'dp', axis=0, tiled=False)]
    all_to_all x2, waiting for transfers between devices: 23.7 us -> 12.2 us  [spread_over(): lax.all_to_all(jnp.broadcast_to(block[None], (count,) + block.shape), axi...]
    all_to_all x0 -> x1, blocking collectives: none -> 10.7 us  [spread_over(): lax.all_to_all(jnp.broadcast_to(block[None], (count,) + block.shape), axi...]
    all_to_all x2, starting transfers between devices: 21.5 us -> 16.6 us  [spread_over(): lax.all_to_all(jnp.broadcast_to(block[None], (count,) + block.shape), axi...]
    slice x3, local copies, waits for them, and re-layouts: 6.94 us -> 3.2 us  [per_device(): values[lower:upper]]
    unnamed x90 -> x67, local copies, waits for them, and re-layouts: 8.68 us -> 11.5 us
  transfers between devices with their start and end apart: 15 -> 15, of which waited for: 9 -> 9; matrix products, arithmetic and copies ran while one was open for 23% -> 26% of each run, Pallas kernels for 0% -> 0%
where the time goes in v7:
time: 258 us; the launch traced here: 256 us
  waiting for transfers between devices  65.1 us (25%)
  starting transfers between devices  50.6 us (20%)
  other arithmetic  49.5 us (19%)
  local copies, waits for them, and re-layouts  33.5 us (13%)
  matrix products  31.9 us (12%)
  between operations  15.1 us (6%)
  blocking collectives  10.7 us (4%)
    ppermute x2, waiting for transfers between devices, ring_of_four(): next_block = lax.ppermute(sent, 'seq', bwd)  22.8 us
    all_to_all x2, starting transfers between devices, spread_over(): lax.all_to_all(jnp.broadcast_to(block[None], (count,) + block.shape), axi...  16.6 us
    ppermute x2, waiting for transfers between devices, ring_of_four(): far_b = lax.ppermute(prev_block[half:], 'seq', fwd)  13.2 us
    all_to_all x2, waiting for transfers between devices, spread_over(): lax.all_to_all(jnp.broadcast_to(block[None], (count,) + block.shape), axi...  12.2 us
    dot_general x2, matrix products, per_device(): jnp.einsum('tn,hpn->thp', read_block, start, precision=lax.Precision.HIGH...  11.7 us
    unnamed x67, local copies, waits for them, and re-layouts  11.5 us
    all_to_all x1, blocking collectives, spread_over(): lax.all_to_all(jnp.broadcast_to(block[None], (count,) + block.shape), axi...  10.7 us
    ppermute x2, starting transfers between devices, ring_of_four(): far_a = lax.ppermute(next_block[:half], 'seq', bwd)  10.2 us
  transfers between devices with their start and end apart: 15, of which 9 were waited for; matrix products, arithmetic and copies ran while one was open for 26% of the time, Pallas kernels for 0%

profile of v7, /device:TPU:1, one launch (start us, length us, event | category | flops | bytes accessed | tf_op | source)
XLA Modules:
  0.0 256.3 jit_solution(10421762542317647596)
XLA Ops:
  7.2 2.1 pad_maximum_fusion.3
  9.4 4.6 %collective-permute-start = (bf16[3,5376]{1,0:T(4,128)(2,1)S(1)}, bf16[3,5376]{1,0:T(4,128)(2,1)S(1)}, u32[]{:S(2)}, u32[]{:S(2)}) collective-permute-start(bf16[3,5376]{1,0:T(4,128)(2,1)S(1)} %slice.294), channel_id=1, source_target_pairs={{0,1},{1,2},{2,3},{3,4},{4,5},{5,6},{6,7},{7,8},{8,9},{9,10},{10,1... | collective-permute-start | bytes 96776 | tf_op jit(solution)/shard_map/ppermute | solution.py:16
  15.8 2.4 maximum_maximum_fusion
  18.2 4.4 %multiply_convert_fusion = bf16[256,5376]{1,0:T(8,128)(2,1)S(1)} fusion(bf16[259,5376]{1,0:T(8,128)(2,1)S(1)} %maximum_maximum_fusion, f32[5376]{0:T(1024)S(1)} %get-tuple-element.35, f32[5376]{0:T(1024)S(1)} %get-tuple-element.36, f32[5376]{0:T(1024)S(1)} %get-tuple-element.34, f32[5376]{0:T(1024)S(1)} %get-tuple-element.33, f32[5376]{0:T(1024)S(1)} %copy-done.29, ...), kind=kLoop, calls=%fused_computation.2 | loop fusion | flops 30277632 | bytes 13870080 | tf_op jit(solution)/shard_map/convert_element_type | solution.py:184
  22.9 1.2 copy-done.1
  24.2 1.5 copy.156
  25.6 1.4 copy.157
  27.1 1.6 fusion.14
  28.7 1.8 multiply_add_fusion.2
  31.4 1.5 collective-permute-start.1
  32.9 5.4 %collective-permute-done.1 = f32[80,65,128]{2,0,1:T(8,128)S(1)} collective-permute-done((f32[80,65,128]{2,0,1:T(8,128)S(1)}, f32[80,65,128]{2,0,1:T(8,128)S(1)}, u32[]{:S(2)}, u32[]{:S(2)}) %collective-permute-start.1) | collective-permute-done | bytes 2662432 | tf_op jit(solution)/shard_map/ppermute | solution.py:111
  38.4 0.9 multiply_add_fusion.1
  39.9 2.6 %copy.204 = bf16[80,64,128]{2,0,1:T(8,128)(2,1)} copy(f32[80,64,128]{2,1,0:T(8,128)S(1)} %multiply_add_fusion.1) | data formatting | bytes 3932160 | tf_op jit(solution)/shard_map/add | solution.py:123
  42.9 1.4 fusion.40
  44.3 4.2 %collective-permute-start.3 = (bf16[80,65,128]{2,0,1:T(8,128)(2,1)S(1)}, bf16[80,65,128]{2,0,1:T(8,128)(2,1)S(1)}, u32[]{:S(2)}, u32[]{:S(2)}) collective-permute-start(bf16[80,65,128]{2,0,1:T(8,128)(2,1)S(1)} %fusion.40), channel_id=1, source_target_pairs={{1,7},{3,1},{5,3},{7,5},{9,15},{11,9},{13,11},{15,13},{17,23},{19,... | collective-permute-start | bytes 3993608 | tf_op jit(solution)/shard_map/ppermute | solution.py:71
  48.5 1.9 collective-permute-start.2
  50.5 12.8 %collective-permute-done.3 = bf16[80,65,128]{2,0,1:T(8,128)(2,1)S(1)} collective-permute-done((bf16[80,65,128]{2,0,1:T(8,128)(2,1)S(1)}, bf16[80,65,128]{2,0,1:T(8,128)(2,1)S(1)}, u32[]{:S(2)}, u32[]{:S(2)}) %collective-permute-start.3) | collective-permute-done | bytes 1331232 | tf_op jit(solution)/shard_map/ppermute | solution.py:71
  63.3 1.1 copy-done.15
  64.4 0.9 slice.319
  65.3 5.0 %collective-permute-start.4 = (bf16[40,65,128]{2,0,1:T(8,128)(2,1)}, bf16[40,65,128]{2,0,1:T(8,128)(2,1)S(1)}, u32[]{:S(2)}, u32[]{:S(2)}) collective-permute-start(bf16[40,65,128]{2,0,1:T(8,128)(2,1)} %slice.319), channel_id=1, source_target_pairs={{1,7},{3,1},{5,3},{7,5},{9,15},{11,9},{13,11},{15,13},{17,23},{19,... | collective-permute-start | bytes 1996808 | tf_op jit(solution)/shard_map/ppermute | solution.py:72
  70.4 1.1 copy-done.17
  71.4 0.9 slice.320
  72.4 1.9 collective-permute-start.5
  74.5 0.9 fusion.61
  76.1 2.2 collective-permute-done.4
  78.3 7.0 %collective-permute-done.5 = bf16[40,65,128]{2,0,1:T(8,128)(2,1)} collective-permute-done((bf16[40,65,128]{2,0,1:T(8,128)(2,1)}, bf16[40,65,128]{2,0,1:T(8,128)(2,1)}, u32[]{:S(2)}, u32[]{:S(2)}) %collective-permute-start.5) | collective-permute-done | bytes 665632 | tf_op jit(solution)/shard_map/ppermute | solution.py:73
  85.3 1.2 constant_dynamic-update-slice_fusion
  87.1 5.1 %fusion.98 = (bf16[80,64,128]{2,0,1:T(8,128)(2,1)S(1)}, f32[80,64,128]{2,0,1:T(8,128)}, f32[80,64,128]{2,0,1:T(8,128)}, f32[80,64,128]{2,0,1:T(8,128)}, f32[80,64,128]{2,0,1:T(8,128)}) fusion(bf16[80,65,128]{2,0,1:T(8,128)(2,1)S(1)} %constant_dynamic-update-slice_fusion, f32[80]{0:T(128)S(1)} %get-tuple-element.95, bf16[80,65,128]{2,0,1:T(8,128)(2,1)S(1)} %copy-done.16, ...), kind=kLoop, calls=%fused_computation.231 | loop fusion | flops 9175040 | bytes 18352320 | tf_op jit(solution)/shard_map/convert.10
  92.2 1.2 fusion.41
  93.4 4.1 %collective-permute-start.7 = (bf16[80,65,128]{2,0,1:T(8,128)(2,1)}, bf16[80,65,128]{2,0,1:T(8,128)(2,1)}, u32[]{:S(2)}, u32[]{:S(2)}) collective-permute-start(bf16[80,65,128]{2,0,1:T(8,128)(2,1)} %fusion.41), channel_id=1, source_target_pairs={{1,25},{3,27},{5,29},{7,31},{9,1},{11,3},{13,5},{15,7},{17,9},{19,... | collective-permute-start | bytes 3993608 | tf_op jit(solution)/shard_map/ppermute | solution.py:71
  97.5 1.9 collective-permute-start.6
  100.2 4.5 %all-to-all-start = ((f32[32,8,256]{2,1,0:T(8,128)}), f32[32,8,256]{2,1,0:T(8,128)S(1)}, u32[]{:S(2)}, u32[]{:S(2)}) async-start(f32[32,8,256]{2,1,0:T(8,128)} %broadcast_in_dim.147), calls=%async_computation | async-start | bytes 524288 | tf_op jit(solution)/shard_map/all_to_all | solution.py:141
  104.7 10.0 %collective-permute-done.7 = bf16[80,65,128]{2,0,1:T(8,128)(2,1)} collective-permute-done((bf16[80,65,128]{2,0,1:T(8,128)(2,1)}, bf16[80,65,128]{2,0,1:T(8,128)(2,1)}, u32[]{:S(2)}, u32[]{:S(2)}) %collective-permute-start.7) | collective-permute-done | bytes 1331232 | tf_op jit(solution)/shard_map/ppermute | solution.py:71
  114.7 2.1 slice.336
  116.8 5.2 %collective-permute-start.8 = (bf16[40,65,128]{2,0,1:T(8,128)(2,1)}, bf16[40,65,128]{2,0,1:T(8,128)(2,1)}, u32[]{:S(2)}, u32[]{:S(2)}) collective-permute-start(bf16[40,65,128]{2,0,1:T(8,128)(2,1)} %slice.336), channel_id=1, source_target_pairs={{1,25},{3,27},{5,29},{7,31},{9,1},{11,3},{13,5},{15,7},{17,9},{19,... | collective-permute-start | bytes 1996808 | tf_op jit(solution)/shard_map/ppermute | solution.py:72
  122.9 1.3 slice.337
  124.2 1.9 collective-permute-start.9
  127.6 2.3 collective-permute-done.8
  129.9 1.2 copy_dynamic-update-slice_fusion.1
  131.1 6.2 %collective-permute-done.9 = bf16[40,65,128]{2,0,1:T(8,128)(2,1)S(1)} collective-permute-done((bf16[40,65,128]{2,0,1:T(8,128)(2,1)S(1)}, bf16[40,65,128]{2,0,1:T(8,128)(2,1)S(1)}, u32[]{:S(2)}, u32[]{:S(2)}) %collective-permute-start.9) | collective-permute-done | bytes 665632 | tf_op jit(solution)/shard_map/ppermute | solution.py:73
  137.9 2.6 %multiply_add_fusion = f32[80,64,128]{2,0,1:T(8,128)S(1)} fusion(f32[80,64,128]{2,0,1:T(8,128)S(1)} %copy-done.10, bf16[80,65,128]{2,0,1:T(8,128)(2,1)} %collective-permute-done.7, bf16[80,65,128]{2,0,1:T(8,128)(2,1)} %collective-permute-done.6, f32[80]{0:T(128)S(1)} %get-tuple-element.103, f32[80]{0:T(128)S(1)} %get-tuple-element.102, ...), kind=kLoop, calls=%fused_computation.56 | loop fusion | flops 4587520 | bytes 7865280 | tf_op jit(solution)/shard_map/add | solution.py:100
  142.1 7.1 %fusion.16 = f32[80,64,128]{2,1,0:T(8,128)} fusion(f32[80,64,128]{2,0,1:T(8,128)S(1)} %copy-done.9, f32[80,64,128]{2,0,1:T(8,128)S(1)} %copy-done.8, f32[80,64,128]{2,0,1:T(8,128)S(1)} %copy-done.7, f32[80,64,128]{2,0,1:T(8,128)S(1)} %multiply_add_fusion, f32[80,64,128]{2,1,0:T(8,128)S(1)} %multiply_add_fusion.1, ...), kind=kLoop, calls=%fused_computation.43 | loop fusion | flops 5898240 | bytes 17040320 | tf_op jit(solution)/shard_map/add | solution.py:128
  149.2 1.7 collective-permute-start.10
  151.1 0.9 fusion.54
  152.0 0.9 fusion.51
  153.0 4.5 %fusion.9 = f32[80,64,128]{2,1,0:T(8,128)} fusion(bf16[128,80,64]{0,2,1:T(8,128)(2,1)} %bitcast.188, f32[80,128]{1,0:T(8,128)S(1)} %copy-done.27, f32[80,128]{1,0:T(8,128)S(1)} %reduce_window_sum.17, f32[128,128]{1,0:T(8,128)S(1)} %fusion.54, pred[128,128]{1,0:T(8,128)(4,1)S(1)} %iota_compare_fusion.1), kind=kOutput, calls=%fused_computation.33 | convolution fusion | flops 174325760 | bytes 4096000 | tf_op jit(solution)/shard_map/hts,shp->thp/dot_general | solution.py:26
  157.4 4.0 %fusion.10 = f32[80,64,128]{2,1,0:T(8,128)} fusion(bf16[128,80,64]{0,2,1:T(8,128)(2,1)S(1)} %bitcast.191, f32[80,128]{1,0:T(8,128)S(1)} %get-tuple-element.77, f32[80,128]{1,0:T(8,128)S(1)} %reduce_window_sum.18, f32[128,128]{1,0:T(8,128)S(1)} %fusion.51, pred[128,128]{1,0:T(8,128)(4,1)S(1)} %iota_compare_fusion.1), kind=kOutput, calls=%fused_computation.34 | convolution fusion | flops 174325760 | bytes 4096000 | tf_op jit(solution)/shard_map/hts,shp->thp/dot_general | solution.py:26
  161.5 1.5 copy-done.19
  163.0 4.6 %add_select_fusion = f32[80,64,128]{2,1,0:T(8,128)} fusion(f32[80,64,128]{2,1,0:T(8,128)} %copy-done.19, f32[80,64,128]{2,1,0:T(8,128)} %fusion.16, f32[80,64,128]{2,0,1:T(8,128)S(1)} %copy-done.6, f32[80]{0:T(128)S(1)} %get-tuple-element.101, pred[]{:T(512)S(6)} %eq.14), kind=kLoop, calls=%fused_computation.55 | loop fusion | flops 1966080 | bytes 10486081 | tf_op jit(solution)/shard_map/jit(_where)/select_n | solution.py:131
  167.6 5.3 %bitcast_add_fusion.1 = f32[128,80,64]{0,2,1:T(8,128)} fusion(f32[80,64,128]{2,1,0:T(8,128)} %fusion.9, f32[80,64,128]{2,1,0:T(8,128)} %add_select_fusion, f32[128,80]{0,1:T(8,128)S(1)} %get-tuple-element.81, bf16[256,5376]{1,0:T(8,128)(2,1)S(1)} %copy-done.2), kind=kOutput, calls=%fused_computation.41 | convolution fusion | flops 1007943680 | bytes 7938048 | tf_op jit(solution)/shard_map/tn,hpn->thp/dot_general | solution.py:227
  172.9 3.3 %copy.174 = f32[128,5120]{1,0:T(8,128)} copy(f32[128,5120]{0,1:T(8,128)} %bitcast.186) | data formatting | bytes 5242880 | tf_op jit(solution)/shard_map/concatenate | solution.py:231
  176.2 6.4 %bitcast_add_fusion = f32[128,80,64]{0,2,1:T(8,128)} fusion(f32[80,64,128]{2,1,0:T(8,128)} %fusion.10, f32[80,64,128]{2,1,0:T(8,128)} %add_select_fusion, f32[80,64,128]{2,1,0:T(8,128)} %copy-done.4, f32[80]{0:T(128)S(1)} %get-tuple-element.96, f32[128,80]{0,1:T(8,128)S(1)} %get-tuple-element.80, f32[80]{0:T(128)S(1)} %get-tuple-element.97, ...), kind=kOutput, calls=%fused_computation.40 | convolution fusion | flops 1009909760 | bytes 10560512 | tf_op jit(solution)/shard_map/tn,hpn->thp/dot_general | solution.py:227
  182.6 3.2 %copy.175 = f32[128,5120]{1,0:T(8,128)} copy(f32[128,5120]{0,1:T(8,128)} %bitcast.187) | data formatting | bytes 5242880 | tf_op jit(solution)/shard_map/concatenate | solution.py:231
  185.8 5.3 %multiply_reduce_fusion = (f32[256]{0:T(256)S(1)}, f32[256,5120]{1,0:T(8,128)S(1)}) fusion(bf16[1,256,5120]{2,1,0:T(8,128)(2,1)} %param.17, bf16[256,5376]{1,0:T(8,128)(2,1)S(1)} %copy-done.2, f32[5120]{0:T(1024)S(1)} %mul.423, f32[128,5120]{1,0:T(8,128)} %copy.175, f32[128,5120]{1,0:T(8,128)} %copy.174), kind=kLoop, calls=%fused_computation.10 | loop fusion | flops 15728384 | bytes 15750144 | tf_op jit(solution)/shard_map/reduce_sum | solution.py:234
  191.1 2.3 copy-done
  193.4 1.0 convert_reduce_fusion
  194.4 7.0 %all-gather.5.cloned.1.call-done = bf16[5120,256]{1,0:T(8,128)(2,1)} async-done(((bf16[640,256]{1,0:T(8,128)(2,1)}), bf16[5120,256]{1,0:T(8,128)(2,1)}) %all-gather.5.cloned.1.call-update) | async-done | bytes 2621456 | tf_op jit(solution)/shard_map/all_gather | solution.py:175
  201.3 2.3 multiply_reduce_fusion.2
  203.7 10.7 %all_to_all.15 = bf16[8,8,256]{2,1,0:T(8,128)(2,1)S(1)} all-to-all(bf16[8,8,256]{2,1,0:T(8,128)(2,1)S(1)} %broadcast_in_dim.153), channel_id=1, replica_groups=mesh['dp'=8,'seq'=32] {'dp'}, dimensions={0} | all-to-all | bytes 65536 | tf_op jit(solution)/shard_map/all_to_all | solution.py:141
  214.3 1.1 broadcast_in_dim.154
  215.5 12.1 %all-to-all-start.2 = ((bf16[32,8,8,256]{3,2,1,0:T(8,128)(2,1)}), bf16[32,8,8,256]{3,2,1,0:T(8,128)(2,1)S(1)}, u32[]{:S(2)}, u32[]{:S(2)}) async-start(bf16[32,8,8,256]{3,2,1,0:T(8,128)(2,1)} %broadcast_in_dim.154), calls=%async_computation.2 | async-start | bytes 2097152 | tf_op jit(solution)/shard_map/all_to_all | solution.py:141
  227.6 4.7 %fusion.96 = bf16[1,256,5120]{2,1,0:T(8,128)(2,1)} fusion(f32[5120]{0:T(1024)S(1)} %copy-done.24, f32[256,5120]{1,0:T(8,128)} %copy-done, f32[256]{0:T(256)S(1)} %add_rsqrt_fusion), kind=kLoop, calls=%fused_computation.230 | loop fusion | flops 3932160 | bytes 7885824 | tf_op jit(solution)/shard_map/broadcast_in_dim | solution.py:248
  232.3 12.2 %all-to-all-done.2 = bf16[32,8,8,256]{3,2,1,0:T(8,128)(2,1)S(1)} async-done(((bf16[32,8,8,256]{3,2,1,0:T(8,128)(2,1)}), bf16[32,8,8,256]{3,2,1,0:T(8,128)(2,1)S(1)}, u32[]{:S(2)}, u32[]{:S(2)}) %all-to-all-start.2) | async-done | bytes 1048608 | tf_op jit(solution)/shard_map/all_to_all | solution.py:141
  245.3 4.2 %fusion.6 = f32[8,4096]{1,0:T(8,128)} fusion(f32[8,256]{1,0:T(8,128)S(1)} %get-tuple-element.104, f32[2048,256]{1,0:T(8,128)S(1)} %copy-done.11, f32[2048,256]{1,0:T(8,128)S(1)} %bitcast.185, f32[4096]{0:T(1024)S(1)} %multiply_reduce_fusion.1, f32[8]{0:T(128)S(1)} %get-tuple-element.86), kind=kOutput, calls=%fused_computation.18 | convolution fusion | flops 101875712 | bytes 4349984 | tf_op jit(solution)/shard_map/dot_general | solution.py:242
  (113 shorter events, 11.6 us)
Async XLA Ops:
  7.2 6.8 %copy-start.25 = (f32[1,80,256]{2,1,0:T(8,128)S(1)}, f32[1,80,256]{2,1,0:T(8,128)}, u32[]{:S(2)}) copy-start(f32[1,80,256]{2,1,0:T(8,128)} %param.21) | copy-start | bytes 245764
  7.2 7.7 %copy-start.26 = (f32[1,80,256]{2,1,0:T(8,128)S(1)}, f32[1,80,256]{2,1,0:T(8,128)}, u32[]{:S(2)}) copy-start(f32[1,80,256]{2,1,0:T(8,128)} %param.20) | copy-start | bytes 245764
  7.2 8.3 %copy-start.23 = (f32[4,5376]{1,0:T(4,128)S(1)}, f32[4,5376]{1,0:T(4,128)}, u32[]{:S(2)}) copy-start(f32[4,5376]{1,0:T(4,128)} %param.22) | copy-start | bytes 258052
  7.2 8.6 %copy-start.3 = (bf16[1,256,5120]{2,1,0:T(8,128)(2,1)S(1)}, bf16[1,256,5120]{2,1,0:T(8,128)(2,1)}, u32[]{:S(2)}) copy-start(bf16[1,256,5120]{2,1,0:T(8,128)(2,1)} %param.16) | copy-start | bytes 7864324
  7.2 8.6 %copy-start.21 = (bf16[1,256,128]{2,1,0:T(8,128)(2,1)S(1)}, bf16[1,256,128]{2,1,0:T(8,128)(2,1)}, u32[]{:S(2)}) copy-start(bf16[1,256,128]{2,1,0:T(8,128)(2,1)} %param.19) | copy-start | bytes 196612
  7.2 8.6 %copy-start.22 = (bf16[1,256,128]{2,1,0:T(8,128)(2,1)S(1)}, bf16[1,256,128]{2,1,0:T(8,128)(2,1)}, u32[]{:S(2)}) copy-start(bf16[1,256,128]{2,1,0:T(8,128)(2,1)} %param.18) | copy-start | bytes 196612
  9.4 6.3 %collective-permute-start = (bf16[3,5376]{1,0:T(4,128)(2,1)S(1)}, bf16[3,5376]{1,0:T(4,128)(2,1)S(1)}, u32[]{:S(2)}, u32[]{:S(2)}) collective-permute-start(bf16[3,5376]{1,0:T(4,128)(2,1)S(1)} %slice.294), channel_id=1, source_target_pairs={{0,1},{1,2},{2,3},{3,4},{4,5},{5,6},{6,7},{7,8},{8,9},{9,10},{10,1... | collective-permute-start | bytes 96776 | tf_op jit(solution)/shard_map/ppermute | solution.py:16
  15.7 2.4 copy-start.29
  22.6 1.5 copy-start.1
  25.6 1.4 copy-start.12
  27.0 1.6 copy-start.13
  28.7 1.8 copy-start.4
  31.4 6.9 %collective-permute-start.1 = (f32[80,65,128]{2,0,1:T(8,128)S(1)}, f32[80,65,128]{2,0,1:T(8,128)S(1)}, u32[]{:S(2)}, u32[]{:S(2)}) collective-permute-start(f32[80,65,128]{2,0,1:T(8,128)S(1)} %copy.158), channel_id=1, source_target_pairs={{0,1},{2,3},{4,5},{6,7},{8,9},{10,11},{12,13},{14,15},{16,17},{18,... | collective-permute-start | bytes 7987208 | tf_op jit(solution)/shard_map/ppermute | solution.py:111
  38.4 1.5 copy-start.5
  44.3 19.0 %collective-permute-start.3 = (bf16[80,65,128]{2,0,1:T(8,128)(2,1)S(1)}, bf16[80,65,128]{2,0,1:T(8,128)(2,1)S(1)}, u32[]{:S(2)}, u32[]{:S(2)}) collective-permute-start(bf16[80,65,128]{2,0,1:T(8,128)(2,1)S(1)} %fusion.40), channel_id=1, source_target_pairs={{1,7},{3,1},{5,3},{7,5},{9,15},{11,9},{13,11},{15,13},{17,23},{19,... | collective-permute-start | bytes 3993608 | tf_op jit(solution)/shard_map/ppermute | solution.py:71
  48.5 21.8 %collective-permute-start.2 = (bf16[80,65,128]{2,0,1:T(8,128)(2,1)S(1)}, bf16[80,65,128]{2,0,1:T(8,128)(2,1)S(1)}, u32[]{:S(2)}, u32[]{:S(2)}) collective-permute-start(bf16[80,65,128]{2,0,1:T(8,128)(2,1)S(1)} %fusion.40), channel_id=1, source_target_pairs={{1,3},{3,5},{5,7},{7,1},{9,11},{11,13},{13,15},{15,9},{17,19},{19,... | collective-permute-start | bytes 3993608 | tf_op jit(solution)/shard_map/ppermute | solution.py:70
  63.3 1.1 copy-start.15
  65.3 13.0 %collective-permute-start.4 = (bf16[40,65,128]{2,0,1:T(8,128)(2,1)}, bf16[40,65,128]{2,0,1:T(8,128)(2,1)S(1)}, u32[]{:S(2)}, u32[]{:S(2)}) collective-permute-start(bf16[40,65,128]{2,0,1:T(8,128)(2,1)} %slice.319), channel_id=1, source_target_pairs={{1,7},{3,1},{5,3},{7,5},{9,15},{11,9},{13,11},{15,13},{17,23},{19,... | collective-permute-start | bytes 1996808 | tf_op jit(solution)/shard_map/ppermute | solution.py:72
  70.3 1.1 copy-start.17
  72.4 13.0 %collective-permute-start.5 = (bf16[40,65,128]{2,0,1:T(8,128)(2,1)}, bf16[40,65,128]{2,0,1:T(8,128)(2,1)}, u32[]{:S(2)}, u32[]{:S(2)}) collective-permute-start(bf16[40,65,128]{2,0,1:T(8,128)(2,1)} %slice.320), channel_id=1, source_target_pairs={{1,3},{3,5},{5,7},{7,1},{9,11},{11,13},{13,15},{15,9},{17,19},{19,... | collective-permute-start | bytes 1996808 | tf_op jit(solution)/shard_map/ppermute | solution.py:73
  74.4 12.6 %copy-start.16 = (bf16[80,65,128]{2,0,1:T(8,128)(2,1)S(1)}, bf16[80,65,128]{2,0,1:T(8,128)(2,1)}, u32[]{:S(2)}) copy-start(bf16[80,65,128]{2,0,1:T(8,128)(2,1)} %copy-done.15) | copy-start | bytes 3993604
  74.5 12.6 %copy-start.18 = (bf16[80,65,128]{2,0,1:T(8,128)(2,1)S(1)}, bf16[80,65,128]{2,0,1:T(8,128)(2,1)}, u32[]{:S(2)}) copy-start(bf16[80,65,128]{2,0,1:T(8,128)(2,1)} %copy-done.17) | copy-start | bytes 3993604
  92.2 7.3 %copy-start.30 = (f32[8,256]{1,0:T(8,128)S(1)}, f32[8,256]{1,0:T(8,128)}, u32[]{:S(2)}) copy-start(f32[8,256]{1,0:T(8,128)} %param.27) | copy-start | bytes 24580
  93.4 21.4 %collective-permute-start.7 = (bf16[80,65,128]{2,0,1:T(8,128)(2,1)}, bf16[80,65,128]{2,0,1:T(8,128)(2,1)}, u32[]{:S(2)}, u32[]{:S(2)}) collective-permute-start(bf16[80,65,128]{2,0,1:T(8,128)(2,1)} %fusion.41), channel_id=1, source_target_pairs={{1,25},{3,27},{5,29},{7,31},{9,1},{11,3},{13,5},{15,7},{17,9},{19,... | collective-permute-start | bytes 3993608 | tf_op jit(solution)/shard_map/ppermute | solution.py:71
  97.5 25.4 %collective-permute-start.6 = (bf16[80,65,128]{2,0,1:T(8,128)(2,1)}, bf16[80,65,128]{2,0,1:T(8,128)(2,1)}, u32[]{:S(2)}, u32[]{:S(2)}) collective-permute-start(bf16[80,65,128]{2,0,1:T(8,128)(2,1)} %fusion.41), channel_id=1, source_target_pairs={{1,9},{3,11},{5,13},{7,15},{9,17},{11,19},{13,21},{15,23},{17,25},... | collective-permute-start | bytes 3993608 | tf_op jit(solution)/shard_map/ppermute | solution.py:70
  100.2 21.9 %all-to-all-start = ((f32[32,8,256]{2,1,0:T(8,128)}), f32[32,8,256]{2,1,0:T(8,128)S(1)}, u32[]{:S(2)}, u32[]{:S(2)}) async-start(f32[32,8,256]{2,1,0:T(8,128)} %broadcast_in_dim.147), calls=%async_computation | async-start | bytes 524288 | tf_op jit(solution)/shard_map/all_to_all | solution.py:141
  104.7 62.9 %all-gather.3.cloned.1.call-start = ((), (), s32[]{:S(2)}) async-start(), calls=%async_computation.3 | async-start | bytes 2359296 | tf_op jit(solution)/shard_map/all_gather | solution.py:146
  116.8 13.1 %collective-permute-start.8 = (bf16[40,65,128]{2,0,1:T(8,128)(2,1)}, bf16[40,65,128]{2,0,1:T(8,128)(2,1)}, u32[]{:S(2)}, u32[]{:S(2)}) collective-permute-start(bf16[40,65,128]{2,0,1:T(8,128)(2,1)} %slice.336), channel_id=1, source_target_pairs={{1,25},{3,27},{5,29},{7,31},{9,1},{11,3},{13,5},{15,7},{17,9},{19,... | collective-permute-start | bytes 1996808 | tf_op jit(solution)/shard_map/ppermute | solution.py:72
  122.1 0.7 copy-start.20
  122.8 78.5 %all-gather.5.cloned.1.call-start = ((), (), s32[]{:S(2)}) async-start(), calls=%async_computation.4 | async-start | bytes 2949120 | tf_op jit(solution)/shard_map/all_gather | solution.py:175
  122.9 15.0 %copy-start.10 = (f32[80,64,128]{2,0,1:T(8,128)S(1)}, f32[80,64,128]{2,0,1:T(8,128)}, u32[]{:S(2)}) copy-start(f32[80,64,128]{2,0,1:T(8,128)} %get-tuple-element.57) | copy-start | bytes 7864324
  124.2 13.1 %collective-permute-start.9 = (bf16[40,65,128]{2,0,1:T(8,128)(2,1)S(1)}, bf16[40,65,128]{2,0,1:T(8,128)(2,1)S(1)}, u32[]{:S(2)}, u32[]{:S(2)}) collective-permute-start(bf16[40,65,128]{2,0,1:T(8,128)(2,1)S(1)} %slice.337), channel_id=1, source_target_pairs={{1,9},{3,11},{5,13},{7,15},{9,17},{11,19},{13,21},{15,23},{17,25},... | collective-permute-start | bytes 1996808 | tf_op jit(solution)/shard_map/ppermute | solution.py:73
  137.9 2.6 %copy-start.7 = (f32[80,64,128]{2,0,1:T(8,128)S(1)}, f32[80,64,128]{2,0,1:T(8,128)}, u32[]{:S(2)}) copy-start(f32[80,64,128]{2,0,1:T(8,128)} %get-tuple-element.71) | copy-start | bytes 7864324
  137.9 3.4 %copy-start.8 = (f32[80,64,128]{2,0,1:T(8,128)S(1)}, f32[80,64,128]{2,0,1:T(8,128)}, u32[]{:S(2)}) copy-start(f32[80,64,128]{2,0,1:T(8,128)} %get-tuple-element.72) | copy-start | bytes 7864324
  137.9 4.2 %copy-start.9 = (f32[80,64,128]{2,0,1:T(8,128)S(1)}, f32[80,64,128]{2,0,1:T(8,128)}, u32[]{:S(2)}) copy-start(f32[80,64,128]{2,0,1:T(8,128)} %get-tuple-element.73) | copy-start | bytes 7864324
  142.1 8.8 %copy-start.31 = (f32[80]{0:T(128)S(1)}, f32[80]{0:T(128)}, u32[]{:S(2)}) copy-start(f32[80]{0:T(128)} %param.24) | copy-start | bytes 964
  142.1 10.9 %copy-start.27 = (f32[80,128]{1,0:T(8,128)S(1)}, f32[80,128]{1,0:T(8,128)}, u32[]{:S(2)}) copy-start(f32[80,128]{1,0:T(8,128)} %get-tuple-element.74) | copy-start | bytes 122884
  149.2 12.3 %collective-permute-start.10 = (f32[80,64,128]{2,1,0:T(8,128)}, f32[80,64,128]{2,1,0:T(8,128)S(1)}, u32[]{:S(2)}, u32[]{:S(2)}) collective-permute-start(f32[80,64,128]{2,1,0:T(8,128)} %fusion.16), channel_id=1, source_target_pairs={{1,0},{3,2},{5,4},{7,6},{9,8},{11,10},{13,12},{15,14},{17,16},{19,... | collective-permute-start | bytes 7864328 | tf_op jit(solution)/shard_map/ppermute | solution.py:129
  152.9 4.5 %copy-start.14 = (bf16[128,5120]{0,1:T(8,128)(2,1)S(1)}, bf16[128,5120]{0,1:T(8,128)(2,1)}, u32[]{:S(2)}) copy-start(bf16[128,5120]{0,1:T(8,128)(2,1)} %copy.157) | copy-start | bytes 3932164
  157.4 5.5 %copy-start.6 = (f32[80,64,128]{2,0,1:T(8,128)S(1)}, f32[80,64,128]{2,0,1:T(8,128)}, u32[]{:S(2)}) copy-start(f32[80,64,128]{2,0,1:T(8,128)} %copy-done.5) | copy-start | bytes 7864324
  161.5 1.5 copy-start.19
  163.0 4.6 %copy-start.2 = (bf16[256,5376]{1,0:T(8,128)(2,1)S(1)}, bf16[256,5376]{1,0:T(8,128)(2,1)}, u32[]{:S(2)}) copy-start(bf16[256,5376]{1,0:T(8,128)(2,1)} %copy-done.1) | copy-start | bytes 8257540
  185.8 7.6 %copy-start.24 = (f32[5120]{0:T(1024)S(1)}, f32[5120]{0:T(1024)}, u32[]{:S(2)}) copy-start(f32[5120]{0:T(1024)} %param.25) | copy-start | bytes 61444
  191.1 2.3 copy-start
  203.6 41.7 %copy-start.28 = (f32[8,256]{1,0:T(8,128)}, f32[8,256]{1,0:T(8,128)S(1)}, u32[]{:S(2)}) copy-start(f32[8,256]{1,0:T(8,128)S(1)} %get-tuple-element.104) | copy-start | bytes 24580
  215.5 29.0 %all-to-all-start.2 = ((bf16[32,8,8,256]{3,2,1,0:T(8,128)(2,1)}), bf16[32,8,8,256]{3,2,1,0:T(8,128)(2,1)S(1)}, u32[]{:S(2)}, u32[]{:S(2)}) async-start(bf16[32,8,8,256]{3,2,1,0:T(8,128)(2,1)} %broadcast_in_dim.154), calls=%async_computation.2 | async-start | bytes 2097152 | tf_op jit(solution)/shard_map/all_to_all | solution.py:141
  232.3 12.4 %copy-start.11 = (f32[2048,256]{1,0:T(8,128)S(1)}, f32[2048,256]{1,0:T(8,128)}, u32[]{:S(2)}) copy-start(f32[2048,256]{1,0:T(8,128)} %all-gather.3.cloned.1.call-done) | copy-start | bytes 6291460
Sparse Core Ops, SparseCore 0:
  123.0 34.7 all-gather.2
  159.6 41.7 all-gather.4

commit v8 on v6

--- a/solution.py
+++ b/solution.py
@@ -36,14 +36,13 @@
     def at(x, y, c):
         return (x * RING + y) * CORES + c
 
-    cells = [(x, y) for x in range(rows) for y in range(RING)]
-    up = [(at(x, y, 0), at(x, y, 1)) for x, y in cells]
-    down = [(b, a) for a, b in up]
-    y_fwd = [(at(x, y, 1), at(x, (y + 1) % RING, 1)) for x, y in cells]
-    y_bwd = [(at(x, y, 1), at(x, (y - 1) % RING, 1)) for x, y in cells]
-    x_fwd = [(at(x, y, 1), at((x + 1) % rows, y, 1)) for x, y in cells]
-    x_bwd = [(at(x, y, 1), at((x - 1) % rows, y, 1)) for x, y in cells]
-    return rows, up, down, (y_fwd, y_bwd), (x_fwd, x_bwd)
+    cells = [(x, y, c) for x in range(rows) for y in range(RING) for c in range(CORES)]
+    partner = [(at(x, y, c), at(x, y, 1 - c)) for x, y, c in cells]
+    y_fwd = [(at(x, y, c), at(x, (y + 1) % RING, c)) for x, y, c in cells]
+    y_bwd = [(at(x, y, c), at(x, (y - 1) % RING, c)) for x, y, c in cells]
+    x_fwd = [(at(x, y, c), at((x + 1) % rows, y, c)) for x, y, c in cells]
+    x_bwd = [(at(x, y, c), at((x - 1) % rows, y, c)) for x, y, c in cells]
+    return rows, partner, (y_fwd, y_bwd), (x_fwd, x_bwd)
 
 
 def ring_of_four(state, fwd, bwd):
@@ -85,27 +84,35 @@
 
 def carried_in(own_state, shard_logs):
     seq = lax.axis_size("seq")
-    rows, up, down, y_routes, x_routes = chip_routes(seq)
+    rows, partner, y_routes, x_routes = chip_routes(seq)
     assert rows == RING and seq == rows * RING * CORES
     place = lax.axis_index("seq")
     core = place % CORES
     y_pos = (place // CORES) % RING
     x_pos = place // (CORES * RING)
+    half = own_state.shape[0] // CORES
+    mine = core * half
+    theirs = (1 - core) * half
     grid_logs = shard_logs.reshape(rows, RING, CORES, -1)
-    chip_logs = grid_logs[:, :, 0] + grid_logs[:, :, 1]
-    own_log = lax.dynamic_index_in_dim(shard_logs, place, 0, False)
-    low_log = lax.dynamic_index_in_dim(shard_logs, place - 1, 0, False)
-    low_state = lax.ppermute(own_state, "seq", up)
-    chip_state = jnp.exp(own_log)[:, None, None] * low_state + own_state
+    chip_logs = lax.dynamic_slice_in_dim(grid_logs[:, :, 0] + grid_logs[:, :, 1], mine, half, 2)
+    low_log = lax.dynamic_slice_in_dim(grid_logs[x_pos, y_pos, 0], mine, half, 0)
+    high_log = lax.dynamic_slice_in_dim(grid_logs[x_pos, y_pos, 1], mine, half, 0)
+    own_half = lax.dynamic_slice_in_dim(own_state, mine, half, 0)
+    other_half = lax.ppermute(lax.dynamic_slice_in_dim(own_state, theirs, half, 0), "seq", partner)
+    low_half = jnp.where(core == 0, own_half, other_half)
+    high_half = jnp.where(core == 0, other_half, own_half)
+    chip_state = jnp.exp(high_log)[:, None, None] * low_half + high_half
     slots = ring_of_four(chip_state, *y_routes)
     row_logs = lax.dynamic_index_in_dim(chip_logs, x_pos, 0, False)
     row_before, row_lead, row_total = fold_ring(slots, y_pos, row_logs)
     slots = ring_of_four(row_total, *x_routes)
     rows_before, _, _ = fold_ring(slots, x_pos, jnp.sum(chip_logs, axis=1))
     chip_in = row_lead[:, None, None] * rows_before + row_before
-    chip_in_low = lax.ppermute(chip_in, "seq", down)
-    high_in = jnp.exp(low_log)[:, None, None] * chip_in + low_state
-    return jnp.where(core == 0, chip_in_low, high_in)
+    high_in = jnp.exp(low_log)[:, None, None] * chip_in + low_half
+    keep = jnp.where(core == 0, chip_in, high_in)
+    give = jnp.where(core == 0, high_in, chip_in)
+    got = lax.ppermute(give, "seq", partner)
+    return jnp.where(core == 0, jnp.concatenate([keep, got], 0), jnp.concatenate([got, keep], 0))
 
 
 def placed(block, slots, index):

time: 251 us -> 226 us (0.900)
  starting transfers between devices: 49.8 us -> 36.4 us
  other arithmetic: 46.2 us -> 40.1 us
  waiting for transfers between devices: 62 us -> 57.5 us
  matrix products: 35.4 us -> 32.5 us
    add x1, other arithmetic: 7.58 us -> 0.01 us  [carried_in(): grid_logs[:, :, 0] + grid_logs[:, :, 1]]
    ppermute x2, waiting for transfers between devices: 14 us -> 8.96 us  [ring_of_four(): far_b = lax.ppermute(prev_state[half:], 'seq', fwd)]
    ppermute x2, starting transfers between devices: 4.97 us -> 0.97 us  [ring_of_four(): prev_state = lax.ppermute(sent, 'seq', fwd)]
    select_n x1 -> x3, other arithmetic: 4.42 us -> 8.01 us  [the longest x1 4.4 us: carried_in(): keep = jnp.where(core == 0, chip_in, high_in)]
    ppermute x2, starting transfers between devices: 5.59 us -> 2.04 us  [ring_of_four(): next_state = lax.ppermute(sent, 'seq', bwd)]
    ppermute x2, starting transfers between devices: 8 us -> 4.47 us  [ring_of_four(): far_a = lax.ppermute(next_state[:half], 'seq', bwd)]
    ppermute x2, starting transfers between devices: 3.82 us -> 0.35 us  [ring_of_four(): far_b = lax.ppermute(prev_state[half:], 'seq', fwd)]
    convert_element_type x2, other arithmetic: 8.5 us -> 5.59 us  [ring_of_four(): sent = state.astype(XFER)]
  transfers between devices with their start and end apart: 16 -> 16, of which waited for: 8 -> 7; matrix products, arithmetic and copies ran while one was open for 26% -> 37% of each run, Pallas kernels for 0% -> 0%
where the time goes in v8:
time: 226 us; the launch traced here: 225 us
  waiting for transfers between devices  57.5 us (25%)
  other arithmetic  40.1 us (18%)
  starting transfers between devices  36.4 us (16%)
  matrix products  32.5 us (14%)
  local copies, waits for them, and re-layouts  28.5 us (13%)
  blocking collectives  14.8 us (7%)
  between operations  14.8 us (7%)
    ppermute x2, waiting for transfers between devices, ring_of_four(): next_state = lax.ppermute(sent, 'seq', bwd)  26 us
    all_to_all x3, starting transfers between devices, spread_over(): lax.all_to_all(jnp.broadcast_to(block[None], (count,) + block.shape), axi...  20.1 us
    all_to_all x3, waiting for transfers between devices, spread_over(): lax.all_to_all(jnp.broadcast_to(block[None], (count,) + block.shape), axi...  19.1 us
    all_to_all x1, blocking collectives, spread_over(): lax.all_to_all(jnp.broadcast_to(block[None], (count,) + block.shape), axi...  14.8 us
    dot_general x2, matrix products, per_device(): jnp.einsum('tn,hpn->thp', read_block, start, precision=lax.Precision.HIGH...  11.9 us
    ppermute x2, waiting for transfers between devices, ring_of_four(): far_b = lax.ppermute(prev_state[half:], 'seq', fwd)  8.96 us
    dot_general x2, matrix products, block_terms(): jnp.einsum('hts,shp->thp', mixing, values, preferred_element_type=jnp.flo...  8.15 us
    slice x3, local copies, waits for them, and re-layouts, per_device(): values[lower:upper]  6.68 us
  transfers between devices with their start and end apart: 16, of which 7 were waited for; matrix products, arithmetic and copies ran while one was open for 37% of the time, Pallas kernels for 0%

profile of v8, /device:TPU:1, one launch (start us, length us, event | category | flops | bytes accessed | tf_op | source)
XLA Modules:
  0.0 224.6 jit_solution(11883042503073168334)
XLA Ops:
  7.2 2.1 pad_maximum_fusion.2
  9.4 4.6 %collective-permute-start = (bf16[3,5376]{1,0:T(4,128)(2,1)S(1)}, bf16[3,5376]{1,0:T(4,128)(2,1)S(1)}, u32[]{:S(2)}, u32[]{:S(2)}) collective-permute-start(bf16[3,5376]{1,0:T(4,128)(2,1)S(1)} %slice.128), channel_id=1, source_target_pairs={{0,1},{1,2},{2,3},{3,4},{4,5},{5,6},{6,7},{7,8},{8,9},{9,10},{10,1... | collective-permute-start | bytes 96776 | tf_op jit(solution)/shard_map/ppermute | solution.py:16
  14.0 0.7 broadcast_in_dim.149
  14.7 6.9 %all-to-all-start = ((f32[32,8,256]{2,1,0:T(8,128)}), f32[32,8,256]{2,1,0:T(8,128)S(1)}, u32[]{:S(2)}, u32[]{:S(2)}) async-start(f32[32,8,256]{2,1,0:T(8,128)} %broadcast_in_dim.149), calls=%async_computation | async-start | bytes 524288 | tf_op jit(solution)/shard_map/all_to_all | solution.py:125
  22.5 0.6 fusion.105
  23.1 0.7 fusion.103
  23.7 1.3 slice_reduce_fusion.5
  25.2 2.4 %maximum_maximum_fusion = bf16[259,5376]{1,0:T(8,128)(2,1)S(1)} fusion(bf16[256,128]{1,0:T(8,128)(2,1)S(1)} %bitcast.87, bf16[256,128]{1,0:T(8,128)(2,1)S(1)} %bitcast.90, bf16[256,5120]{1,0:T(8,128)(2,1)S(1)} %bitcast.75, bf16[3,5376]{1,0:T(4,128)(2,1)S(1)} %collective-permute-done), kind=kLoop, calls=%fused_computation.21 | loop fusion | flops 11139072 | bytes 5569536 | tf_op jit(solution)/shard_map/concatenate | solution.py:162
  27.6 4.4 %multiply_convert_fusion = bf16[256,5376]{1,0:T(8,128)(2,1)S(1)} fusion(bf16[259,5376]{1,0:T(8,128)(2,1)S(1)} %maximum_maximum_fusion, f32[5376]{0:T(1024)S(1)} %get-tuple-element.9, f32[5376]{0:T(1024)S(1)} %get-tuple-element.10, f32[5376]{0:T(1024)S(1)} %get-tuple-element.8, f32[5376]{0:T(1024)S(1)} %get-tuple-element.7, f32[5376]{0:T(1024)S(1)} %copy-done.25, ...), kind=kLoop, calls=%fused_computation.2 | loop fusion | flops 30277632 | bytes 13870080 | tf_op jit(solution)/shard_map/convert_element_type | solution.py:168
  32.0 1.8 fusion.102
  33.8 2.4 %copy.39 = bf16[128,5120]{0,1:T(8,128)(2,1)} copy(bf16[128,5120]{1,0:T(8,128)(2,1)} %get-tuple-element.24) | data formatting | bytes 2621440 | tf_op jit(solution)/shard_map/slice | solution.py:182
  36.3 2.4 %copy.40 = bf16[128,5120]{0,1:T(8,128)(2,1)} copy(bf16[128,5120]{1,0:T(8,128)(2,1)} %get-tuple-element.25) | data formatting | bytes 2621440 | tf_op jit(solution)/shard_map/slice | solution.py:182
  38.7 3.9 %fusion.9 = f32[80,64,128]{2,1,0:T(8,128)S(1)} fusion(bf16[128,80,64]{0,2,1:T(8,128)(2,1)} %bitcast.81, f32[128,128]{1,0:T(8,128)S(1)} %get-tuple-element.23, f32[80,128]{1,0:T(8,128)S(1)} %get-tuple-element.27), kind=kOutput, calls=%fused_computation.25 | convolution fusion | flops 170393600 | bytes 4038656 | tf_op jit(solution)/shard_map/hsn,shp->hpn/dot_general | solution.py:29
  42.6 1.8 multiply_add_fusion
  44.4 1.3 constant_dynamic-slice_fusion.2
  45.7 0.6 copy-done.4
  46.6 0.7 copy-done.14
  47.3 0.6 broadcast_in_dim.150
  47.9 7.3 %all-to-all-start.1 = ((f32[32,1,80]{2,1,0:T(1,128)}), f32[32,1,80]{2,1,0:T(1,128)S(1)}, u32[]{:S(2)}, u32[]{:S(2)}) async-start(f32[32,1,80]{2,1,0:T(1,128)} %broadcast_in_dim.150), calls=%async_computation.1 | async-start | bytes 32768 | tf_op jit(solution)/shard_map/all_to_all | solution.py:125
  55.3 6.8 %all-to-all-done.1 = f32[32,1,80]{2,1,0:T(1,128)S(1)} async-done(((f32[32,1,80]{2,1,0:T(1,128)}), f32[32,1,80]{2,1,0:T(1,128)S(1)}, u32[]{:S(2)}, u32[]{:S(2)}) %all-to-all-start.1) | async-done | bytes 10272 | tf_op jit(solution)/shard_map/all_to_all | solution.py:125
  62.2 3.3 %fusion.101 = (bf16[40,64,128]{2,1,0:T(8,128)(2,1)}, f32[40,64,128]{2,1,0:T(8,128)}) fusion(f32[40,64,128]{2,1,0:T(8,128)} %collective-permute-done.1, f32[80,64,128]{2,1,0:T(8,128)} %copy-done.4, s32[]{:T(128)S(6)} %select_n.708, pred[]{:T(512)S(6)} %eq.18, f32[40]{0:T(128)S(1)} %get-tuple-element.34), kind=kLoop, calls=%fused_computation.211 | loop fusion | flops 1638400 | bytes 4587685 | tf_op jit(solution)/shard_map/convert_element_type | solution.py:50
  65.5 1.0 collective-permute-start.3
  67.0 0.7 exponential_bitcast_fusion.2
  67.6 13.8 %collective-permute-done.3 = bf16[40,64,128]{2,1,0:T(8,128)(2,1)S(1)} collective-permute-done((bf16[40,64,128]{2,1,0:T(8,128)(2,1)}, bf16[40,64,128]{2,1,0:T(8,128)(2,1)S(1)}, u32[]{:S(2)}, u32[]{:S(2)}) %collective-permute-start.3) | collective-permute-done | bytes 655392 | tf_op jit(solution)/shard_map/ppermute | solution.py:52
  81.5 2.2 collective-permute-start.4
  83.7 1.0 slice.146
  84.9 0.6 exponential_bitcast_fusion.5
  85.5 0.6 exponential_bitcast_fusion.6
  86.1 3.4 %collective-permute-done.4 = bf16[20,64,128]{2,1,0:T(8,128)(2,1)S(1)} collective-permute-done((bf16[20,64,128]{2,1,0:T(8,128)(2,1)S(1)}, bf16[20,64,128]{2,1,0:T(8,128)(2,1)S(1)}, u32[]{:S(2)}, u32[]{:S(2)}) %collective-permute-start.4) | collective-permute-done | bytes 327712 | tf_op jit(solution)/shard_map/ppermute | solution.py:53
  89.5 4.1 %collective-permute-done.5 = bf16[20,64,128]{2,1,0:T(8,128)(2,1)S(1)} collective-permute-done((bf16[20,64,128]{2,1,0:T(8,128)(2,1)S(1)}, bf16[20,64,128]{2,1,0:T(8,128)(2,1)S(1)}, u32[]{:S(2)}, u32[]{:S(2)}) %collective-permute-start.5) | collective-permute-done | bytes 327712 | tf_op jit(solution)/shard_map/ppermute | solution.py:54
  93.6 2.3 %fusion.43 = bf16[40,64,128]{2,1,0:T(8,128)(2,1)S(1)} fusion(bf16[40,64,128]{2,1,0:T(8,128)(2,1)S(1)} %collective-permute-done.3, bf16[40,64,128]{2,1,0:T(8,128)(2,1)} %collective-permute-done.2, f32[40,64,128]{2,1,0:T(8,128)} %get-tuple-element.21, f32[40]{0:T(128)S(1)} %get-tuple-element.50, f32[40]{0:T(128)S(1)} %get-tuple-element.52, ...), kind=kLoop, calls=%fused_computation.68 | loop fusion | flops 3932160 | bytes 3932800 | tf_op jit(solution)/shard_map/convert_element_type | solution.py:50
  95.9 1.1 collective-permute-start.7
  97.5 12.2 %collective-permute-done.7 = bf16[40,64,128]{2,1,0:T(8,128)(2,1)S(1)} collective-permute-done((bf16[40,64,128]{2,1,0:T(8,128)(2,1)S(1)}, bf16[40,64,128]{2,1,0:T(8,128)(2,1)S(1)}, u32[]{:S(2)}, u32[]{:S(2)}) %collective-permute-start.7) | collective-permute-done | bytes 655392 | tf_op jit(solution)/shard_map/ppermute | solution.py:52
  109.7 0.8 copy-done.10
  110.5 0.8 slice.147
  111.3 2.3 %collective-permute-start.8 = (bf16[20,64,128]{2,1,0:T(8,128)(2,1)}, bf16[20,64,128]{2,1,0:T(8,128)(2,1)}, u32[]{:S(2)}, u32[]{:S(2)}) collective-permute-start(bf16[20,64,128]{2,1,0:T(8,128)(2,1)} %slice.147), channel_id=1, source_target_pairs={{0,24},{1,25},{2,26},{3,27},{4,28},{5,29},{6,30},{7,31},{8,0},{9,1... | collective-permute-start | bytes 983048 | tf_op jit(solution)/shard_map/ppermute | solution.py:53
  113.5 0.9 copy-done.11
  114.4 0.7 slice.148
  115.5 0.7 mul.397
  116.1 0.8 mul.398
  117.0 0.8 dynamic-slice_reduce_fusion
  117.9 4.8 %collective-permute-done.9 = bf16[20,64,128]{2,1,0:T(8,128)(2,1)} collective-permute-done((bf16[20,64,128]{2,1,0:T(8,128)(2,1)}, bf16[20,64,128]{2,1,0:T(8,128)(2,1)}, u32[]{:S(2)}, u32[]{:S(2)}) %collective-permute-start.9) | collective-permute-done | bytes 327712 | tf_op jit(solution)/shard_map/ppermute | solution.py:54
  122.7 4.4 %fusion.42 = (f32[40,64,128]{2,1,0:T(8,128)S(1)}, f32[40,64,128]{2,1,0:T(8,128)S(1)}) fusion(f32[40]{0:T(128)S(1)} %get-tuple-element.35, pred[]{:T(512)S(6)} %eq.18, f32[40,64,128]{2,1,0:T(8,128)} %collective-permute-done.1, f32[80,64,128]{2,1,0:T(8,128)} %copy-done.4, s32[]{:T(128)S(6)} %select_n.708, f32[40]{0:T(128)} %get-tuple-element.49, ...), kind=kLoop, calls=%fused_computation.67 | loop fusion | flops 11468800 | bytes 10488005 | tf_op jit(solution)/shard_map/jit(_where)/select_n | solution.py:112
  127.1 1.7 fusion.41
  128.8 3.5 %collective-permute-start.10 = (f32[40,64,128]{2,1,0:T(8,128)S(1)}, f32[40,64,128]{2,1,0:T(8,128)S(1)}, u32[]{:S(2)}, u32[]{:S(2)}) collective-permute-start(f32[40,64,128]{2,1,0:T(8,128)S(1)} %fusion.41), channel_id=1, source_target_pairs={{0,1},{1,0},{2,3},{3,2},{4,5},{5,4},{6,7},{7,6},{8,9},{9,8},{10,11... | collective-permute-start | bytes 3932168 | tf_op jit(solution)/shard_map/ppermute | solution.py:114
  132.7 4.1 %fusion.7 = f32[80,64,128]{2,1,0:T(8,128)} fusion(bf16[128,80,64]{0,2,1:T(8,128)(2,1)S(1)} %bitcast.82, f32[80,128]{1,0:T(8,128)S(1)} %copy-done.23, f32[80,128]{1,0:T(8,128)S(1)} %reduce_window_sum.17, f32[128,128]{1,0:T(8,128)S(1)} %fusion.53, pred[128,128]{1,0:T(8,128)(4,1)S(1)} %iota_compare_fusion), kind=kOutput, calls=%fused_computation.23 | convolution fusion | flops 174325760 | bytes 4096000 | tf_op jit(solution)/shard_map/hts,shp->thp/dot_general | solution.py:26
  136.8 4.0 %fusion.8 = f32[80,64,128]{2,1,0:T(8,128)} fusion(bf16[128,80,64]{0,2,1:T(8,128)(2,1)S(1)} %bitcast.84, f32[80,128]{1,0:T(8,128)S(1)} %copy-done.22, f32[80,128]{1,0:T(8,128)S(1)} %reduce_window_sum.18, f32[128,128]{1,0:T(8,128)S(1)} %fusion.50, pred[128,128]{1,0:T(8,128)(4,1)S(1)} %iota_compare_fusion), kind=kOutput, calls=%fused_computation.24 | convolution fusion | flops 174325760 | bytes 4096000 | tf_op jit(solution)/shard_map/hts,shp->thp/dot_general | solution.py:26
  140.9 1.9 maximum_select_fusion
  142.8 5.4 %bitcast_add_fusion.1 = f32[128,80,64]{0,2,1:T(8,128)} fusion(f32[80,64,128]{2,1,0:T(8,128)} %fusion.7, f32[80,64,128]{2,1,0:T(8,128)} %maximum_select_fusion, f32[128,80]{0,1:T(8,128)S(1)} %copy-done.17, bf16[256,5376]{1,0:T(8,128)(2,1)S(1)} %multiply_convert_fusion), kind=kOutput, calls=%fused_computation.29 | convolution fusion | flops 1007943680 | bytes 7938048 | tf_op jit(solution)/shard_map/tn,hpn->thp/dot_general | solution.py:211
  148.2 3.3 %copy.45 = f32[128,5120]{1,0:T(8,128)} copy(f32[128,5120]{0,1:T(8,128)} %bitcast.79) | data formatting | bytes 5242880 | tf_op jit(solution)/shard_map/concatenate | solution.py:215
  151.5 6.4 %bitcast_add_fusion = f32[128,80,64]{0,2,1:T(8,128)} fusion(f32[80,64,128]{2,1,0:T(8,128)} %fusion.8, f32[80,64,128]{2,1,0:T(8,128)} %maximum_select_fusion, f32[80,64,128]{2,1,0:T(8,128)} %copy-done.3, f32[80]{0:T(128)S(1)} %copy-done.33, f32[128,80]{0,1:T(8,128)S(1)} %get-tuple-element.32, f32[80]{0:T(128)S(1)} %copy-done.32, ...), kind=kOutput, calls=%fused_computation.28 | convolution fusion | flops 1009909760 | bytes 10560512 | tf_op jit(solution)/shard_map/tn,hpn->thp/dot_general | solution.py:211
  158.0 3.2 %copy.46 = f32[128,5120]{1,0:T(8,128)} copy(f32[128,5120]{0,1:T(8,128)} %bitcast.80) | data formatting | bytes 5242880 | tf_op jit(solution)/shard_map/concatenate | solution.py:215
  161.2 5.2 %multiply_reduce_fusion = (f32[256]{0:T(256)S(1)}, f32[256,5120]{1,0:T(8,128)S(1)}) fusion(bf16[1,256,5120]{2,1,0:T(8,128)(2,1)} %param.13, bf16[256,5376]{1,0:T(8,128)(2,1)S(1)} %multiply_convert_fusion, f32[5120]{0:T(1024)S(1)} %mul.398, f32[128,5120]{1,0:T(8,128)} %copy.46, f32[128,5120]{1,0:T(8,128)} %copy.45), kind=kLoop, calls=%fused_computation.10 | loop fusion | flops 15728384 | bytes 15750144 | tf_op jit(solution)/shard_map/reduce_sum | solution.py:218
  166.5 2.3 %copy-done = f32[256,5120]{1,0:T(8,128)} copy-done((f32[256,5120]{1,0:T(8,128)}, f32[256,5120]{1,0:T(8,128)S(1)}, u32[]{:S(2)}) %copy-start) | copy-done | bytes 5242904
  168.8 1.0 convert_reduce_fusion
  169.8 2.3 %multiply_reduce_fusion.2 = (f32[8]{0:T(128)S(1)}, bf16[8,256]{1,0:T(8,128)(2,1)S(1)}, f32[8,256]{1,0:T(8,128)S(1)}) fusion(bf16[5120,256]{1,0:T(8,128)(2,1)} %all-gather.5.cloned.1.call-done, f32[8,5120]{1,0:T(8,128)S(1)} %convert_reduce_fusion), kind=kOutput, calls=%fused_computation.101 | convolution fusion | flops 21059576 | bytes 2797600 | tf_op jit(solution)/shard_map/dot_general | solution.py:223
  172.1 14.8 %all_to_all.21 = bf16[8,8,256]{2,1,0:T(8,128)(2,1)S(1)} all-to-all(bf16[8,8,256]{2,1,0:T(8,128)(2,1)S(1)} %broadcast_in_dim.156), channel_id=1, replica_groups=mesh['dp'=8,'seq'=32] {'dp'}, dimensions={0} | all-to-all | bytes 65536 | tf_op jit(solution)/shard_map/all_to_all | solution.py:125
  187.0 1.1 broadcast_in_dim.157
  188.0 6.0 %all-to-all-start.3 = ((bf16[32,8,8,256]{3,2,1,0:T(8,128)(2,1)}), bf16[32,8,8,256]{3,2,1,0:T(8,128)(2,1)}, u32[]{:S(2)}, u32[]{:S(2)}) async-start(bf16[32,8,8,256]{3,2,1,0:T(8,128)(2,1)} %broadcast_in_dim.157), calls=%async_computation.3 | async-start | bytes 2097152 | tf_op jit(solution)/shard_map/all_to_all | solution.py:125
  194.0 4.7 %fusion.98 = bf16[1,256,5120]{2,1,0:T(8,128)(2,1)} fusion(f32[5120]{0:T(1024)S(1)} %copy-done.18, f32[256,5120]{1,0:T(8,128)} %copy-done, f32[256]{0:T(256)S(1)} %add_rsqrt_fusion), kind=kLoop, calls=%fused_computation.210 | loop fusion | flops 3932160 | bytes 7885824 | tf_op jit(solution)/shard_map/broadcast_in_dim | solution.py:232
  198.7 12.4 %all-to-all-done.3 = bf16[32,8,8,256]{3,2,1,0:T(8,128)(2,1)} async-done(((bf16[32,8,8,256]{3,2,1,0:T(8,128)(2,1)}), bf16[32,8,8,256]{3,2,1,0:T(8,128)(2,1)}, u32[]{:S(2)}, u32[]{:S(2)}) %all-to-all-start.3) | async-done | bytes 1048608 | tf_op jit(solution)/shard_map/all_to_all | solution.py:125
  211.1 1.6 copy_convert_fusion
  213.0 0.6 multiply_reduce_fusion.1
  213.6 4.2 %fusion.6 = f32[8,4096]{1,0:T(8,128)} fusion(f32[8,256]{1,0:T(8,128)S(1)} %get-tuple-element.57, f32[2048,256]{1,0:T(8,128)S(1)} %copy-done.6, f32[2048,256]{1,0:T(8,128)S(1)} %bitcast.78, f32[4096]{0:T(1024)S(1)} %multiply_reduce_fusion.1, f32[8]{0:T(128)S(1)} %get-tuple-element.36), kind=kOutput, calls=%fused_computation.18 | convolution fusion | flops 101875712 | bytes 4349984 | tf_op jit(solution)/shard_map/dot_general | solution.py:226
  (99 shorter events, 3.5 us)
Async XLA Ops:
  7.2 6.8 %copy-start.26 = (f32[8,256]{1,0:T(8,128)S(1)}, f32[8,256]{1,0:T(8,128)}, u32[]{:S(2)}) copy-start(f32[8,256]{1,0:T(8,128)} %param.23) | copy-start | bytes 24580
  7.2 14.5 %copy-start.19 = (f32[1,80,256]{2,1,0:T(8,128)S(1)}, f32[1,80,256]{2,1,0:T(8,128)}, u32[]{:S(2)}) copy-start(f32[1,80,256]{2,1,0:T(8,128)} %param.17) | copy-start | bytes 245764
  7.2 15.9 %copy-start.20 = (f32[1,80,256]{2,1,0:T(8,128)S(1)}, f32[1,80,256]{2,1,0:T(8,128)}, u32[]{:S(2)}) copy-start(f32[1,80,256]{2,1,0:T(8,128)} %param.16) | copy-start | bytes 245764
  7.2 17.9 %copy-start.1 = (bf16[1,256,5120]{2,1,0:T(8,128)(2,1)S(1)}, bf16[1,256,5120]{2,1,0:T(8,128)(2,1)}, u32[]{:S(2)}) copy-start(bf16[1,256,5120]{2,1,0:T(8,128)(2,1)} %param.12) | copy-start | bytes 7864324
  7.2 17.9 %copy-start.15 = (bf16[1,256,128]{2,1,0:T(8,128)(2,1)S(1)}, bf16[1,256,128]{2,1,0:T(8,128)(2,1)}, u32[]{:S(2)}) copy-start(bf16[1,256,128]{2,1,0:T(8,128)(2,1)} %param.15) | copy-start | bytes 196612
  7.2 17.9 %copy-start.16 = (bf16[1,256,128]{2,1,0:T(8,128)(2,1)S(1)}, bf16[1,256,128]{2,1,0:T(8,128)(2,1)}, u32[]{:S(2)}) copy-start(bf16[1,256,128]{2,1,0:T(8,128)(2,1)} %param.14) | copy-start | bytes 196612
  9.4 15.7 %collective-permute-start = (bf16[3,5376]{1,0:T(4,128)(2,1)S(1)}, bf16[3,5376]{1,0:T(4,128)(2,1)S(1)}, u32[]{:S(2)}, u32[]{:S(2)}) collective-permute-start(bf16[3,5376]{1,0:T(4,128)(2,1)S(1)} %slice.128), channel_id=1, source_target_pairs={{0,1},{1,2},{2,3},{3,4},{4,5},{5,6},{6,7},{7,8},{8,9},{9,10},{10,1... | collective-permute-start | bytes 96776 | tf_op jit(solution)/shard_map/ppermute | solution.py:16
  14.7 31.8 %all-to-all-start = ((f32[32,8,256]{2,1,0:T(8,128)}), f32[32,8,256]{2,1,0:T(8,128)S(1)}, u32[]{:S(2)}, u32[]{:S(2)}) async-start(f32[32,8,256]{2,1,0:T(8,128)} %broadcast_in_dim.149), calls=%async_computation | async-start | bytes 524288 | tf_op jit(solution)/shard_map/all_to_all | solution.py:125
  21.7 121.1 %all-gather.3.cloned.1.call-start = ((), (), s32[]{:S(2)}) async-start(), calls=%async_computation.4 | async-start | bytes 2359296 | tf_op jit(solution)/shard_map/all_gather | solution.py:130
  23.1 19.5 %copy-start.31 = (f32[80]{0:T(128)}, f32[80]{0:T(128)S(1)}, u32[]{:S(2)}) copy-start(f32[80]{0:T(128)S(1)} %get-tuple-element.54) | copy-start | bytes 964
  25.1 2.4 %copy-start.2 = (bf16[1,256,5120]{2,1,0:T(8,128)(2,1)S(1)}, bf16[1,256,5120]{2,1,0:T(8,128)(2,1)}, u32[]{:S(2)}) copy-start(bf16[1,256,5120]{2,1,0:T(8,128)(2,1)} %param.12) | copy-start | bytes 7864324
  25.1 2.4 %copy-start.25 = (f32[5376]{0:T(1024)S(1)}, f32[5376]{0:T(1024)}, u32[]{:S(2)}) copy-start(f32[5376]{0:T(1024)} %param.19) | copy-start | bytes 64516
  38.7 4.0 %copy-start.8 = (bf16[128,5120]{0,1:T(8,128)(2,1)S(1)}, bf16[128,5120]{0,1:T(8,128)(2,1)}, u32[]{:S(2)}) copy-start(bf16[128,5120]{0,1:T(8,128)(2,1)} %copy.40) | copy-start | bytes 3932164
  42.6 1.8 copy-start.3
  44.4 1.9 copy-start.4
  46.3 15.8 %collective-permute-start.1 = (f32[40,64,128]{2,1,0:T(8,128)}, f32[40,64,128]{2,1,0:T(8,128)}, u32[]{:S(2)}, u32[]{:S(2)}) collective-permute-start(f32[40,64,128]{2,1,0:T(8,128)} %constant_dynamic-slice_fusion.2), channel_id=1, source_target_pairs={{0,1},{1,0},{2,3},{3,2},{4,5},{5,4},{6,7},{7,6},{8,9},{9,8},{10,11... | collective-permute-start | bytes 3932168 | tf_op jit(solution)/shard_map/ppermute | solution.py:101
  46.6 0.7 copy-start.14
  47.9 14.2 %all-to-all-start.1 = ((f32[32,1,80]{2,1,0:T(1,128)}), f32[32,1,80]{2,1,0:T(1,128)S(1)}, u32[]{:S(2)}, u32[]{:S(2)}) async-start(f32[32,1,80]{2,1,0:T(1,128)} %broadcast_in_dim.150), calls=%async_computation.1 | async-start | bytes 32768 | tf_op jit(solution)/shard_map/all_to_all | solution.py:125
  55.2 114.6 %all-gather.5.cloned.1.call-start = ((), (), s32[]{:S(2)}) async-start(), calls=%async_computation.5 | async-start | bytes 2949120 | tf_op jit(solution)/shard_map/all_gather | solution.py:159
  65.5 15.9 %collective-permute-start.3 = (bf16[40,64,128]{2,1,0:T(8,128)(2,1)}, bf16[40,64,128]{2,1,0:T(8,128)(2,1)S(1)}, u32[]{:S(2)}, u32[]{:S(2)}) collective-permute-start(bf16[40,64,128]{2,1,0:T(8,128)(2,1)} %get-tuple-element.20), channel_id=1, source_target_pairs={{0,6},{1,7},{2,0},{3,1},{4,2},{5,3},{6,4},{7,5},{8,14},{9,15},{10,... | collective-permute-start | bytes 1966088 | tf_op jit(solution)/shard_map/ppermute | solution.py:52
  66.5 17.2 %collective-permute-start.2 = (bf16[40,64,128]{2,1,0:T(8,128)(2,1)}, bf16[40,64,128]{2,1,0:T(8,128)(2,1)}, u32[]{:S(2)}, u32[]{:S(2)}) collective-permute-start(bf16[40,64,128]{2,1,0:T(8,128)(2,1)} %get-tuple-element.20), channel_id=1, source_target_pairs={{0,2},{1,3},{2,4},{3,5},{4,6},{5,7},{6,0},{7,1},{8,10},{9,11},{10,... | collective-permute-start | bytes 1966088 | tf_op jit(solution)/shard_map/ppermute | solution.py:51
  67.0 0.7 copy-start.21
  81.5 8.0 %collective-permute-start.4 = (bf16[20,64,128]{2,1,0:T(8,128)(2,1)S(1)}, bf16[20,64,128]{2,1,0:T(8,128)(2,1)S(1)}, u32[]{:S(2)}, u32[]{:S(2)}) collective-permute-start(bf16[20,64,128]{2,1,0:T(8,128)(2,1)S(1)} %slice.145), channel_id=1, source_target_pairs={{0,6},{1,7},{2,0},{3,1},{4,2},{5,3},{6,4},{7,5},{8,14},{9,15},{10,... | collective-permute-start | bytes 983048 | tf_op jit(solution)/shard_map/ppermute | solution.py:53
  84.7 9.0 %collective-permute-start.5 = (bf16[20,64,128]{2,1,0:T(8,128)(2,1)S(1)}, bf16[20,64,128]{2,1,0:T(8,128)(2,1)S(1)}, u32[]{:S(2)}, u32[]{:S(2)}) collective-permute-start(bf16[20,64,128]{2,1,0:T(8,128)(2,1)S(1)} %slice.146), channel_id=1, source_target_pairs={{0,2},{1,3},{2,4},{3,5},{4,6},{5,7},{6,0},{7,1},{8,10},{9,11},{10,... | collective-permute-start | bytes 983048 | tf_op jit(solution)/shard_map/ppermute | solution.py:54
  85.5 29.6 %copy-start.27 = (f32[40]{0:T(128)}, f32[40]{0:T(128)S(1)}, u32[]{:S(2)}) copy-start(f32[40]{0:T(128)S(1)} %get-tuple-element.43) | copy-start | bytes 484
  85.5 29.6 %copy-start.28 = (f32[40]{0:T(128)}, f32[40]{0:T(128)S(1)}, u32[]{:S(2)}) copy-start(f32[40]{0:T(128)S(1)} %get-tuple-element.52) | copy-start | bytes 484
  86.1 29.0 %copy-start.29 = (f32[40]{0:T(128)}, f32[40]{0:T(128)S(1)}, u32[]{:S(2)}) copy-start(f32[40]{0:T(128)S(1)} %get-tuple-element.41) | copy-start | bytes 484
  86.1 29.0 %copy-start.30 = (f32[40]{0:T(128)}, f32[40]{0:T(128)S(1)}, u32[]{:S(2)}) copy-start(f32[40]{0:T(128)S(1)} %get-tuple-element.50) | copy-start | bytes 484
  89.5 25.7 %copy-start.12 = (bf16[20,64,128]{2,1,0:T(8,128)(2,1)}, bf16[20,64,128]{2,1,0:T(8,128)(2,1)S(1)}, u32[]{:S(2)}) copy-start(bf16[20,64,128]{2,1,0:T(8,128)(2,1)S(1)} %collective-permute-done.4) | copy-start | bytes 983044
  93.6 21.5 %copy-start.13 = (bf16[20,64,128]{2,1,0:T(8,128)(2,1)}, bf16[20,64,128]{2,1,0:T(8,128)(2,1)S(1)}, u32[]{:S(2)}) copy-start(bf16[20,64,128]{2,1,0:T(8,128)(2,1)S(1)} %collective-permute-done.5) | copy-start | bytes 983044
  93.6 21.8 %copy-start.34 = (f32[80]{0:T(128)S(1)}, f32[80]{0:T(128)}, u32[]{:S(2)}) copy-start(f32[80]{0:T(128)} %param.20) | copy-start | bytes 964
  95.9 13.7 %collective-permute-start.7 = (bf16[40,64,128]{2,1,0:T(8,128)(2,1)S(1)}, bf16[40,64,128]{2,1,0:T(8,128)(2,1)S(1)}, u32[]{:S(2)}, u32[]{:S(2)}) collective-permute-start(bf16[40,64,128]{2,1,0:T(8,128)(2,1)S(1)} %fusion.43), channel_id=1, source_target_pairs={{0,24},{1,25},{2,26},{3,27},{4,28},{5,29},{6,30},{7,31},{8,0},{9,1... | collective-permute-start | bytes 1966088 | tf_op jit(solution)/shard_map/ppermute | solution.py:52
  97.0 16.6 %collective-permute-start.6 = (bf16[40,64,128]{2,1,0:T(8,128)(2,1)S(1)}, bf16[40,64,128]{2,1,0:T(8,128)(2,1)S(1)}, u32[]{:S(2)}, u32[]{:S(2)}) collective-permute-start(bf16[40,64,128]{2,1,0:T(8,128)(2,1)S(1)} %fusion.43), channel_id=1, source_target_pairs={{0,8},{1,9},{2,10},{3,11},{4,12},{5,13},{6,14},{7,15},{8,16},{9,17... | collective-permute-start | bytes 1966088 | tf_op jit(solution)/shard_map/ppermute | solution.py:51
  109.7 0.8 copy-start.10
  111.3 6.6 %collective-permute-start.8 = (bf16[20,64,128]{2,1,0:T(8,128)(2,1)}, bf16[20,64,128]{2,1,0:T(8,128)(2,1)}, u32[]{:S(2)}, u32[]{:S(2)}) collective-permute-start(bf16[20,64,128]{2,1,0:T(8,128)(2,1)} %slice.147), channel_id=1, source_target_pairs={{0,24},{1,25},{2,26},{3,27},{4,28},{5,29},{6,30},{7,31},{8,0},{9,1... | collective-permute-start | bytes 983048 | tf_op jit(solution)/shard_map/ppermute | solution.py:53
  113.5 0.9 copy-start.11
  115.2 7.5 %collective-permute-start.9 = (bf16[20,64,128]{2,1,0:T(8,128)(2,1)}, bf16[20,64,128]{2,1,0:T(8,128)(2,1)}, u32[]{:S(2)}, u32[]{:S(2)}) collective-permute-start(bf16[20,64,128]{2,1,0:T(8,128)(2,1)} %slice.148), channel_id=1, source_target_pairs={{0,8},{1,9},{2,10},{3,11},{4,12},{5,13},{6,14},{7,15},{8,16},{9,17... | collective-permute-start | bytes 983048 | tf_op jit(solution)/shard_map/ppermute | solution.py:54
  122.7 4.4 %copy-start.5 = (f32[80,64,128]{2,1,0:T(8,128)S(1)}, f32[80,64,128]{2,1,0:T(8,128)}, u32[]{:S(2)}) copy-start(f32[80,64,128]{2,1,0:T(8,128)} %copy-done.4) | copy-start | bytes 7864324
  127.1 5.5 %copy-start.7 = (bf16[128,5120]{0,1:T(8,128)(2,1)S(1)}, bf16[128,5120]{0,1:T(8,128)(2,1)}, u32[]{:S(2)}) copy-start(bf16[128,5120]{0,1:T(8,128)(2,1)} %copy.39) | copy-start | bytes 3932164
  127.1 5.6 %copy-start.23 = (f32[80,128]{1,0:T(8,128)S(1)}, f32[80,128]{1,0:T(8,128)}, u32[]{:S(2)}) copy-start(f32[80,128]{1,0:T(8,128)} %get-tuple-element.26) | copy-start | bytes 122884
  128.8 12.0 %collective-permute-start.10 = (f32[40,64,128]{2,1,0:T(8,128)S(1)}, f32[40,64,128]{2,1,0:T(8,128)S(1)}, u32[]{:S(2)}, u32[]{:S(2)}) collective-permute-start(f32[40,64,128]{2,1,0:T(8,128)S(1)} %fusion.41), channel_id=1, source_target_pairs={{0,1},{1,0},{2,3},{3,2},{4,5},{5,4},{6,7},{7,6},{8,9},{9,8},{10,11... | collective-permute-start | bytes 3932168 | tf_op jit(solution)/shard_map/ppermute | solution.py:114
  132.7 4.1 %copy-start.9 = (bf16[128,5120]{0,1:T(8,128)(2,1)S(1)}, bf16[128,5120]{0,1:T(8,128)(2,1)}, u32[]{:S(2)}) copy-start(bf16[128,5120]{0,1:T(8,128)(2,1)} %copy.40) | copy-start | bytes 3932164
  132.7 4.1 %copy-start.22 = (f32[80,128]{1,0:T(8,128)S(1)}, f32[80,128]{1,0:T(8,128)}, u32[]{:S(2)}) copy-start(f32[80,128]{1,0:T(8,128)} %get-tuple-element.29) | copy-start | bytes 122884
  140.9 1.9 copy-start.17
  148.2 3.3 %copy-start.32 = (f32[80]{0:T(128)S(1)}, f32[80]{0:T(128)}, u32[]{:S(2)}) copy-start(f32[80]{0:T(128)} %copy-done.31) | copy-start | bytes 964
  148.2 3.3 %copy-start.33 = (f32[80]{0:T(128)S(1)}, f32[80]{0:T(128)}, u32[]{:S(2)}) copy-start(f32[80]{0:T(128)} %get-tuple-element.53) | copy-start | bytes 964
  161.2 7.6 %copy-start.18 = (f32[5120]{0:T(1024)S(1)}, f32[5120]{0:T(1024)}, u32[]{:S(2)}) copy-start(f32[5120]{0:T(1024)} %param.21) | copy-start | bytes 61444
  166.5 2.3 %copy-start = (f32[256,5120]{1,0:T(8,128)}, f32[256,5120]{1,0:T(8,128)S(1)}, u32[]{:S(2)}) copy-start(f32[256,5120]{1,0:T(8,128)S(1)} %get-tuple-element.12) | copy-start | bytes 15728644
  172.1 41.5 %copy-start.24 = (f32[8,256]{1,0:T(8,128)}, f32[8,256]{1,0:T(8,128)S(1)}, u32[]{:S(2)}) copy-start(f32[8,256]{1,0:T(8,128)S(1)} %get-tuple-element.57) | copy-start | bytes 24580
  188.0 23.0 %all-to-all-start.3 = ((bf16[32,8,8,256]{3,2,1,0:T(8,128)(2,1)}), bf16[32,8,8,256]{3,2,1,0:T(8,128)(2,1)}, u32[]{:S(2)}, u32[]{:S(2)}) async-start(bf16[32,8,8,256]{3,2,1,0:T(8,128)(2,1)} %broadcast_in_dim.157), calls=%async_computation.3 | async-start | bytes 2097152 | tf_op jit(solution)/shard_map/all_to_all | solution.py:125
  211.1 1.9 copy-start.6
Sparse Core Ops, SparseCore 0:
  47.4 39.1 all-gather.2
  115.4 42.4 all-gather.4

commit v9 on v8

--- a/solution.py
+++ b/solution.py
@@ -82,7 +82,7 @@
     return before, jnp.exp(lead), total
 
 
-def carried_in(own_state, shard_logs):
+def carried_in(own_state, shard_logs, prior_block):
     seq = lax.axis_size("seq")
     rows, partner, y_routes, x_routes = chip_routes(seq)
     assert rows == RING and seq == rows * RING * CORES
@@ -105,6 +105,8 @@
     slots = ring_of_four(chip_state, *y_routes)
     row_logs = lax.dynamic_index_in_dim(chip_logs, x_pos, 0, False)
     row_before, row_lead, row_total = fold_ring(slots, y_pos, row_logs)
+    prior_block, row_total = lax.optimization_barrier((prior_block, row_total))
+    all_prior = prior_everywhere(prior_block)
     slots = ring_of_four(row_total, *x_routes)
     rows_before, _, _ = fold_ring(slots, x_pos, jnp.sum(chip_logs, axis=1))
     chip_in = row_lead[:, None, None] * rows_before + row_before
@@ -112,7 +114,8 @@
     keep = jnp.where(core == 0, chip_in, high_in)
     give = jnp.where(core == 0, high_in, chip_in)
     got = lax.ppermute(give, "seq", partner)
-    return jnp.where(core == 0, jnp.concatenate([keep, got], 0), jnp.concatenate([got, keep], 0))
+    carry = jnp.where(core == 0, jnp.concatenate([keep, got], 0), jnp.concatenate([got, keep], 0))
+    return carry, all_prior
 
 
 def placed(block, slots, index):
@@ -198,9 +201,8 @@
         block_total = cum_list[block][:, -1]
         running = jnp.exp(block_total)[:, None, None] * running + state_list[block]
         before = before + block_total
-    all_prior = prior_everywhere(prior_draw)
     shard_logs = spread_over(before, "seq")
-    carry_in = carried_in(running, shard_logs)
+    carry_in, all_prior = carried_in(running, shard_logs, prior_draw)
     all_prior, carry_in = lax.optimization_barrier((all_prior, carry_in))
     outputs = []
     for block in range(blocks):

time: 226 us -> 239 us (1.058)
  blocking collectives: 14.8 us -> 27.6 us
  waiting for transfers between devices: 57.5 us -> 64.3 us
  starting transfers between devices: 36.4 us -> 30.2 us
  local copies, waits for them, and re-layouts: 28.5 us -> 25.9 us
  other arithmetic: 40.1 us -> 42.6 us
    all_to_all x1 -> x2, blocking collectives: 14.8 us -> 27.6 us  [spread_over(): lax.all_to_all(jnp.broadcast_to(block[None], (count,) + block.shape), axi...]
    add x0 -> x1, other arithmetic: none -> 3.2 us  [fold_ring(): total = w_total * v if total is None else total + w_total * v]
    ppermute x1, starting transfers between devices: 3.52 us -> 0.77 us  [carried_in(): got = lax.ppermute(give, 'seq', partner)]
    ppermute x2, waiting for transfers between devices: 3.38 us -> 5.98 us  [ring_of_four(): far_a = lax.ppermute(next_state[:half], 'seq', bwd)]
    ppermute x2, waiting for transfers between devices: 26 us -> 28.6 us  [ring_of_four(): next_state = lax.ppermute(sent, 'seq', bwd)]
    all_to_all x3 -> x2, starting transfers between devices: 20.1 us -> 17.6 us  [spread_over(): lax.all_to_all(jnp.broadcast_to(block[None], (count,) + block.shape), axi...]
    unnamed x70 -> x62, local copies, waits for them, and re-layouts: 5.84 us -> 5.17 us
    all_to_all x3 -> x2, waiting for transfers between devices: 19.1 us -> 19 us  [spread_over(): lax.all_to_all(jnp.broadcast_to(block[None], (count,) + block.shape), axi...]
  transfers between devices with their start and end apart: 16 -> 15, of which waited for: 7 -> 9; matrix products, arithmetic and copies ran while one was open for 37% -> 24% of each run, Pallas kernels for 0% -> 0%
where the time goes in v9:
time: 239 us; the launch traced here: 238 us
  waiting for transfers between devices  64.3 us (27%)
  other arithmetic  42.6 us (18%)
  matrix products  32.6 us (14%)
  starting transfers between devices  30.2 us (13%)
  blocking collectives  27.6 us (12%)
  local copies, waits for them, and re-layouts  25.9 us (11%)
  between operations  14.8 us (6%)
    ppermute x2, waiting for transfers between devices, ring_of_four(): next_state = lax.ppermute(sent, 'seq', bwd)  28.6 us
    all_to_all x2, blocking collectives, spread_over(): lax.all_to_all(jnp.broadcast_to(block[None], (count,) + block.shape), axi...  27.6 us
    all_to_all x2, waiting for transfers between devices, spread_over(): lax.all_to_all(jnp.broadcast_to(block[None], (count,) + block.shape), axi...  19 us
    all_to_all x2, starting transfers between devices, spread_over(): lax.all_to_all(jnp.broadcast_to(block[None], (count,) + block.shape), axi...  17.6 us
    dot_general x2, matrix products, per_device(): jnp.einsum('tn,hpn->thp', read_block, start, precision=lax.Precision.HIGH...  12 us
    ppermute x2, waiting for transfers between devices, ring_of_four(): far_b = lax.ppermute(prev_state[half:], 'seq', fwd)  8.33 us
    dot_general x2, matrix products, block_terms(): jnp.einsum('hts,shp->thp', mixing, values, preferred_element_type=jnp.flo...  8.19 us
    slice x3, local copies, waits for them, and re-layouts, per_device(): values[lower:upper]  6.67 us
  transfers between devices with their start and end apart: 15, of which 9 were waited for; matrix products, arithmetic and copies ran while one was open for 24% of the time, Pallas kernels for 0%

profile of v9, /device:TPU:1, one launch (start us, length us, event | category | flops | bytes accessed | tf_op | source)
XLA Modules:
  0.0 238.0 jit_solution(7832864366876967816)
XLA Ops:
  7.2 2.1 pad_maximum_fusion.2
  9.4 4.6 %collective-permute-start = (bf16[3,5376]{1,0:T(4,128)(2,1)S(1)}, bf16[3,5376]{1,0:T(4,128)(2,1)S(1)}, u32[]{:S(2)}, u32[]{:S(2)}) collective-permute-start(bf16[3,5376]{1,0:T(4,128)(2,1)S(1)} %slice.128), channel_id=1, source_target_pairs={{0,1},{1,2},{2,3},{3,4},{4,5},{5,6},{6,7},{7,8},{8,9},{9,10},{10,1... | collective-permute-start | bytes 96776 | tf_op jit(solution)/shard_map/ppermute | solution.py:16
  15.3 0.7 fusion.102
  16.3 2.4 maximum_maximum_fusion
  18.7 4.4 %multiply_convert_fusion = bf16[256,5376]{1,0:T(8,128)(2,1)S(1)} fusion(bf16[259,5376]{1,0:T(8,128)(2,1)S(1)} %maximum_maximum_fusion, f32[5376]{0:T(1024)S(1)} %get-tuple-element.13, f32[5376]{0:T(1024)S(1)} %get-tuple-element.14, f32[5376]{0:T(1024)S(1)} %get-tuple-element.12, f32[5376]{0:T(1024)S(1)} %get-tuple-element.11, f32[5376]{0:T(1024)S(1)} %copy-done.25, ...), kind=kLoop, calls=%fused_computation.2 | loop fusion | flops 30277632 | bytes 13870080 | tf_op jit(solution)/shard_map/convert_element_type | solution.py:171
  23.1 1.8 fusion.101
  25.0 2.4 %copy.39 = bf16[128,5120]{0,1:T(8,128)(2,1)} copy(bf16[128,5120]{1,0:T(8,128)(2,1)} %get-tuple-element.28) | data formatting | bytes 2621440 | tf_op jit(solution)/shard_map/slice | solution.py:185
  27.4 2.4 %copy.40 = bf16[128,5120]{0,1:T(8,128)(2,1)} copy(bf16[128,5120]{1,0:T(8,128)(2,1)} %get-tuple-element.29) | data formatting | bytes 2621440 | tf_op jit(solution)/shard_map/slice | solution.py:185
  29.8 3.9 %fusion.9 = f32[80,64,128]{2,1,0:T(8,128)S(1)} fusion(bf16[128,80,64]{0,2,1:T(8,128)(2,1)} %bitcast.81, f32[128,128]{1,0:T(8,128)S(1)} %get-tuple-element.27, f32[80,128]{1,0:T(8,128)S(1)} %get-tuple-element.31), kind=kOutput, calls=%fused_computation.25 | convolution fusion | flops 170393600 | bytes 4038656 | tf_op jit(solution)/shard_map/hsn,shp->hpn/dot_general | solution.py:29
  33.8 1.8 multiply_add_fusion
  35.6 1.3 constant_dynamic-slice_fusion.6
  36.9 0.6 copy-done.4
  37.5 0.6 broadcast_in_dim.149
  38.1 7.3 %all-to-all-start = ((f32[32,1,80]{2,1,0:T(1,128)}), f32[32,1,80]{2,1,0:T(1,128)S(1)}, u32[]{:S(2)}, u32[]{:S(2)}) async-start(f32[32,1,80]{2,1,0:T(1,128)} %broadcast_in_dim.149), calls=%async_computation | async-start | bytes 32768 | tf_op jit(solution)/shard_map/all_to_all | solution.py:128
  45.5 6.8 %all-to-all-done = f32[32,1,80]{2,1,0:T(1,128)S(1)} async-done(((f32[32,1,80]{2,1,0:T(1,128)}), f32[32,1,80]{2,1,0:T(1,128)S(1)}, u32[]{:S(2)}, u32[]{:S(2)}) %all-to-all-start) | async-done | bytes 10272 | tf_op jit(solution)/shard_map/all_to_all | solution.py:128
  52.4 3.3 %fusion.100 = (bf16[40,64,128]{2,1,0:T(8,128)(2,1)}, f32[40,64,128]{2,1,0:T(8,128)}) fusion(f32[40,64,128]{2,1,0:T(8,128)} %collective-permute-done.1, f32[80,64,128]{2,1,0:T(8,128)} %copy-done.4, s32[]{:T(128)S(6)} %select_n.707, pred[]{:T(512)S(6)} %eq.18, f32[40]{0:T(128)S(1)} %get-tuple-element.39), kind=kLoop, calls=%fused_computation.210 | loop fusion | flops 1638400 | bytes 4587685 | tf_op jit(solution)/shard_map/convert_element_type | solution.py:50
  55.7 0.9 collective-permute-start.3
  57.2 0.6 exponential_bitcast_fusion.2
  57.8 13.8 %collective-permute-done.3 = bf16[40,64,128]{2,1,0:T(8,128)(2,1)S(1)} collective-permute-done((bf16[40,64,128]{2,1,0:T(8,128)(2,1)}, bf16[40,64,128]{2,1,0:T(8,128)(2,1)S(1)}, u32[]{:S(2)}, u32[]{:S(2)}) %collective-permute-start.3) | collective-permute-done | bytes 655392 | tf_op jit(solution)/shard_map/ppermute | solution.py:52
  71.7 2.1 collective-permute-start.4
  73.8 1.0 slice.146
  75.0 0.6 fusion.68
  75.6 0.6 fusion.67
  76.2 3.3 %collective-permute-done.4 = bf16[20,64,128]{2,1,0:T(8,128)(2,1)S(1)} collective-permute-done((bf16[20,64,128]{2,1,0:T(8,128)(2,1)S(1)}, bf16[20,64,128]{2,1,0:T(8,128)(2,1)S(1)}, u32[]{:S(2)}, u32[]{:S(2)}) %collective-permute-start.4) | collective-permute-done | bytes 327712 | tf_op jit(solution)/shard_map/ppermute | solution.py:53
  79.6 4.1 %collective-permute-done.5 = bf16[20,64,128]{2,1,0:T(8,128)(2,1)S(1)} collective-permute-done((bf16[20,64,128]{2,1,0:T(8,128)(2,1)S(1)}, bf16[20,64,128]{2,1,0:T(8,128)(2,1)S(1)}, u32[]{:S(2)}, u32[]{:S(2)}) %collective-permute-start.5) | collective-permute-done | bytes 327712 | tf_op jit(solution)/shard_map/ppermute | solution.py:54
  83.7 3.2 %fusion.35 = f32[40,64,128]{2,1,0:T(8,128)} fusion(bf16[40,64,128]{2,1,0:T(8,128)(2,1)} %collective-permute-done.2, bf16[40,64,128]{2,1,0:T(8,128)(2,1)S(1)} %collective-permute-done.3, f32[40,64,128]{2,1,0:T(8,128)} %get-tuple-element.25, f32[40]{0:T(128)S(1)} %get-tuple-element.53, f32[40]{0:T(128)S(1)} %get-tuple-element.55, f32[40]{0:T(128)S(1)} %get-tuple-element.48, ...), kind=kLoop, calls=%fused_computation.59 | loop fusion | flops 3604480 | bytes 4588160 | tf_op jit(solution)/shard_map/add | solution.py:78
  87.0 15.0 %all_to_all.21 = f32[32,8,256]{2,1,0:T(8,128)} all-to-all(f32[32,8,256]{2,1,0:T(8,128)S(1)} %broadcast_in_dim.152), channel_id=1, replica_groups=mesh['dp'=8,'seq'=32] {'seq'}, dimensions={0} | all-to-all | bytes 524288 | tf_op jit(solution)/shard_map/all_to_all | solution.py:128
  102.1 1.4 convert_element_type.102
  103.5 0.8 collective-permute-start.7
  104.3 0.7 collective-permute-start.6
  105.0 14.7 %collective-permute-done.7 = bf16[40,64,128]{2,1,0:T(8,128)(2,1)S(1)} collective-permute-done((bf16[40,64,128]{2,1,0:T(8,128)(2,1)S(1)}, bf16[40,64,128]{2,1,0:T(8,128)(2,1)S(1)}, u32[]{:S(2)}, u32[]{:S(2)}) %collective-permute-start.7) | collective-permute-done | bytes 655392 | tf_op jit(solution)/shard_map/ppermute | solution.py:52
  119.8 0.9 copy-done.10
  120.7 0.7 slice.147
  121.4 1.8 collective-permute-start.8
  123.2 0.8 copy-done.11
  124.1 0.8 slice.148
  125.0 0.7 mul.397
  125.7 0.8 mul.398
  126.6 0.8 dynamic-slice_reduce_fusion
  127.4 2.6 %collective-permute-done.8 = bf16[20,64,128]{2,1,0:T(8,128)(2,1)} collective-permute-done((bf16[20,64,128]{2,1,0:T(8,128)(2,1)}, bf16[20,64,128]{2,1,0:T(8,128)(2,1)}, u32[]{:S(2)}, u32[]{:S(2)}) %collective-permute-start.8) | collective-permute-done | bytes 327712 | tf_op jit(solution)/shard_map/ppermute | solution.py:53
  130.1 4.2 %collective-permute-done.9 = bf16[20,64,128]{2,1,0:T(8,128)(2,1)} collective-permute-done((bf16[20,64,128]{2,1,0:T(8,128)(2,1)}, bf16[20,64,128]{2,1,0:T(8,128)(2,1)}, u32[]{:S(2)}, u32[]{:S(2)}) %collective-permute-start.9) | collective-permute-done | bytes 327712 | tf_op jit(solution)/shard_map/ppermute | solution.py:54
  134.3 4.5 %fusion.42 = (f32[40,64,128]{2,1,0:T(8,128)S(1)}, f32[40,64,128]{2,1,0:T(8,128)S(1)}) fusion(f32[40]{0:T(128)S(1)} %get-tuple-element.38, pred[]{:T(512)S(6)} %eq.18, f32[40,64,128]{2,1,0:T(8,128)} %collective-permute-done.1, f32[80,64,128]{2,1,0:T(8,128)} %copy-done.4, s32[]{:T(128)S(6)} %select_n.707, bf16[20,64,128]{2,1,0:T(8,128)(2,1)} %copy-done.13, ...), kind=kLoop, calls=%fused_computation.67 | loop fusion | flops 9175040 | bytes 11798085 | tf_op jit(solution)/shard_map/jit(_where)/select_n | solution.py:114
  138.8 1.7 fusion.41
  140.5 0.8 collective-permute-start.10
  141.7 4.1 %fusion.7 = f32[80,64,128]{2,1,0:T(8,128)} fusion(bf16[128,80,64]{0,2,1:T(8,128)(2,1)S(1)} %bitcast.82, f32[80,128]{1,0:T(8,128)S(1)} %copy-done.23, f32[80,128]{1,0:T(8,128)S(1)} %reduce_window_sum.17, f32[128,128]{1,0:T(8,128)S(1)} %fusion.52, pred[128,128]{1,0:T(8,128)(4,1)S(1)} %iota_compare_fusion), kind=kOutput, calls=%fused_computation.23 | convolution fusion | flops 174325760 | bytes 4096000 | tf_op jit(solution)/shard_map/hts,shp->thp/dot_general | solution.py:26
  145.8 4.0 %fusion.8 = f32[80,64,128]{2,1,0:T(8,128)} fusion(bf16[128,80,64]{0,2,1:T(8,128)(2,1)S(1)} %bitcast.84, f32[80,128]{1,0:T(8,128)S(1)} %copy-done.22, f32[80,128]{1,0:T(8,128)S(1)} %reduce_window_sum.18, f32[128,128]{1,0:T(8,128)S(1)} %fusion.49, pred[128,128]{1,0:T(8,128)(4,1)S(1)} %iota_compare_fusion), kind=kOutput, calls=%fused_computation.24 | convolution fusion | flops 174325760 | bytes 4096000 | tf_op jit(solution)/shard_map/hts,shp->thp/dot_general | solution.py:26
  149.9 1.9 maximum_select_fusion
  151.8 5.5 %bitcast_add_fusion.1 = f32[128,80,64]{0,2,1:T(8,128)} fusion(f32[80,64,128]{2,1,0:T(8,128)} %fusion.7, f32[80,64,128]{2,1,0:T(8,128)} %maximum_select_fusion, f32[128,80]{0,1:T(8,128)S(1)} %copy-done.16, bf16[256,5376]{1,0:T(8,128)(2,1)S(1)} %multiply_convert_fusion), kind=kOutput, calls=%fused_computation.29 | convolution fusion | flops 1007943680 | bytes 7938048 | tf_op jit(solution)/shard_map/tn,hpn->thp/dot_general | solution.py:213
  157.3 3.3 %copy.45 = f32[128,5120]{1,0:T(8,128)} copy(f32[128,5120]{0,1:T(8,128)} %bitcast.79) | data formatting | bytes 5242880 | tf_op jit(solution)/shard_map/concatenate | solution.py:217
  160.6 6.5 %bitcast_add_fusion = f32[128,80,64]{0,2,1:T(8,128)} fusion(f32[80,64,128]{2,1,0:T(8,128)} %fusion.8, f32[80,64,128]{2,1,0:T(8,128)} %maximum_select_fusion, f32[80,64,128]{2,1,0:T(8,128)} %copy-done.3, f32[80]{0:T(128)S(1)} %copy-done.29, f32[128,80]{0,1:T(8,128)S(1)} %get-tuple-element.36, f32[80]{0:T(128)S(1)} %copy-done.28, ...), kind=kOutput, calls=%fused_computation.28 | convolution fusion | flops 1009909760 | bytes 10560512 | tf_op jit(solution)/shard_map/tn,hpn->thp/dot_general | solution.py:213
  167.1 3.2 %copy.46 = f32[128,5120]{1,0:T(8,128)} copy(f32[128,5120]{0,1:T(8,128)} %bitcast.80) | data formatting | bytes 5242880 | tf_op jit(solution)/shard_map/concatenate | solution.py:217
  170.3 5.3 %multiply_reduce_fusion = (f32[256]{0:T(256)S(1)}, f32[256,5120]{1,0:T(8,128)S(1)}) fusion(bf16[1,256,5120]{2,1,0:T(8,128)(2,1)} %param.13, bf16[256,5376]{1,0:T(8,128)(2,1)S(1)} %multiply_convert_fusion, f32[5120]{0:T(1024)S(1)} %mul.398, f32[128,5120]{1,0:T(8,128)} %copy.46, f32[128,5120]{1,0:T(8,128)} %copy.45), kind=kLoop, calls=%fused_computation.10 | loop fusion | flops 15728384 | bytes 15750144 | tf_op jit(solution)/shard_map/reduce_sum | solution.py:220
  175.6 2.3 copy-done
  177.9 1.0 convert_reduce_fusion
  178.9 2.4 all-gather.5.cloned.1.call-done
  181.3 2.3 multiply_reduce_fusion.2
  183.6 12.6 %all_to_all.22 = bf16[8,8,256]{2,1,0:T(8,128)(2,1)S(1)} all-to-all(bf16[8,8,256]{2,1,0:T(8,128)(2,1)S(1)} %broadcast_in_dim.156), channel_id=1, replica_groups=mesh['dp'=8,'seq'=32] {'dp'}, dimensions={0} | all-to-all | bytes 65536 | tf_op jit(solution)/shard_map/all_to_all | solution.py:128
  196.2 1.1 broadcast_in_dim.157
  197.2 10.3 %all-to-all-start.3 = ((bf16[32,8,8,256]{3,2,1,0:T(8,128)(2,1)}), bf16[32,8,8,256]{3,2,1,0:T(8,128)(2,1)}, u32[]{:S(2)}, u32[]{:S(2)}) async-start(bf16[32,8,8,256]{3,2,1,0:T(8,128)(2,1)} %broadcast_in_dim.157), calls=%async_computation.3 | async-start | bytes 2097152 | tf_op jit(solution)/shard_map/all_to_all | solution.py:128
  207.5 4.7 %fusion.97 = bf16[1,256,5120]{2,1,0:T(8,128)(2,1)} fusion(f32[5120]{0:T(1024)S(1)} %copy-done.18, f32[256,5120]{1,0:T(8,128)} %copy-done, f32[256]{0:T(256)S(1)} %add_rsqrt_fusion), kind=kLoop, calls=%fused_computation.209 | loop fusion | flops 3932160 | bytes 7885824 | tf_op jit(solution)/shard_map/broadcast_in_dim | solution.py:234
  212.2 12.3 %all-to-all-done.3 = bf16[32,8,8,256]{3,2,1,0:T(8,128)(2,1)} async-done(((bf16[32,8,8,256]{3,2,1,0:T(8,128)(2,1)}), bf16[32,8,8,256]{3,2,1,0:T(8,128)(2,1)}, u32[]{:S(2)}, u32[]{:S(2)}) %all-to-all-start.3) | async-done | bytes 1048608 | tf_op jit(solution)/shard_map/all_to_all | solution.py:128
  224.5 1.6 copy_convert_fusion
  226.4 0.6 multiply_reduce_fusion.1
  227.0 4.2 %fusion.6 = f32[8,4096]{1,0:T(8,128)} fusion(f32[8,256]{1,0:T(8,128)S(1)} %get-tuple-element.61, f32[2048,256]{1,0:T(8,128)S(1)} %copy-done.6, f32[2048,256]{1,0:T(8,128)S(1)} %bitcast.78, f32[4096]{0:T(1024)S(1)} %multiply_reduce_fusion.1, f32[8]{0:T(128)S(1)} %get-tuple-element.40), kind=kOutput, calls=%fused_computation.18 | convolution fusion | flops 101875712 | bytes 4349984 | tf_op jit(solution)/shard_map/dot_general | solution.py:228
  (91 shorter events, 3.5 us)
Async XLA Ops:
  7.2 6.8 %copy-start.19 = (f32[1,80,256]{2,1,0:T(8,128)S(1)}, f32[1,80,256]{2,1,0:T(8,128)}, u32[]{:S(2)}) copy-start(f32[1,80,256]{2,1,0:T(8,128)} %param.17) | copy-start | bytes 245764
  7.2 8.2 %copy-start.20 = (f32[1,80,256]{2,1,0:T(8,128)S(1)}, f32[1,80,256]{2,1,0:T(8,128)}, u32[]{:S(2)}) copy-start(f32[1,80,256]{2,1,0:T(8,128)} %param.16) | copy-start | bytes 245764
  7.2 8.8 %copy-start.17 = (f32[4,5376]{1,0:T(4,128)S(1)}, f32[4,5376]{1,0:T(4,128)}, u32[]{:S(2)}) copy-start(f32[4,5376]{1,0:T(4,128)} %param.18) | copy-start | bytes 258052
  7.2 9.1 %copy-start.1 = (bf16[1,256,5120]{2,1,0:T(8,128)(2,1)S(1)}, bf16[1,256,5120]{2,1,0:T(8,128)(2,1)}, u32[]{:S(2)}) copy-start(bf16[1,256,5120]{2,1,0:T(8,128)(2,1)} %param.12) | copy-start | bytes 7864324
  7.2 9.1 %copy-start.14 = (bf16[1,256,128]{2,1,0:T(8,128)(2,1)S(1)}, bf16[1,256,128]{2,1,0:T(8,128)(2,1)}, u32[]{:S(2)}) copy-start(bf16[1,256,128]{2,1,0:T(8,128)(2,1)} %param.15) | copy-start | bytes 196612
  7.2 9.1 %copy-start.15 = (bf16[1,256,128]{2,1,0:T(8,128)(2,1)S(1)}, bf16[1,256,128]{2,1,0:T(8,128)(2,1)}, u32[]{:S(2)}) copy-start(bf16[1,256,128]{2,1,0:T(8,128)(2,1)} %param.14) | copy-start | bytes 196612
  9.4 6.9 %collective-permute-start = (bf16[3,5376]{1,0:T(4,128)(2,1)S(1)}, bf16[3,5376]{1,0:T(4,128)(2,1)S(1)}, u32[]{:S(2)}, u32[]{:S(2)}) collective-permute-start(bf16[3,5376]{1,0:T(4,128)(2,1)S(1)} %slice.128), channel_id=1, source_target_pairs={{0,1},{1,2},{2,3},{3,4},{4,5},{5,6},{6,7},{7,8},{8,9},{9,10},{10,1... | collective-permute-start | bytes 96776 | tf_op jit(solution)/shard_map/ppermute | solution.py:16
  15.3 18.4 %copy-start.27 = (f32[80]{0:T(128)}, f32[80]{0:T(128)S(1)}, u32[]{:S(2)}) copy-start(f32[80]{0:T(128)S(1)} %get-tuple-element.58) | copy-start | bytes 964
  16.3 2.4 %copy-start.2 = (bf16[1,256,5120]{2,1,0:T(8,128)(2,1)S(1)}, bf16[1,256,5120]{2,1,0:T(8,128)(2,1)}, u32[]{:S(2)}) copy-start(bf16[1,256,5120]{2,1,0:T(8,128)(2,1)} %param.12) | copy-start | bytes 7864324
  16.3 2.4 %copy-start.25 = (f32[5376]{0:T(1024)S(1)}, f32[5376]{0:T(1024)}, u32[]{:S(2)}) copy-start(f32[5376]{0:T(1024)} %param.19) | copy-start | bytes 64516
  29.8 4.0 %copy-start.8 = (bf16[128,5120]{0,1:T(8,128)(2,1)S(1)}, bf16[128,5120]{0,1:T(8,128)(2,1)}, u32[]{:S(2)}) copy-start(bf16[128,5120]{0,1:T(8,128)(2,1)} %copy.40) | copy-start | bytes 3932164
  33.8 1.8 copy-start.3
  35.6 1.9 copy-start.4
  37.5 14.9 %collective-permute-start.1 = (f32[40,64,128]{2,1,0:T(8,128)}, f32[40,64,128]{2,1,0:T(8,128)}, u32[]{:S(2)}, u32[]{:S(2)}) collective-permute-start(f32[40,64,128]{2,1,0:T(8,128)} %constant_dynamic-slice_fusion.6), channel_id=1, source_target_pairs={{0,1},{1,0},{2,3},{3,2},{4,5},{5,4},{6,7},{7,6},{8,9},{9,8},{10,11... | collective-permute-start | bytes 3932168 | tf_op jit(solution)/shard_map/ppermute | solution.py:101
  38.1 14.2 %all-to-all-start = ((f32[32,1,80]{2,1,0:T(1,128)}), f32[32,1,80]{2,1,0:T(1,128)S(1)}, u32[]{:S(2)}, u32[]{:S(2)}) async-start(f32[32,1,80]{2,1,0:T(1,128)} %broadcast_in_dim.149), calls=%async_computation | async-start | bytes 32768 | tf_op jit(solution)/shard_map/all_to_all | solution.py:128
  45.4 106.4 %all-gather.3.cloned.1.call-start = ((), (), s32[]{:S(2)}) async-start(), calls=%async_computation.4 | async-start | bytes 2359296 | tf_op jit(solution)/shard_map/all_gather | solution.py:133
  55.7 15.9 %collective-permute-start.3 = (bf16[40,64,128]{2,1,0:T(8,128)(2,1)}, bf16[40,64,128]{2,1,0:T(8,128)(2,1)S(1)}, u32[]{:S(2)}, u32[]{:S(2)}) collective-permute-start(bf16[40,64,128]{2,1,0:T(8,128)(2,1)} %get-tuple-element.24), channel_id=1, source_target_pairs={{0,6},{1,7},{2,0},{3,1},{4,2},{5,3},{6,4},{7,5},{8,14},{9,15},{10,... | collective-permute-start | bytes 1966088 | tf_op jit(solution)/shard_map/ppermute | solution.py:52
  56.6 17.2 %collective-permute-start.2 = (bf16[40,64,128]{2,1,0:T(8,128)(2,1)}, bf16[40,64,128]{2,1,0:T(8,128)(2,1)}, u32[]{:S(2)}, u32[]{:S(2)}) collective-permute-start(bf16[40,64,128]{2,1,0:T(8,128)(2,1)} %get-tuple-element.24), channel_id=1, source_target_pairs={{0,2},{1,3},{2,4},{3,5},{4,6},{5,7},{6,0},{7,1},{8,10},{9,11},{10,... | collective-permute-start | bytes 1966088 | tf_op jit(solution)/shard_map/ppermute | solution.py:51
  57.2 0.6 copy-start.21
  71.6 15.3 %copy-start.26 = (f32[8,256]{1,0:T(8,128)S(1)}, f32[8,256]{1,0:T(8,128)}, u32[]{:S(2)}) copy-start(f32[8,256]{1,0:T(8,128)} %param.23) | copy-start | bytes 24580
  71.7 7.9 %collective-permute-start.4 = (bf16[20,64,128]{2,1,0:T(8,128)(2,1)S(1)}, bf16[20,64,128]{2,1,0:T(8,128)(2,1)S(1)}, u32[]{:S(2)}, u32[]{:S(2)}) collective-permute-start(bf16[20,64,128]{2,1,0:T(8,128)(2,1)S(1)} %slice.145), channel_id=1, source_target_pairs={{0,6},{1,7},{2,0},{3,1},{4,2},{5,3},{6,4},{7,5},{8,14},{9,15},{10,... | collective-permute-start | bytes 983048 | tf_op jit(solution)/shard_map/ppermute | solution.py:53
  74.8 9.0 %collective-permute-start.5 = (bf16[20,64,128]{2,1,0:T(8,128)(2,1)S(1)}, bf16[20,64,128]{2,1,0:T(8,128)(2,1)S(1)}, u32[]{:S(2)}, u32[]{:S(2)}) collective-permute-start(bf16[20,64,128]{2,1,0:T(8,128)(2,1)S(1)} %slice.146), channel_id=1, source_target_pairs={{0,2},{1,3},{2,4},{3,5},{4,6},{5,7},{6,0},{7,1},{8,10},{9,11},{10,... | collective-permute-start | bytes 983048 | tf_op jit(solution)/shard_map/ppermute | solution.py:54
  79.6 22.4 %copy-start.12 = (bf16[20,64,128]{2,1,0:T(8,128)(2,1)}, bf16[20,64,128]{2,1,0:T(8,128)(2,1)S(1)}, u32[]{:S(2)}) copy-start(bf16[20,64,128]{2,1,0:T(8,128)(2,1)S(1)} %collective-permute-done.4) | copy-start | bytes 983044
  83.7 18.3 %copy-start.13 = (bf16[20,64,128]{2,1,0:T(8,128)(2,1)}, bf16[20,64,128]{2,1,0:T(8,128)(2,1)S(1)}, u32[]{:S(2)}) copy-start(bf16[20,64,128]{2,1,0:T(8,128)(2,1)S(1)} %collective-permute-done.5) | copy-start | bytes 983044
  86.9 38.1 %copy-start.30 = (f32[80]{0:T(128)S(1)}, f32[80]{0:T(128)}, u32[]{:S(2)}) copy-start(f32[80]{0:T(128)} %param.20) | copy-start | bytes 964
  102.0 79.3 %all-gather.5.cloned.1.call-start = ((), (), s32[]{:S(2)}) async-start(), calls=%async_computation.5 | async-start | bytes 2949120 | tf_op jit(solution)/shard_map/all_gather | solution.py:162
  103.5 16.3 %collective-permute-start.7 = (bf16[40,64,128]{2,1,0:T(8,128)(2,1)S(1)}, bf16[40,64,128]{2,1,0:T(8,128)(2,1)S(1)}, u32[]{:S(2)}, u32[]{:S(2)}) collective-permute-start(bf16[40,64,128]{2,1,0:T(8,128)(2,1)S(1)} %convert_element_type.102), channel_id=1, source_target_pairs={{0,24},{1,25},{2,26},{3,27},{4,28},{5,29},{6,30},{7,31},{8,0},{9,1... | collective-permute-start | bytes 1966088 | tf_op jit(solution)/shard_map/ppermute | solution.py:52
  104.3 18.9 %collective-permute-start.6 = (bf16[40,64,128]{2,1,0:T(8,128)(2,1)S(1)}, bf16[40,64,128]{2,1,0:T(8,128)(2,1)S(1)}, u32[]{:S(2)}, u32[]{:S(2)}) collective-permute-start(bf16[40,64,128]{2,1,0:T(8,128)(2,1)S(1)} %convert_element_type.102), channel_id=1, source_target_pairs={{0,8},{1,9},{2,10},{3,11},{4,12},{5,13},{6,14},{7,15},{8,16},{9,17... | collective-permute-start | bytes 1966088 | tf_op jit(solution)/shard_map/ppermute | solution.py:51
  119.8 0.9 copy-start.10
  121.4 8.6 %collective-permute-start.8 = (bf16[20,64,128]{2,1,0:T(8,128)(2,1)}, bf16[20,64,128]{2,1,0:T(8,128)(2,1)}, u32[]{:S(2)}, u32[]{:S(2)}) collective-permute-start(bf16[20,64,128]{2,1,0:T(8,128)(2,1)} %slice.147), channel_id=1, source_target_pairs={{0,24},{1,25},{2,26},{3,27},{4,28},{5,29},{6,30},{7,31},{8,0},{9,1... | collective-permute-start | bytes 983048 | tf_op jit(solution)/shard_map/ppermute | solution.py:53
  123.2 0.8 copy-start.11
  124.8 9.4 %collective-permute-start.9 = (bf16[20,64,128]{2,1,0:T(8,128)(2,1)}, bf16[20,64,128]{2,1,0:T(8,128)(2,1)}, u32[]{:S(2)}, u32[]{:S(2)}) collective-permute-start(bf16[20,64,128]{2,1,0:T(8,128)(2,1)} %slice.148), channel_id=1, source_target_pairs={{0,8},{1,9},{2,10},{3,11},{4,12},{5,13},{6,14},{7,15},{8,16},{9,17... | collective-permute-start | bytes 983048 | tf_op jit(solution)/shard_map/ppermute | solution.py:54
  134.3 4.6 %copy-start.5 = (f32[80,64,128]{2,1,0:T(8,128)S(1)}, f32[80,64,128]{2,1,0:T(8,128)}, u32[]{:S(2)}) copy-start(f32[80,64,128]{2,1,0:T(8,128)} %copy-done.4) | copy-start | bytes 7864324
  138.8 2.8 %copy-start.7 = (bf16[128,5120]{0,1:T(8,128)(2,1)S(1)}, bf16[128,5120]{0,1:T(8,128)(2,1)}, u32[]{:S(2)}) copy-start(bf16[128,5120]{0,1:T(8,128)(2,1)} %copy.39) | copy-start | bytes 3932164
  138.8 2.8 %copy-start.23 = (f32[80,128]{1,0:T(8,128)S(1)}, f32[80,128]{1,0:T(8,128)}, u32[]{:S(2)}) copy-start(f32[80,128]{1,0:T(8,128)} %get-tuple-element.30) | copy-start | bytes 122884
  140.5 9.3 %collective-permute-start.10 = (f32[40,64,128]{2,1,0:T(8,128)S(1)}, f32[40,64,128]{2,1,0:T(8,128)S(1)}, u32[]{:S(2)}, u32[]{:S(2)}) collective-permute-start(f32[40,64,128]{2,1,0:T(8,128)S(1)} %fusion.41), channel_id=1, source_target_pairs={{0,1},{1,0},{2,3},{3,2},{4,5},{5,4},{6,7},{7,6},{8,9},{9,8},{10,11... | collective-permute-start | bytes 3932168 | tf_op jit(solution)/shard_map/ppermute | solution.py:116
  141.6 4.2 %copy-start.9 = (bf16[128,5120]{0,1:T(8,128)(2,1)S(1)}, bf16[128,5120]{0,1:T(8,128)(2,1)}, u32[]{:S(2)}) copy-start(bf16[128,5120]{0,1:T(8,128)(2,1)} %copy.40) | copy-start | bytes 3932164
  141.7 4.2 %copy-start.22 = (f32[80,128]{1,0:T(8,128)S(1)}, f32[80,128]{1,0:T(8,128)}, u32[]{:S(2)}) copy-start(f32[80,128]{1,0:T(8,128)} %get-tuple-element.33) | copy-start | bytes 122884
  149.9 1.9 copy-start.16
  157.3 3.3 %copy-start.28 = (f32[80]{0:T(128)S(1)}, f32[80]{0:T(128)}, u32[]{:S(2)}) copy-start(f32[80]{0:T(128)} %copy-done.27) | copy-start | bytes 964
  157.3 3.3 %copy-start.29 = (f32[80]{0:T(128)S(1)}, f32[80]{0:T(128)}, u32[]{:S(2)}) copy-start(f32[80]{0:T(128)} %get-tuple-element.57) | copy-start | bytes 964
  170.3 7.6 %copy-start.18 = (f32[5120]{0:T(1024)S(1)}, f32[5120]{0:T(1024)}, u32[]{:S(2)}) copy-start(f32[5120]{0:T(1024)} %param.21) | copy-start | bytes 61444
  175.6 2.3 copy-start
  183.6 43.4 %copy-start.24 = (f32[8,256]{1,0:T(8,128)}, f32[8,256]{1,0:T(8,128)S(1)}, u32[]{:S(2)}) copy-start(f32[8,256]{1,0:T(8,128)S(1)} %get-tuple-element.61) | copy-start | bytes 24580
  197.2 27.2 %all-to-all-start.3 = ((bf16[32,8,8,256]{3,2,1,0:T(8,128)(2,1)}), bf16[32,8,8,256]{3,2,1,0:T(8,128)(2,1)}, u32[]{:S(2)}, u32[]{:S(2)}) async-start(bf16[32,8,8,256]{3,2,1,0:T(8,128)(2,1)} %broadcast_in_dim.157), calls=%async_computation.3 | async-start | bytes 2097152 | tf_op jit(solution)/shard_map/all_to_all | solution.py:128
  224.5 1.9 copy-start.6
Sparse Core Ops, SparseCore 0:
  102.1 35.5 all-gather.2
  139.5 41.7 all-gather.4

commit v10 on v8

--- a/solution.py
+++ b/solution.py
@@ -130,10 +130,10 @@
     return lax.all_gather(rows, "dp", axis=0, tiled=True)
 
 
-def codes_everywhere(block):
+def rows_everywhere(block):
     rows = spread_over(block.astype(XFER), "dp")
     got = spread_over(rows, "seq")
-    return jnp.swapaxes(got, 0, 1).reshape((-1,) + block.shape[1:]).astype(jnp.float32)
+    return jnp.swapaxes(got, 0, 1).astype(jnp.float32)
 
 
 def per_device(
@@ -198,10 +198,8 @@
         block_total = cum_list[block][:, -1]
         running = jnp.exp(block_total)[:, None, None] * running + state_list[block]
         before = before + block_total
-    all_prior = prior_everywhere(prior_draw)
     shard_logs = spread_over(before, "seq")
     carry_in = carried_in(running, shard_logs)
-    all_prior, carry_in = lax.optimization_barrier((all_prior, carry_in))
     outputs = []
     for block in range(blocks):
         lower = block * SPAN
@@ -221,7 +219,11 @@
         jnp.bfloat16
     )
     codes_local = jnp.dot(pooled, full_code_weight, preferred_element_type=jnp.float32)
-    all_codes = codes_everywhere(codes_local)
+    local_rows = codes_local.shape[0]
+    code_dim = codes_local.shape[1]
+    both = rows_everywhere(jnp.concatenate([codes_local, prior_draw], axis=0))
+    all_codes = both[:, :, :local_rows].reshape(-1, code_dim)
+    all_prior = both[:, :, local_rows:].reshape(-1, code_dim)
     columns = jnp.concatenate([all_codes, all_prior], axis=0)
     cross = jnp.dot(codes_local, columns.T, precision=lax.Precision.HIGHEST)
     row_sq = jnp.sum(codes_local * codes_local, axis=1)

time: 226 us -> 222 us (0.982)
  waiting for transfers between devices: 57.5 us -> 68.1 us
  starting transfers between devices: 36.4 us -> 28.6 us
  matrix products: 32.5 us -> 28.9 us
    all_to_all x3 -> x2, waiting for transfers between devices: 19.1 us -> 30.5 us  [spread_over(): lax.all_to_all(jnp.broadcast_to(block[None], (count,) + block.shape), axi...]
    all_to_all x3 -> x2, starting transfers between devices: 20.1 us -> 13.4 us  [spread_over(): lax.all_to_all(jnp.broadcast_to(block[None], (count,) + block.shape), axi...]
    unnamed x70 -> x72, local copies, waits for them, and re-layouts: 5.84 us -> 4.88 us
  transfers between devices with their start and end apart: 16 -> 14, of which waited for: 7 -> 7; matrix products, arithmetic and copies ran while one was open for 37% -> 23% of each run, Pallas kernels for 0% -> 0%
where the time goes in v10:
time: 222 us; the launch traced here: 221 us
  waiting for transfers between devices  68.1 us (31%)
  other arithmetic  38.4 us (17%)
  matrix products  28.9 us (13%)
  starting transfers between devices  28.6 us (13%)
  local copies, waits for them, and re-layouts  27.2 us (12%)
  blocking collectives  15.2 us (7%)
  between operations  14.8 us (7%)
    all_to_all x2, waiting for transfers between devices, spread_over(): lax.all_to_all(jnp.broadcast_to(block[None], (count,) + block.shape), axi...  30.5 us
    ppermute x2, waiting for transfers between devices, ring_of_four(): next_state = lax.ppermute(sent, 'seq', bwd)  26 us
    all_to_all x1, blocking collectives, spread_over(): lax.all_to_all(jnp.broadcast_to(block[None], (count,) + block.shape), axi...  15.2 us
    all_to_all x2, starting transfers between devices, spread_over(): lax.all_to_all(jnp.broadcast_to(block[None], (count,) + block.shape), axi...  13.4 us
    dot_general x2, matrix products, per_device(): jnp.einsum('tn,hpn->thp', read_block, start, precision=lax.Precision.HIGH...  10.5 us
    ppermute x2, waiting for transfers between devices, ring_of_four(): far_b = lax.ppermute(prev_state[half:], 'seq', fwd)  8.26 us
    slice x3, local copies, waits for them, and re-layouts, per_device(): values[lower:upper]  6.69 us
    concatenate x2, local copies, waits for them, and re-layouts, per_device(): ssd_out = jnp.concatenate(outputs, axis=0)  6.51 us
  transfers between devices with their start and end apart: 14, of which 7 were waited for; matrix products, arithmetic and copies ran while one was open for 23% of the time, Pallas kernels for 0%

profile of v10, /device:TPU:1, one launch (start us, length us, event | category | flops | bytes accessed | tf_op | source)
XLA Modules:
  0.0 221.3 jit_solution(15984802298255015569)
XLA Ops:
  7.2 2.1 pad_maximum_fusion.2
  9.4 4.6 %collective-permute-start = (bf16[3,5376]{1,0:T(4,128)(2,1)S(1)}, bf16[3,5376]{1,0:T(4,128)(2,1)S(1)}, u32[]{:S(2)}, u32[]{:S(2)}) collective-permute-start(bf16[3,5376]{1,0:T(4,128)(2,1)S(1)} %slice.136), channel_id=1, source_target_pairs={{0,1},{1,2},{2,3},{3,4},{4,5},{5,6},{6,7},{7,8},{8,9},{9,10},{10,1... | collective-permute-start | bytes 96776 | tf_op jit(solution)/shard_map/ppermute | solution.py:16
  14.8 0.5 fusion.110
  15.3 0.7 fusion.108
  16.3 2.4 %maximum_maximum_fusion = bf16[259,5376]{1,0:T(8,128)(2,1)S(1)} fusion(bf16[256,128]{1,0:T(8,128)(2,1)S(1)} %bitcast.87, bf16[256,128]{1,0:T(8,128)(2,1)S(1)} %bitcast.90, bf16[256,5120]{1,0:T(8,128)(2,1)S(1)} %bitcast.74, bf16[3,5376]{1,0:T(4,128)(2,1)S(1)} %collective-permute-done), kind=kLoop, calls=%fused_computation.22 | loop fusion | flops 11139072 | bytes 5569536 | tf_op jit(solution)/shard_map/concatenate | solution.py:162
  18.7 4.4 %multiply_convert_fusion = bf16[256,5376]{1,0:T(8,128)(2,1)S(1)} fusion(bf16[259,5376]{1,0:T(8,128)(2,1)S(1)} %maximum_maximum_fusion, f32[5376]{0:T(1024)S(1)} %get-tuple-element.5, f32[5376]{0:T(1024)S(1)} %get-tuple-element.6, f32[5376]{0:T(1024)S(1)} %get-tuple-element.4, f32[5376]{0:T(1024)S(1)} %get-tuple-element.3, f32[5376]{0:T(1024)S(1)} %copy-done.26, ...), kind=kLoop, calls=%fused_computation.2 | loop fusion | flops 30277632 | bytes 13870080 | tf_op jit(solution)/shard_map/convert_element_type | solution.py:168
  23.1 1.8 fusion.107
  25.0 2.4 %copy.31 = bf16[128,5120]{0,1:T(8,128)(2,1)} copy(bf16[128,5120]{1,0:T(8,128)(2,1)} %get-tuple-element.22) | data formatting | bytes 2621440 | tf_op jit(solution)/shard_map/slice | solution.py:182
  27.4 2.4 %copy.32 = bf16[128,5120]{0,1:T(8,128)(2,1)} copy(bf16[128,5120]{1,0:T(8,128)(2,1)} %get-tuple-element.23) | data formatting | bytes 2621440 | tf_op jit(solution)/shard_map/slice | solution.py:182
  29.9 3.9 %fusion.9 = f32[80,64,128]{2,1,0:T(8,128)S(1)} fusion(bf16[128,80,64]{0,2,1:T(8,128)(2,1)} %bitcast.82, f32[128,128]{1,0:T(8,128)S(1)} %get-tuple-element.21, f32[80,128]{1,0:T(8,128)S(1)} %get-tuple-element.25), kind=kOutput, calls=%fused_computation.26 | convolution fusion | flops 170393600 | bytes 4038656 | tf_op jit(solution)/shard_map/hsn,shp->hpn/dot_general | solution.py:29
  33.8 1.8 multiply_add_fusion
  35.6 1.2 constant_dynamic-slice_fusion.2
  36.8 0.7 copy-done.4
  37.5 0.6 broadcast_in_dim.143
  38.1 7.3 %all-to-all-start = ((f32[32,1,80]{2,1,0:T(1,128)}), f32[32,1,80]{2,1,0:T(1,128)S(1)}, u32[]{:S(2)}, u32[]{:S(2)}) async-start(f32[32,1,80]{2,1,0:T(1,128)} %broadcast_in_dim.143), calls=%async_computation | async-start | bytes 32768 | tf_op jit(solution)/shard_map/all_to_all | solution.py:125
  45.6 6.8 %all-to-all-done = f32[32,1,80]{2,1,0:T(1,128)S(1)} async-done(((f32[32,1,80]{2,1,0:T(1,128)}), f32[32,1,80]{2,1,0:T(1,128)S(1)}, u32[]{:S(2)}, u32[]{:S(2)}) %all-to-all-start) | async-done | bytes 10272 | tf_op jit(solution)/shard_map/all_to_all | solution.py:125
  52.3 0.7 exponential_bitcast_fusion.7
  53.0 3.4 %fusion.105 = (bf16[40,64,128]{2,1,0:T(8,128)(2,1)}, f32[40,64,128]{2,1,0:T(8,128)}) fusion(f32[40,64,128]{2,1,0:T(8,128)} %collective-permute-done.1, f32[80,64,128]{2,1,0:T(8,128)} %copy-done.4, s32[]{:T(128)S(6)} %select_n.708, pred[]{:T(512)S(6)} %eq.18, f32[40]{0:T(128)S(1)} %get-tuple-element.32), kind=kLoop, calls=%fused_computation.216 | loop fusion | flops 1638400 | bytes 4587685 | tf_op jit(solution)/shard_map/convert_element_type | solution.py:50
  56.4 0.9 collective-permute-start.3
  57.3 0.6 collective-permute-start.2
  57.9 0.7 exponential_bitcast_fusion.2
  58.6 13.8 %collective-permute-done.3 = bf16[40,64,128]{2,1,0:T(8,128)(2,1)S(1)} collective-permute-done((bf16[40,64,128]{2,1,0:T(8,128)(2,1)}, bf16[40,64,128]{2,1,0:T(8,128)(2,1)S(1)}, u32[]{:S(2)}, u32[]{:S(2)}) %collective-permute-start.3) | collective-permute-done | bytes 655392 | tf_op jit(solution)/shard_map/ppermute | solution.py:52
  72.4 2.1 collective-permute-start.4
  74.5 1.0 slice.154
  75.7 0.6 exponential_bitcast_fusion.5
  76.3 0.6 exponential_bitcast_fusion.6
  77.0 3.3 %collective-permute-done.4 = bf16[20,64,128]{2,1,0:T(8,128)(2,1)S(1)} collective-permute-done((bf16[20,64,128]{2,1,0:T(8,128)(2,1)S(1)}, bf16[20,64,128]{2,1,0:T(8,128)(2,1)S(1)}, u32[]{:S(2)}, u32[]{:S(2)}) %collective-permute-start.4) | collective-permute-done | bytes 327712 | tf_op jit(solution)/shard_map/ppermute | solution.py:53
  80.3 4.1 %collective-permute-done.5 = bf16[20,64,128]{2,1,0:T(8,128)(2,1)S(1)} collective-permute-done((bf16[20,64,128]{2,1,0:T(8,128)(2,1)S(1)}, bf16[20,64,128]{2,1,0:T(8,128)(2,1)S(1)}, u32[]{:S(2)}, u32[]{:S(2)}) %collective-permute-start.5) | collective-permute-done | bytes 327712 | tf_op jit(solution)/shard_map/ppermute | solution.py:54
  84.4 2.3 %fusion.43 = bf16[40,64,128]{2,1,0:T(8,128)(2,1)S(1)} fusion(bf16[40,64,128]{2,1,0:T(8,128)(2,1)S(1)} %collective-permute-done.3, bf16[40,64,128]{2,1,0:T(8,128)(2,1)} %collective-permute-done.2, f32[40,64,128]{2,1,0:T(8,128)} %get-tuple-element.17, f32[40]{0:T(128)S(1)} %get-tuple-element.48, f32[40]{0:T(128)S(1)} %get-tuple-element.50, ...), kind=kLoop, calls=%fused_computation.69 | loop fusion | flops 3932160 | bytes 3932800 | tf_op jit(solution)/shard_map/convert_element_type | solution.py:50
  86.7 1.0 collective-permute-start.7
  87.7 0.6 collective-permute-start.6
  88.3 12.2 %collective-permute-done.7 = bf16[40,64,128]{2,1,0:T(8,128)(2,1)S(1)} collective-permute-done((bf16[40,64,128]{2,1,0:T(8,128)(2,1)S(1)}, bf16[40,64,128]{2,1,0:T(8,128)(2,1)S(1)}, u32[]{:S(2)}, u32[]{:S(2)}) %collective-permute-start.7) | collective-permute-done | bytes 655392 | tf_op jit(solution)/shard_map/ppermute | solution.py:52
  100.5 0.9 copy-done.11
  101.3 0.8 slice.155
  102.1 2.1 collective-permute-start.8
  104.2 0.9 copy-done.12
  105.0 0.7 slice.156
  106.1 0.7 mul.397
  106.8 0.8 mul.398
  107.6 0.7 convert.10
  108.3 0.8 dynamic-slice_reduce_fusion
  109.2 4.1 %collective-permute-done.9 = bf16[20,64,128]{2,1,0:T(8,128)(2,1)} collective-permute-done((bf16[20,64,128]{2,1,0:T(8,128)(2,1)}, bf16[20,64,128]{2,1,0:T(8,128)(2,1)}, u32[]{:S(2)}, u32[]{:S(2)}) %collective-permute-start.9) | collective-permute-done | bytes 327712 | tf_op jit(solution)/shard_map/ppermute | solution.py:54
  113.3 4.4 %fusion.42 = (f32[40,64,128]{2,1,0:T(8,128)S(1)}, f32[40,64,128]{2,1,0:T(8,128)S(1)}) fusion(f32[40]{0:T(128)} %get-tuple-element.33, pred[]{:T(512)S(6)} %eq.18, f32[40,64,128]{2,1,0:T(8,128)} %collective-permute-done.1, f32[80,64,128]{2,1,0:T(8,128)} %copy-done.4, s32[]{:T(128)S(6)} %select_n.708, f32[40]{0:T(128)} %get-tuple-element.47, ...), kind=kLoop, calls=%fused_computation.68 | loop fusion | flops 11468800 | bytes 10488005 | tf_op jit(solution)/shard_map/jit(_where)/select_n | solution.py:112
  117.8 2.1 fusion.41
  119.9 3.0 %collective-permute-start.10 = (f32[40,64,128]{2,1,0:T(8,128)S(1)}, f32[40,64,128]{2,1,0:T(8,128)S(1)}, u32[]{:S(2)}, u32[]{:S(2)}) collective-permute-start(f32[40,64,128]{2,1,0:T(8,128)S(1)} %fusion.41), channel_id=1, source_target_pairs={{0,1},{1,0},{2,3},{3,2},{4,5},{5,4},{6,7},{7,6},{8,9},{9,8},{10,11... | collective-permute-start | bytes 3932168 | tf_op jit(solution)/shard_map/ppermute | solution.py:114
  123.2 2.0 fusion.7
  125.2 4.1 %fusion.8 = f32[80,64,128]{2,1,0:T(8,128)} fusion(bf16[128,80,64]{0,2,1:T(8,128)(2,1)S(1)} %bitcast.85, f32[80,128]{1,0:T(8,128)S(1)} %copy-done.23, f32[80,128]{1,0:T(8,128)S(1)} %reduce_window_sum.18, f32[128,128]{1,0:T(8,128)S(1)} %fusion.52, pred[128,128]{1,0:T(8,128)(4,1)S(1)} %iota_compare_fusion), kind=kOutput, calls=%fused_computation.25 | convolution fusion | flops 174325760 | bytes 4096000 | tf_op jit(solution)/shard_map/hts,shp->thp/dot_general | solution.py:26
  129.3 3.0 %bitcast_add_fusion.1 = f32[128,80,64]{0,2,1:T(8,128)} fusion(f32[80,64,128]{2,1,0:T(8,128)S(1)} %fusion.7, f32[40,64,128]{2,1,0:T(8,128)S(1)} %collective-permute-done.10, f32[40,64,128]{2,1,0:T(8,128)S(1)} %get-tuple-element.9, f32[128,80]{0,1:T(8,128)S(1)} %copy-done.17, pred[]{:T(512)S(6)} %eq.18, bf16[256,5376]{1,0:T(8,128)(2,1)S(1)} %multiply_convert_fusion), kind=kOutput, calls=%fused_computation.30 | convolution fusion | flops 1009909760 | bytes 7938049 | tf_op jit(solution)/shard_map/tn,hpn->thp/dot_general | solution.py:209
  132.3 3.3 %copy.37 = f32[128,5120]{1,0:T(8,128)} copy(f32[128,5120]{0,1:T(8,128)} %bitcast.80) | data formatting | bytes 5242880 | tf_op jit(solution)/shard_map/concatenate | solution.py:213
  135.6 7.5 %bitcast_add_fusion = f32[128,80,64]{0,2,1:T(8,128)} fusion(f32[80,64,128]{2,1,0:T(8,128)} %fusion.8, f32[80,64,128]{2,1,0:T(8,128)} %copy-done.3, f32[40,64,128]{2,1,0:T(8,128)} %copy-done.7, f32[40,64,128]{2,1,0:T(8,128)} %copy-done.6, f32[80]{0:T(128)S(1)} %copy-done.34, f32[128,80]{0,1:T(8,128)S(1)} %get-tuple-element.30, f32[80]{0:T(128)S(1)} %copy-done.33, ...), kind=kOutput, calls=%fused_computation.29 | convolution fusion | flops 1011875840 | bytes 10560513 | tf_op jit(solution)/shard_map/tn,hpn->thp/dot_general | solution.py:209
  143.1 3.2 %copy.38 = f32[128,5120]{1,0:T(8,128)} copy(f32[128,5120]{0,1:T(8,128)} %bitcast.81) | data formatting | bytes 5242880 | tf_op jit(solution)/shard_map/concatenate | solution.py:213
  146.3 5.2 %multiply_reduce_fusion = (f32[256]{0:T(256)S(1)}, f32[256,5120]{1,0:T(8,128)S(1)}) fusion(bf16[1,256,5120]{2,1,0:T(8,128)(2,1)} %param.13, bf16[256,5376]{1,0:T(8,128)(2,1)S(1)} %multiply_convert_fusion, f32[5120]{0:T(1024)S(1)} %mul.398, f32[128,5120]{1,0:T(8,128)} %copy.38, f32[128,5120]{1,0:T(8,128)} %copy.37), kind=kLoop, calls=%fused_computation.10 | loop fusion | flops 15728384 | bytes 15750144 | tf_op jit(solution)/shard_map/reduce_sum | solution.py:216
  151.6 2.3 %copy-done = f32[256,5120]{1,0:T(8,128)} copy-done((f32[256,5120]{1,0:T(8,128)}, f32[256,5120]{1,0:T(8,128)S(1)}, u32[]{:S(2)}) %copy-start) | copy-done | bytes 5242904
  153.9 1.0 convert_reduce_fusion
  154.9 2.3 %multiply_reduce_fusion.2 = (f32[8]{0:T(128)S(1)}, bf16[8,256]{1,0:T(8,128)(2,1)S(1)}, f32[8,256]{1,0:T(8,128)S(1)}) fusion(bf16[5120,256]{1,0:T(8,128)(2,1)} %all-gather.2.cloned.1.call-done, f32[8,5120]{1,0:T(8,128)S(1)} %convert_reduce_fusion), kind=kOutput, calls=%fused_computation.104 | convolution fusion | flops 21059576 | bytes 2797600 | tf_op jit(solution)/shard_map/dot_general | solution.py:221
  157.2 15.2 %all_to_all.16 = bf16[8,16,256]{2,1,0:T(8,128)(2,1)S(1)} all-to-all(bf16[8,16,256]{2,1,0:T(8,128)(2,1)S(1)} %broadcast_in_dim.149), channel_id=1, replica_groups=mesh['dp'=8,'seq'=32] {'dp'}, dimensions={0} | all-to-all | bytes 131072 | tf_op jit(solution)/shard_map/all_to_all | solution.py:125
  172.4 1.6 broadcast_in_dim.150
  174.0 6.2 %all-to-all-start.2 = ((bf16[32,8,16,256]{3,2,1,0:T(8,128)(2,1)}), bf16[32,8,16,256]{3,2,1,0:T(8,128)(2,1)S(1)}, u32[]{:S(2)}, u32[]{:S(2)}) async-start(bf16[32,8,16,256]{3,2,1,0:T(8,128)(2,1)} %broadcast_in_dim.150), calls=%async_computation.2 | async-start | bytes 4194304 | tf_op jit(solution)/shard_map/all_to_all | solution.py:125
  180.2 4.7 %fusion.102 = bf16[1,256,5120]{2,1,0:T(8,128)(2,1)} fusion(f32[5120]{0:T(1024)S(1)} %copy-done.19, f32[256,5120]{1,0:T(8,128)} %copy-done, f32[256]{0:T(256)S(1)} %add_rsqrt_fusion), kind=kLoop, calls=%fused_computation.215 | loop fusion | flops 3932160 | bytes 7885824 | tf_op jit(solution)/shard_map/broadcast_in_dim | solution.py:234
  184.8 23.7 %all-to-all-done.2 = bf16[32,8,16,256]{3,2,1,0:T(8,128)(2,1)S(1)} async-done(((bf16[32,8,16,256]{3,2,1,0:T(8,128)(2,1)}), bf16[32,8,16,256]{3,2,1,0:T(8,128)(2,1)S(1)}, u32[]{:S(2)}, u32[]{:S(2)}) %all-to-all-start.2) | async-done | bytes 2097184 | tf_op jit(solution)/shard_map/all_to_all | solution.py:125
  208.6 0.6 convert_bitcast_fusion
  209.2 0.5 fusion.106
  209.7 0.6 multiply_reduce_fusion.1
  210.3 4.2 %fusion.6 = f32[8,4096]{1,0:T(8,128)} fusion(f32[8,256]{1,0:T(8,128)S(1)} %get-tuple-element.55, f32[2048,256]{1,0:T(8,128)S(1)} %bitcast.79, f32[2048,256]{1,0:T(8,128)S(1)} %bitcast.77, f32[4096]{0:T(1024)S(1)} %multiply_reduce_fusion.1, f32[8]{0:T(128)S(1)} %get-tuple-element.34), kind=kOutput, calls=%fused_computation.18 | convolution fusion | flops 101875712 | bytes 4349984 | tf_op jit(solution)/shard_map/dot_general | solution.py:228
  (97 shorter events, 2.1 us)
Async XLA Ops:
  7.2 6.8 %copy-start.20 = (f32[1,80,256]{2,1,0:T(8,128)S(1)}, f32[1,80,256]{2,1,0:T(8,128)}, u32[]{:S(2)}) copy-start(f32[1,80,256]{2,1,0:T(8,128)} %param.17) | copy-start | bytes 245764
  7.2 8.2 %copy-start.21 = (f32[1,80,256]{2,1,0:T(8,128)S(1)}, f32[1,80,256]{2,1,0:T(8,128)}, u32[]{:S(2)}) copy-start(f32[1,80,256]{2,1,0:T(8,128)} %param.16) | copy-start | bytes 245764
  7.2 8.8 %copy-start.18 = (f32[4,5376]{1,0:T(4,128)S(1)}, f32[4,5376]{1,0:T(4,128)}, u32[]{:S(2)}) copy-start(f32[4,5376]{1,0:T(4,128)} %param.18) | copy-start | bytes 258052
  7.2 9.1 %copy-start.1 = (bf16[1,256,5120]{2,1,0:T(8,128)(2,1)S(1)}, bf16[1,256,5120]{2,1,0:T(8,128)(2,1)}, u32[]{:S(2)}) copy-start(bf16[1,256,5120]{2,1,0:T(8,128)(2,1)} %param.12) | copy-start | bytes 7864324
  7.2 9.1 %copy-start.15 = (bf16[1,256,128]{2,1,0:T(8,128)(2,1)S(1)}, bf16[1,256,128]{2,1,0:T(8,128)(2,1)}, u32[]{:S(2)}) copy-start(bf16[1,256,128]{2,1,0:T(8,128)(2,1)} %param.15) | copy-start | bytes 196612
  7.2 9.1 %copy-start.16 = (bf16[1,256,128]{2,1,0:T(8,128)(2,1)S(1)}, bf16[1,256,128]{2,1,0:T(8,128)(2,1)}, u32[]{:S(2)}) copy-start(bf16[1,256,128]{2,1,0:T(8,128)(2,1)} %param.14) | copy-start | bytes 196612
  9.4 6.9 %collective-permute-start = (bf16[3,5376]{1,0:T(4,128)(2,1)S(1)}, bf16[3,5376]{1,0:T(4,128)(2,1)S(1)}, u32[]{:S(2)}, u32[]{:S(2)}) collective-permute-start(bf16[3,5376]{1,0:T(4,128)(2,1)S(1)} %slice.136), channel_id=1, source_target_pairs={{0,1},{1,2},{2,3},{3,4},{4,5},{5,6},{6,7},{7,8},{8,9},{9,10},{10,1... | collective-permute-start | bytes 96776 | tf_op jit(solution)/shard_map/ppermute | solution.py:16
  15.3 18.5 %copy-start.32 = (f32[80]{0:T(128)}, f32[80]{0:T(128)S(1)}, u32[]{:S(2)}) copy-start(f32[80]{0:T(128)S(1)} %get-tuple-element.52) | copy-start | bytes 964
  16.3 2.4 %copy-start.2 = (bf16[1,256,5120]{2,1,0:T(8,128)(2,1)S(1)}, bf16[1,256,5120]{2,1,0:T(8,128)(2,1)}, u32[]{:S(2)}) copy-start(bf16[1,256,5120]{2,1,0:T(8,128)(2,1)} %param.12) | copy-start | bytes 7864324
  16.3 2.4 %copy-start.26 = (f32[5376]{0:T(1024)S(1)}, f32[5376]{0:T(1024)}, u32[]{:S(2)}) copy-start(f32[5376]{0:T(1024)} %param.19) | copy-start | bytes 64516
  29.9 4.0 %copy-start.9 = (bf16[128,5120]{0,1:T(8,128)(2,1)S(1)}, bf16[128,5120]{0,1:T(8,128)(2,1)}, u32[]{:S(2)}) copy-start(bf16[128,5120]{0,1:T(8,128)(2,1)} %copy.32) | copy-start | bytes 3932164
  33.8 1.8 copy-start.3
  35.6 1.9 copy-start.4
  37.5 15.5 %collective-permute-start.1 = (f32[40,64,128]{2,1,0:T(8,128)}, f32[40,64,128]{2,1,0:T(8,128)}, u32[]{:S(2)}, u32[]{:S(2)}) collective-permute-start(f32[40,64,128]{2,1,0:T(8,128)} %constant_dynamic-slice_fusion.2), channel_id=1, source_target_pairs={{0,1},{1,0},{2,3},{3,2},{4,5},{5,4},{6,7},{7,6},{8,9},{9,8},{10,11... | collective-permute-start | bytes 3932168 | tf_op jit(solution)/shard_map/ppermute | solution.py:101
  38.1 14.2 %all-to-all-start = ((f32[32,1,80]{2,1,0:T(1,128)}), f32[32,1,80]{2,1,0:T(1,128)S(1)}, u32[]{:S(2)}, u32[]{:S(2)}) async-start(f32[32,1,80]{2,1,0:T(1,128)} %broadcast_in_dim.143), calls=%async_computation | async-start | bytes 32768 | tf_op jit(solution)/shard_map/all_to_all | solution.py:125
  45.4 109.4 %all-gather.2.cloned.1.call-start = ((), (), s32[]{:S(2)}) async-start(), calls=%async_computation.3 | async-start | bytes 2949120 | tf_op jit(solution)/shard_map/all_gather | solution.py:159
  56.4 15.9 %collective-permute-start.3 = (bf16[40,64,128]{2,1,0:T(8,128)(2,1)}, bf16[40,64,128]{2,1,0:T(8,128)(2,1)S(1)}, u32[]{:S(2)}, u32[]{:S(2)}) collective-permute-start(bf16[40,64,128]{2,1,0:T(8,128)(2,1)} %get-tuple-element.16), channel_id=1, source_target_pairs={{0,6},{1,7},{2,0},{3,1},{4,2},{5,3},{6,4},{7,5},{8,14},{9,15},{10,... | collective-permute-start | bytes 1966088 | tf_op jit(solution)/shard_map/ppermute | solution.py:52
  57.3 17.2 %collective-permute-start.2 = (bf16[40,64,128]{2,1,0:T(8,128)(2,1)}, bf16[40,64,128]{2,1,0:T(8,128)(2,1)}, u32[]{:S(2)}, u32[]{:S(2)}) collective-permute-start(bf16[40,64,128]{2,1,0:T(8,128)(2,1)} %get-tuple-element.16), channel_id=1, source_target_pairs={{0,2},{1,3},{2,4},{3,5},{4,6},{5,7},{6,0},{7,1},{8,10},{9,11},{10,... | collective-permute-start | bytes 1966088 | tf_op jit(solution)/shard_map/ppermute | solution.py:51
  57.9 0.7 copy-start.22
  72.4 7.9 %collective-permute-start.4 = (bf16[20,64,128]{2,1,0:T(8,128)(2,1)S(1)}, bf16[20,64,128]{2,1,0:T(8,128)(2,1)S(1)}, u32[]{:S(2)}, u32[]{:S(2)}) collective-permute-start(bf16[20,64,128]{2,1,0:T(8,128)(2,1)S(1)} %slice.153), channel_id=1, source_target_pairs={{0,6},{1,7},{2,0},{3,1},{4,2},{5,3},{6,4},{7,5},{8,14},{9,15},{10,... | collective-permute-start | bytes 983048 | tf_op jit(solution)/shard_map/ppermute | solution.py:53
  75.5 9.0 %collective-permute-start.5 = (bf16[20,64,128]{2,1,0:T(8,128)(2,1)S(1)}, bf16[20,64,128]{2,1,0:T(8,128)(2,1)S(1)}, u32[]{:S(2)}, u32[]{:S(2)}) collective-permute-start(bf16[20,64,128]{2,1,0:T(8,128)(2,1)S(1)} %slice.154), channel_id=1, source_target_pairs={{0,2},{1,3},{2,4},{3,5},{4,6},{5,7},{6,0},{7,1},{8,10},{9,11},{10,... | collective-permute-start | bytes 983048 | tf_op jit(solution)/shard_map/ppermute | solution.py:54
  76.3 29.4 %copy-start.28 = (f32[40]{0:T(128)}, f32[40]{0:T(128)S(1)}, u32[]{:S(2)}) copy-start(f32[40]{0:T(128)S(1)} %get-tuple-element.41) | copy-start | bytes 484
  76.3 29.4 %copy-start.29 = (f32[40]{0:T(128)}, f32[40]{0:T(128)S(1)}, u32[]{:S(2)}) copy-start(f32[40]{0:T(128)S(1)} %get-tuple-element.50) | copy-start | bytes 484
  77.0 28.8 %copy-start.30 = (f32[40]{0:T(128)}, f32[40]{0:T(128)S(1)}, u32[]{:S(2)}) copy-start(f32[40]{0:T(128)S(1)} %get-tuple-element.39) | copy-start | bytes 484
  77.0 28.8 %copy-start.31 = (f32[40]{0:T(128)}, f32[40]{0:T(128)S(1)}, u32[]{:S(2)}) copy-start(f32[40]{0:T(128)S(1)} %get-tuple-element.48) | copy-start | bytes 484
  80.3 25.5 %copy-start.13 = (bf16[20,64,128]{2,1,0:T(8,128)(2,1)}, bf16[20,64,128]{2,1,0:T(8,128)(2,1)S(1)}, u32[]{:S(2)}) copy-start(bf16[20,64,128]{2,1,0:T(8,128)(2,1)S(1)} %collective-permute-done.4) | copy-start | bytes 983044
  84.4 21.4 %copy-start.14 = (bf16[20,64,128]{2,1,0:T(8,128)(2,1)}, bf16[20,64,128]{2,1,0:T(8,128)(2,1)S(1)}, u32[]{:S(2)}) copy-start(bf16[20,64,128]{2,1,0:T(8,128)(2,1)S(1)} %collective-permute-done.5) | copy-start | bytes 983044
  84.4 21.6 %copy-start.35 = (f32[80]{0:T(128)S(1)}, f32[80]{0:T(128)}, u32[]{:S(2)}) copy-start(f32[80]{0:T(128)} %param.20) | copy-start | bytes 964
  86.7 13.7 %collective-permute-start.7 = (bf16[40,64,128]{2,1,0:T(8,128)(2,1)S(1)}, bf16[40,64,128]{2,1,0:T(8,128)(2,1)S(1)}, u32[]{:S(2)}, u32[]{:S(2)}) collective-permute-start(bf16[40,64,128]{2,1,0:T(8,128)(2,1)S(1)} %fusion.43), channel_id=1, source_target_pairs={{0,24},{1,25},{2,26},{3,27},{4,28},{5,29},{6,30},{7,31},{8,0},{9,1... | collective-permute-start | bytes 1966088 | tf_op jit(solution)/shard_map/ppermute | solution.py:52
  87.7 16.5 %collective-permute-start.6 = (bf16[40,64,128]{2,1,0:T(8,128)(2,1)S(1)}, bf16[40,64,128]{2,1,0:T(8,128)(2,1)S(1)}, u32[]{:S(2)}, u32[]{:S(2)}) collective-permute-start(bf16[40,64,128]{2,1,0:T(8,128)(2,1)S(1)} %fusion.43), channel_id=1, source_target_pairs={{0,8},{1,9},{2,10},{3,11},{4,12},{5,13},{6,14},{7,15},{8,16},{9,17... | collective-permute-start | bytes 1966088 | tf_op jit(solution)/shard_map/ppermute | solution.py:51
  100.5 0.9 copy-start.11
  102.1 7.1 %collective-permute-start.8 = (bf16[20,64,128]{2,1,0:T(8,128)(2,1)}, bf16[20,64,128]{2,1,0:T(8,128)(2,1)}, u32[]{:S(2)}, u32[]{:S(2)}) collective-permute-start(bf16[20,64,128]{2,1,0:T(8,128)(2,1)} %slice.155), channel_id=1, source_target_pairs={{0,24},{1,25},{2,26},{3,27},{4,28},{5,29},{6,30},{7,31},{8,0},{9,1... | collective-permute-start | bytes 983048 | tf_op jit(solution)/shard_map/ppermute | solution.py:53
  104.2 0.9 copy-start.12
  105.8 7.5 %collective-permute-start.9 = (bf16[20,64,128]{2,1,0:T(8,128)(2,1)}, bf16[20,64,128]{2,1,0:T(8,128)(2,1)}, u32[]{:S(2)}, u32[]{:S(2)}) collective-permute-start(bf16[20,64,128]{2,1,0:T(8,128)(2,1)} %slice.156), channel_id=1, source_target_pairs={{0,8},{1,9},{2,10},{3,11},{4,12},{5,13},{6,14},{7,15},{8,16},{9,17... | collective-permute-start | bytes 983048 | tf_op jit(solution)/shard_map/ppermute | solution.py:54
  113.3 4.4 %copy-start.5 = (f32[80,64,128]{2,1,0:T(8,128)S(1)}, f32[80,64,128]{2,1,0:T(8,128)}, u32[]{:S(2)}) copy-start(f32[80,64,128]{2,1,0:T(8,128)} %copy-done.4) | copy-start | bytes 7864324
  113.3 4.4 %copy-start.27 = (f32[40]{0:T(128)S(1)}, f32[40]{0:T(128)}, u32[]{:S(2)}) copy-start(f32[40]{0:T(128)} %get-tuple-element.33) | copy-start | bytes 484
  117.7 11.6 %copy-start.6 = (f32[40,64,128]{2,1,0:T(8,128)}, f32[40,64,128]{2,1,0:T(8,128)S(1)}, u32[]{:S(2)}) copy-start(f32[40,64,128]{2,1,0:T(8,128)S(1)} %get-tuple-element.9) | copy-start | bytes 3932164
  117.8 5.4 %copy-start.8 = (bf16[128,5120]{0,1:T(8,128)(2,1)S(1)}, bf16[128,5120]{0,1:T(8,128)(2,1)}, u32[]{:S(2)}) copy-start(bf16[128,5120]{0,1:T(8,128)(2,1)} %copy.31) | copy-start | bytes 3932164
  117.8 5.4 %copy-start.24 = (f32[80,128]{1,0:T(8,128)S(1)}, f32[80,128]{1,0:T(8,128)}, u32[]{:S(2)}) copy-start(f32[80,128]{1,0:T(8,128)} %get-tuple-element.24) | copy-start | bytes 122884
  119.9 9.4 %collective-permute-start.10 = (f32[40,64,128]{2,1,0:T(8,128)S(1)}, f32[40,64,128]{2,1,0:T(8,128)S(1)}, u32[]{:S(2)}, u32[]{:S(2)}) collective-permute-start(f32[40,64,128]{2,1,0:T(8,128)S(1)} %fusion.41), channel_id=1, source_target_pairs={{0,1},{1,0},{2,3},{3,2},{4,5},{5,4},{6,7},{7,6},{8,9},{9,8},{10,11... | collective-permute-start | bytes 3932168 | tf_op jit(solution)/shard_map/ppermute | solution.py:114
  123.2 2.0 copy-start.10
  123.2 2.0 copy-start.23
  125.2 4.1 %copy-start.17 = (f32[128,80]{0,1:T(8,128)S(1)}, f32[128,80]{0,1:T(8,128)}, u32[]{:S(2)}) copy-start(f32[128,80]{0,1:T(8,128)} %get-tuple-element.31) | copy-start | bytes 122884
  129.3 3.0 %copy-start.7 = (f32[40,64,128]{2,1,0:T(8,128)}, f32[40,64,128]{2,1,0:T(8,128)S(1)}, u32[]{:S(2)}) copy-start(f32[40,64,128]{2,1,0:T(8,128)S(1)} %collective-permute-done.10) | copy-start | bytes 3932164
  132.3 3.3 %copy-start.33 = (f32[80]{0:T(128)S(1)}, f32[80]{0:T(128)}, u32[]{:S(2)}) copy-start(f32[80]{0:T(128)} %copy-done.32) | copy-start | bytes 964
  132.3 3.3 %copy-start.34 = (f32[80]{0:T(128)S(1)}, f32[80]{0:T(128)}, u32[]{:S(2)}) copy-start(f32[80]{0:T(128)} %get-tuple-element.51) | copy-start | bytes 964
  146.3 7.6 %copy-start.19 = (f32[5120]{0:T(1024)S(1)}, f32[5120]{0:T(1024)}, u32[]{:S(2)}) copy-start(f32[5120]{0:T(1024)} %param.21) | copy-start | bytes 61444
  151.6 2.3 %copy-start = (f32[256,5120]{1,0:T(8,128)}, f32[256,5120]{1,0:T(8,128)S(1)}, u32[]{:S(2)}) copy-start(f32[256,5120]{1,0:T(8,128)S(1)} %get-tuple-element.8) | copy-start | bytes 15728644
  157.2 53.1 %copy-start.25 = (f32[8,256]{1,0:T(8,128)}, f32[8,256]{1,0:T(8,128)S(1)}, u32[]{:S(2)}) copy-start(f32[8,256]{1,0:T(8,128)S(1)} %get-tuple-element.55) | copy-start | bytes 24580
  174.0 34.6 %all-to-all-start.2 = ((bf16[32,8,16,256]{3,2,1,0:T(8,128)(2,1)}), bf16[32,8,16,256]{3,2,1,0:T(8,128)(2,1)S(1)}, u32[]{:S(2)}, u32[]{:S(2)}) async-start(bf16[32,8,16,256]{3,2,1,0:T(8,128)(2,1)} %broadcast_in_dim.150), calls=%async_computation.2 | async-start | bytes 4194304 | tf_op jit(solution)/shard_map/all_to_all | solution.py:125
Sparse Core Ops, SparseCore 0:
  106.0 42.7 all-gather.1

commit v11 on v10

--- a/solution.py
+++ b/solution.py
@@ -166,6 +166,10 @@
             jnp.float32
         )
     active = jax.nn.silu(summed).astype(jnp.bfloat16)
+    shard_total = jnp.zeros((heads,), jnp.float32)
+    for block in range(length // SPAN):
+        shard_total = shard_total + jnp.cumsum(log_forget[0][:, block * SPAN : (block + 1) * SPAN], axis=1)[:, -1]
+    active, shard_logs = lax.optimization_barrier((active, spread_over(shard_total, "seq")))
     values = active[:, :width].reshape(length, heads, head_dim)
     write_all = active[:, width : width + state_dim]
     read_all = active[:, width + state_dim :]
@@ -198,7 +202,6 @@
         block_total = cum_list[block][:, -1]
         running = jnp.exp(block_total)[:, None, None] * running + state_list[block]
         before = before + block_total
-    shard_logs = spread_over(before, "seq")
     carry_in = carried_in(running, shard_logs)
     outputs = []
     for block in range(blocks):

time: 222 us -> 221 us (level)
  waiting for transfers between devices: 68.1 us -> 63.2 us
  starting transfers between devices: 28.6 us -> 33 us
    all_to_all x2, waiting for transfers between devices: 30.5 us -> 23.7 us  [spread_over(): lax.all_to_all(jnp.broadcast_to(block[None], (count,) + block.shape), axi...]
    ppermute x2, starting transfers between devices: 1.86 us -> 5.14 us  [ring_of_four(): next_state = lax.ppermute(sent, 'seq', bwd)]
    ppermute x2, starting transfers between devices: 4.19 us -> 6.79 us  [ring_of_four(): far_a = lax.ppermute(next_state[:half], 'seq', bwd)]
    ppermute x1, waiting for transfers between devices: 0.01 us -> 2.47 us  [carried_in(): lax.ppermute(lax.dynamic_slice_in_dim(own_state, theirs, half, 0), 'seq',...]
  transfers between devices with their start and end apart: 14 -> 14, of which waited for: 7 -> 7; matrix products, arithmetic and copies ran while one was open for 23% -> 26% of each run, Pallas kernels for 0% -> 0%
where the time goes in v11:
time: 221 us
  waiting for transfers between devices  63.2 us (29%)
  other arithmetic  38.4 us (17%)
  starting transfers between devices  33 us (15%)
  matrix products  29 us (13%)
  local copies, waits for them, and re-layouts  27.1 us (12%)
  blocking collectives  15.2 us (7%)
  between operations  14.8 us (7%)
    ppermute x2, waiting for transfers between devices, ring_of_four(): next_state = lax.ppermute(sent, 'seq', bwd)  25.1 us
    all_to_all x2, waiting for transfers between devices, spread_over(): lax.all_to_all(jnp.broadcast_to(block[None], (count,) + block.shape), axi...  23.7 us
    all_to_all x1, blocking collectives, spread_over(): lax.all_to_all(jnp.broadcast_to(block[None], (count,) + block.shape), axi...  15.2 us
    all_to_all x2, starting transfers between devices, spread_over(): lax.all_to_all(jnp.broadcast_to(block[None], (count,) + block.shape), axi...  13.1 us
    dot_general x2, matrix products, per_device(): jnp.einsum('tn,hpn->thp', read_block, start, precision=lax.Precision.HIGH...  10.5 us
    ppermute x2, waiting for transfers between devices, ring_of_four(): far_b = lax.ppermute(prev_state[half:], 'seq', fwd)  8.53 us
    ppermute x2, starting transfers between devices, ring_of_four(): far_a = lax.ppermute(next_state[:half], 'seq', bwd)  6.79 us
    slice x3, local copies, waits for them, and re-layouts, per_device(): values[lower:upper]  6.69 us
  transfers between devices with their start and end apart: 14, of which 7 were waited for; matrix products, arithmetic and copies ran while one was open for 26% of the time, Pallas kernels for 0%

profile of v11, /device:TPU:1, one launch (start us, length us, event | category | flops | bytes accessed | tf_op | source)
XLA Modules:
  0.0 220.6 jit_solution(13801206404179070932)
XLA Ops:
  7.2 2.1 pad_maximum_fusion.2
  9.4 4.6 %collective-permute-start = (bf16[3,5376]{1,0:T(4,128)(2,1)S(1)}, bf16[3,5376]{1,0:T(4,128)(2,1)S(1)}, u32[]{:S(2)}, u32[]{:S(2)}) collective-permute-start(bf16[3,5376]{1,0:T(4,128)(2,1)S(1)} %slice.140), channel_id=1, source_target_pairs={{0,1},{1,2},{2,3},{3,4},{4,5},{5,6},{6,7},{7,8},{8,9},{9,10},{10,1... | collective-permute-start | bytes 96776 | tf_op jit(solution)/shard_map/ppermute | solution.py:16
  14.0 0.3 reduce_window_sum.19
  14.3 0.3 reduce_window_sum.20
  14.8 0.5 fusion.110
  15.3 0.6 broadcast_in_dim.141
  16.0 6.9 %all-to-all-start = ((f32[32,1,80]{2,1,0:T(1,128)}), f32[32,1,80]{2,1,0:T(1,128)S(1)}, u32[]{:S(2)}, u32[]{:S(2)}) async-start(f32[32,1,80]{2,1,0:T(1,128)} %broadcast_in_dim.141), calls=%async_computation | async-start | bytes 32768 | tf_op jit(solution)/shard_map/all_to_all | solution.py:125
  22.9 0.7 fusion.108
  23.9 2.4 %maximum_maximum_fusion = bf16[259,5376]{1,0:T(8,128)(2,1)S(1)} fusion(bf16[256,128]{1,0:T(8,128)(2,1)S(1)} %bitcast.88, bf16[256,128]{1,0:T(8,128)(2,1)S(1)} %bitcast.91, bf16[256,5120]{1,0:T(8,128)(2,1)S(1)} %bitcast.75, bf16[3,5376]{1,0:T(4,128)(2,1)S(1)} %collective-permute-done), kind=kLoop, calls=%fused_computation.22 | loop fusion | flops 11139072 | bytes 5569536 | tf_op jit(solution)/shard_map/concatenate | solution.py:162
  26.3 4.4 %multiply_convert_fusion = bf16[256,5376]{1,0:T(8,128)(2,1)S(1)} fusion(bf16[259,5376]{1,0:T(8,128)(2,1)S(1)} %maximum_maximum_fusion, f32[5376]{0:T(1024)S(1)} %get-tuple-element.9, f32[5376]{0:T(1024)S(1)} %get-tuple-element.10, f32[5376]{0:T(1024)S(1)} %get-tuple-element.8, f32[5376]{0:T(1024)S(1)} %get-tuple-element.7, f32[5376]{0:T(1024)S(1)} %copy-done.26, ...), kind=kLoop, calls=%fused_computation.2 | loop fusion | flops 30277632 | bytes 13870080 | tf_op jit(solution)/shard_map/convert_element_type | solution.py:168
  30.7 1.8 fusion.107
  32.6 2.4 %copy.31 = bf16[128,5120]{0,1:T(8,128)(2,1)} copy(bf16[128,5120]{1,0:T(8,128)(2,1)} %get-tuple-element.26) | data formatting | bytes 2621440 | tf_op jit(solution)/shard_map/slice | solution.py:186
  35.0 2.4 %copy.32 = bf16[128,5120]{0,1:T(8,128)(2,1)} copy(bf16[128,5120]{1,0:T(8,128)(2,1)} %get-tuple-element.27) | data formatting | bytes 2621440 | tf_op jit(solution)/shard_map/slice | solution.py:186
  37.4 3.9 %fusion.9 = f32[80,64,128]{2,1,0:T(8,128)S(1)} fusion(bf16[128,80,64]{0,2,1:T(8,128)(2,1)} %bitcast.83, f32[128,128]{1,0:T(8,128)S(1)} %get-tuple-element.25, f32[80,128]{1,0:T(8,128)S(1)} %get-tuple-element.29), kind=kOutput, calls=%fused_computation.26 | convolution fusion | flops 170393600 | bytes 4038656 | tf_op jit(solution)/shard_map/hsn,shp->hpn/dot_general | solution.py:29
  41.4 1.8 multiply_add_fusion
  43.2 1.2 constant_dynamic-slice_fusion.2
  44.4 0.7 copy-done.4
  45.4 0.7 exponential_bitcast_fusion.7
  46.0 2.5 %collective-permute-done.1 = f32[40,64,128]{2,1,0:T(8,128)} collective-permute-done((f32[40,64,128]{2,1,0:T(8,128)}, f32[40,64,128]{2,1,0:T(8,128)}, u32[]{:S(2)}, u32[]{:S(2)}) %collective-permute-start.1) | collective-permute-done | bytes 1310752 | tf_op jit(solution)/shard_map/ppermute | solution.py:101
  48.5 3.4 %fusion.105 = (bf16[40,64,128]{2,1,0:T(8,128)(2,1)}, f32[40,64,128]{2,1,0:T(8,128)}) fusion(f32[40,64,128]{2,1,0:T(8,128)} %collective-permute-done.1, f32[80,64,128]{2,1,0:T(8,128)} %copy-done.4, s32[]{:T(128)S(6)} %select_n.708, pred[]{:T(512)S(6)} %eq.18, f32[40]{0:T(128)S(1)} %get-tuple-element.36), kind=kLoop, calls=%fused_computation.216 | loop fusion | flops 1638400 | bytes 4587685 | tf_op jit(solution)/shard_map/convert_element_type | solution.py:50
  51.9 2.6 %collective-permute-start.3 = (bf16[40,64,128]{2,1,0:T(8,128)(2,1)}, bf16[40,64,128]{2,1,0:T(8,128)(2,1)S(1)}, u32[]{:S(2)}, u32[]{:S(2)}) collective-permute-start(bf16[40,64,128]{2,1,0:T(8,128)(2,1)} %get-tuple-element.20), channel_id=1, source_target_pairs={{0,6},{1,7},{2,0},{3,1},{4,2},{5,3},{6,4},{7,5},{8,14},{9,15},{10,... | collective-permute-start | bytes 1966088 | tf_op jit(solution)/shard_map/ppermute | solution.py:52
  54.5 0.7 exponential_bitcast_fusion.2
  55.2 13.3 %collective-permute-done.3 = bf16[40,64,128]{2,1,0:T(8,128)(2,1)S(1)} collective-permute-done((bf16[40,64,128]{2,1,0:T(8,128)(2,1)}, bf16[40,64,128]{2,1,0:T(8,128)(2,1)S(1)}, u32[]{:S(2)}, u32[]{:S(2)}) %collective-permute-start.3) | collective-permute-done | bytes 655392 | tf_op jit(solution)/shard_map/ppermute | solution.py:52
  68.5 3.4 %collective-permute-start.4 = (bf16[20,64,128]{2,1,0:T(8,128)(2,1)S(1)}, bf16[20,64,128]{2,1,0:T(8,128)(2,1)S(1)}, u32[]{:S(2)}, u32[]{:S(2)}) collective-permute-start(bf16[20,64,128]{2,1,0:T(8,128)(2,1)S(1)} %slice.152), channel_id=1, source_target_pairs={{0,6},{1,7},{2,0},{3,1},{4,2},{5,3},{6,4},{7,5},{8,14},{9,15},{10,... | collective-permute-start | bytes 983048 | tf_op jit(solution)/shard_map/ppermute | solution.py:53
  71.9 1.0 slice.153
  73.2 0.6 exponential_bitcast_fusion.5
  73.8 0.6 exponential_bitcast_fusion.6
  74.4 3.3 %collective-permute-done.4 = bf16[20,64,128]{2,1,0:T(8,128)(2,1)S(1)} collective-permute-done((bf16[20,64,128]{2,1,0:T(8,128)(2,1)S(1)}, bf16[20,64,128]{2,1,0:T(8,128)(2,1)S(1)}, u32[]{:S(2)}, u32[]{:S(2)}) %collective-permute-start.4) | collective-permute-done | bytes 327712 | tf_op jit(solution)/shard_map/ppermute | solution.py:53
  77.7 4.4 %collective-permute-done.5 = bf16[20,64,128]{2,1,0:T(8,128)(2,1)S(1)} collective-permute-done((bf16[20,64,128]{2,1,0:T(8,128)(2,1)S(1)}, bf16[20,64,128]{2,1,0:T(8,128)(2,1)S(1)}, u32[]{:S(2)}, u32[]{:S(2)}) %collective-permute-start.5) | collective-permute-done | bytes 327712 | tf_op jit(solution)/shard_map/ppermute | solution.py:54
  82.1 2.3 %fusion.43 = bf16[40,64,128]{2,1,0:T(8,128)(2,1)S(1)} fusion(bf16[40,64,128]{2,1,0:T(8,128)(2,1)S(1)} %collective-permute-done.3, bf16[40,64,128]{2,1,0:T(8,128)(2,1)} %collective-permute-done.2, f32[40,64,128]{2,1,0:T(8,128)} %get-tuple-element.21, f32[40]{0:T(128)S(1)} %get-tuple-element.52, f32[40]{0:T(128)S(1)} %get-tuple-element.54, ...), kind=kLoop, calls=%fused_computation.69 | loop fusion | flops 3932160 | bytes 3932800 | tf_op jit(solution)/shard_map/convert_element_type | solution.py:50
  84.4 2.6 %collective-permute-start.7 = (bf16[40,64,128]{2,1,0:T(8,128)(2,1)S(1)}, bf16[40,64,128]{2,1,0:T(8,128)(2,1)S(1)}, u32[]{:S(2)}, u32[]{:S(2)}) collective-permute-start(bf16[40,64,128]{2,1,0:T(8,128)(2,1)S(1)} %fusion.43), channel_id=1, source_target_pairs={{0,24},{1,25},{2,26},{3,27},{4,28},{5,29},{6,30},{7,31},{8,0},{9,1... | collective-permute-start | bytes 1966088 | tf_op jit(solution)/shard_map/ppermute | solution.py:52
  87.0 11.7 %collective-permute-done.7 = bf16[40,64,128]{2,1,0:T(8,128)(2,1)S(1)} collective-permute-done((bf16[40,64,128]{2,1,0:T(8,128)(2,1)S(1)}, bf16[40,64,128]{2,1,0:T(8,128)(2,1)S(1)}, u32[]{:S(2)}, u32[]{:S(2)}) %collective-permute-start.7) | collective-permute-done | bytes 655392 | tf_op jit(solution)/shard_map/ppermute | solution.py:52
  98.7 0.9 copy-done.11
  99.6 0.8 slice.154
  100.3 3.4 %collective-permute-start.8 = (bf16[20,64,128]{2,1,0:T(8,128)(2,1)}, bf16[20,64,128]{2,1,0:T(8,128)(2,1)}, u32[]{:S(2)}, u32[]{:S(2)}) collective-permute-start(bf16[20,64,128]{2,1,0:T(8,128)(2,1)} %slice.154), channel_id=1, source_target_pairs={{0,24},{1,25},{2,26},{3,27},{4,28},{5,29},{6,30},{7,31},{8,0},{9,1... | collective-permute-start | bytes 983048 | tf_op jit(solution)/shard_map/ppermute | solution.py:53
  103.7 0.9 copy-done.12
  104.6 0.7 slice.155
  105.6 0.7 mul.397
  106.3 0.8 mul.398
  107.2 0.7 convert.10
  107.9 0.8 dynamic-slice_reduce_fusion
  108.8 4.1 %collective-permute-done.9 = bf16[20,64,128]{2,1,0:T(8,128)(2,1)} collective-permute-done((bf16[20,64,128]{2,1,0:T(8,128)(2,1)}, bf16[20,64,128]{2,1,0:T(8,128)(2,1)}, u32[]{:S(2)}, u32[]{:S(2)}) %collective-permute-start.9) | collective-permute-done | bytes 327712 | tf_op jit(solution)/shard_map/ppermute | solution.py:54
  112.9 4.4 %fusion.42 = (f32[40,64,128]{2,1,0:T(8,128)S(1)}, f32[40,64,128]{2,1,0:T(8,128)S(1)}) fusion(f32[40]{0:T(128)} %get-tuple-element.37, pred[]{:T(512)S(6)} %eq.18, f32[40,64,128]{2,1,0:T(8,128)} %collective-permute-done.1, f32[80,64,128]{2,1,0:T(8,128)} %copy-done.4, s32[]{:T(128)S(6)} %select_n.708, f32[40]{0:T(128)} %get-tuple-element.51, ...), kind=kLoop, calls=%fused_computation.68 | loop fusion | flops 11468800 | bytes 10488005 | tf_op jit(solution)/shard_map/jit(_where)/select_n | solution.py:112
  117.4 2.1 fusion.41
  119.4 2.7 %collective-permute-start.10 = (f32[40,64,128]{2,1,0:T(8,128)S(1)}, f32[40,64,128]{2,1,0:T(8,128)S(1)}, u32[]{:S(2)}, u32[]{:S(2)}) collective-permute-start(f32[40,64,128]{2,1,0:T(8,128)S(1)} %fusion.41), channel_id=1, source_target_pairs={{0,1},{1,0},{2,3},{3,2},{4,5},{5,4},{6,7},{7,6},{8,9},{9,8},{10,11... | collective-permute-start | bytes 3932168 | tf_op jit(solution)/shard_map/ppermute | solution.py:114
  122.5 2.0 fusion.7
  124.5 4.1 %fusion.8 = f32[80,64,128]{2,1,0:T(8,128)} fusion(bf16[128,80,64]{0,2,1:T(8,128)(2,1)S(1)} %bitcast.86, f32[80,128]{1,0:T(8,128)S(1)} %copy-done.23, f32[80,128]{1,0:T(8,128)S(1)} %reduce_window_sum.20, f32[128,128]{1,0:T(8,128)S(1)} %fusion.52, pred[128,128]{1,0:T(8,128)(4,1)S(1)} %iota_compare_fusion), kind=kOutput, calls=%fused_computation.25 | convolution fusion | flops 174325760 | bytes 4096000 | tf_op jit(solution)/shard_map/hts,shp->thp/dot_general | solution.py:26
  128.6 3.0 %bitcast_add_fusion.1 = f32[128,80,64]{0,2,1:T(8,128)} fusion(f32[80,64,128]{2,1,0:T(8,128)S(1)} %fusion.7, f32[40,64,128]{2,1,0:T(8,128)S(1)} %collective-permute-done.10, f32[40,64,128]{2,1,0:T(8,128)S(1)} %get-tuple-element.13, f32[128,80]{0,1:T(8,128)S(1)} %copy-done.17, pred[]{:T(512)S(6)} %eq.18, bf16[256,5376]{1,0:T(8,128)(2,1)S(1)} %multiply_convert_fusion), kind=kOutput, calls=%fused_computation.30 | convolution fusion | flops 1009909760 | bytes 7938049 | tf_op jit(solution)/shard_map/tn,hpn->thp/dot_general | solution.py:212
  131.6 3.3 %copy.37 = f32[128,5120]{1,0:T(8,128)} copy(f32[128,5120]{0,1:T(8,128)} %bitcast.81) | data formatting | bytes 5242880 | tf_op jit(solution)/shard_map/concatenate | solution.py:216
  134.9 7.5 %bitcast_add_fusion = f32[128,80,64]{0,2,1:T(8,128)} fusion(f32[80,64,128]{2,1,0:T(8,128)} %fusion.8, f32[80,64,128]{2,1,0:T(8,128)} %copy-done.3, f32[40,64,128]{2,1,0:T(8,128)} %copy-done.7, f32[40,64,128]{2,1,0:T(8,128)} %copy-done.6, f32[80]{0:T(128)S(1)} %copy-done.34, f32[128,80]{0,1:T(8,128)S(1)} %get-tuple-element.34, f32[80]{0:T(128)S(1)} %copy-done.33, ...), kind=kOutput, calls=%fused_computation.29 | convolution fusion | flops 1011875840 | bytes 10560513 | tf_op jit(solution)/shard_map/tn,hpn->thp/dot_general | solution.py:212
  142.4 3.2 %copy.38 = f32[128,5120]{1,0:T(8,128)} copy(f32[128,5120]{0,1:T(8,128)} %bitcast.82) | data formatting | bytes 5242880 | tf_op jit(solution)/shard_map/concatenate | solution.py:216
  145.6 5.2 %multiply_reduce_fusion = (f32[256]{0:T(256)S(1)}, f32[256,5120]{1,0:T(8,128)S(1)}) fusion(bf16[1,256,5120]{2,1,0:T(8,128)(2,1)} %param.13, bf16[256,5376]{1,0:T(8,128)(2,1)S(1)} %multiply_convert_fusion, f32[5120]{0:T(1024)S(1)} %mul.398, f32[128,5120]{1,0:T(8,128)} %copy.38, f32[128,5120]{1,0:T(8,128)} %copy.37), kind=kLoop, calls=%fused_computation.10 | loop fusion | flops 15728384 | bytes 15750144 | tf_op jit(solution)/shard_map/reduce_sum | solution.py:219
  150.9 2.3 %copy-done = f32[256,5120]{1,0:T(8,128)} copy-done((f32[256,5120]{1,0:T(8,128)}, f32[256,5120]{1,0:T(8,128)S(1)}, u32[]{:S(2)}) %copy-start) | copy-done | bytes 5242904
  153.2 1.0 convert_reduce_fusion
  154.2 2.3 %multiply_reduce_fusion.2 = (f32[8]{0:T(128)S(1)}, bf16[8,256]{1,0:T(8,128)(2,1)S(1)}, f32[8,256]{1,0:T(8,128)S(1)}) fusion(bf16[5120,256]{1,0:T(8,128)(2,1)} %all-gather.2.cloned.1.call-done, f32[8,5120]{1,0:T(8,128)S(1)} %convert_reduce_fusion), kind=kOutput, calls=%fused_computation.104 | convolution fusion | flops 21059576 | bytes 2797600 | tf_op jit(solution)/shard_map/dot_general | solution.py:224
  156.5 15.2 %all_to_all.19 = bf16[8,16,256]{2,1,0:T(8,128)(2,1)S(1)} all-to-all(bf16[8,16,256]{2,1,0:T(8,128)(2,1)S(1)} %broadcast_in_dim.149), channel_id=1, replica_groups=mesh['dp'=8,'seq'=32] {'dp'}, dimensions={0} | all-to-all | bytes 131072 | tf_op jit(solution)/shard_map/all_to_all | solution.py:125
  171.7 1.6 broadcast_in_dim.150
  173.3 6.2 %all-to-all-start.2 = ((bf16[32,8,16,256]{3,2,1,0:T(8,128)(2,1)}), bf16[32,8,16,256]{3,2,1,0:T(8,128)(2,1)S(1)}, u32[]{:S(2)}, u32[]{:S(2)}) async-start(bf16[32,8,16,256]{3,2,1,0:T(8,128)(2,1)} %broadcast_in_dim.150), calls=%async_computation.2 | async-start | bytes 4194304 | tf_op jit(solution)/shard_map/all_to_all | solution.py:125
  179.5 4.7 %fusion.102 = bf16[1,256,5120]{2,1,0:T(8,128)(2,1)} fusion(f32[5120]{0:T(1024)S(1)} %copy-done.19, f32[256,5120]{1,0:T(8,128)} %copy-done, f32[256]{0:T(256)S(1)} %add_rsqrt_fusion), kind=kLoop, calls=%fused_computation.215 | loop fusion | flops 3932160 | bytes 7885824 | tf_op jit(solution)/shard_map/broadcast_in_dim | solution.py:237
  184.1 23.7 %all-to-all-done.2 = bf16[32,8,16,256]{3,2,1,0:T(8,128)(2,1)S(1)} async-done(((bf16[32,8,16,256]{3,2,1,0:T(8,128)(2,1)}), bf16[32,8,16,256]{3,2,1,0:T(8,128)(2,1)S(1)}, u32[]{:S(2)}, u32[]{:S(2)}) %all-to-all-start.2) | async-done | bytes 2097184 | tf_op jit(solution)/shard_map/all_to_all | solution.py:125
  207.9 0.6 convert_bitcast_fusion
  208.5 0.5 fusion.106
  209.0 0.6 multiply_reduce_fusion.1
  209.6 4.2 %fusion.6 = f32[8,4096]{1,0:T(8,128)} fusion(f32[8,256]{1,0:T(8,128)S(1)} %get-tuple-element.59, f32[2048,256]{1,0:T(8,128)S(1)} %bitcast.80, f32[2048,256]{1,0:T(8,128)S(1)} %bitcast.78, f32[4096]{0:T(1024)S(1)} %multiply_reduce_fusion.1, f32[8]{0:T(128)S(1)} %get-tuple-element.38), kind=kOutput, calls=%fused_computation.18 | convolution fusion | flops 101875712 | bytes 4349984 | tf_op jit(solution)/shard_map/dot_general | solution.py:231
  (97 shorter events, 1.7 us)
Async XLA Ops:
  7.2 6.8 %copy-start.20 = (f32[1,80,256]{2,1,0:T(8,128)S(1)}, f32[1,80,256]{2,1,0:T(8,128)}, u32[]{:S(2)}) copy-start(f32[1,80,256]{2,1,0:T(8,128)} %param.17) | copy-start | bytes 245764
  7.2 15.7 %copy-start.21 = (f32[1,80,256]{2,1,0:T(8,128)S(1)}, f32[1,80,256]{2,1,0:T(8,128)}, u32[]{:S(2)}) copy-start(f32[1,80,256]{2,1,0:T(8,128)} %param.16) | copy-start | bytes 245764
  7.2 16.4 %copy-start.18 = (f32[4,5376]{1,0:T(4,128)S(1)}, f32[4,5376]{1,0:T(4,128)}, u32[]{:S(2)}) copy-start(f32[4,5376]{1,0:T(4,128)} %param.18) | copy-start | bytes 258052
  7.2 16.7 %copy-start.1 = (bf16[1,256,5120]{2,1,0:T(8,128)(2,1)S(1)}, bf16[1,256,5120]{2,1,0:T(8,128)(2,1)}, u32[]{:S(2)}) copy-start(bf16[1,256,5120]{2,1,0:T(8,128)(2,1)} %param.12) | copy-start | bytes 7864324
  7.2 16.7 %copy-start.15 = (bf16[1,256,128]{2,1,0:T(8,128)(2,1)S(1)}, bf16[1,256,128]{2,1,0:T(8,128)(2,1)}, u32[]{:S(2)}) copy-start(bf16[1,256,128]{2,1,0:T(8,128)(2,1)} %param.15) | copy-start | bytes 196612
  7.2 16.7 %copy-start.16 = (bf16[1,256,128]{2,1,0:T(8,128)(2,1)S(1)}, bf16[1,256,128]{2,1,0:T(8,128)(2,1)}, u32[]{:S(2)}) copy-start(bf16[1,256,128]{2,1,0:T(8,128)(2,1)} %param.14) | copy-start | bytes 196612
  9.4 14.5 %collective-permute-start = (bf16[3,5376]{1,0:T(4,128)(2,1)S(1)}, bf16[3,5376]{1,0:T(4,128)(2,1)S(1)}, u32[]{:S(2)}, u32[]{:S(2)}) collective-permute-start(bf16[3,5376]{1,0:T(4,128)(2,1)S(1)} %slice.140), channel_id=1, source_target_pairs={{0,1},{1,2},{2,3},{3,4},{4,5},{5,6},{6,7},{7,8},{8,9},{9,10},{10,1... | collective-permute-start | bytes 96776 | tf_op jit(solution)/shard_map/ppermute | solution.py:16
  15.3 26.1 %copy-start.32 = (f32[80]{0:T(128)}, f32[80]{0:T(128)S(1)}, u32[]{:S(2)}) copy-start(f32[80]{0:T(128)S(1)} %get-tuple-element.56) | copy-start | bytes 964
  16.0 14.8 %all-to-all-start = ((f32[32,1,80]{2,1,0:T(1,128)}), f32[32,1,80]{2,1,0:T(1,128)S(1)}, u32[]{:S(2)}, u32[]{:S(2)}) async-start(f32[32,1,80]{2,1,0:T(1,128)} %broadcast_in_dim.141), calls=%async_computation | async-start | bytes 32768 | tf_op jit(solution)/shard_map/all_to_all | solution.py:125
  22.9 131.3 %all-gather.2.cloned.1.call-start = ((), (), s32[]{:S(2)}) async-start(), calls=%async_computation.3 | async-start | bytes 2949120 | tf_op jit(solution)/shard_map/all_gather | solution.py:159
  23.8 2.4 %copy-start.2 = (bf16[1,256,5120]{2,1,0:T(8,128)(2,1)S(1)}, bf16[1,256,5120]{2,1,0:T(8,128)(2,1)}, u32[]{:S(2)}) copy-start(bf16[1,256,5120]{2,1,0:T(8,128)(2,1)} %param.12) | copy-start | bytes 7864324
  23.9 2.4 %copy-start.26 = (f32[5376]{0:T(1024)S(1)}, f32[5376]{0:T(1024)}, u32[]{:S(2)}) copy-start(f32[5376]{0:T(1024)} %param.19) | copy-start | bytes 64516
  37.4 4.0 %copy-start.9 = (bf16[128,5120]{0,1:T(8,128)(2,1)S(1)}, bf16[128,5120]{0,1:T(8,128)(2,1)}, u32[]{:S(2)}) copy-start(bf16[128,5120]{0,1:T(8,128)(2,1)} %copy.32) | copy-start | bytes 3932164
  41.4 1.8 copy-start.3
  43.2 1.9 copy-start.4
  45.1 3.4 %collective-permute-start.1 = (f32[40,64,128]{2,1,0:T(8,128)}, f32[40,64,128]{2,1,0:T(8,128)}, u32[]{:S(2)}, u32[]{:S(2)}) collective-permute-start(f32[40,64,128]{2,1,0:T(8,128)} %constant_dynamic-slice_fusion.2), channel_id=1, source_target_pairs={{0,1},{1,0},{2,3},{3,2},{4,5},{5,4},{6,7},{7,6},{8,9},{9,8},{10,11... | collective-permute-start | bytes 3932168 | tf_op jit(solution)/shard_map/ppermute | solution.py:101
  51.9 16.6 %collective-permute-start.3 = (bf16[40,64,128]{2,1,0:T(8,128)(2,1)}, bf16[40,64,128]{2,1,0:T(8,128)(2,1)S(1)}, u32[]{:S(2)}, u32[]{:S(2)}) collective-permute-start(bf16[40,64,128]{2,1,0:T(8,128)(2,1)} %get-tuple-element.20), channel_id=1, source_target_pairs={{0,6},{1,7},{2,0},{3,1},{4,2},{5,3},{6,4},{7,5},{8,14},{9,15},{10,... | collective-permute-start | bytes 1966088 | tf_op jit(solution)/shard_map/ppermute | solution.py:52
  54.5 17.4 %collective-permute-start.2 = (bf16[40,64,128]{2,1,0:T(8,128)(2,1)}, bf16[40,64,128]{2,1,0:T(8,128)(2,1)}, u32[]{:S(2)}, u32[]{:S(2)}) collective-permute-start(bf16[40,64,128]{2,1,0:T(8,128)(2,1)} %get-tuple-element.20), channel_id=1, source_target_pairs={{0,2},{1,3},{2,4},{3,5},{4,6},{5,7},{6,0},{7,1},{8,10},{9,11},{10,... | collective-permute-start | bytes 1966088 | tf_op jit(solution)/shard_map/ppermute | solution.py:51
  54.5 0.7 copy-start.22
  68.5 9.2 %collective-permute-start.4 = (bf16[20,64,128]{2,1,0:T(8,128)(2,1)S(1)}, bf16[20,64,128]{2,1,0:T(8,128)(2,1)S(1)}, u32[]{:S(2)}, u32[]{:S(2)}) collective-permute-start(bf16[20,64,128]{2,1,0:T(8,128)(2,1)S(1)} %slice.152), channel_id=1, source_target_pairs={{0,6},{1,7},{2,0},{3,1},{4,2},{5,3},{6,4},{7,5},{8,14},{9,15},{10,... | collective-permute-start | bytes 983048 | tf_op jit(solution)/shard_map/ppermute | solution.py:53
  72.9 9.2 %collective-permute-start.5 = (bf16[20,64,128]{2,1,0:T(8,128)(2,1)S(1)}, bf16[20,64,128]{2,1,0:T(8,128)(2,1)S(1)}, u32[]{:S(2)}, u32[]{:S(2)}) collective-permute-start(bf16[20,64,128]{2,1,0:T(8,128)(2,1)S(1)} %slice.153), channel_id=1, source_target_pairs={{0,2},{1,3},{2,4},{3,5},{4,6},{5,7},{6,0},{7,1},{8,10},{9,11},{10,... | collective-permute-start | bytes 983048 | tf_op jit(solution)/shard_map/ppermute | solution.py:54
  73.8 31.6 %copy-start.28 = (f32[40]{0:T(128)}, f32[40]{0:T(128)S(1)}, u32[]{:S(2)}) copy-start(f32[40]{0:T(128)S(1)} %get-tuple-element.45) | copy-start | bytes 484
  73.8 31.6 %copy-start.29 = (f32[40]{0:T(128)}, f32[40]{0:T(128)S(1)}, u32[]{:S(2)}) copy-start(f32[40]{0:T(128)S(1)} %get-tuple-element.54) | copy-start | bytes 484
  74.4 30.9 %copy-start.30 = (f32[40]{0:T(128)}, f32[40]{0:T(128)S(1)}, u32[]{:S(2)}) copy-start(f32[40]{0:T(128)S(1)} %get-tuple-element.43) | copy-start | bytes 484
  74.4 30.9 %copy-start.31 = (f32[40]{0:T(128)}, f32[40]{0:T(128)S(1)}, u32[]{:S(2)}) copy-start(f32[40]{0:T(128)S(1)} %get-tuple-element.52) | copy-start | bytes 484
  77.7 27.6 %copy-start.13 = (bf16[20,64,128]{2,1,0:T(8,128)(2,1)}, bf16[20,64,128]{2,1,0:T(8,128)(2,1)S(1)}, u32[]{:S(2)}) copy-start(bf16[20,64,128]{2,1,0:T(8,128)(2,1)S(1)} %collective-permute-done.4) | copy-start | bytes 983044
  82.1 23.2 %copy-start.14 = (bf16[20,64,128]{2,1,0:T(8,128)(2,1)}, bf16[20,64,128]{2,1,0:T(8,128)(2,1)S(1)}, u32[]{:S(2)}) copy-start(bf16[20,64,128]{2,1,0:T(8,128)(2,1)S(1)} %collective-permute-done.5) | copy-start | bytes 983044
  82.1 23.5 %copy-start.35 = (f32[80]{0:T(128)S(1)}, f32[80]{0:T(128)}, u32[]{:S(2)}) copy-start(f32[80]{0:T(128)} %param.20) | copy-start | bytes 964
  84.4 14.3 %collective-permute-start.7 = (bf16[40,64,128]{2,1,0:T(8,128)(2,1)S(1)}, bf16[40,64,128]{2,1,0:T(8,128)(2,1)S(1)}, u32[]{:S(2)}, u32[]{:S(2)}) collective-permute-start(bf16[40,64,128]{2,1,0:T(8,128)(2,1)S(1)} %fusion.43), channel_id=1, source_target_pairs={{0,24},{1,25},{2,26},{3,27},{4,28},{5,29},{6,30},{7,31},{8,0},{9,1... | collective-permute-start | bytes 1966088 | tf_op jit(solution)/shard_map/ppermute | solution.py:52
  87.0 16.8 %collective-permute-start.6 = (bf16[40,64,128]{2,1,0:T(8,128)(2,1)S(1)}, bf16[40,64,128]{2,1,0:T(8,128)(2,1)S(1)}, u32[]{:S(2)}, u32[]{:S(2)}) collective-permute-start(bf16[40,64,128]{2,1,0:T(8,128)(2,1)S(1)} %fusion.43), channel_id=1, source_target_pairs={{0,8},{1,9},{2,10},{3,11},{4,12},{5,13},{6,14},{7,15},{8,16},{9,17... | collective-permute-start | bytes 1966088 | tf_op jit(solution)/shard_map/ppermute | solution.py:51
  98.7 0.9 copy-start.11
  100.3 8.4 %collective-permute-start.8 = (bf16[20,64,128]{2,1,0:T(8,128)(2,1)}, bf16[20,64,128]{2,1,0:T(8,128)(2,1)}, u32[]{:S(2)}, u32[]{:S(2)}) collective-permute-start(bf16[20,64,128]{2,1,0:T(8,128)(2,1)} %slice.154), channel_id=1, source_target_pairs={{0,24},{1,25},{2,26},{3,27},{4,28},{5,29},{6,30},{7,31},{8,0},{9,1... | collective-permute-start | bytes 983048 | tf_op jit(solution)/shard_map/ppermute | solution.py:53
  103.7 0.9 copy-start.12
  105.4 7.5 %collective-permute-start.9 = (bf16[20,64,128]{2,1,0:T(8,128)(2,1)}, bf16[20,64,128]{2,1,0:T(8,128)(2,1)}, u32[]{:S(2)}, u32[]{:S(2)}) collective-permute-start(bf16[20,64,128]{2,1,0:T(8,128)(2,1)} %slice.155), channel_id=1, source_target_pairs={{0,8},{1,9},{2,10},{3,11},{4,12},{5,13},{6,14},{7,15},{8,16},{9,17... | collective-permute-start | bytes 983048 | tf_op jit(solution)/shard_map/ppermute | solution.py:54
  112.9 4.4 %copy-start.5 = (f32[80,64,128]{2,1,0:T(8,128)S(1)}, f32[80,64,128]{2,1,0:T(8,128)}, u32[]{:S(2)}) copy-start(f32[80,64,128]{2,1,0:T(8,128)} %copy-done.4) | copy-start | bytes 7864324
  112.9 4.4 %copy-start.27 = (f32[40]{0:T(128)S(1)}, f32[40]{0:T(128)}, u32[]{:S(2)}) copy-start(f32[40]{0:T(128)} %get-tuple-element.37) | copy-start | bytes 484
  117.3 11.3 %copy-start.6 = (f32[40,64,128]{2,1,0:T(8,128)}, f32[40,64,128]{2,1,0:T(8,128)S(1)}, u32[]{:S(2)}) copy-start(f32[40,64,128]{2,1,0:T(8,128)S(1)} %get-tuple-element.13) | copy-start | bytes 3932164
  117.3 5.1 %copy-start.8 = (bf16[128,5120]{0,1:T(8,128)(2,1)S(1)}, bf16[128,5120]{0,1:T(8,128)(2,1)}, u32[]{:S(2)}) copy-start(bf16[128,5120]{0,1:T(8,128)(2,1)} %copy.31) | copy-start | bytes 3932164
  117.3 5.2 %copy-start.24 = (f32[80,128]{1,0:T(8,128)S(1)}, f32[80,128]{1,0:T(8,128)}, u32[]{:S(2)}) copy-start(f32[80,128]{1,0:T(8,128)} %get-tuple-element.28) | copy-start | bytes 122884
  119.4 9.2 %collective-permute-start.10 = (f32[40,64,128]{2,1,0:T(8,128)S(1)}, f32[40,64,128]{2,1,0:T(8,128)S(1)}, u32[]{:S(2)}, u32[]{:S(2)}) collective-permute-start(f32[40,64,128]{2,1,0:T(8,128)S(1)} %fusion.41), channel_id=1, source_target_pairs={{0,1},{1,0},{2,3},{3,2},{4,5},{5,4},{6,7},{7,6},{8,9},{9,8},{10,11... | collective-permute-start | bytes 3932168 | tf_op jit(solution)/shard_map/ppermute | solution.py:114
  122.5 2.0 copy-start.10
  122.5 2.0 copy-start.23
  124.5 4.1 %copy-start.17 = (f32[128,80]{0,1:T(8,128)S(1)}, f32[128,80]{0,1:T(8,128)}, u32[]{:S(2)}) copy-start(f32[128,80]{0,1:T(8,128)} %get-tuple-element.35) | copy-start | bytes 122884
  128.6 3.0 %copy-start.7 = (f32[40,64,128]{2,1,0:T(8,128)}, f32[40,64,128]{2,1,0:T(8,128)S(1)}, u32[]{:S(2)}) copy-start(f32[40,64,128]{2,1,0:T(8,128)S(1)} %collective-permute-done.10) | copy-start | bytes 3932164
  131.6 3.3 %copy-start.33 = (f32[80]{0:T(128)S(1)}, f32[80]{0:T(128)}, u32[]{:S(2)}) copy-start(f32[80]{0:T(128)} %copy-done.32) | copy-start | bytes 964
  131.6 3.3 %copy-start.34 = (f32[80]{0:T(128)S(1)}, f32[80]{0:T(128)}, u32[]{:S(2)}) copy-start(f32[80]{0:T(128)} %get-tuple-element.55) | copy-start | bytes 964
  145.6 7.6 %copy-start.19 = (f32[5120]{0:T(1024)S(1)}, f32[5120]{0:T(1024)}, u32[]{:S(2)}) copy-start(f32[5120]{0:T(1024)} %param.21) | copy-start | bytes 61444
  150.9 2.3 %copy-start = (f32[256,5120]{1,0:T(8,128)}, f32[256,5120]{1,0:T(8,128)S(1)}, u32[]{:S(2)}) copy-start(f32[256,5120]{1,0:T(8,128)S(1)} %get-tuple-element.12) | copy-start | bytes 15728644
  156.5 53.1 %copy-start.25 = (f32[8,256]{1,0:T(8,128)}, f32[8,256]{1,0:T(8,128)S(1)}, u32[]{:S(2)}) copy-start(f32[8,256]{1,0:T(8,128)S(1)} %get-tuple-element.59) | copy-start | bytes 24580
  173.3 34.6 %all-to-all-start.2 = ((bf16[32,8,16,256]{3,2,1,0:T(8,128)(2,1)}), bf16[32,8,16,256]{3,2,1,0:T(8,128)(2,1)S(1)}, u32[]{:S(2)}, u32[]{:S(2)}) async-start(bf16[32,8,16,256]{3,2,1,0:T(8,128)(2,1)} %broadcast_in_dim.150), calls=%async_computation.2 | async-start | bytes 4194304 | tf_op jit(solution)/shard_map/all_to_all | solution.py:125
Sparse Core Ops, SparseCore 0:
  105.6 42.3 all-gather.1

commit v12 on v11

--- a/solution.py
+++ b/solution.py
@@ -208,10 +208,11 @@
         lower = block * SPAN
         upper = lower + SPAN
         start = start_list[block] + jnp.exp(before_list[block])[:, None, None] * carry_in
-        read_block = read_all[lower:upper].astype(jnp.float32)
-        outer_out = jnp.exp(cum_list[block]).T[:, :, None] * jnp.einsum(
-            "tn,hpn->thp", read_block, start, precision=lax.Precision.HIGHEST
-        )
+        read_block = read_all[lower:upper]
+        start_hi = lax.reduce_precision(start, exponent_bits=8, mantissa_bits=7)
+        start_lo = start - start_hi
+        pieces = [jnp.einsum("tn,hpn->thp", read_block, piece.astype(jnp.bfloat16), preferred_element_type=jnp.float32) for piece in (start_hi, start_lo)]
+        outer_out = jnp.exp(cum_list[block]).T[:, :, None] * (pieces[0] + pieces[1])
         outputs.append(inner_list[block] + outer_out)
     ssd_out = jnp.concatenate(outputs, axis=0)
     total = ssd_out + skip_gain[None, :, None] * values.astype(jnp.float32)

time: 221 us -> 221 us (level)
    ppermute x2, waiting for transfers between devices: 25.1 us -> 22 us  [ring_of_four(): next_state = lax.ppermute(sent, 'seq', bwd)]
    ppermute x2, waiting for transfers between devices: 3.34 us -> 6.22 us  [ring_of_four(): far_a = lax.ppermute(next_state[:half], 'seq', bwd)]
    select_n x1, other arithmetic: 4.39 us -> 1.63 us  [carried_in(): keep = jnp.where(core == 0, chip_in, high_in)]
    select_n x1, other arithmetic: 2.07 us -> 4.4 us  [carried_in(): give = jnp.where(core == 0, high_in, chip_in)]
    dot_general x2 -> x4, matrix products: 10.5 us -> 9.55 us  [per_device(): jnp.einsum('tn,hpn->thp', read_block, piece.astype(jnp.bfloat16), preferr...]
    unnamed x72 -> x76, local copies, waits for them, and re-layouts: 4.88 us -> 5.46 us
  transfers between devices with their start and end apart: 14 -> 14, of which waited for: 7 -> 8; matrix products, arithmetic and copies ran while one was open for 26% -> 26% of each run, Pallas kernels for 0% -> 0%
where the time goes in v12:
time: 221 us
  waiting for transfers between devices  62.7 us (28%)
  other arithmetic  38.7 us (18%)
  starting transfers between devices  32.6 us (15%)
  local copies, waits for them, and re-layouts  28.3 us (13%)
  matrix products  28 us (13%)
  blocking collectives  15.4 us (7%)
  between operations  14.8 us (7%)
    all_to_all x2, waiting for transfers between devices, spread_over(): lax.all_to_all(jnp.broadcast_to(block[None], (count,) + block.shape), axi...  23.4 us
    ppermute x2, waiting for transfers between devices, ring_of_four(): next_state = lax.ppermute(sent, 'seq', bwd)  22 us
    all_to_all x1, blocking collectives, spread_over(): lax.all_to_all(jnp.broadcast_to(block[None], (count,) + block.shape), axi...  15.4 us
    all_to_all x2, starting transfers between devices, spread_over(): lax.all_to_all(jnp.broadcast_to(block[None], (count,) + block.shape), axi...  10.9 us
    dot_general x4, matrix products, per_device(): jnp.einsum('tn,hpn->thp', read_block, piece.astype(jnp.bfloat16), preferr...  9.55 us
    ppermute x2, waiting for transfers between devices, ring_of_four(): far_b = lax.ppermute(prev_state[half:], 'seq', fwd)  8.63 us
    ppermute x2, starting transfers between devices, ring_of_four(): far_a = lax.ppermute(next_state[:half], 'seq', bwd)  6.87 us
    slice x3, local copies, waits for them, and re-layouts, per_device(): values[lower:upper]  6.7 us
  transfers between devices with their start and end apart: 14, of which 8 were waited for; matrix products, arithmetic and copies ran while one was open for 26% of the time, Pallas kernels for 0%

profile of v12, /device:TPU:1, one launch (start us, length us, event | category | flops | bytes accessed | tf_op | source)
XLA Modules:
  0.0 220.6 jit_solution(3876927987649932100)
XLA Ops:
  7.2 2.1 pad_maximum_fusion.2
  9.4 4.6 %collective-permute-start = (bf16[3,5376]{1,0:T(4,128)(2,1)S(1)}, bf16[3,5376]{1,0:T(4,128)(2,1)S(1)}, u32[]{:S(2)}, u32[]{:S(2)}) collective-permute-start(bf16[3,5376]{1,0:T(4,128)(2,1)S(1)} %slice.140), channel_id=1, source_target_pairs={{0,1},{1,2},{2,3},{3,4},{4,5},{5,6},{6,7},{7,8},{8,9},{9,10},{10,1... | collective-permute-start | bytes 96776 | tf_op jit(solution)/shard_map/ppermute | solution.py:16
  14.8 0.6 fusion.110
  15.4 0.6 broadcast_in_dim.141
  16.0 6.9 %all-to-all-start = ((f32[32,1,80]{2,1,0:T(1,128)}), f32[32,1,80]{2,1,0:T(1,128)S(1)}, u32[]{:S(2)}, u32[]{:S(2)}) async-start(f32[32,1,80]{2,1,0:T(1,128)} %broadcast_in_dim.141), calls=%async_computation | async-start | bytes 32768 | tf_op jit(solution)/shard_map/all_to_all | solution.py:125
  23.0 0.7 fusion.108
  24.0 2.4 %maximum_maximum_fusion = bf16[259,5376]{1,0:T(8,128)(2,1)S(1)} fusion(bf16[256,128]{1,0:T(8,128)(2,1)S(1)} %bitcast.92, bf16[256,128]{1,0:T(8,128)(2,1)S(1)} %bitcast.95, bf16[256,5120]{1,0:T(8,128)(2,1)S(1)} %bitcast.79, bf16[3,5376]{1,0:T(4,128)(2,1)S(1)} %collective-permute-done), kind=kLoop, calls=%fused_computation.26 | loop fusion | flops 11139072 | bytes 5569536 | tf_op jit(solution)/shard_map/concatenate | solution.py:162
  26.4 4.4 %multiply_convert_fusion = bf16[256,5376]{1,0:T(8,128)(2,1)S(1)} fusion(bf16[259,5376]{1,0:T(8,128)(2,1)S(1)} %maximum_maximum_fusion, f32[5376]{0:T(1024)S(1)} %get-tuple-element.9, f32[5376]{0:T(1024)S(1)} %get-tuple-element.10, f32[5376]{0:T(1024)S(1)} %get-tuple-element.8, f32[5376]{0:T(1024)S(1)} %get-tuple-element.7, f32[5376]{0:T(1024)S(1)} %copy-done.28, ...), kind=kLoop, calls=%fused_computation.2 | loop fusion | flops 30277632 | bytes 13870080 | tf_op jit(solution)/shard_map/convert_element_type | solution.py:168
  30.8 1.8 fusion.107
  32.7 2.5 %copy.39 = bf16[128,5120]{0,1:T(8,128)(2,1)} copy(bf16[128,5120]{1,0:T(8,128)(2,1)} %get-tuple-element.26) | data formatting | bytes 2621440 | tf_op jit(solution)/shard_map/slice | solution.py:186
  35.1 2.4 %copy.40 = bf16[128,5120]{0,1:T(8,128)(2,1)} copy(bf16[128,5120]{1,0:T(8,128)(2,1)} %get-tuple-element.27) | data formatting | bytes 2621440 | tf_op jit(solution)/shard_map/slice | solution.py:186
  37.5 3.9 %fusion.11 = f32[80,64,128]{2,1,0:T(8,128)S(1)} fusion(bf16[128,80,64]{0,2,1:T(8,128)(2,1)} %bitcast.87, f32[128,128]{1,0:T(8,128)S(1)} %get-tuple-element.25, f32[80,128]{1,0:T(8,128)S(1)} %get-tuple-element.29), kind=kOutput, calls=%fused_computation.32 | convolution fusion | flops 170393600 | bytes 4038656 | tf_op jit(solution)/shard_map/hsn,shp->hpn/dot_general | solution.py:29
  41.5 1.8 multiply_add_fusion.1
  43.3 1.3 constant_dynamic-slice_fusion.2
  44.6 0.7 copy-done.5
  45.5 0.6 exponential_bitcast_fusion.7
  46.1 2.5 %collective-permute-done.1 = f32[40,64,128]{2,1,0:T(8,128)} collective-permute-done((f32[40,64,128]{2,1,0:T(8,128)}, f32[40,64,128]{2,1,0:T(8,128)}, u32[]{:S(2)}, u32[]{:S(2)}) %collective-permute-start.1) | collective-permute-done | bytes 1310752 | tf_op jit(solution)/shard_map/ppermute | solution.py:101
  48.6 3.3 %fusion.105 = (bf16[40,64,128]{2,1,0:T(8,128)(2,1)}, f32[40,64,128]{2,1,0:T(8,128)}) fusion(f32[40,64,128]{2,1,0:T(8,128)} %collective-permute-done.1, f32[80,64,128]{2,1,0:T(8,128)} %copy-done.5, s32[]{:T(128)S(6)} %select_n.708, pred[]{:T(512)S(6)} %eq.18, f32[40]{0:T(128)S(1)} %get-tuple-element.36), kind=kLoop, calls=%fused_computation.221 | loop fusion | flops 1638400 | bytes 4587685 | tf_op jit(solution)/shard_map/convert_element_type | solution.py:50
  51.9 2.6 %collective-permute-start.3 = (bf16[40,64,128]{2,1,0:T(8,128)(2,1)}, bf16[40,64,128]{2,1,0:T(8,128)(2,1)S(1)}, u32[]{:S(2)}, u32[]{:S(2)}) collective-permute-start(bf16[40,64,128]{2,1,0:T(8,128)(2,1)} %get-tuple-element.20), channel_id=1, source_target_pairs={{0,6},{1,7},{2,0},{3,1},{4,2},{5,3},{6,4},{7,5},{8,14},{9,15},{10,... | collective-permute-start | bytes 1966088 | tf_op jit(solution)/shard_map/ppermute | solution.py:52
  54.5 0.7 exponential_bitcast_fusion.2
  55.2 13.3 %collective-permute-done.3 = bf16[40,64,128]{2,1,0:T(8,128)(2,1)S(1)} collective-permute-done((bf16[40,64,128]{2,1,0:T(8,128)(2,1)}, bf16[40,64,128]{2,1,0:T(8,128)(2,1)S(1)}, u32[]{:S(2)}, u32[]{:S(2)}) %collective-permute-start.3) | collective-permute-done | bytes 655392 | tf_op jit(solution)/shard_map/ppermute | solution.py:52
  68.5 3.4 %collective-permute-start.4 = (bf16[20,64,128]{2,1,0:T(8,128)(2,1)S(1)}, bf16[20,64,128]{2,1,0:T(8,128)(2,1)S(1)}, u32[]{:S(2)}, u32[]{:S(2)}) collective-permute-start(bf16[20,64,128]{2,1,0:T(8,128)(2,1)S(1)} %slice.152), channel_id=1, source_target_pairs={{0,6},{1,7},{2,0},{3,1},{4,2},{5,3},{6,4},{7,5},{8,14},{9,15},{10,... | collective-permute-start | bytes 983048 | tf_op jit(solution)/shard_map/ppermute | solution.py:53
  71.9 1.0 slice.153
  73.2 0.6 exponential_bitcast_fusion.5
  73.8 0.6 exponential_bitcast_fusion.6
  74.3 3.4 %collective-permute-done.4 = bf16[20,64,128]{2,1,0:T(8,128)(2,1)S(1)} collective-permute-done((bf16[20,64,128]{2,1,0:T(8,128)(2,1)S(1)}, bf16[20,64,128]{2,1,0:T(8,128)(2,1)S(1)}, u32[]{:S(2)}, u32[]{:S(2)}) %collective-permute-start.4) | collective-permute-done | bytes 327712 | tf_op jit(solution)/shard_map/ppermute | solution.py:53
  77.8 4.4 %collective-permute-done.5 = bf16[20,64,128]{2,1,0:T(8,128)(2,1)S(1)} collective-permute-done((bf16[20,64,128]{2,1,0:T(8,128)(2,1)S(1)}, bf16[20,64,128]{2,1,0:T(8,128)(2,1)S(1)}, u32[]{:S(2)}, u32[]{:S(2)}) %collective-permute-start.5) | collective-permute-done | bytes 327712 | tf_op jit(solution)/shard_map/ppermute | solution.py:54
  82.2 3.1 %fusion.42 = bf16[40,64,128]{2,1,0:T(8,128)(2,1)} fusion(bf16[40,64,128]{2,1,0:T(8,128)(2,1)S(1)} %collective-permute-done.3, bf16[40,64,128]{2,1,0:T(8,128)(2,1)} %collective-permute-done.2, f32[40,64,128]{2,1,0:T(8,128)} %get-tuple-element.21, f32[40]{0:T(128)S(1)} %get-tuple-element.52, f32[40]{0:T(128)S(1)} %get-tuple-element.54, ...), kind=kLoop, calls=%fused_computation.73 | loop fusion | flops 3932160 | bytes 3932800 | tf_op jit(solution)/shard_map/convert_element_type | solution.py:50
  85.3 2.5 %collective-permute-start.7 = (bf16[40,64,128]{2,1,0:T(8,128)(2,1)}, bf16[40,64,128]{2,1,0:T(8,128)(2,1)}, u32[]{:S(2)}, u32[]{:S(2)}) collective-permute-start(bf16[40,64,128]{2,1,0:T(8,128)(2,1)} %fusion.42), channel_id=1, source_target_pairs={{0,24},{1,25},{2,26},{3,27},{4,28},{5,29},{6,30},{7,31},{8,0},{9,1... | collective-permute-start | bytes 1966088 | tf_op jit(solution)/shard_map/ppermute | solution.py:52
  88.1 0.7 mul.397
  88.8 0.8 mul.398
  89.6 0.7 convert.10
  90.3 0.8 dynamic-slice_reduce_fusion
  91.2 8.7 %collective-permute-done.7 = bf16[40,64,128]{2,1,0:T(8,128)(2,1)} collective-permute-done((bf16[40,64,128]{2,1,0:T(8,128)(2,1)}, bf16[40,64,128]{2,1,0:T(8,128)(2,1)}, u32[]{:S(2)}, u32[]{:S(2)}) %collective-permute-start.7) | collective-permute-done | bytes 655392 | tf_op jit(solution)/shard_map/ppermute | solution.py:52
  99.8 1.0 slice.154
  100.8 3.5 %collective-permute-start.8 = (bf16[20,64,128]{2,1,0:T(8,128)(2,1)S(1)}, bf16[20,64,128]{2,1,0:T(8,128)(2,1)S(1)}, u32[]{:S(2)}, u32[]{:S(2)}) collective-permute-start(bf16[20,64,128]{2,1,0:T(8,128)(2,1)S(1)} %slice.154), channel_id=1, source_target_pairs={{0,24},{1,25},{2,26},{3,27},{4,28},{5,29},{6,30},{7,31},{8,0},{9,1... | collective-permute-start | bytes 983048 | tf_op jit(solution)/shard_map/ppermute | solution.py:53
  104.3 1.0 slice.155
  105.5 2.8 %collective-permute-done.8 = bf16[20,64,128]{2,1,0:T(8,128)(2,1)S(1)} collective-permute-done((bf16[20,64,128]{2,1,0:T(8,128)(2,1)S(1)}, bf16[20,64,128]{2,1,0:T(8,128)(2,1)S(1)}, u32[]{:S(2)}, u32[]{:S(2)}) %collective-permute-start.8) | collective-permute-done | bytes 327712 | tf_op jit(solution)/shard_map/ppermute | solution.py:53
  108.3 4.2 %collective-permute-done.9 = bf16[20,64,128]{2,1,0:T(8,128)(2,1)S(1)} collective-permute-done((bf16[20,64,128]{2,1,0:T(8,128)(2,1)S(1)}, bf16[20,64,128]{2,1,0:T(8,128)(2,1)S(1)}, u32[]{:S(2)}, u32[]{:S(2)}) %collective-permute-start.9) | collective-permute-done | bytes 327712 | tf_op jit(solution)/shard_map/ppermute | solution.py:54
  112.6 4.4 %fusion.40 = (f32[40,64,128]{2,1,0:T(8,128)S(1)}, f32[40,64,128]{2,1,0:T(8,128)S(1)}) fusion(f32[40]{0:T(128)} %get-tuple-element.37, pred[]{:T(512)S(6)} %eq.18, f32[40,64,128]{2,1,0:T(8,128)} %collective-permute-done.1, f32[80,64,128]{2,1,0:T(8,128)} %copy-done.5, s32[]{:T(128)S(6)} %select_n.708, f32[40]{0:T(128)} %get-tuple-element.51, ...), kind=kLoop, calls=%fused_computation.71 | loop fusion | flops 11468800 | bytes 10488005 | tf_op jit(solution)/shard_map/jit(_where)/select_n | solution.py:113
  117.0 4.5 %collective-permute-start.10 = (f32[40,64,128]{2,1,0:T(8,128)S(1)}, f32[40,64,128]{2,1,0:T(8,128)S(1)}, u32[]{:S(2)}, u32[]{:S(2)}) collective-permute-start(f32[40,64,128]{2,1,0:T(8,128)S(1)} %get-tuple-element.13), channel_id=1, source_target_pairs={{0,1},{1,0},{2,3},{3,2},{4,5},{5,4},{6,7},{7,6},{8,9},{9,8},{10,11... | collective-permute-start | bytes 3932168 | tf_op jit(solution)/shard_map/ppermute | solution.py:114
  121.6 2.0 fusion.7
  123.7 4.1 %fusion.8 = f32[80,64,128]{2,1,0:T(8,128)} fusion(bf16[128,80,64]{0,2,1:T(8,128)(2,1)S(1)} %bitcast.90, f32[80,128]{1,0:T(8,128)S(1)} %copy-done.25, f32[80,128]{1,0:T(8,128)S(1)} %reduce_window_sum.20, f32[128,128]{1,0:T(8,128)S(1)} %fusion.49, pred[128,128]{1,0:T(8,128)(4,1)S(1)} %iota_compare_fusion), kind=kOutput, calls=%fused_computation.29 | convolution fusion | flops 174325760 | bytes 4096000 | tf_op jit(solution)/shard_map/hts,shp->thp/dot_general | solution.py:26
  127.7 1.6 fusion.41
  129.4 0.5 fusion.38
  130.4 0.5 copy-done.9
  131.0 2.1 bitcast_add_fusion.1
  133.1 3.3 %copy.49 = f32[128,5120]{1,0:T(8,128)} copy(f32[128,5120]{0,1:T(8,128)} %bitcast.86) | data formatting | bytes 5242880 | tf_op jit(solution)/shard_map/concatenate | solution.py:217
  136.4 4.3 %fusion.36 = f32[128,80,64]{0,2,1:T(8,128)S(1)} fusion(bf16[256,5376]{1,0:T(8,128)(2,1)S(1)} %multiply_convert_fusion, f32[80,64,128]{2,1,0:T(8,128)} %copy-done.3, f32[80]{0:T(128)S(1)} %copy-done.36, f32[80]{0:T(128)S(1)} %copy-done.35, f32[40,64,128]{2,1,0:T(8,128)} %copy-done.7, f32[40,64,128]{2,1,0:T(8,128)} %copy-done.9, pred[]{:T(512)S(6)} %eq.18), kind=kOutput, calls=%fused_computation.68 | convolution fusion | flops 173670400 | bytes 7898113 | tf_op jit(solution)/shard_map/tn,hpn->thp/dot_general | solution.py:214
  141.2 0.8 copy-done.14
  142.1 2.6 %bitcast_add_fusion = f32[128,80,64]{0,2,1:T(8,128)} fusion(f32[80,64,128]{2,1,0:T(8,128)S(1)} %copy-done.14, f32[128,80,64]{0,2,1:T(8,128)S(1)} %fusion.36, f32[128,80]{0,1:T(8,128)S(1)} %get-tuple-element.34, bf16[256,5376]{1,0:T(8,128)(2,1)S(1)} %multiply_convert_fusion, f32[80,64,128]{2,1,0:T(8,128)S(1)} %copy-done.4, f32[80]{0:T(128)S(1)} %copy-done.36, ...), kind=kOutput, calls=%fused_computation.35 | convolution fusion | flops 174981120 | bytes 13181953 | tf_op jit(solution)/shard_map/tn,hpn->thp/dot_general | solution.py:214
  144.6 3.3 %copy.50 = f32[128,5120]{1,0:T(8,128)} copy(f32[128,5120]{0,1:T(8,128)} %bitcast.85) | data formatting | bytes 5242880 | tf_op jit(solution)/shard_map/concatenate | solution.py:217
  147.9 5.2 %multiply_reduce_fusion = (f32[256]{0:T(256)S(1)}, f32[256,5120]{1,0:T(8,128)S(1)}) fusion(bf16[1,256,5120]{2,1,0:T(8,128)(2,1)} %param.13, bf16[256,5376]{1,0:T(8,128)(2,1)S(1)} %multiply_convert_fusion, f32[5120]{0:T(1024)S(1)} %mul.398, f32[128,5120]{1,0:T(8,128)} %copy.50, f32[128,5120]{1,0:T(8,128)} %copy.49), kind=kLoop, calls=%fused_computation.10 | loop fusion | flops 15728384 | bytes 15750144 | tf_op jit(solution)/shard_map/reduce_sum | solution.py:220
  153.1 2.3 %copy-done = f32[256,5120]{1,0:T(8,128)} copy-done((f32[256,5120]{1,0:T(8,128)}, f32[256,5120]{1,0:T(8,128)S(1)}, u32[]{:S(2)}) %copy-start) | copy-done | bytes 5242904
  155.5 1.0 convert_reduce_fusion
  156.5 2.3 %multiply_reduce_fusion.2 = (f32[8]{0:T(128)S(1)}, bf16[8,256]{1,0:T(8,128)(2,1)S(1)}, f32[8,256]{1,0:T(8,128)S(1)}) fusion(bf16[5120,256]{1,0:T(8,128)(2,1)} %all-gather.2.cloned.1.call-done, f32[8,5120]{1,0:T(8,128)S(1)} %convert_reduce_fusion), kind=kOutput, calls=%fused_computation.109 | convolution fusion | flops 21059576 | bytes 2797600 | tf_op jit(solution)/shard_map/dot_general | solution.py:225
  158.8 15.4 %all_to_all.19 = bf16[8,16,256]{2,1,0:T(8,128)(2,1)S(1)} all-to-all(bf16[8,16,256]{2,1,0:T(8,128)(2,1)S(1)} %broadcast_in_dim.149), channel_id=1, replica_groups=mesh['dp'=8,'seq'=32] {'dp'}, dimensions={0} | all-to-all | bytes 131072 | tf_op jit(solution)/shard_map/all_to_all | solution.py:125
  174.2 1.6 broadcast_in_dim.150
  175.7 4.0 %all-to-all-start.2 = ((bf16[32,8,16,256]{3,2,1,0:T(8,128)(2,1)}), bf16[32,8,16,256]{3,2,1,0:T(8,128)(2,1)S(1)}, u32[]{:S(2)}, u32[]{:S(2)}) async-start(bf16[32,8,16,256]{3,2,1,0:T(8,128)(2,1)} %broadcast_in_dim.150), calls=%async_computation.2 | async-start | bytes 4194304 | tf_op jit(solution)/shard_map/all_to_all | solution.py:125
  179.7 4.7 %fusion.102 = bf16[1,256,5120]{2,1,0:T(8,128)(2,1)} fusion(f32[5120]{0:T(1024)S(1)} %copy-done.21, f32[256,5120]{1,0:T(8,128)} %copy-done, f32[256]{0:T(256)S(1)} %add_rsqrt_fusion), kind=kLoop, calls=%fused_computation.220 | loop fusion | flops 3932160 | bytes 7885824 | tf_op jit(solution)/shard_map/broadcast_in_dim | solution.py:238
  184.4 23.4 %all-to-all-done.2 = bf16[32,8,16,256]{3,2,1,0:T(8,128)(2,1)S(1)} async-done(((bf16[32,8,16,256]{3,2,1,0:T(8,128)(2,1)}), bf16[32,8,16,256]{3,2,1,0:T(8,128)(2,1)S(1)}, u32[]{:S(2)}, u32[]{:S(2)}) %all-to-all-start.2) | async-done | bytes 2097184 | tf_op jit(solution)/shard_map/all_to_all | solution.py:125
  207.8 0.6 convert_bitcast_fusion
  208.9 0.6 multiply_reduce_fusion.1
  209.5 4.2 %fusion.6 = f32[8,4096]{1,0:T(8,128)} fusion(f32[8,256]{1,0:T(8,128)S(1)} %get-tuple-element.59, f32[2048,256]{1,0:T(8,128)S(1)} %bitcast.84, f32[2048,256]{1,0:T(8,128)S(1)} %bitcast.82, f32[4096]{0:T(1024)S(1)} %multiply_reduce_fusion.1, f32[8]{0:T(128)S(1)} %get-tuple-element.38), kind=kOutput, calls=%fused_computation.18 | convolution fusion | flops 101875712 | bytes 4349984 | tf_op jit(solution)/shard_map/dot_general | solution.py:232
  (103 shorter events, 3.8 us)
Async XLA Ops:
  7.2 6.8 %copy-start.22 = (f32[1,80,256]{2,1,0:T(8,128)S(1)}, f32[1,80,256]{2,1,0:T(8,128)}, u32[]{:S(2)}) copy-start(f32[1,80,256]{2,1,0:T(8,128)} %param.17) | copy-start | bytes 245764
  7.2 15.8 %copy-start.23 = (f32[1,80,256]{2,1,0:T(8,128)S(1)}, f32[1,80,256]{2,1,0:T(8,128)}, u32[]{:S(2)}) copy-start(f32[1,80,256]{2,1,0:T(8,128)} %param.16) | copy-start | bytes 245764
  7.2 16.5 %copy-start.20 = (f32[4,5376]{1,0:T(4,128)S(1)}, f32[4,5376]{1,0:T(4,128)}, u32[]{:S(2)}) copy-start(f32[4,5376]{1,0:T(4,128)} %param.18) | copy-start | bytes 258052
  7.2 16.8 %copy-start.1 = (bf16[1,256,5120]{2,1,0:T(8,128)(2,1)S(1)}, bf16[1,256,5120]{2,1,0:T(8,128)(2,1)}, u32[]{:S(2)}) copy-start(bf16[1,256,5120]{2,1,0:T(8,128)(2,1)} %param.12) | copy-start | bytes 7864324
  7.2 16.8 %copy-start.17 = (bf16[1,256,128]{2,1,0:T(8,128)(2,1)S(1)}, bf16[1,256,128]{2,1,0:T(8,128)(2,1)}, u32[]{:S(2)}) copy-start(bf16[1,256,128]{2,1,0:T(8,128)(2,1)} %param.15) | copy-start | bytes 196612
  7.2 16.8 %copy-start.18 = (bf16[1,256,128]{2,1,0:T(8,128)(2,1)S(1)}, bf16[1,256,128]{2,1,0:T(8,128)(2,1)}, u32[]{:S(2)}) copy-start(bf16[1,256,128]{2,1,0:T(8,128)(2,1)} %param.14) | copy-start | bytes 196612
  9.4 14.5 %collective-permute-start = (bf16[3,5376]{1,0:T(4,128)(2,1)S(1)}, bf16[3,5376]{1,0:T(4,128)(2,1)S(1)}, u32[]{:S(2)}, u32[]{:S(2)}) collective-permute-start(bf16[3,5376]{1,0:T(4,128)(2,1)S(1)} %slice.140), channel_id=1, source_target_pairs={{0,1},{1,2},{2,3},{3,4},{4,5},{5,6},{6,7},{7,8},{8,9},{9,10},{10,1... | collective-permute-start | bytes 96776 | tf_op jit(solution)/shard_map/ppermute | solution.py:16
  15.4 26.1 %copy-start.34 = (f32[80]{0:T(128)}, f32[80]{0:T(128)S(1)}, u32[]{:S(2)}) copy-start(f32[80]{0:T(128)S(1)} %get-tuple-element.57) | copy-start | bytes 964
  16.0 14.8 %all-to-all-start = ((f32[32,1,80]{2,1,0:T(1,128)}), f32[32,1,80]{2,1,0:T(1,128)S(1)}, u32[]{:S(2)}, u32[]{:S(2)}) async-start(f32[32,1,80]{2,1,0:T(1,128)} %broadcast_in_dim.141), calls=%async_computation | async-start | bytes 32768 | tf_op jit(solution)/shard_map/all_to_all | solution.py:125
  22.9 133.5 %all-gather.2.cloned.1.call-start = ((), (), s32[]{:S(2)}) async-start(), calls=%async_computation.3 | async-start | bytes 2949120 | tf_op jit(solution)/shard_map/all_gather | solution.py:159
  23.9 2.4 %copy-start.2 = (bf16[1,256,5120]{2,1,0:T(8,128)(2,1)S(1)}, bf16[1,256,5120]{2,1,0:T(8,128)(2,1)}, u32[]{:S(2)}) copy-start(bf16[1,256,5120]{2,1,0:T(8,128)(2,1)} %param.12) | copy-start | bytes 7864324
  23.9 2.4 %copy-start.28 = (f32[5376]{0:T(1024)S(1)}, f32[5376]{0:T(1024)}, u32[]{:S(2)}) copy-start(f32[5376]{0:T(1024)} %param.19) | copy-start | bytes 64516
  37.5 4.0 %copy-start.12 = (bf16[128,5120]{0,1:T(8,128)(2,1)S(1)}, bf16[128,5120]{0,1:T(8,128)(2,1)}, u32[]{:S(2)}) copy-start(bf16[128,5120]{0,1:T(8,128)(2,1)} %copy.40) | copy-start | bytes 3932164
  41.5 1.8 copy-start.3
  43.3 1.9 copy-start.5
  45.2 3.4 %collective-permute-start.1 = (f32[40,64,128]{2,1,0:T(8,128)}, f32[40,64,128]{2,1,0:T(8,128)}, u32[]{:S(2)}, u32[]{:S(2)}) collective-permute-start(f32[40,64,128]{2,1,0:T(8,128)} %constant_dynamic-slice_fusion.2), channel_id=1, source_target_pairs={{0,1},{1,0},{2,3},{3,2},{4,5},{5,4},{6,7},{7,6},{8,9},{9,8},{10,11... | collective-permute-start | bytes 3932168 | tf_op jit(solution)/shard_map/ppermute | solution.py:101
  51.9 16.6 %collective-permute-start.3 = (bf16[40,64,128]{2,1,0:T(8,128)(2,1)}, bf16[40,64,128]{2,1,0:T(8,128)(2,1)S(1)}, u32[]{:S(2)}, u32[]{:S(2)}) collective-permute-start(bf16[40,64,128]{2,1,0:T(8,128)(2,1)} %get-tuple-element.20), channel_id=1, source_target_pairs={{0,6},{1,7},{2,0},{3,1},{4,2},{5,3},{6,4},{7,5},{8,14},{9,15},{10,... | collective-permute-start | bytes 1966088 | tf_op jit(solution)/shard_map/ppermute | solution.py:52
  54.5 17.5 %collective-permute-start.2 = (bf16[40,64,128]{2,1,0:T(8,128)(2,1)}, bf16[40,64,128]{2,1,0:T(8,128)(2,1)}, u32[]{:S(2)}, u32[]{:S(2)}) collective-permute-start(bf16[40,64,128]{2,1,0:T(8,128)(2,1)} %get-tuple-element.20), channel_id=1, source_target_pairs={{0,2},{1,3},{2,4},{3,5},{4,6},{5,7},{6,0},{7,1},{8,10},{9,11},{10,... | collective-permute-start | bytes 1966088 | tf_op jit(solution)/shard_map/ppermute | solution.py:51
  54.5 0.7 copy-start.24
  68.5 19.5 %copy-start.37 = (f32[80]{0:T(128)S(1)}, f32[80]{0:T(128)}, u32[]{:S(2)}) copy-start(f32[80]{0:T(128)} %param.20) | copy-start | bytes 964
  68.5 9.2 %collective-permute-start.4 = (bf16[20,64,128]{2,1,0:T(8,128)(2,1)S(1)}, bf16[20,64,128]{2,1,0:T(8,128)(2,1)S(1)}, u32[]{:S(2)}, u32[]{:S(2)}) collective-permute-start(bf16[20,64,128]{2,1,0:T(8,128)(2,1)S(1)} %slice.152), channel_id=1, source_target_pairs={{0,6},{1,7},{2,0},{3,1},{4,2},{5,3},{6,4},{7,5},{8,14},{9,15},{10,... | collective-permute-start | bytes 983048 | tf_op jit(solution)/shard_map/ppermute | solution.py:53
  72.9 9.2 %collective-permute-start.5 = (bf16[20,64,128]{2,1,0:T(8,128)(2,1)S(1)}, bf16[20,64,128]{2,1,0:T(8,128)(2,1)S(1)}, u32[]{:S(2)}, u32[]{:S(2)}) collective-permute-start(bf16[20,64,128]{2,1,0:T(8,128)(2,1)S(1)} %slice.153), channel_id=1, source_target_pairs={{0,2},{1,3},{2,4},{3,5},{4,6},{5,7},{6,0},{7,1},{8,10},{9,11},{10,... | collective-permute-start | bytes 983048 | tf_op jit(solution)/shard_map/ppermute | solution.py:54
  73.8 14.0 %copy-start.30 = (f32[40]{0:T(128)}, f32[40]{0:T(128)S(1)}, u32[]{:S(2)}) copy-start(f32[40]{0:T(128)S(1)} %get-tuple-element.45) | copy-start | bytes 484
  73.8 14.0 %copy-start.31 = (f32[40]{0:T(128)}, f32[40]{0:T(128)S(1)}, u32[]{:S(2)}) copy-start(f32[40]{0:T(128)S(1)} %get-tuple-element.54) | copy-start | bytes 484
  74.3 13.5 %copy-start.32 = (f32[40]{0:T(128)}, f32[40]{0:T(128)S(1)}, u32[]{:S(2)}) copy-start(f32[40]{0:T(128)S(1)} %get-tuple-element.43) | copy-start | bytes 484
  74.3 13.5 %copy-start.33 = (f32[40]{0:T(128)}, f32[40]{0:T(128)S(1)}, u32[]{:S(2)}) copy-start(f32[40]{0:T(128)S(1)} %get-tuple-element.52) | copy-start | bytes 484
  77.8 4.4 %copy-start.15 = (bf16[20,64,128]{2,1,0:T(8,128)(2,1)}, bf16[20,64,128]{2,1,0:T(8,128)(2,1)S(1)}, u32[]{:S(2)}) copy-start(bf16[20,64,128]{2,1,0:T(8,128)(2,1)S(1)} %collective-permute-done.4) | copy-start | bytes 983044
  82.2 3.1 %copy-start.16 = (bf16[20,64,128]{2,1,0:T(8,128)(2,1)}, bf16[20,64,128]{2,1,0:T(8,128)(2,1)S(1)}, u32[]{:S(2)}) copy-start(bf16[20,64,128]{2,1,0:T(8,128)(2,1)S(1)} %collective-permute-done.5) | copy-start | bytes 983044
  85.3 14.5 %collective-permute-start.7 = (bf16[40,64,128]{2,1,0:T(8,128)(2,1)}, bf16[40,64,128]{2,1,0:T(8,128)(2,1)}, u32[]{:S(2)}, u32[]{:S(2)}) collective-permute-start(bf16[40,64,128]{2,1,0:T(8,128)(2,1)} %fusion.42), channel_id=1, source_target_pairs={{0,24},{1,25},{2,26},{3,27},{4,28},{5,29},{6,30},{7,31},{8,0},{9,1... | collective-permute-start | bytes 1966088 | tf_op jit(solution)/shard_map/ppermute | solution.py:52
  87.8 16.5 %collective-permute-start.6 = (bf16[40,64,128]{2,1,0:T(8,128)(2,1)}, bf16[40,64,128]{2,1,0:T(8,128)(2,1)}, u32[]{:S(2)}, u32[]{:S(2)}) collective-permute-start(bf16[40,64,128]{2,1,0:T(8,128)(2,1)} %fusion.42), channel_id=1, source_target_pairs={{0,8},{1,9},{2,10},{3,11},{4,12},{5,13},{6,14},{7,15},{8,16},{9,17... | collective-permute-start | bytes 1966088 | tf_op jit(solution)/shard_map/ppermute | solution.py:51
  100.8 7.5 %collective-permute-start.8 = (bf16[20,64,128]{2,1,0:T(8,128)(2,1)S(1)}, bf16[20,64,128]{2,1,0:T(8,128)(2,1)S(1)}, u32[]{:S(2)}, u32[]{:S(2)}) collective-permute-start(bf16[20,64,128]{2,1,0:T(8,128)(2,1)S(1)} %slice.154), channel_id=1, source_target_pairs={{0,24},{1,25},{2,26},{3,27},{4,28},{5,29},{6,30},{7,31},{8,0},{9,1... | collective-permute-start | bytes 983048 | tf_op jit(solution)/shard_map/ppermute | solution.py:53
  105.3 7.3 %collective-permute-start.9 = (bf16[20,64,128]{2,1,0:T(8,128)(2,1)S(1)}, bf16[20,64,128]{2,1,0:T(8,128)(2,1)S(1)}, u32[]{:S(2)}, u32[]{:S(2)}) collective-permute-start(bf16[20,64,128]{2,1,0:T(8,128)(2,1)S(1)} %slice.155), channel_id=1, source_target_pairs={{0,8},{1,9},{2,10},{3,11},{4,12},{5,13},{6,14},{7,15},{8,16},{9,17... | collective-permute-start | bytes 983048 | tf_op jit(solution)/shard_map/ppermute | solution.py:54
  112.6 9.0 %copy-start.11 = (bf16[128,5120]{0,1:T(8,128)(2,1)S(1)}, bf16[128,5120]{0,1:T(8,128)(2,1)}, u32[]{:S(2)}) copy-start(bf16[128,5120]{0,1:T(8,128)(2,1)} %copy.39) | copy-start | bytes 3932164
  112.6 9.0 %copy-start.26 = (f32[80,128]{1,0:T(8,128)S(1)}, f32[80,128]{1,0:T(8,128)}, u32[]{:S(2)}) copy-start(f32[80,128]{1,0:T(8,128)} %get-tuple-element.28) | copy-start | bytes 122884
  117.0 12.4 %collective-permute-start.10 = (f32[40,64,128]{2,1,0:T(8,128)S(1)}, f32[40,64,128]{2,1,0:T(8,128)S(1)}, u32[]{:S(2)}, u32[]{:S(2)}) collective-permute-start(f32[40,64,128]{2,1,0:T(8,128)S(1)} %get-tuple-element.13), channel_id=1, source_target_pairs={{0,1},{1,0},{2,3},{3,2},{4,5},{5,4},{6,7},{7,6},{8,9},{9,8},{10,11... | collective-permute-start | bytes 3932168 | tf_op jit(solution)/shard_map/ppermute | solution.py:114
  121.6 2.0 copy-start.13
  121.6 2.0 copy-start.25
  123.6 4.1 %copy-start.6 = (f32[80,64,128]{2,1,0:T(8,128)S(1)}, f32[80,64,128]{2,1,0:T(8,128)}, u32[]{:S(2)}) copy-start(f32[80,64,128]{2,1,0:T(8,128)} %copy-done.5) | copy-start | bytes 7864324
  123.7 4.1 %copy-start.29 = (f32[40]{0:T(128)S(1)}, f32[40]{0:T(128)}, u32[]{:S(2)}) copy-start(f32[40]{0:T(128)} %get-tuple-element.37) | copy-start | bytes 484
  129.4 1.0 copy-start.7
  129.4 1.6 copy-start.19
  129.4 1.6 copy-start.9
  133.1 3.3 %copy-start.35 = (f32[80]{0:T(128)S(1)}, f32[80]{0:T(128)}, u32[]{:S(2)}) copy-start(f32[80]{0:T(128)} %copy-done.34) | copy-start | bytes 964
  133.1 3.3 %copy-start.36 = (f32[80]{0:T(128)S(1)}, f32[80]{0:T(128)}, u32[]{:S(2)}) copy-start(f32[80]{0:T(128)} %get-tuple-element.58) | copy-start | bytes 964
  136.4 4.4 %copy-start.4 = (f32[80,64,128]{2,1,0:T(8,128)S(1)}, f32[80,64,128]{2,1,0:T(8,128)}, u32[]{:S(2)}) copy-start(f32[80,64,128]{2,1,0:T(8,128)} %copy-done.3) | copy-start | bytes 7864324
  136.4 4.4 %copy-start.8 = (f32[40,64,128]{2,1,0:T(8,128)S(1)}, f32[40,64,128]{2,1,0:T(8,128)}, u32[]{:S(2)}) copy-start(f32[40,64,128]{2,1,0:T(8,128)} %copy-done.7) | copy-start | bytes 3932164
  136.4 4.8 %copy-start.10 = (f32[40,64,128]{2,1,0:T(8,128)S(1)}, f32[40,64,128]{2,1,0:T(8,128)}, u32[]{:S(2)}) copy-start(f32[40,64,128]{2,1,0:T(8,128)} %copy-done.9) | copy-start | bytes 3932164
  136.4 5.6 %copy-start.14 = (f32[80,64,128]{2,1,0:T(8,128)S(1)}, f32[80,64,128]{2,1,0:T(8,128)}, u32[]{:S(2)}) copy-start(f32[80,64,128]{2,1,0:T(8,128)} %fusion.8) | copy-start | bytes 7864324
  147.9 7.6 %copy-start.21 = (f32[5120]{0:T(1024)S(1)}, f32[5120]{0:T(1024)}, u32[]{:S(2)}) copy-start(f32[5120]{0:T(1024)} %param.21) | copy-start | bytes 61444
  153.1 2.3 %copy-start = (f32[256,5120]{1,0:T(8,128)}, f32[256,5120]{1,0:T(8,128)S(1)}, u32[]{:S(2)}) copy-start(f32[256,5120]{1,0:T(8,128)S(1)} %get-tuple-element.12) | copy-start | bytes 15728644
  158.8 50.8 %copy-start.27 = (f32[8,256]{1,0:T(8,128)}, f32[8,256]{1,0:T(8,128)S(1)}, u32[]{:S(2)}) copy-start(f32[8,256]{1,0:T(8,128)S(1)} %get-tuple-element.59) | copy-start | bytes 24580
  175.7 32.1 %all-to-all-start.2 = ((bf16[32,8,16,256]{3,2,1,0:T(8,128)(2,1)}), bf16[32,8,16,256]{3,2,1,0:T(8,128)(2,1)S(1)}, u32[]{:S(2)}, u32[]{:S(2)}) async-start(bf16[32,8,16,256]{3,2,1,0:T(8,128)(2,1)} %broadcast_in_dim.150), calls=%async_computation.2 | async-start | bytes 4194304 | tf_op jit(solution)/shard_map/all_to_all | solution.py:125
Sparse Core Ops, SparseCore 0:
  88.0 41.5 all-gather.1
